TPU v7x, 32 devices: a whole 2x2x4 slice. The times are simulated.
32 devices in a mesh: cells: 32 (over z, y, x, core).
Axes of the slice: x: 2, y: 2, z: 4, core: 2. Of those that a mesh axis runs over, the one named last changes fastest.
Arguments:
- concentration: float32 [9, 256, 4096], P(None, None, 'cells'), may hold values from 0.05 to 4
- flux_weight: float32 [8, 9, 4096], P(None, None, 'cells'), may hold values from 0.01 to 0.08
- vertical_mixing: float32 [8, 4096], P(None, 'cells'), may hold values from 0.02 to 0.15
- deposition: float32 [9, 4096], P(None, 'cells'), may hold values from 0.02 to 0.3
- halo_index: int32 [8, 4096], P(None, 'cells'), may hold values from 0 to 639, as said below
- send_cells: int32 [32, 32, 16], P('cells'), may hold values from 0 to 127, as said below
- live_count: int32 [32], P('cells'), may hold values from 32 to 128, as said below
Outputs:
- advanced: float32 [9, 256, 4096], P(None, None, 'cells')
Inputs may be any that keep to these rules, and one draw needn't show every extreme that they name: Device d's live cells are its slots 0 to live_count[d] - 1; some device is full in every draw. send_cells[d, p, h] is a live slot of device d. `halo_index`: every entry of a live cell of device d is a live slot of d below 128, or 128 + p * 16 + h for a sender p equal to d - 2, d - 1, d + 1 or d + 2 within the axis, or to (d + 16) mod 32.
All inputs are finite; a program needn't handle non-finite values.
Results may differ from a plain program's by a relative error of at most 0.00002.
Values sent between devices are 32-bit elements; how exact they have to be, the bound alone decides.
No kernel may reach another device: no remote copies, remote signals or barrier semaphores. Data moves between devices by JAX's collectives and lax.ppermute only.
A program may use at most 128 MiB of HBM per device.

v0:
```python
import jax
import jax.numpy as jnp
from jax import lax
from jax.sharding import PartitionSpec as P

STEPS = 2


def advance(values, extended, lookup, flux_weight, vertical_mixing, deposition, occupied, length):
    levels, pulses = (values.shape[0], values.shape[1])
    summed = jnp.zeros_like(values)
    for neighbour in range(flux_weight.shape[0]):
        columns = lookup[neighbour]
        nearby = jnp.take(extended, columns, axis=1).reshape(levels, pulses, length)
        weight = flux_weight[neighbour]
        summed = summed + weight[:, None, :] * (nearby - values)
    upward = vertical_mixing[:, None, :] * (values[1:] - values[:-1])
    nothing = jnp.zeros_like(values[:1])
    vertical = jnp.concatenate([upward, nothing], axis=0) - jnp.concatenate(
        [nothing, upward], axis=0
    )
    living = jnp.arange(length, dtype=jnp.int32) < occupied
    return jnp.where(
        living[None, None, :], (values + summed + vertical) * (1.0 - deposition[:, None, :]), 0.0
    )


def per_device(
    concentration, flux_weight, vertical_mixing, deposition, halo_index, send_cells, live_count
):
    levels, pulses, capacity = concentration.shape
    sender_rows = send_cells[0]
    occupied = live_count[0]
    values = concentration
    for sweep in range(STEPS):
        flat_values = values.reshape(levels * pulses, capacity)
        outgoing = jnp.take(flat_values, sender_rows.reshape(-1), axis=1)
        incoming = lax.all_to_all(outgoing, "cells", split_axis=1, concat_axis=1, tiled=True)
        extended = jnp.concatenate([flat_values, incoming], axis=1)
        values = advance(
            values,
            extended,
            halo_index,
            flux_weight,
            vertical_mixing,
            deposition,
            occupied,
            capacity,
        )
    return values


def solution(mesh):
    in_specs = (
        P(None, None, "cells"),
        P(None, None, "cells"),
        P(None, "cells"),
        P(None, "cells"),
        P(None, "cells"),
        P("cells", None, None),
        P("cells"),
    )
    out_specs = P(None, None, "cells")
    return jax.shard_map(
        per_device, mesh=mesh, in_specs=in_specs, out_specs=out_specs, check_vma=False
    )
```

profile of v0, /device:TPU:25, one launch (start us, length us, event | category | flops | bytes accessed | tf_op | source)
XLA Modules:
  0.0 376.7 jit_solution(717401835810015343)
XLA Ops:
  0.9 1.6 copy.29
  2.6 4.0 %gather_fusion = f32[512,2304]{1,0:T(8,128)} fusion(f32[2304,128]{0,1:T(8,128)S(1)} %copy.29, s32[1024]{0:T(1024)S(1)} %pad_clamp_fusion.8), kind=kCustom, calls=%fused_computation.clone | custom fusion | bytes 9439232 | tf_op jit(solution)/shard_map/jit(_take)/gather | solution.py:37
  6.6 4.8 %broadcast_select_fusion.1 = f32[512,2304]{1,0:T(8,128)} fusion(f32[512,2304]{1,0:T(8,128)} %gather_fusion, pred[512]{0:T(512)(128)(4,1)S(1)} %compare_and_fusion.8), kind=kLoop, calls=%fused_computation.21 | loop fusion | flops 1179648 | bytes 9437696 | tf_op jit(solution)/shard_map/jit(_take)/select_n | solution.py:37
  11.4 6.2 %all-to-all-start = ((f32[2304,32,16]{0,2,1:T(8,128)}), f32[2304,32,16]{0,2,1:T(8,128)}, u32[]{:S(2)}, u32[]{:S(2)}) async-start(f32[2304,32,16]{0,2,1:T(8,128)} %bitcast.109), calls=%async_computation | async-start | bytes 9437184 | tf_op jit(solution)/shard_map/all_to_all | solution.py:38
  29.6 91.3 %all-to-all-done = f32[2304,32,16]{0,2,1:T(8,128)} async-done(((f32[2304,32,16]{0,2,1:T(8,128)}), f32[2304,32,16]{0,2,1:T(8,128)}, u32[]{:S(2)}, u32[]{:S(2)}) %all-to-all-start) | async-done | bytes 4718624 | tf_op jit(solution)/shard_map/all_to_all | solution.py:38
  120.9 5.2 %pad_maximum_fusion = f32[2304,640]{0,1:T(8,128)} fusion(f32[2304,512]{0,1:T(8,128)} %bitcast.6, f32[2304,128]{0,1:T(8,128)S(1)} %copy.29), kind=kLoop, calls=%fused_computation.18 | loop fusion | flops 1474560 | bytes 11796480 | tf_op jit(solution)/shard_map/concatenate | solution.py:39
  126.2 4.4 %gather_fusion.2 = f32[128,2304]{1,0:T(8,128)S(1)} fusion(f32[2304,640]{0,1:T(8,128)} %pad_maximum_fusion, s32[1024]{0:T(1024)} %pad_clamp_fusion.6), kind=kCustom, calls=%fused_computation.3.clone | custom fusion | bytes 2359808 | tf_op jit(solution)/shard_map/jit(_take)/gather | solution.py:14
  131.3 1.4 copy.32
  132.6 4.4 %gather_fusion.3 = f32[128,2304]{1,0:T(8,128)S(1)} fusion(f32[2304,640]{0,1:T(8,128)} %pad_maximum_fusion, s32[1024]{0:T(1024)} %pad_clamp_fusion.5), kind=kCustom, calls=%fused_computation.4.clone | custom fusion | bytes 2359808 | tf_op jit(solution)/shard_map/jit(_take)/gather | solution.py:14
  137.8 1.4 copy.34
  139.2 4.4 %gather_fusion.4 = f32[128,2304]{1,0:T(8,128)S(1)} fusion(f32[2304,640]{0,1:T(8,128)} %pad_maximum_fusion, s32[1024]{0:T(1024)} %pad_clamp_fusion.4), kind=kCustom, calls=%fused_computation.5.clone | custom fusion | bytes 2359808 | tf_op jit(solution)/shard_map/jit(_take)/gather | solution.py:14
  144.3 1.4 copy.36
  145.7 4.4 %gather_fusion.5 = f32[128,2304]{1,0:T(8,128)S(1)} fusion(f32[2304,640]{0,1:T(8,128)} %pad_maximum_fusion, s32[1024]{0:T(1024)} %pad_clamp_fusion.3), kind=kCustom, calls=%fused_computation.6.clone | custom fusion | bytes 2359808 | tf_op jit(solution)/shard_map/jit(_take)/gather | solution.py:14
  150.8 1.5 copy.38
  152.3 4.4 %gather_fusion.6 = f32[128,2304]{1,0:T(8,128)S(1)} fusion(f32[2304,640]{0,1:T(8,128)} %pad_maximum_fusion, s32[1024]{0:T(1024)} %pad_clamp_fusion.2), kind=kCustom, calls=%fused_computation.7.clone | custom fusion | bytes 2359808 | tf_op jit(solution)/shard_map/jit(_take)/gather | solution.py:14
  157.4 1.4 copy.40
  158.8 4.4 %gather_fusion.7 = f32[128,2304]{1,0:T(8,128)S(1)} fusion(f32[2304,640]{0,1:T(8,128)} %pad_maximum_fusion, s32[1024]{0:T(1024)} %pad_clamp_fusion.1), kind=kCustom, calls=%fused_computation.8.clone | custom fusion | bytes 2359808 | tf_op jit(solution)/shard_map/jit(_take)/gather | solution.py:14
  164.0 1.4 copy.42
  165.4 4.4 %gather_fusion.1 = f32[128,2304]{1,0:T(8,128)S(1)} fusion(f32[2304,640]{0,1:T(8,128)} %pad_maximum_fusion, s32[1024]{0:T(1024)} %pad_clamp_fusion.7), kind=kCustom, calls=%fused_computation.1.clone | custom fusion | bytes 2359808 | tf_op jit(solution)/shard_map/jit(_take)/gather | solution.py:14
  170.5 1.4 copy.30
  171.9 4.4 %gather_fusion.8 = f32[128,2304]{1,0:T(8,128)S(1)} fusion(f32[2304,640]{0,1:T(8,128)} %pad_maximum_fusion, s32[1024]{0:T(1024)} %pad_clamp_fusion), kind=kCustom, calls=%fused_computation.9.clone | custom fusion | bytes 2359808 | tf_op jit(solution)/shard_map/jit(_take)/gather | solution.py:14
  177.1 1.4 copy.44
  178.5 6.0 %multiply_select_fusion.1 = f32[9,256,128]{2,1,0:T(8,128)S(1)} fusion(f32[8,256,128]{2,1,0:T(8,128)} %subtract_multiply_fusion, f32[9,256,128]{2,1,0:T(8,128)S(1)} %copy-done, f32[9,256,128]{2,1,0:T(8,128)} %bitcast.127, f32[9,256,128]{2,1,0:T(8,128)} %bitcast.125, f32[9,256,128]{2,1,0:T(8,128)} %bitcast.122, f32[9,256,128]{2,1,0:T(8,128)} %bitcast.121, ...), kind=kLoop, calls=%fused_computation.39 | loop fusion | flops 8257536 | bytes 12886656 | tf_op jit(solution)/shard_map/jit(_where)/select_n | solution.py:23
  185.2 4.0 %gather_fusion.9 = f32[512,2304]{1,0:T(8,128)} fusion(f32[2304,128]{0,1:T(8,128)S(1)} %copy.46, s32[1024]{0:T(1024)S(1)} %copy-done.7), kind=kCustom, calls=%fused_computation.2.clone | custom fusion | bytes 9439232 | tf_op jit(solution)/shard_map/jit(_take)/gather | solution.py:37
  189.2 4.8 %broadcast_select_fusion = f32[512,2304]{1,0:T(8,128)} fusion(f32[512,2304]{1,0:T(8,128)} %gather_fusion.9, pred[512]{0:T(512)(128)(4,1)S(1)} %copy-done.10), kind=kLoop, calls=%fused_computation.20 | loop fusion | flops 1179648 | bytes 9437696 | tf_op jit(solution)/shard_map/jit(_take)/select_n | solution.py:37
  194.0 6.0 %all-to-all-start.1 = ((f32[2304,32,16]{0,2,1:T(8,128)}), f32[2304,32,16]{0,2,1:T(8,128)}, u32[]{:S(2)}, u32[]{:S(2)}) async-start(f32[2304,32,16]{0,2,1:T(8,128)} %bitcast.110), calls=%async_computation.1 | async-start | bytes 9437184 | tf_op jit(solution)/shard_map/all_to_all | solution.py:38
  201.1 102.1 %all-to-all-done.1 = f32[2304,32,16]{0,2,1:T(8,128)} async-done(((f32[2304,32,16]{0,2,1:T(8,128)}), f32[2304,32,16]{0,2,1:T(8,128)}, u32[]{:S(2)}, u32[]{:S(2)}) %all-to-all-start.1) | async-done | bytes 4718624 | tf_op jit(solution)/shard_map/all_to_all | solution.py:38
  303.2 5.2 %pad_maximum_fusion.1 = f32[2304,640]{0,1:T(8,128)} fusion(f32[2304,512]{0,1:T(8,128)} %bitcast.40, f32[2304,128]{0,1:T(8,128)S(1)} %copy.46), kind=kLoop, calls=%fused_computation.19 | loop fusion | flops 1474560 | bytes 11796480 | tf_op jit(solution)/shard_map/concatenate | solution.py:39
  308.5 5.4 %gather_fusion.10 = f32[128,2304]{1,0:T(8,128)} fusion(f32[2304,640]{0,1:T(8,128)} %pad_maximum_fusion.1, s32[1024]{0:T(1024)} %pad_clamp_fusion.7), kind=kCustom, calls=%fused_computation.10.clone | custom fusion | bytes 2359808 | tf_op jit(solution)/shard_map/jit(_take)/gather | solution.py:14
  313.9 5.3 %gather_fusion.11 = f32[128,2304]{1,0:T(8,128)} fusion(f32[2304,640]{0,1:T(8,128)} %pad_maximum_fusion.1, s32[1024]{0:T(1024)} %pad_clamp_fusion.6), kind=kCustom, calls=%fused_computation.11.clone | custom fusion | bytes 2359808 | tf_op jit(solution)/shard_map/jit(_take)/gather | solution.py:14
  319.2 5.3 %gather_fusion.12 = f32[128,2304]{1,0:T(8,128)} fusion(f32[2304,640]{0,1:T(8,128)} %pad_maximum_fusion.1, s32[1024]{0:T(1024)} %pad_clamp_fusion.5), kind=kCustom, calls=%fused_computation.12.clone | custom fusion | bytes 2359808 | tf_op jit(solution)/shard_map/jit(_take)/gather | solution.py:14
  324.5 5.3 %gather_fusion.13 = f32[128,2304]{1,0:T(8,128)} fusion(f32[2304,640]{0,1:T(8,128)} %pad_maximum_fusion.1, s32[1024]{0:T(1024)} %pad_clamp_fusion.4), kind=kCustom, calls=%fused_computation.13.clone | custom fusion | bytes 2359808 | tf_op jit(solution)/shard_map/jit(_take)/gather | solution.py:14
  329.8 5.3 %gather_fusion.14 = f32[128,2304]{1,0:T(8,128)} fusion(f32[2304,640]{0,1:T(8,128)} %pad_maximum_fusion.1, s32[1024]{0:T(1024)} %pad_clamp_fusion.3), kind=kCustom, calls=%fused_computation.14.clone | custom fusion | bytes 2359808 | tf_op jit(solution)/shard_map/jit(_take)/gather | solution.py:14
  335.2 5.4 %gather_fusion.15 = f32[128,2304]{1,0:T(8,128)} fusion(f32[2304,640]{0,1:T(8,128)} %pad_maximum_fusion.1, s32[1024]{0:T(1024)} %pad_clamp_fusion.2), kind=kCustom, calls=%fused_computation.15.clone | custom fusion | bytes 2359808 | tf_op jit(solution)/shard_map/jit(_take)/gather | solution.py:14
  340.6 5.3 %gather_fusion.16 = f32[128,2304]{1,0:T(8,128)} fusion(f32[2304,640]{0,1:T(8,128)} %pad_maximum_fusion.1, s32[1024]{0:T(1024)} %pad_clamp_fusion.1), kind=kCustom, calls=%fused_computation.16.clone | custom fusion | bytes 2359808 | tf_op jit(solution)/shard_map/jit(_take)/gather | solution.py:14
  345.9 5.3 %gather_fusion.17 = f32[128,2304]{1,0:T(8,128)} fusion(f32[2304,640]{0,1:T(8,128)} %pad_maximum_fusion.1, s32[1024]{0:T(1024)} %pad_clamp_fusion), kind=kCustom, calls=%fused_computation.17.clone | custom fusion | bytes 2359808 | tf_op jit(solution)/shard_map/jit(_take)/gather | solution.py:14
  351.2 1.9 select_bitcast_fusion.6
  353.1 1.4 copy.47
  354.5 1.4 copy.48
  355.9 1.9 select_bitcast_fusion.4
  357.8 1.4 copy.49
  360.6 1.9 select_bitcast_fusion.2
  362.4 1.4 copy.51
  363.9 1.4 copy.52
  365.3 1.9 select_bitcast_fusion
  367.1 1.4 copy.53
  368.5 1.4 copy.54
  369.9 6.8 %multiply_select_fusion = f32[9,256,128]{2,1,0:T(8,128)} fusion(f32[8,256,128]{2,1,0:T(8,128)} %fusion, f32[9,256,128]{2,1,0:T(8,128)S(1)} %multiply_select_fusion.1, f32[9,256,128]{2,1,0:T(8,128)} %bitcast.124, f32[9,256,128]{2,1,0:T(8,128)} %bitcast.123, f32[9,256,128]{2,1,0:T(8,128)} %bitcast.120, f32[9,256,128]{2,1,0:T(8,128)} %bitcast.118, ...), kind=kLoop, calls=%fused_computation.38 | loop fusion | flops 8257536 | bytes 12886656 | tf_op jit(solution)/shard_map/jit(_where)/select_n | solution.py:23
  (61 shorter events, 21.3 us)
Async XLA Ops:
  0.9 5.7 %copy-start.9 = (pred[512]{0:T(512)(128)(4,1)}, pred[512]{0:T(512)(128)(4,1)S(1)}, u32[]{:S(2)}) copy-start(pred[512]{0:T(512)(128)(4,1)S(1)} %compare_and_fusion.8) | copy-start | bytes 1540
  0.9 1.7 copy-start.6
  11.4 6.3 %copy-start.3 = (f32[8,9,128]{2,0,1:T(8,128)S(1)}, f32[8,9,128]{2,0,1:T(8,128)}, u32[]{:S(2)}) copy-start(f32[8,9,128]{2,0,1:T(8,128)} %param.12) | copy-start | bytes 110596
  11.4 11.1 %copy-start.11 = (s32[8,128]{1,0:T(8,128)S(1)}, s32[8,128]{1,0:T(8,128)}, u32[]{:S(2)}) copy-start(s32[8,128]{1,0:T(8,128)} %param.15) | copy-start | bytes 12292
  11.4 16.5 %copy-start.8 = (f32[9,128]{1,0:T(8,128)S(1)}, f32[9,128]{1,0:T(8,128)}, u32[]{:S(2)}) copy-start(f32[9,128]{1,0:T(8,128)} %param.14) | copy-start | bytes 13828
  11.4 17.1 %copy-start = (f32[9,256,128]{2,1,0:T(8,128)S(1)}, f32[9,256,128]{2,1,0:T(8,128)}, u32[]{:S(2)}) copy-start(f32[9,256,128]{2,1,0:T(8,128)} %param.11) | copy-start | bytes 3538948
  11.4 17.1 %copy-start.4 = (f32[8,128]{1,0:T(8,128)S(1)}, f32[8,128]{1,0:T(8,128)}, u32[]{:S(2)}) copy-start(f32[8,128]{1,0:T(8,128)} %param.13) | copy-start | bytes 12292
  11.4 109.5 %all-to-all-start = ((f32[2304,32,16]{0,2,1:T(8,128)}), f32[2304,32,16]{0,2,1:T(8,128)}, u32[]{:S(2)}, u32[]{:S(2)}) async-start(f32[2304,32,16]{0,2,1:T(8,128)} %bitcast.109), calls=%async_computation | async-start | bytes 9437184 | tf_op jit(solution)/shard_map/all_to_all | solution.py:38
  177.1 1.4 copy-start.2
  184.5 0.7 copy-start.7
  185.2 4.0 %copy-start.10 = (pred[512]{0:T(512)(128)(4,1)S(1)}, pred[512]{0:T(512)(128)(4,1)}, u32[]{:S(2)}) copy-start(pred[512]{0:T(512)(128)(4,1)} %copy-done.9) | copy-start | bytes 1540
  194.0 6.0 %copy-start.5 = (f32[8,128]{1,0:T(8,128)S(1)}, f32[8,128]{1,0:T(8,128)}, u32[]{:S(2)}) copy-start(f32[8,128]{1,0:T(8,128)} %param.13) | copy-start | bytes 12292
  194.0 109.2 %all-to-all-start.1 = ((f32[2304,32,16]{0,2,1:T(8,128)}), f32[2304,32,16]{0,2,1:T(8,128)}, u32[]{:S(2)}, u32[]{:S(2)}) async-start(f32[2304,32,16]{0,2,1:T(8,128)} %bitcast.110), calls=%async_computation.1 | async-start | bytes 9437184 | tf_op jit(solution)/shard_map/all_to_all | solution.py:38
  368.5 1.4 copy-start.1
where the time goes:
time: 381 us; the launch traced here: 377 us
  waiting for transfers between devices  193 us (51%)
  local copies, waits for them, and re-layouts  115 us (30%)
  other arithmetic  55.2 us (14%)
  starting transfers between devices  12.2 us (3%)
    all_to_all x2, waiting for transfers between devices, per_device(): lax.all_to_all(outgoing, 'cells', split_axis=1, concat_axis=1, tiled=True)  193 us
    gather x16, local copies, waits for them, and re-layouts, advance(): nearby = jnp.take(extended, columns, axis=1).reshape(levels, pulses, length)  77.6 us
    select_n x16, local copies, waits for them, and re-layouts, advance(): nearby = jnp.take(extended, columns, axis=1).reshape(levels, pulses, length)  22.6 us
    select_n x12, other arithmetic, advance(): nearby = jnp.take(extended, columns, axis=1).reshape(levels, pulses, length)  13.5 us
    select_n x2, other arithmetic, advance(): jnp.where(living[None, None, :], (values + summed + vertical) * (1.0 - de...  12.8 us
    all_to_all x2, starting transfers between devices, per_device(): lax.all_to_all(outgoing, 'cells', split_axis=1, concat_axis=1, tiled=True)  12.2 us
    concatenate x2, other arithmetic, per_device(): extended = jnp.concatenate([flat_values, incoming], axis=1)  10.5 us
    select_n x3, other arithmetic, per_device(): outgoing = jnp.take(flat_values, sender_rows.reshape(-1), axis=1)  9.7 us
  transfers between devices with their start and end apart: 2, of which 2 were waited for; matrix products, arithmetic and copies ran while one was open for 3% of the time, Pallas kernels for 0%

commit v1 on v0

v1 whole, which is shorter than its diff:
```python
import jax
import jax.numpy as jnp
from jax import lax
from jax.sharding import PartitionSpec as P

STEPS = 2
HIGHEST = lax.Precision.HIGHEST


def peer_shifts(n):
    return (1, -1, 2, -2, n // 2)


def permutation(n, shift):
    if shift == n // 2:
        return [(p, (p + shift) % n) for p in range(n)]
    return [(p, p + shift) for p in range(n) if 0 <= p + shift < n]


def per_device(
    n, concentration, flux_weight, vertical_mixing, deposition, halo_index, send_cells, live_count
):
    levels, pulses, capacity = concentration.shape
    hslot = send_cells.shape[2]
    shifts = peer_shifts(n)
    groups = len(shifts)
    me = lax.axis_index("cells")
    f32 = jnp.float32

    peers = (me + jnp.array(shifts, dtype=jnp.int32)) % n
    picked = send_cells[0][peers].reshape(groups * hslot)
    select = (picked[:, None] == jnp.arange(capacity, dtype=jnp.int32)[None, :]).astype(f32)

    beyond = halo_index - capacity
    sender = beyond // hslot
    place = beyond % hslot
    shift = (me - sender) % n
    group = jnp.full(halo_index.shape, -1, dtype=jnp.int32)
    for g, s in enumerate(shifts):
        group = jnp.where(shift == s % n, g, group)
    local_col = jnp.where(beyond < 0, halo_index, -1)
    remote_col = jnp.where((beyond >= 0) & (group >= 0), group * hslot + place, -1)
    onehot_local = (local_col[:, None, :] == jnp.arange(capacity)[None, :, None]).astype(f32)
    onehot_remote = (
        remote_col[:, None, :] == jnp.arange(groups * hslot)[None, :, None]
    ).astype(f32)
    local_matrix = sum(
        flux_weight[k][:, None, :] * onehot_local[k][None] for k in range(flux_weight.shape[0])
    )
    remote_matrix = sum(
        flux_weight[k][:, None, :] * onehot_remote[k][None] for k in range(flux_weight.shape[0])
    )
    weight_sum = jnp.sum(flux_weight, axis=0)

    living = jnp.arange(capacity, dtype=jnp.int32) < live_count[0]
    keep = 1.0 - deposition

    values = concentration
    for sweep in range(STEPS):
        outgoing = jnp.einsum("sc,lqc->slq", select, values, precision=HIGHEST)
        outgoing = outgoing.reshape(groups, hslot, levels * pulses)
        incoming = jnp.stack(
            [
                lax.ppermute(outgoing[g], "cells", perm=permutation(n, s))
                for g, s in enumerate(shifts)
            ]
        ).reshape(groups * hslot, levels, pulses)
        near = jnp.einsum("lqs,lsc->lqc", values, local_matrix, precision=HIGHEST)
        far = jnp.einsum("slq,lsc->lqc", incoming, remote_matrix, precision=HIGHEST)
        summed = near + far - weight_sum[:, None, :] * values
        upward = vertical_mixing[:, None, :] * (values[1:] - values[:-1])
        nothing = jnp.zeros_like(values[:1])
        vertical = jnp.concatenate([upward, nothing], axis=0) - jnp.concatenate(
            [nothing, upward], axis=0
        )
        values = jnp.where(
            living[None, None, :], (values + summed + vertical) * keep[:, None, :], 0.0
        )
    return values


def solution(mesh):
    n = mesh.shape["cells"]
    in_specs = (
        P(None, None, "cells"),
        P(None, None, "cells"),
        P(None, "cells"),
        P(None, "cells"),
        P(None, "cells"),
        P("cells", None, None),
        P("cells"),
    )
    out_specs = P(None, None, "cells")

    def body(*args):
        return per_device(n, *args)

    return jax.shard_map(body, mesh=mesh, in_specs=in_specs, out_specs=out_specs, check_vma=False)
```

time: 381 us -> 77.2 us (0.20)
  the two profiles are of different devices: /device:TPU:25 before, /device:TPU:0 now
where the time goes in v1:
time: 77.2 us; the launch traced here: 76.5 us
  starting transfers between devices  34.4 us (45%)
  local copies, waits for them, and re-layouts  15.4 us (20%)
  matrix products  13.9 us (18%)
  other arithmetic  5.69 us (7%)
  waiting for transfers between devices  5.67 us (7%)
  between operations  1.46 us (2%)
    ppermute x10, starting transfers between devices, per_device(): lax.ppermute(outgoing[g], 'cells', perm=permutation(n, s))  34.4 us
    dot_general x2, matrix products, per_device(): far = jnp.einsum('slq,lsc->lqc', incoming, remote_matrix, precision=HIGHEST)  8.31 us
    ppermute x10, waiting for transfers between devices, per_device(): lax.ppermute(outgoing[g], 'cells', perm=permutation(n, s))  5.67 us
    unnamed x84, local copies, waits for them, and re-layouts  5.64 us
    squeeze x10, local copies, waits for them, and re-layouts, per_device(): outgoing[g]  3.41 us
    dot_general x2, matrix products, per_device(): near = jnp.einsum('lqs,lsc->lqc', values, local_matrix, precision=HIGHEST)  2.96 us
    dot_general x2, matrix products, per_device(): outgoing = jnp.einsum('sc,lqc->slq', select, values, precision=HIGHEST)  2.67 us
    reshape x2, local copies, waits for them, and re-layouts, per_device(): incoming = jnp.stack([lax.ppermute(outgoing[g], 'cells', perm=permutation...  2.51 us
  transfers between devices with their start and end apart: 10, of which 1 were waited for; matrix products, arithmetic and copies ran while one was open for 18% of the time, Pallas kernels for 0%

profile of v1, /device:TPU:0, one launch (start us, length us, event | category | flops | bytes accessed | tf_op | source)
XLA Modules:
  0.0 76.5 jit_solution(10268253749757132217)
XLA Ops:
  0.0 0.7 compare_select_fusion.1
  0.7 0.8 %copy.30 = s32[1,32,16]{2,1,0:T(8,128)S(1)} copy(s32[1,32,16]{1,2,0:T(8,128)} %param.13) | data formatting | bytes 4096 | tf_op args[5]
  1.4 0.6 gather_fusion
  2.0 0.1 eq.72
  2.1 0.5 copy-done.33
  2.6 2.1 %fusion.84 = f32[80,9,256]{2,0,1:T(8,128)S(1)} fusion(f32[9,256,128]{2,1,0:T(8,128)} %param.8, s32[80]{0:T(128)S(1)} %eq.72), kind=kOutput, calls=%fused_computation.130 | convolution fusion | flops 283125760 | bytes 1917248 | tf_op jit(solution)/shard_map/sc,lqc->slq/dot_general | solution.py:60
  4.7 0.0 copy-start
  4.7 0.1 slice_bitcast_fusion.5
  4.7 0.7 copy.67
  5.4 3.0 %collective-permute-start = (f32[16,2304]{1,0:T(8,128)}, f32[16,2304]{1,0:T(8,128)}, u32[]{:S(2)}, u32[]{:S(2)}) collective-permute-start(f32[16,2304]{1,0:T(8,128)} %bitcast.39), channel_id=1, source_target_pairs={{0,1},{1,2},{2,3},{3,4},{4,5},{5,6},{6,7},{7,8},{8,9},{9,10},{10,1... | collective-permute-start | bytes 442376 | tf_op jit(solution)/shard_map/ppermute | solution.py:64
  8.4 0.7 copy.68
  9.1 1.3 %collective-permute-start.1 = (f32[16,2304]{1,0:T(8,128)}, f32[16,2304]{1,0:T(8,128)}, u32[]{:S(2)}, u32[]{:S(2)}) collective-permute-start(f32[16,2304]{1,0:T(8,128)} %bitcast.41), channel_id=1, source_target_pairs={{1,0},{2,1},{3,2},{4,3},{5,4},{6,5},{7,6},{8,7},{9,8},{10,9},{11,1... | collective-permute-start | bytes 442376 | tf_op jit(solution)/shard_map/ppermute | solution.py:64
  10.4 0.7 copy.69
  11.0 6.8 %collective-permute-start.2 = (f32[16,2304]{1,0:T(8,128)}, f32[16,2304]{1,0:T(8,128)}, u32[]{:S(2)}, u32[]{:S(2)}) collective-permute-start(f32[16,2304]{1,0:T(8,128)} %bitcast.43), channel_id=1, source_target_pairs={{0,2},{1,3},{2,4},{3,5},{4,6},{5,7},{6,8},{7,9},{8,10},{9,11},{10,... | collective-permute-start | bytes 442376 | tf_op jit(solution)/shard_map/ppermute | solution.py:64
  17.8 0.7 copy.70
  18.5 1.3 %collective-permute-start.3 = (f32[16,2304]{1,0:T(8,128)}, f32[16,2304]{1,0:T(8,128)}, u32[]{:S(2)}, u32[]{:S(2)}) collective-permute-start(f32[16,2304]{1,0:T(8,128)} %bitcast.45), channel_id=1, source_target_pairs={{2,0},{3,1},{4,2},{5,3},{6,4},{7,5},{8,6},{9,7},{10,8},{11,9},{12,... | collective-permute-start | bytes 442376 | tf_op jit(solution)/shard_map/ppermute | solution.py:64
  19.8 0.7 copy.71
  20.4 6.7 %collective-permute-start.4 = (f32[16,2304]{1,0:T(8,128)}, f32[16,2304]{1,0:T(8,128)}, u32[]{:S(2)}, u32[]{:S(2)}) collective-permute-start(f32[16,2304]{1,0:T(8,128)} %bitcast.47), channel_id=1, source_target_pairs={{0,16},{1,17},{2,18},{3,19},{4,20},{5,21},{6,22},{7,23},{8,24},{9,... | collective-permute-start | bytes 442376 | tf_op jit(solution)/shard_map/ppermute | solution.py:64
  27.1 0.4 copy.39
  27.6 0.0 copy-start.30
  27.6 0.8 %slice_bitcast_fusion.25 = (f32[80,128]{1,0:T(8,128)}, f32[80,128]{1,0:T(8,128)}, f32[80,128]{1,0:T(8,128)}, f32[80,128]{1,0:T(8,128)}, f32[80,128]{1,0:T(8,128)...) fusion(f32[8,80,128]{2,1,0:T(8,128)S(1)} %fusion.16), kind=kLoop, calls=%fused_computation.126 | loop fusion | bytes 655360 | tf_op jit(solution)/shard_map/mul | solution.py:51
  28.7 1.2 %fusion.11 = f32[8,256,128]{1,2,0:T(8,128)} fusion(f32[9,256,128]{1,2,0:T(8,128)S(1)} %copy.39, f32[8,128]{1,0:T(8,128)S(1)} %copy-done.30), kind=kLoop, calls=%fused_computation.17 | loop fusion | flops 524288 | bytes 3149824 | tf_op jit(solution)/shard_map/mul | solution.py:71
  30.0 0.0 copy-start.32
  30.0 1.5 %convolution_bitcast_fusion = f32[9,256,128]{1,2,0:T(8,128)S(1)} fusion(f32[9,256,128]{2,1,0:T(8,128)S(1)} %copy-done, f32[128,128]{1,0:T(8,128)S(1)} %get-tuple-element.16, f32[9,128]{1,0:T(8,128)S(1)} %get-tuple-element.41, f32[128,128]{1,0:T(8,128)S(1)} %get-tuple-element.17, f32[9,128]{1,0:T(8,128)S(1)} %get-tuple-element.42, ...), kind=kOutput, calls=%fused_computation.1 | convolution fusion | flops 455196672 | bytes 2920448 | tf_op jit(solution)/shard_map/lqs,lsc->lqc/dot_general | solution.py:68
  31.5 0.6 broadcast_subtract_fusion
  32.7 1.4 %reduce_sum.9 = f32[9,128]{1,0:T(8,128)} reduce(f32[8,9,128]{2,0,1:T(8,128)} %param.9, f32[]{:T(128)} %constant.77.clone.1), dimensions={0}, to_apply=%region_0.1 | reduce | flops 8064 | bytes 41476 | tf_op jit(solution)/shard_map/reduce_sum | solution.py:53
  34.1 0.6 iota_compare_fusion.3
  34.7 0.9 %bitcast_dynamic-update-slice_fusion.9 = f32[5,16,2304]{2,1,0:T(8,128)S(1)} fusion(f32[16,2304]{1,0:T(8,128)} %collective-permute-done), kind=kLoop, calls=%fused_computation.110 | loop fusion | bytes 294912
  35.6 0.9 %bitcast_dynamic-update-slice_fusion.8 = f32[5,16,2304]{2,1,0:T(8,128)S(1)} fusion(f32[5,16,2304]{2,1,0:T(8,128)S(1)} %bitcast_dynamic-update-slice_fusion.9, f32[16,2304]{1,0:T(8,128)} %collective-permute-done.1), kind=kLoop, calls=%fused_computation.109 | loop fusion | bytes 294912
  36.6 0.9 %bitcast_dynamic-update-slice_fusion.7 = f32[5,16,2304]{2,1,0:T(8,128)S(1)} fusion(f32[5,16,2304]{2,1,0:T(8,128)S(1)} %bitcast_dynamic-update-slice_fusion.8, f32[16,2304]{1,0:T(8,128)} %collective-permute-done.2), kind=kLoop, calls=%fused_computation.108 | loop fusion | bytes 294912
  37.5 0.9 %bitcast_dynamic-update-slice_fusion.6 = f32[5,16,2304]{2,1,0:T(8,128)S(1)} fusion(f32[5,16,2304]{2,1,0:T(8,128)S(1)} %bitcast_dynamic-update-slice_fusion.7, f32[16,2304]{1,0:T(8,128)} %collective-permute-done.3), kind=kLoop, calls=%fused_computation.107 | loop fusion | bytes 294912
  38.4 0.9 %bitcast_dynamic-update-slice_fusion.5 = f32[5,16,2304]{2,1,0:T(8,128)S(1)} fusion(f32[5,16,2304]{2,1,0:T(8,128)S(1)} %bitcast_dynamic-update-slice_fusion.6, f32[16,2304]{1,0:T(8,128)} %collective-permute-done.4), kind=kLoop, calls=%fused_computation.106 | loop fusion | bytes 294912 | tf_op jit(solution)/shard_map/stack | solution.py:62
  39.4 1.3 %reshape.46 = f32[80,9,256]{2,1,0:T(8,128)} reshape(f32[5,16,2304]{2,1,0:T(8,128)S(1)} %bitcast_dynamic-update-slice_fusion.5) | data formatting | bytes 1474560 | tf_op jit(solution)/shard_map/reshape | solution.py:67
  40.7 4.2 %fusion.8 = f32[9,256,128]{1,2,0:T(8,128)S(1)} fusion(f32[9,256,128]{1,2,0:T(8,128)S(1)} %copy.39, f32[9,256,128]{1,2,0:T(8,128)S(1)} %convolution_bitcast_fusion, f32[8,256,128]{1,2,0:T(8,128)} %fusion.11, f32[80,9,256]{2,1,0:T(8,128)} %reshape.46, f32[9,128]{1,0:T(8,128)} %broadcast_subtract_fusion, f32[9,128]{1,0:T(8,128)} %reduce_sum.9, ...), kind=kOutput, calls=%fused_computation.12 | convolution fusion | flops 286857216 | bytes 5698688 | tf_op jit(solution)/shard_map/slq,lsc->lqc/dot_general | solution.py:69
  45.1 1.5 %fusion.15 = f32[9,256,128]{1,2,0:T(8,128)S(1)} fusion(f32[9,256,128]{1,2,0:T(8,128)S(1)} %fusion.8, f32[128,128]{1,0:T(8,128)S(1)} %copy-done.4, f32[9,128]{1,0:T(8,128)S(1)} %copy-done.18, f32[128,128]{1,0:T(8,128)S(1)} %copy-done.6, f32[9,128]{1,0:T(8,128)S(1)} %copy-done.20, f32[128,128]{1,0:T(8,128)S(1)} %copy-done.8, f32[9,128]{1,0:T(8,128)S(1)} %copy-done.22, ...), kind=kOutput, calls=%fused_computation.24 | convolution fusion | flops 455196672 | bytes 2920448 | tf_op jit(solution)/shard_map/lqs,lsc->lqc/dot_general | solution.py:68
  46.6 0.6 fusion.82
  47.2 0.0 copy-start.31
  47.2 0.1 slice_bitcast_fusion
  47.4 1.3 %collective-permute-start.5 = (f32[16,2304]{1,0:T(8,128)S(1)}, f32[16,2304]{1,0:T(8,128)S(1)}, u32[]{:S(2)}, u32[]{:S(2)}) collective-permute-start(f32[16,2304]{1,0:T(8,128)S(1)} %bitcast.116), channel_id=1, source_target_pairs={{0,1},{1,2},{2,3},{3,4},{4,5},{5,6},{6,7},{7,8},{8,9},{9,10},{10,1... | collective-permute-start | bytes 442376 | tf_op jit(solution)/shard_map/ppermute | solution.py:64
  48.7 1.3 %collective-permute-start.6 = (f32[16,2304]{1,0:T(8,128)S(1)}, f32[16,2304]{1,0:T(8,128)S(1)}, u32[]{:S(2)}, u32[]{:S(2)}) collective-permute-start(f32[16,2304]{1,0:T(8,128)S(1)} %bitcast.115), channel_id=1, source_target_pairs={{1,0},{2,1},{3,2},{4,3},{5,4},{6,5},{7,6},{8,7},{9,8},{10,9},{11,1... | collective-permute-start | bytes 442376 | tf_op jit(solution)/shard_map/ppermute | solution.py:64
  50.0 3.2 %collective-permute-start.7 = (f32[16,2304]{1,0:T(8,128)S(1)}, f32[16,2304]{1,0:T(8,128)S(1)}, u32[]{:S(2)}, u32[]{:S(2)}) collective-permute-start(f32[16,2304]{1,0:T(8,128)S(1)} %bitcast.114), channel_id=1, source_target_pairs={{0,2},{1,3},{2,4},{3,5},{4,6},{5,7},{6,8},{7,9},{8,10},{9,11},{10,... | collective-permute-start | bytes 442376 | tf_op jit(solution)/shard_map/ppermute | solution.py:64
  53.2 1.3 %collective-permute-start.8 = (f32[16,2304]{1,0:T(8,128)S(1)}, f32[16,2304]{1,0:T(8,128)S(1)}, u32[]{:S(2)}, u32[]{:S(2)}) collective-permute-start(f32[16,2304]{1,0:T(8,128)S(1)} %bitcast.113), channel_id=1, source_target_pairs={{2,0},{3,1},{4,2},{5,3},{6,4},{7,5},{8,6},{9,7},{10,8},{11,9},{12,... | collective-permute-start | bytes 442376 | tf_op jit(solution)/shard_map/ppermute | solution.py:64
  54.5 8.4 %collective-permute-start.9 = (f32[16,2304]{1,0:T(8,128)S(1)}, f32[16,2304]{1,0:T(8,128)S(1)}, u32[]{:S(2)}, u32[]{:S(2)}) collective-permute-start(f32[16,2304]{1,0:T(8,128)S(1)} %bitcast.112), channel_id=1, source_target_pairs={{0,16},{1,17},{2,18},{3,19},{4,20},{5,21},{6,22},{7,23},{8,24},{9,... | collective-permute-start | bytes 442376 | tf_op jit(solution)/shard_map/ppermute | solution.py:64
  62.9 1.2 %fusion.10 = f32[8,256,128]{1,2,0:T(8,128)} fusion(f32[9,256,128]{1,2,0:T(8,128)S(1)} %fusion.8, f32[8,128]{1,0:T(8,128)S(1)} %copy-done.31), kind=kLoop, calls=%fused_computation.15 | loop fusion | flops 524288 | bytes 3149824 | tf_op jit(solution)/shard_map/mul | solution.py:71
  64.1 5.7 %collective-permute-done.9 = f32[16,2304]{1,0:T(8,128)S(1)} collective-permute-done((f32[16,2304]{1,0:T(8,128)S(1)}, f32[16,2304]{1,0:T(8,128)S(1)}, u32[]{:S(2)}, u32[]{:S(2)}) %collective-permute-start.9) | collective-permute-done | bytes 147488 | tf_op jit(solution)/shard_map/ppermute | solution.py:64
  69.8 1.3 %reshape.47 = f32[80,9,256]{2,1,0:T(8,128)} reshape(f32[5,16,2304]{2,1,0:T(8,128)S(1)} %bitcast_dynamic-update-slice_fusion) | data formatting | bytes 1474560 | tf_op jit(solution)/shard_map/reshape | solution.py:67
  71.1 4.1 %fusion.9 = f32[9,256,128]{1,2,0:T(8,128)S(1)} fusion(f32[9,256,128]{1,2,0:T(8,128)S(1)} %fusion.8, f32[9,256,128]{1,2,0:T(8,128)S(1)} %fusion.15, f32[8,256,128]{1,2,0:T(8,128)} %fusion.10, f32[80,9,256]{2,1,0:T(8,128)} %reshape.47, f32[9,128]{1,0:T(8,128)} %broadcast_subtract_fusion, f32[9,128]{1,0:T(8,128)} %reduce_sum.9, ...), kind=kOutput, calls=%fused_computation.13 | convolution fusion | flops 286857216 | bytes 5698688 | tf_op jit(solution)/shard_map/slq,lsc->lqc/dot_general | solution.py:69
  75.2 1.4 %copy.52 = f32[9,256,128]{2,1,0:T(8,128)} copy(f32[9,256,128]{1,2,0:T(8,128)S(1)} %fusion.9) | data formatting | bytes 2359296 | tf_op jit(solution)/shard_map/jit(_where)/select_n | solution.py:76
  (96 shorter events, 0.5 us)
Async XLA Ops:
  2.1 0.5 copy-start.33
  4.7 22.5 %copy-start = (f32[9,256,128]{2,1,0:T(8,128)S(1)}, f32[9,256,128]{2,1,0:T(8,128)}, u32[]{:S(2)}) copy-start(f32[9,256,128]{2,1,0:T(8,128)} %param.8) | copy-start | bytes 3538948
  5.4 29.3 %collective-permute-start = (f32[16,2304]{1,0:T(8,128)}, f32[16,2304]{1,0:T(8,128)}, u32[]{:S(2)}, u32[]{:S(2)}) collective-permute-start(f32[16,2304]{1,0:T(8,128)} %bitcast.39), channel_id=1, source_target_pairs={{0,1},{1,2},{2,3},{3,4},{4,5},{5,6},{6,7},{7,8},{8,9},{9,10},{10,1... | collective-permute-start | bytes 442376 | tf_op jit(solution)/shard_map/ppermute | solution.py:64
  9.1 26.5 %collective-permute-start.1 = (f32[16,2304]{1,0:T(8,128)}, f32[16,2304]{1,0:T(8,128)}, u32[]{:S(2)}, u32[]{:S(2)}) collective-permute-start(f32[16,2304]{1,0:T(8,128)} %bitcast.41), channel_id=1, source_target_pairs={{1,0},{2,1},{3,2},{4,3},{5,4},{6,5},{7,6},{8,7},{9,8},{10,9},{11,1... | collective-permute-start | bytes 442376 | tf_op jit(solution)/shard_map/ppermute | solution.py:64
  11.0 25.5 %collective-permute-start.2 = (f32[16,2304]{1,0:T(8,128)}, f32[16,2304]{1,0:T(8,128)}, u32[]{:S(2)}, u32[]{:S(2)}) collective-permute-start(f32[16,2304]{1,0:T(8,128)} %bitcast.43), channel_id=1, source_target_pairs={{0,2},{1,3},{2,4},{3,5},{4,6},{5,7},{6,8},{7,9},{8,10},{9,11},{10,... | collective-permute-start | bytes 442376 | tf_op jit(solution)/shard_map/ppermute | solution.py:64
  18.5 19.0 %collective-permute-start.3 = (f32[16,2304]{1,0:T(8,128)}, f32[16,2304]{1,0:T(8,128)}, u32[]{:S(2)}, u32[]{:S(2)}) collective-permute-start(f32[16,2304]{1,0:T(8,128)} %bitcast.45), channel_id=1, source_target_pairs={{2,0},{3,1},{4,2},{5,3},{6,4},{7,5},{8,6},{9,7},{10,8},{11,9},{12,... | collective-permute-start | bytes 442376 | tf_op jit(solution)/shard_map/ppermute | solution.py:64
  20.4 7.1 %copy-start.35 = (s32[8,128]{1,0:T(8,128)S(1)}, s32[8,128]{1,0:T(8,128)}, u32[]{:S(2)}) copy-start(s32[8,128]{1,0:T(8,128)} %param.12) | copy-start | bytes 12292
  20.4 7.1 %copy-start.29 = (f32[8,9,128]{2,0,1:T(8,128)S(1)}, f32[8,9,128]{2,0,1:T(8,128)}, u32[]{:S(2)}) copy-start(f32[8,9,128]{2,0,1:T(8,128)} %param.9) | copy-start | bytes 110596
  20.4 18.0 %collective-permute-start.4 = (f32[16,2304]{1,0:T(8,128)}, f32[16,2304]{1,0:T(8,128)}, u32[]{:S(2)}, u32[]{:S(2)}) collective-permute-start(f32[16,2304]{1,0:T(8,128)} %bitcast.47), channel_id=1, source_target_pairs={{0,16},{1,17},{2,18},{3,19},{4,20},{5,21},{6,22},{7,23},{8,24},{9,... | collective-permute-start | bytes 442376 | tf_op jit(solution)/shard_map/ppermute | solution.py:64
  27.6 1.0 %copy-start.30 = (f32[8,128]{1,0:T(8,128)S(1)}, f32[8,128]{1,0:T(8,128)}, u32[]{:S(2)}) copy-start(f32[8,128]{1,0:T(8,128)} %param.10) | copy-start | bytes 12292
  28.5 1.4 %copy-start.1 = (f32[128,128]{1,0:T(8,128)}, f32[128,128]{1,0:T(8,128)S(1)}, u32[]{:S(2)}) copy-start(f32[128,128]{1,0:T(8,128)S(1)} %get-tuple-element.15) | copy-start | bytes 196612
  28.5 1.4 %copy-start.3 = (f32[128,128]{1,0:T(8,128)}, f32[128,128]{1,0:T(8,128)S(1)}, u32[]{:S(2)}) copy-start(f32[128,128]{1,0:T(8,128)S(1)} %get-tuple-element.16) | copy-start | bytes 196612
  28.5 1.4 %copy-start.5 = (f32[128,128]{1,0:T(8,128)}, f32[128,128]{1,0:T(8,128)S(1)}, u32[]{:S(2)}) copy-start(f32[128,128]{1,0:T(8,128)S(1)} %get-tuple-element.17) | copy-start | bytes 196612
  28.5 1.4 %copy-start.7 = (f32[128,128]{1,0:T(8,128)}, f32[128,128]{1,0:T(8,128)S(1)}, u32[]{:S(2)}) copy-start(f32[128,128]{1,0:T(8,128)S(1)} %get-tuple-element.18) | copy-start | bytes 196612
  28.5 1.3 %copy-start.9 = (f32[128,128]{1,0:T(8,128)}, f32[128,128]{1,0:T(8,128)S(1)}, u32[]{:S(2)}) copy-start(f32[128,128]{1,0:T(8,128)S(1)} %get-tuple-element.19) | copy-start | bytes 196612
  28.5 1.3 %copy-start.11 = (f32[128,128]{1,0:T(8,128)}, f32[128,128]{1,0:T(8,128)S(1)}, u32[]{:S(2)}) copy-start(f32[128,128]{1,0:T(8,128)S(1)} %get-tuple-element.20) | copy-start | bytes 196612
  28.6 1.3 %copy-start.13 = (f32[128,128]{1,0:T(8,128)}, f32[128,128]{1,0:T(8,128)S(1)}, u32[]{:S(2)}) copy-start(f32[128,128]{1,0:T(8,128)S(1)} %get-tuple-element.21) | copy-start | bytes 196612
  28.6 1.3 %copy-start.15 = (f32[128,128]{1,0:T(8,128)}, f32[128,128]{1,0:T(8,128)S(1)}, u32[]{:S(2)}) copy-start(f32[128,128]{1,0:T(8,128)S(1)} %get-tuple-element.22) | copy-start | bytes 196612
  28.6 1.3 %copy-start.17 = (f32[9,128]{1,0:T(8,128)}, f32[9,128]{1,0:T(8,128)S(1)}, u32[]{:S(2)}) copy-start(f32[9,128]{1,0:T(8,128)S(1)} %get-tuple-element.41) | copy-start | bytes 13828
  28.6 1.3 %copy-start.19 = (f32[9,128]{1,0:T(8,128)}, f32[9,128]{1,0:T(8,128)S(1)}, u32[]{:S(2)}) copy-start(f32[9,128]{1,0:T(8,128)S(1)} %get-tuple-element.42) | copy-start | bytes 13828
  28.6 1.3 %copy-start.21 = (f32[9,128]{1,0:T(8,128)}, f32[9,128]{1,0:T(8,128)S(1)}, u32[]{:S(2)}) copy-start(f32[9,128]{1,0:T(8,128)S(1)} %get-tuple-element.43) | copy-start | bytes 13828
  28.6 1.3 %copy-start.23 = (f32[9,128]{1,0:T(8,128)}, f32[9,128]{1,0:T(8,128)S(1)}, u32[]{:S(2)}) copy-start(f32[9,128]{1,0:T(8,128)S(1)} %get-tuple-element.44) | copy-start | bytes 13828
  28.7 1.3 %copy-start.25 = (f32[9,128]{1,0:T(8,128)}, f32[9,128]{1,0:T(8,128)S(1)}, u32[]{:S(2)}) copy-start(f32[9,128]{1,0:T(8,128)S(1)} %get-tuple-element.45) | copy-start | bytes 13828
  28.7 1.3 %copy-start.27 = (f32[9,128]{1,0:T(8,128)}, f32[9,128]{1,0:T(8,128)S(1)}, u32[]{:S(2)}) copy-start(f32[9,128]{1,0:T(8,128)S(1)} %get-tuple-element.46) | copy-start | bytes 13828
  30.0 1.5 %copy-start.32 = (f32[9,128]{1,0:T(8,128)S(1)}, f32[9,128]{1,0:T(8,128)}, u32[]{:S(2)}) copy-start(f32[9,128]{1,0:T(8,128)} %param.11) | copy-start | bytes 13828
  40.6 4.3 %copy-start.2 = (f32[128,128]{1,0:T(8,128)S(1)}, f32[128,128]{1,0:T(8,128)}, u32[]{:S(2)}) copy-start(f32[128,128]{1,0:T(8,128)} %copy-done.1) | copy-start | bytes 196612
  40.6 4.3 %copy-start.4 = (f32[128,128]{1,0:T(8,128)S(1)}, f32[128,128]{1,0:T(8,128)}, u32[]{:S(2)}) copy-start(f32[128,128]{1,0:T(8,128)} %copy-done.3) | copy-start | bytes 196612
  40.6 4.4 %copy-start.6 = (f32[128,128]{1,0:T(8,128)S(1)}, f32[128,128]{1,0:T(8,128)}, u32[]{:S(2)}) copy-start(f32[128,128]{1,0:T(8,128)} %copy-done.5) | copy-start | bytes 196612
  40.6 4.4 %copy-start.8 = (f32[128,128]{1,0:T(8,128)S(1)}, f32[128,128]{1,0:T(8,128)}, u32[]{:S(2)}) copy-start(f32[128,128]{1,0:T(8,128)} %copy-done.7) | copy-start | bytes 196612
  40.6 4.4 %copy-start.10 = (f32[128,128]{1,0:T(8,128)S(1)}, f32[128,128]{1,0:T(8,128)}, u32[]{:S(2)}) copy-start(f32[128,128]{1,0:T(8,128)} %copy-done.9) | copy-start | bytes 196612
  40.6 4.4 %copy-start.12 = (f32[128,128]{1,0:T(8,128)S(1)}, f32[128,128]{1,0:T(8,128)}, u32[]{:S(2)}) copy-start(f32[128,128]{1,0:T(8,128)} %copy-done.11) | copy-start | bytes 196612
  40.7 4.4 %copy-start.14 = (f32[128,128]{1,0:T(8,128)S(1)}, f32[128,128]{1,0:T(8,128)}, u32[]{:S(2)}) copy-start(f32[128,128]{1,0:T(8,128)} %copy-done.13) | copy-start | bytes 196612
  40.7 4.4 %copy-start.16 = (f32[128,128]{1,0:T(8,128)S(1)}, f32[128,128]{1,0:T(8,128)}, u32[]{:S(2)}) copy-start(f32[128,128]{1,0:T(8,128)} %copy-done.15) | copy-start | bytes 196612
  40.7 4.4 %copy-start.18 = (f32[9,128]{1,0:T(8,128)S(1)}, f32[9,128]{1,0:T(8,128)}, u32[]{:S(2)}) copy-start(f32[9,128]{1,0:T(8,128)} %copy-done.17) | copy-start | bytes 13828
  40.7 4.4 %copy-start.20 = (f32[9,128]{1,0:T(8,128)S(1)}, f32[9,128]{1,0:T(8,128)}, u32[]{:S(2)}) copy-start(f32[9,128]{1,0:T(8,128)} %copy-done.19) | copy-start | bytes 13828
  40.7 4.4 %copy-start.22 = (f32[9,128]{1,0:T(8,128)S(1)}, f32[9,128]{1,0:T(8,128)}, u32[]{:S(2)}) copy-start(f32[9,128]{1,0:T(8,128)} %copy-done.21) | copy-start | bytes 13828
  40.7 4.4 %copy-start.24 = (f32[9,128]{1,0:T(8,128)S(1)}, f32[9,128]{1,0:T(8,128)}, u32[]{:S(2)}) copy-start(f32[9,128]{1,0:T(8,128)} %copy-done.23) | copy-start | bytes 13828
  40.7 4.4 %copy-start.26 = (f32[9,128]{1,0:T(8,128)S(1)}, f32[9,128]{1,0:T(8,128)}, u32[]{:S(2)}) copy-start(f32[9,128]{1,0:T(8,128)} %copy-done.25) | copy-start | bytes 13828
  40.7 4.4 %copy-start.28 = (f32[9,128]{1,0:T(8,128)S(1)}, f32[9,128]{1,0:T(8,128)}, u32[]{:S(2)}) copy-start(f32[9,128]{1,0:T(8,128)} %copy-done.27) | copy-start | bytes 13828
  45.1 1.5 %copy-start.34 = (s32[80]{0:T(128)S(1)}, s32[80]{0:T(128)}, u32[]{:S(2)}) copy-start(s32[80]{0:T(128)} %copy-done.33) | copy-start | bytes 964
  47.2 15.6 %copy-start.31 = (f32[8,128]{1,0:T(8,128)S(1)}, f32[8,128]{1,0:T(8,128)}, u32[]{:S(2)}) copy-start(f32[8,128]{1,0:T(8,128)} %param.10) | copy-start | bytes 12292
  47.4 16.6 %collective-permute-start.5 = (f32[16,2304]{1,0:T(8,128)S(1)}, f32[16,2304]{1,0:T(8,128)S(1)}, u32[]{:S(2)}, u32[]{:S(2)}) collective-permute-start(f32[16,2304]{1,0:T(8,128)S(1)} %bitcast.116), channel_id=1, source_target_pairs={{0,1},{1,2},{2,3},{3,4},{4,5},{5,6},{6,7},{7,8},{8,9},{9,10},{10,1... | collective-permute-start | bytes 442376 | tf_op jit(solution)/shard_map/ppermute | solution.py:64
  48.7 15.3 %collective-permute-start.6 = (f32[16,2304]{1,0:T(8,128)S(1)}, f32[16,2304]{1,0:T(8,128)S(1)}, u32[]{:S(2)}, u32[]{:S(2)}) collective-permute-start(f32[16,2304]{1,0:T(8,128)S(1)} %bitcast.115), channel_id=1, source_target_pairs={{1,0},{2,1},{3,2},{4,3},{5,4},{6,5},{7,6},{8,7},{9,8},{10,9},{11,1... | collective-permute-start | bytes 442376 | tf_op jit(solution)/shard_map/ppermute | solution.py:64
  50.0 14.1 %collective-permute-start.7 = (f32[16,2304]{1,0:T(8,128)S(1)}, f32[16,2304]{1,0:T(8,128)S(1)}, u32[]{:S(2)}, u32[]{:S(2)}) collective-permute-start(f32[16,2304]{1,0:T(8,128)S(1)} %bitcast.114), channel_id=1, source_target_pairs={{0,2},{1,3},{2,4},{3,5},{4,6},{5,7},{6,8},{7,9},{8,10},{9,11},{10,... | collective-permute-start | bytes 442376 | tf_op jit(solution)/shard_map/ppermute | solution.py:64
  53.2 10.9 %collective-permute-start.8 = (f32[16,2304]{1,0:T(8,128)S(1)}, f32[16,2304]{1,0:T(8,128)S(1)}, u32[]{:S(2)}, u32[]{:S(2)}) collective-permute-start(f32[16,2304]{1,0:T(8,128)S(1)} %bitcast.113), channel_id=1, source_target_pairs={{2,0},{3,1},{4,2},{5,3},{6,4},{7,5},{8,6},{9,7},{10,8},{11,9},{12,... | collective-permute-start | bytes 442376 | tf_op jit(solution)/shard_map/ppermute | solution.py:64
  54.5 15.3 %collective-permute-start.9 = (f32[16,2304]{1,0:T(8,128)S(1)}, f32[16,2304]{1,0:T(8,128)S(1)}, u32[]{:S(2)}, u32[]{:S(2)}) collective-permute-start(f32[16,2304]{1,0:T(8,128)S(1)} %bitcast.112), channel_id=1, source_target_pairs={{0,16},{1,17},{2,18},{3,19},{4,20},{5,21},{6,22},{7,23},{8,24},{9,... | collective-permute-start | bytes 442376 | tf_op jit(solution)/shard_map/ppermute | solution.py:64

commit v2 on v1

v2 whole, which is shorter than its diff:
```python
import functools

import jax
import jax.numpy as jnp
from jax import lax
from jax.experimental import pallas as pl
from jax.sharding import PartitionSpec as P

STEPS = 2
HIGHEST = lax.Precision.HIGHEST
INTERPRET = False
NT = (((1,), (1,)), ((), ()))
TN = (((0,), (0,)), ((), ()))


def peer_shifts(n):
    return (n // 2, 1, -1, 2, -2)


def permutation(n, shift):
    if shift == n // 2:
        return [(p, (p + shift) % n) for p in range(n)]
    return [(p, p + shift) for p in range(n) if 0 <= p + shift < n]


def select_kernel(groups, hslot, pulses, values_ref, select_ref, *out_refs):
    select = select_ref[...]
    for level in range(values_ref.shape[0]):
        block = lax.dot_general(
            select, values_ref[level], NT, precision=HIGHEST, preferred_element_type=jnp.float32
        )
        for g in range(groups):
            out_refs[g][:, level * pulses : (level + 1) * pulses] = block[g * hslot : (g + 1) * hslot]


def gather_send(values, select, groups, hslot):
    levels, pulses, capacity = values.shape
    return pl.pallas_call(
        functools.partial(select_kernel, groups, hslot, pulses),
        out_shape=[jax.ShapeDtypeStruct((hslot, levels * pulses), jnp.float32)] * groups,
        interpret=INTERPRET,
        name="gather_send",
    )(values, select)


def local_kernel(values_ref, local_ref, weight_sum_ref, mixing_ref, out_ref):
    levels = values_ref.shape[0]
    for level in range(levels):
        v = values_ref[level]
        x = v - weight_sum_ref[level : level + 1, :] * v
        x = x + jnp.dot(
            v, local_ref[level], precision=HIGHEST, preferred_element_type=jnp.float32
        )
        if level + 1 < levels:
            x = x + mixing_ref[level : level + 1, :] * (values_ref[level + 1] - v)
        if level > 0:
            x = x - mixing_ref[level - 1 : level, :] * (v - values_ref[level - 1])
        out_ref[level] = x


def local_part(values, local_matrix, weight_sum, mixing):
    return pl.pallas_call(
        local_kernel,
        out_shape=jax.ShapeDtypeStruct(values.shape, jnp.float32),
        interpret=INTERPRET,
        name="local_part",
    )(values, local_matrix, weight_sum, mixing)


def finish_kernel(groups, hslot, pulses, send, *refs):
    partial_ref = refs[0]
    incoming = refs[1 : 1 + groups]
    remote_ref, keep_ref, living_ref, select_ref = refs[1 + groups : 5 + groups]
    out_ref = refs[5 + groups]
    send_refs = refs[6 + groups :]
    living = living_ref[...] > 0.5
    for level in range(partial_ref.shape[0]):
        columns = slice(level * pulses, (level + 1) * pulses)
        received = jnp.concatenate([incoming[g][:, columns] for g in range(groups)], axis=0)
        far = lax.dot_general(
            received, remote_ref[level], TN, precision=HIGHEST, preferred_element_type=jnp.float32
        )
        x = (partial_ref[level] + far) * keep_ref[level : level + 1, :]
        x = jnp.where(living, x, 0.0)
        out_ref[level] = x
        if send:
            block = lax.dot_general(
                select_ref[...], x, NT, precision=HIGHEST, preferred_element_type=jnp.float32
            )
            for g in range(groups):
                send_refs[g][:, columns] = block[g * hslot : (g + 1) * hslot]


def finish(partial, incoming, remote_matrix, keep, living, select, send):
    levels, pulses, capacity = partial.shape
    groups = len(incoming)
    hslot = incoming[0].shape[0]
    shapes = [jax.ShapeDtypeStruct(partial.shape, jnp.float32)]
    if send:
        shapes += [jax.ShapeDtypeStruct((hslot, levels * pulses), jnp.float32)] * groups
    outs = pl.pallas_call(
        functools.partial(finish_kernel, groups, hslot, pulses, send),
        out_shape=shapes,
        interpret=INTERPRET,
        name="finish_send" if send else "finish",
    )(partial, *incoming, remote_matrix, keep, living, select)
    return outs[0], outs[1:]


def per_device(
    n, concentration, flux_weight, vertical_mixing, deposition, halo_index, send_cells, live_count
):
    levels, pulses, capacity = concentration.shape
    hslot = send_cells.shape[2]
    nbr = flux_weight.shape[0]
    shifts = peer_shifts(n)
    groups = len(shifts)
    me = lax.axis_index("cells")
    f32 = jnp.float32

    peers = (me + jnp.array(shifts, dtype=jnp.int32)) % n
    picked = send_cells[0][peers].reshape(groups * hslot)
    select = (picked[:, None] == jnp.arange(capacity, dtype=jnp.int32)[None, :]).astype(f32)

    values = concentration
    outgoing = gather_send(values, select, groups, hslot)

    beyond = halo_index - capacity
    sender = beyond // hslot
    place = beyond % hslot
    shift = (me - sender) % n
    group = jnp.full(halo_index.shape, -1, dtype=jnp.int32)
    for g, s in enumerate(shifts):
        group = jnp.where(shift == s % n, g, group)
    local_col = jnp.where(beyond < 0, halo_index, -1)
    remote_col = jnp.where((beyond >= 0) & (group >= 0), group * hslot + place, -1)
    onehot_local = (local_col[:, None, :] == jnp.arange(capacity)[None, :, None]).astype(f32)
    onehot_remote = (
        remote_col[:, None, :] == jnp.arange(groups * hslot)[None, :, None]
    ).astype(f32)
    local_matrix = sum(flux_weight[k][:, None, :] * onehot_local[k][None] for k in range(nbr))
    remote_matrix = sum(flux_weight[k][:, None, :] * onehot_remote[k][None] for k in range(nbr))
    weight_sum = sum(flux_weight[k] for k in range(nbr))

    living = (jnp.arange(capacity, dtype=jnp.int32) < live_count[0]).astype(f32)[None, :]
    keep = 1.0 - deposition

    for sweep in range(STEPS):
        incoming = [
            lax.ppermute(outgoing[g], "cells", perm=permutation(n, s))
            for g, s in enumerate(shifts)
        ]
        partial = local_part(values, local_matrix, weight_sum, vertical_mixing)
        values, outgoing = finish(
            partial, incoming, remote_matrix, keep, living, select, sweep + 1 < STEPS
        )
    return values


def solution(mesh):
    n = mesh.shape["cells"]
    in_specs = (
        P(None, None, "cells"),
        P(None, None, "cells"),
        P(None, "cells"),
        P(None, "cells"),
        P(None, "cells"),
        P("cells", None, None),
        P("cells"),
    )
    out_specs = P(None, None, "cells")

    def body(*args):
        return per_device(n, *args)

    return jax.shard_map(body, mesh=mesh, in_specs=in_specs, out_specs=out_specs, check_vma=False)
```

time: 77.2 us -> 64.2 us (0.83)
  the two profiles are of different devices: /device:TPU:0 before, /device:TPU:6 now
where the time goes in v2:
time: 64.2 us; the launch traced here: 63.6 us
  starting transfers between devices  30.6 us (48%)
  Pallas kernels  19.8 us (31%)
  other arithmetic  5.36 us (8%)
  local copies, waits for them, and re-layouts  3.61 us (6%)
  waiting for transfers between devices  3.34 us (5%)
  between operations  0.93 us (1%)
    ppermute x10, starting transfers between devices, per_device(): lax.ppermute(outgoing[g], 'cells', perm=permutation(n, s))  30.6 us
    pallas_call x2, Pallas kernels, finish(): pl.pallas_call(functools.partial(finish_kernel, groups, hslot, pulses, se...  8.89 us
    pallas_call x2, Pallas kernels, local_part(): pl.pallas_call(local_kernel, out_shape=jax.ShapeDtypeStruct(values.shape,...  7.48 us
    pallas_call x1, Pallas kernels, gather_send(): pl.pallas_call(functools.partial(select_kernel, groups, hslot, pulses), o...  3.46 us
    ppermute x10, waiting for transfers between devices, per_device(): lax.ppermute(outgoing[g], 'cells', perm=permutation(n, s))  3.34 us
    unnamed x27, local copies, waits for them, and re-layouts  2.87 us
  transfers between devices with their start and end apart: 10, of which 1 were waited for; matrix products, arithmetic and copies ran while one was open for 6% of the time, Pallas kernels for 12%

profile of v2, /device:TPU:6, one launch (start us, length us, event | category | flops | bytes accessed | tf_op | source)
XLA Modules:
  0.0 63.6 jit_solution(9418966885490631497)
XLA Ops:
  0.0 0.7 %compare_select_fusion.1 = s32[5]{0:T(128)S(1)} fusion(s32[5]{0:T(128)} %constant.76.clone, s32[]{:T(128)S(6)} %axis_index.12), kind=kLoop, calls=%fused_computation.52 | loop fusion | flops 75 | bytes 44 | tf_op jit(solution)/shard_map/select_n | solution.py:122
  0.7 0.8 %copy.17 = s32[1,32,16]{2,1,0:T(8,128)S(1)} copy(s32[1,32,16]{1,2,0:T(8,128)} %param.13) | data formatting | bytes 4096 | tf_op args[5]
  1.5 0.6 gather_fusion
  2.0 0.1 eq.72
  2.1 0.7 %fusion.2.select_ref.refs_9_ = f32[80,128]{1,0:T(8,128)} fusion(s32[80]{0:T(128)S(1)} %eq.72), kind=kLoop, calls=%fused_computation.24 | loop fusion | flops 20480 | bytes 41280 | tf_op jit(solution)/shard_map/convert_element_type | solution.py:123
  2.8 3.5 %gather_send.1 = (f32[16,2304]{1,0:T(8,128)}, f32[16,2304]{1,0:T(8,128)}, f32[16,2304]{1,0:T(8,128)}, f32[16,2304]{1,0:T(8,128)}, f32[16,2304]{1,0:T(8,128)}) custom-call(f32[9,256,128]{2,1,0:T(8,128)} %values_ref.3, f32[80,128]{1,0:T(8,128)} %fusion.2.select_ref.refs_9_), custom_call_target="tpu_custom_call" | custom-call | tf_op jit(solution)/shard_map/gather_send/pallas_call | solution.py:38
  6.3 2.6 %collective-permute-start = (f32[16,2304]{1,0:T(8,128)}, f32[16,2304]{1,0:T(8,128)S(1)}, u32[]{:S(2)}, u32[]{:S(2)}) collective-permute-start(f32[16,2304]{1,0:T(8,128)} %get-tuple-element.16), channel_id=1, source_target_pairs={{0,16},{1,17},{2,18},{3,19},{4,20},{5,21},{6,22},{7,23},{8,24},{9,... | collective-permute-start | bytes 442376 | tf_op jit(solution)/shard_map/ppermute | solution.py:150
  8.8 1.9 %collective-permute-start.1 = (f32[16,2304]{1,0:T(8,128)}, f32[16,2304]{1,0:T(8,128)S(1)}, u32[]{:S(2)}, u32[]{:S(2)}) collective-permute-start(f32[16,2304]{1,0:T(8,128)} %get-tuple-element.17), channel_id=1, source_target_pairs={{0,1},{1,2},{2,3},{3,4},{4,5},{5,6},{6,7},{7,8},{8,9},{9,10},{10,1... | collective-permute-start | bytes 442376 | tf_op jit(solution)/shard_map/ppermute | solution.py:150
  10.8 3.6 %collective-permute-start.2 = (f32[16,2304]{1,0:T(8,128)}, f32[16,2304]{1,0:T(8,128)S(1)}, u32[]{:S(2)}, u32[]{:S(2)}) collective-permute-start(f32[16,2304]{1,0:T(8,128)} %get-tuple-element.18), channel_id=1, source_target_pairs={{1,0},{2,1},{3,2},{4,3},{5,4},{6,5},{7,6},{8,7},{9,8},{10,9},{11,1... | collective-permute-start | bytes 442376 | tf_op jit(solution)/shard_map/ppermute | solution.py:150
  14.4 5.2 %collective-permute-start.3 = (f32[16,2304]{1,0:T(8,128)}, f32[16,2304]{1,0:T(8,128)S(1)}, u32[]{:S(2)}, u32[]{:S(2)}) collective-permute-start(f32[16,2304]{1,0:T(8,128)} %get-tuple-element.19), channel_id=1, source_target_pairs={{0,2},{1,3},{2,4},{3,5},{4,6},{5,7},{6,8},{7,9},{8,10},{9,11},{10,... | collective-permute-start | bytes 442376 | tf_op jit(solution)/shard_map/ppermute | solution.py:150
  19.6 1.9 %collective-permute-start.4 = (f32[16,2304]{1,0:T(8,128)}, f32[16,2304]{1,0:T(8,128)S(1)}, u32[]{:S(2)}, u32[]{:S(2)}) collective-permute-start(f32[16,2304]{1,0:T(8,128)} %get-tuple-element.20), channel_id=1, source_target_pairs={{2,0},{3,1},{4,2},{5,3},{6,4},{7,5},{8,6},{9,7},{10,8},{11,9},{12,... | collective-permute-start | bytes 442376 | tf_op jit(solution)/shard_map/ppermute | solution.py:150
  21.5 0.0 copy-done.10
  21.6 0.6 add_add_fusion.weight_sum_ref
  22.2 0.0 copy-done.12
  22.4 0.0 copy-start.11
  22.4 1.0 %multiply_add_fusion.1.refs_6_ = f32[9,80,128]{2,1,0:T(8,128)} fusion(f32[80,128]{1,0:T(8,128)S(1)} %get-tuple-element.36, f32[9,128]{1,0:T(8,128)S(1)} %get-tuple-element.53, f32[80,128]{1,0:T(8,128)S(1)} %get-tuple-element.37, f32[9,128]{1,0:T(8,128)S(1)} %get-tuple-element.54, f32[80,128]{1,0:T(8,128)S(1)} %get-tuple-element.38, ...), kind=kLoop, calls=%fused_computation.4 | loop fusion | flops 1382400 | bytes 733184 | tf_op jit(solution)/shard_map/add | solution.py:142
  23.4 1.1 %multiply_add_fusion.local_ref = f32[9,128,128]{2,1,0:T(8,128)} fusion(f32[128,128]{1,0:T(8,128)S(1)} %get-tuple-element.28, f32[9,128]{1,0:T(8,128)S(1)} %get-tuple-element.53, f32[128,128]{1,0:T(8,128)S(1)} %get-tuple-element.29, f32[9,128]{1,0:T(8,128)S(1)} %get-tuple-element.54, f32[128,128]{1,0:T(8,128)S(1)} %get-tuple-element.30, ...), kind=kLoop, calls=%fused_computation.1 | loop fusion | flops 2211840 | bytes 1150976 | tf_op jit(solution)/shard_map/add | solution.py:141
  24.5 0.0 copy-done.11
  24.5 0.6 broadcast_subtract_fusion.refs_7_
  25.8 3.7 %local_part.2.refs_0_ = f32[9,256,128]{2,1,0:T(8,128)} custom-call(f32[9,256,128]{2,1,0:T(8,128)} %values_ref.3, f32[9,128,128]{2,1,0:T(8,128)} %multiply_add_fusion.local_ref, f32[9,128]{1,0:T(8,128)} %add_add_fusion.weight_sum_ref, f32[8,128]{1,0:T(8,128)} %mixing_ref.3), custom_call_target="tpu_custom_call" | custom-call | tf_op jit(solution)/shard_map/local_part/pallas_call | solution.py:62
  29.5 0.6 compare_convert_fusion.refs_8_
  30.1 0.0 collective-permute-done.refs_1_
  30.1 0.0 collective-permute-done.1.refs_2_
  30.1 0.0 collective-permute-done.2.refs_3_
  30.2 0.0 collective-permute-done.3.refs_4_
  30.2 0.0 copy-start.3
  30.2 0.0 collective-permute-done.4.refs_5_
  30.2 0.6 copy-done
  30.8 0.1 copy-done.1
  30.8 0.0 copy-done.2
  30.9 0.1 copy-done.3
  30.9 0.7 %copy-done.4 = f32[16,2304]{1,0:T(8,128)} copy-done((f32[16,2304]{1,0:T(8,128)}, f32[16,2304]{1,0:T(8,128)S(1)}, u32[]{:S(2)}) %copy-start.4) | copy-done | bytes 147480
  31.6 5.0 %finish_send.1 = (f32[9,256,128]{2,1,0:T(8,128)}, f32[16,2304]{1,0:T(8,128)}, f32[16,2304]{1,0:T(8,128)}, f32[16,2304]{1,0:T(8,128)}, f32[16,2304]{1,0:T(8,128)}, /*index=5*/f32[16,2304]{1,0:T(8,128)}) custom-call(f32[9,256,128]{2,1,0:T(8,128)} %local_part.2.refs_0_, f32[16,2304]{1,0:T(8,128)} %copy-done, f32[16,2304]{1,0:T(8,128)} %copy-done.1, ...), custom_call_target="tpu_custom_call" | custom-call | tf_op jit(solution)/shard_map/finish_send/pallas_call | solution.py:101
  36.6 0.3 collective-permute-start.5
  37.0 1.9 %collective-permute-start.6 = (f32[16,2304]{1,0:T(8,128)}, f32[16,2304]{1,0:T(8,128)S(1)}, u32[]{:S(2)}, u32[]{:S(2)}) collective-permute-start(f32[16,2304]{1,0:T(8,128)} %get-tuple-element.23), channel_id=1, source_target_pairs={{0,1},{1,2},{2,3},{3,4},{4,5},{5,6},{6,7},{7,8},{8,9},{9,10},{10,1... | collective-permute-start | bytes 442376 | tf_op jit(solution)/shard_map/ppermute | solution.py:150
  38.9 3.6 %collective-permute-start.7 = (f32[16,2304]{1,0:T(8,128)}, f32[16,2304]{1,0:T(8,128)S(1)}, u32[]{:S(2)}, u32[]{:S(2)}) collective-permute-start(f32[16,2304]{1,0:T(8,128)} %get-tuple-element.24), channel_id=1, source_target_pairs={{1,0},{2,1},{3,2},{4,3},{5,4},{6,5},{7,6},{8,7},{9,8},{10,9},{11,1... | collective-permute-start | bytes 442376 | tf_op jit(solution)/shard_map/ppermute | solution.py:150
  42.5 7.5 %collective-permute-start.8 = (f32[16,2304]{1,0:T(8,128)}, f32[16,2304]{1,0:T(8,128)S(1)}, u32[]{:S(2)}, u32[]{:S(2)}) collective-permute-start(f32[16,2304]{1,0:T(8,128)} %get-tuple-element.25), channel_id=1, source_target_pairs={{0,2},{1,3},{2,4},{3,5},{4,6},{5,7},{6,8},{7,9},{8,10},{9,11},{10,... | collective-permute-start | bytes 442376 | tf_op jit(solution)/shard_map/ppermute | solution.py:150
  50.1 1.9 %collective-permute-start.9 = (f32[16,2304]{1,0:T(8,128)}, f32[16,2304]{1,0:T(8,128)S(1)}, u32[]{:S(2)}, u32[]{:S(2)}) collective-permute-start(f32[16,2304]{1,0:T(8,128)} %get-tuple-element.26), channel_id=1, source_target_pairs={{2,0},{3,1},{4,2},{5,3},{6,4},{7,5},{8,6},{9,7},{10,8},{11,9},{12,... | collective-permute-start | bytes 442376 | tf_op jit(solution)/shard_map/ppermute | solution.py:150
  52.0 3.7 %local_part.3.refs_0_ = f32[9,256,128]{2,1,0:T(8,128)} custom-call(f32[9,256,128]{2,1,0:T(8,128)} %get-tuple-element.21.values_ref, f32[9,128,128]{2,1,0:T(8,128)} %multiply_add_fusion.local_ref, f32[9,128]{1,0:T(8,128)} %add_add_fusion.weight_sum_ref, f32[8,128]{1,0:T(8,128)} %mixing_ref.3), custom_call_target="tpu_custom_call" | custom-call | tf_op jit(solution)/shard_map/local_part/pallas_call | solution.py:62
  55.7 0.0 collective-permute-done.5.refs_1_
  55.7 0.0 collective-permute-done.6.refs_2_
  55.8 0.0 collective-permute-done.7.refs_3_
  55.8 0.0 collective-permute-done.8.refs_4_
  55.8 0.0 copy-start.8
  55.8 3.3 %collective-permute-done.9.refs_5_ = f32[16,2304]{1,0:T(8,128)S(1)} collective-permute-done((f32[16,2304]{1,0:T(8,128)}, f32[16,2304]{1,0:T(8,128)S(1)}, u32[]{:S(2)}, u32[]{:S(2)}) %collective-permute-start.9) | collective-permute-done | bytes 147488 | tf_op jit(solution)/shard_map/ppermute | solution.py:150
  59.1 0.0 copy-done.5
  59.1 0.6 %copy-done.9 = f32[16,2304]{1,0:T(8,128)} copy-done((f32[16,2304]{1,0:T(8,128)}, f32[16,2304]{1,0:T(8,128)S(1)}, u32[]{:S(2)}) %copy-start.9) | copy-done | bytes 147480
  59.8 3.9 %finish.1 = f32[9,256,128]{2,1,0:T(8,128)} custom-call(f32[9,256,128]{2,1,0:T(8,128)} %local_part.3.refs_0_, f32[16,2304]{1,0:T(8,128)} %copy-done.5, f32[16,2304]{1,0:T(8,128)} %copy-done.6, f32[16,2304]{1,0:T(8,128)} %copy-done.7, f32[16,2304]{1,0:T(8,128)} %copy-done.8, f32[16,2304]{1,0:T(8,128)} %copy-done.9, f32[9,80,128]{2,1,0:T(8,128)} %multiply_add_fusion.1.refs_6_, ...), custom_call_target="tpu_custom_call" | custom-call | tf_op jit(solution)/shard_map/finish/pallas_call | solution.py:101
  (24 shorter events, 0.2 us)
Async XLA Ops:
  0.0 21.5 %copy-start.10 = (f32[8,9,128]{2,0,1:T(8,128)S(1)}, f32[8,9,128]{2,0,1:T(8,128)}, u32[]{:S(2)}) copy-start(f32[8,9,128]{2,0,1:T(8,128)} %param.9) | copy-start | bytes 110596
  0.0 22.2 %copy-start.12 = (s32[8,128]{1,0:T(8,128)S(1)}, s32[8,128]{1,0:T(8,128)}, u32[]{:S(2)}) copy-start(s32[8,128]{1,0:T(8,128)} %param.12) | copy-start | bytes 12292
  6.3 23.9 %collective-permute-start = (f32[16,2304]{1,0:T(8,128)}, f32[16,2304]{1,0:T(8,128)S(1)}, u32[]{:S(2)}, u32[]{:S(2)}) collective-permute-start(f32[16,2304]{1,0:T(8,128)} %get-tuple-element.16), channel_id=1, source_target_pairs={{0,16},{1,17},{2,18},{3,19},{4,20},{5,21},{6,22},{7,23},{8,24},{9,... | collective-permute-start | bytes 442376 | tf_op jit(solution)/shard_map/ppermute | solution.py:150
  8.8 21.3 %collective-permute-start.1 = (f32[16,2304]{1,0:T(8,128)}, f32[16,2304]{1,0:T(8,128)S(1)}, u32[]{:S(2)}, u32[]{:S(2)}) collective-permute-start(f32[16,2304]{1,0:T(8,128)} %get-tuple-element.17), channel_id=1, source_target_pairs={{0,1},{1,2},{2,3},{3,4},{4,5},{5,6},{6,7},{7,8},{8,9},{9,10},{10,1... | collective-permute-start | bytes 442376 | tf_op jit(solution)/shard_map/ppermute | solution.py:150
  10.8 19.4 %collective-permute-start.2 = (f32[16,2304]{1,0:T(8,128)}, f32[16,2304]{1,0:T(8,128)S(1)}, u32[]{:S(2)}, u32[]{:S(2)}) collective-permute-start(f32[16,2304]{1,0:T(8,128)} %get-tuple-element.18), channel_id=1, source_target_pairs={{1,0},{2,1},{3,2},{4,3},{5,4},{6,5},{7,6},{8,7},{9,8},{10,9},{11,1... | collective-permute-start | bytes 442376 | tf_op jit(solution)/shard_map/ppermute | solution.py:150
  14.4 15.8 %collective-permute-start.3 = (f32[16,2304]{1,0:T(8,128)}, f32[16,2304]{1,0:T(8,128)S(1)}, u32[]{:S(2)}, u32[]{:S(2)}) collective-permute-start(f32[16,2304]{1,0:T(8,128)} %get-tuple-element.19), channel_id=1, source_target_pairs={{0,2},{1,3},{2,4},{3,5},{4,6},{5,7},{6,8},{7,9},{8,10},{9,11},{10,... | collective-permute-start | bytes 442376 | tf_op jit(solution)/shard_map/ppermute | solution.py:150
  19.6 10.6 %collective-permute-start.4 = (f32[16,2304]{1,0:T(8,128)}, f32[16,2304]{1,0:T(8,128)S(1)}, u32[]{:S(2)}, u32[]{:S(2)}) collective-permute-start(f32[16,2304]{1,0:T(8,128)} %get-tuple-element.20), channel_id=1, source_target_pairs={{2,0},{3,1},{4,2},{5,3},{6,4},{7,5},{8,6},{9,7},{10,8},{11,9},{12,... | collective-permute-start | bytes 442376 | tf_op jit(solution)/shard_map/ppermute | solution.py:150
  22.4 2.1 %copy-start.11 = (f32[9,128]{1,0:T(8,128)S(1)}, f32[9,128]{1,0:T(8,128)}, u32[]{:S(2)}) copy-start(f32[9,128]{1,0:T(8,128)} %param.11) | copy-start | bytes 13828
  30.1 0.7 %copy-start = (f32[16,2304]{1,0:T(8,128)}, f32[16,2304]{1,0:T(8,128)S(1)}, u32[]{:S(2)}) copy-start(f32[16,2304]{1,0:T(8,128)S(1)} %collective-permute-done.refs_1_) | copy-start | bytes 442372
  30.1 0.7 %copy-start.1 = (f32[16,2304]{1,0:T(8,128)}, f32[16,2304]{1,0:T(8,128)S(1)}, u32[]{:S(2)}) copy-start(f32[16,2304]{1,0:T(8,128)S(1)} %collective-permute-done.1.refs_2_) | copy-start | bytes 442372
  30.1 0.7 %copy-start.2 = (f32[16,2304]{1,0:T(8,128)}, f32[16,2304]{1,0:T(8,128)S(1)}, u32[]{:S(2)}) copy-start(f32[16,2304]{1,0:T(8,128)S(1)} %collective-permute-done.2.refs_3_) | copy-start | bytes 442372
  30.2 0.8 %copy-start.3 = (f32[16,2304]{1,0:T(8,128)}, f32[16,2304]{1,0:T(8,128)S(1)}, u32[]{:S(2)}) copy-start(f32[16,2304]{1,0:T(8,128)S(1)} %collective-permute-done.3.refs_4_) | copy-start | bytes 442372
  30.9 0.7 %copy-start.4 = (f32[16,2304]{1,0:T(8,128)}, f32[16,2304]{1,0:T(8,128)S(1)}, u32[]{:S(2)}) copy-start(f32[16,2304]{1,0:T(8,128)S(1)} %collective-permute-done.4.refs_5_) | copy-start | bytes 442372
  36.6 19.1 %collective-permute-start.5 = (f32[16,2304]{1,0:T(8,128)}, f32[16,2304]{1,0:T(8,128)S(1)}, u32[]{:S(2)}, u32[]{:S(2)}) collective-permute-start(f32[16,2304]{1,0:T(8,128)} %get-tuple-element.22), channel_id=1, source_target_pairs={{0,16},{1,17},{2,18},{3,19},{4,20},{5,21},{6,22},{7,23},{8,24},{9,... | collective-permute-start | bytes 442376 | tf_op jit(solution)/shard_map/ppermute | solution.py:150
  37.0 18.8 %collective-permute-start.6 = (f32[16,2304]{1,0:T(8,128)}, f32[16,2304]{1,0:T(8,128)S(1)}, u32[]{:S(2)}, u32[]{:S(2)}) collective-permute-start(f32[16,2304]{1,0:T(8,128)} %get-tuple-element.23), channel_id=1, source_target_pairs={{0,1},{1,2},{2,3},{3,4},{4,5},{5,6},{6,7},{7,8},{8,9},{9,10},{10,1... | collective-permute-start | bytes 442376 | tf_op jit(solution)/shard_map/ppermute | solution.py:150
  38.9 16.9 %collective-permute-start.7 = (f32[16,2304]{1,0:T(8,128)}, f32[16,2304]{1,0:T(8,128)S(1)}, u32[]{:S(2)}, u32[]{:S(2)}) collective-permute-start(f32[16,2304]{1,0:T(8,128)} %get-tuple-element.24), channel_id=1, source_target_pairs={{1,0},{2,1},{3,2},{4,3},{5,4},{6,5},{7,6},{8,7},{9,8},{10,9},{11,1... | collective-permute-start | bytes 442376 | tf_op jit(solution)/shard_map/ppermute | solution.py:150
  42.5 13.2 %collective-permute-start.8 = (f32[16,2304]{1,0:T(8,128)}, f32[16,2304]{1,0:T(8,128)S(1)}, u32[]{:S(2)}, u32[]{:S(2)}) collective-permute-start(f32[16,2304]{1,0:T(8,128)} %get-tuple-element.25), channel_id=1, source_target_pairs={{0,2},{1,3},{2,4},{3,5},{4,6},{5,7},{6,8},{7,9},{8,10},{9,11},{10,... | collective-permute-start | bytes 442376 | tf_op jit(solution)/shard_map/ppermute | solution.py:150
  50.1 9.0 %collective-permute-start.9 = (f32[16,2304]{1,0:T(8,128)}, f32[16,2304]{1,0:T(8,128)S(1)}, u32[]{:S(2)}, u32[]{:S(2)}) collective-permute-start(f32[16,2304]{1,0:T(8,128)} %get-tuple-element.26), channel_id=1, source_target_pairs={{2,0},{3,1},{4,2},{5,3},{6,4},{7,5},{8,6},{9,7},{10,8},{11,9},{12,... | collective-permute-start | bytes 442376 | tf_op jit(solution)/shard_map/ppermute | solution.py:150
  55.7 3.4 %copy-start.5 = (f32[16,2304]{1,0:T(8,128)}, f32[16,2304]{1,0:T(8,128)S(1)}, u32[]{:S(2)}) copy-start(f32[16,2304]{1,0:T(8,128)S(1)} %collective-permute-done.5.refs_1_) | copy-start | bytes 442372
  55.7 3.4 %copy-start.6 = (f32[16,2304]{1,0:T(8,128)}, f32[16,2304]{1,0:T(8,128)S(1)}, u32[]{:S(2)}) copy-start(f32[16,2304]{1,0:T(8,128)S(1)} %collective-permute-done.6.refs_2_) | copy-start | bytes 442372
  55.8 3.4 %copy-start.7 = (f32[16,2304]{1,0:T(8,128)}, f32[16,2304]{1,0:T(8,128)S(1)}, u32[]{:S(2)}) copy-start(f32[16,2304]{1,0:T(8,128)S(1)} %collective-permute-done.7.refs_3_) | copy-start | bytes 442372
  55.8 3.3 %copy-start.8 = (f32[16,2304]{1,0:T(8,128)}, f32[16,2304]{1,0:T(8,128)S(1)}, u32[]{:S(2)}) copy-start(f32[16,2304]{1,0:T(8,128)S(1)} %collective-permute-done.8.refs_4_) | copy-start | bytes 442372
  59.1 0.7 %copy-start.9 = (f32[16,2304]{1,0:T(8,128)}, f32[16,2304]{1,0:T(8,128)S(1)}, u32[]{:S(2)}) copy-start(f32[16,2304]{1,0:T(8,128)S(1)} %collective-permute-done.9.refs_5_) | copy-start | bytes 442372

commit v3 on v2

--- a/solution.py
+++ b/solution.py
@@ -1,6 +1,7 @@
 import functools
 
 import jax
+import numpy as np
 import jax.numpy as jnp
 from jax import lax
 from jax.experimental import pallas as pl
@@ -13,14 +14,24 @@
 TN = (((0,), (0,)), ((), ()))
 
 
-def peer_shifts(n):
-    return (n // 2, 1, -1, 2, -2)
+def pairings(n):
+    half = n // 2
+    return (
+        lambda d, xp: (d + half) % n,
+        lambda d, xp: d ^ 1,
+        lambda d, xp: xp.where(d % 2 == 1, d + 1, d - 1),
+        lambda d, xp: xp.where(d % 4 < 2, d + 2, d - 2),
+        lambda d, xp: xp.where(d % 4 < 2, d - 2, d + 2),
+    )
 
 
-def permutation(n, shift):
-    if shift == n // 2:
-        return [(p, (p + shift) % n) for p in range(n)]
-    return [(p, p + shift) for p in range(n) if 0 <= p + shift < n]
+def pair_list(n, partner):
+    pairs = []
+    for d in range(n):
+        p = int(partner(d, np))
+        if 0 <= p < n and p != d:
+            pairs.append((d, p))
+    return pairs
 
 
 def select_kernel(groups, hslot, pulses, values_ref, select_ref, *out_refs):
@@ -113,12 +124,12 @@
     levels, pulses, capacity = concentration.shape
     hslot = send_cells.shape[2]
     nbr = flux_weight.shape[0]
-    shifts = peer_shifts(n)
-    groups = len(shifts)
+    partners = pairings(n)
+    groups = len(partners)
     me = lax.axis_index("cells")
     f32 = jnp.float32
 
-    peers = (me + jnp.array(shifts, dtype=jnp.int32)) % n
+    peers = jnp.clip(jnp.stack([partner(me, jnp) for partner in partners]), 0, n - 1)
     picked = send_cells[0][peers].reshape(groups * hslot)
     select = (picked[:, None] == jnp.arange(capacity, dtype=jnp.int32)[None, :]).astype(f32)
 
@@ -128,10 +139,9 @@
     beyond = halo_index - capacity
     sender = beyond // hslot
     place = beyond % hslot
-    shift = (me - sender) % n
     group = jnp.full(halo_index.shape, -1, dtype=jnp.int32)
-    for g, s in enumerate(shifts):
-        group = jnp.where(shift == s % n, g, group)
+    for g, partner in enumerate(partners):
+        group = jnp.where(sender == partner(me, jnp), g, group)
     local_col = jnp.where(beyond < 0, halo_index, -1)
     remote_col = jnp.where((beyond >= 0) & (group >= 0), group * hslot + place, -1)
     onehot_local = (local_col[:, None, :] == jnp.arange(capacity)[None, :, None]).astype(f32)
@@ -147,8 +157,8 @@
 
     for sweep in range(STEPS):
         incoming = [
-            lax.ppermute(outgoing[g], "cells", perm=permutation(n, s))
-            for g, s in enumerate(shifts)
+            lax.ppermute(outgoing[g], "cells", perm=pair_list(n, partner))
+            for g, partner in enumerate(partners)
         ]
         partial = local_part(values, local_matrix, weight_sum, vertical_mixing)
         values, outgoing = finish(

time: 64.2 us -> 54.6 us (0.85)
  the two profiles are of different devices: /device:TPU:6 before, /device:TPU:0 now
where the time goes in v3:
time: 54.6 us; the launch traced here: 54.2 us
  Pallas kernels  19.8 us (36%)
  starting transfers between devices  19.6 us (36%)
  waiting for transfers between devices  4.77 us (9%)
  other arithmetic  4.69 us (9%)
  local copies, waits for them, and re-layouts  4.35 us (8%)
  between operations  0.88 us (2%)
    ppermute x10, starting transfers between devices, per_device(): lax.ppermute(outgoing[g], 'cells', perm=pair_list(n, partner))  19.6 us
    pallas_call x2, Pallas kernels, finish(): pl.pallas_call(functools.partial(finish_kernel, groups, hslot, pulses, se...  8.9 us
    pallas_call x2, Pallas kernels, local_part(): pl.pallas_call(local_kernel, out_shape=jax.ShapeDtypeStruct(values.shape,...  7.48 us
    ppermute x10, waiting for transfers between devices, per_device(): lax.ppermute(outgoing[g], 'cells', perm=pair_list(n, partner))  4.77 us
    unnamed x27, local copies, waits for them, and re-layouts  3.52 us
    pallas_call x1, Pallas kernels, gather_send(): pl.pallas_call(functools.partial(select_kernel, groups, hslot, pulses), o...  3.46 us
    add x1, other arithmetic, per_device(): sum((flux_weight[k][:, None, :] * onehot_local[k][None] for k in range(nb...  1.14 us
  transfers between devices with their start and end apart: 10, of which 1 were waited for; matrix products, arithmetic and copies ran while one was open for 8% of the time, Pallas kernels for 14%

profile of v3, /device:TPU:0, one launch (start us, length us, event | category | flops | bytes accessed | tf_op | source)
XLA Modules:
  0.0 54.2 jit_solution(3936008344204791537)
XLA Ops:
  0.0 0.1 stack.23
  0.1 0.8 %copy.16 = s32[1,32,16]{2,1,0:T(8,128)S(1)} copy(s32[1,32,16]{1,2,0:T(8,128)} %param.12) | data formatting | bytes 4096 | tf_op args[5]
  0.9 0.6 %gather_fusion = s32[5,16]{1,0:T(8,128)S(1)} fusion(s32[32,16]{1,0:T(8,128)S(1)} %bitcast.74, s32[1024]{0:T(1024)S(1)} %pad_clamp_fusion), kind=kCustom, calls=%fused_computation | custom fusion | bytes 660 | tf_op jit(solution)/shard_map/gather | solution.py:133
  1.5 0.1 eq.90
  1.5 0.7 %fusion.2.select_ref.refs_9_ = f32[80,128]{1,0:T(8,128)} fusion(s32[80]{0:T(128)S(1)} %eq.90), kind=kLoop, calls=%fused_computation.24 | loop fusion | flops 20480 | bytes 41280 | tf_op jit(solution)/shard_map/convert_element_type | solution.py:134
  2.2 3.5 %gather_send.1 = (f32[16,2304]{1,0:T(8,128)}, f32[16,2304]{1,0:T(8,128)}, f32[16,2304]{1,0:T(8,128)}, f32[16,2304]{1,0:T(8,128)}, f32[16,2304]{1,0:T(8,128)}) custom-call(f32[9,256,128]{2,1,0:T(8,128)} %values_ref.3, f32[80,128]{1,0:T(8,128)} %fusion.2.select_ref.refs_9_), custom_call_target="tpu_custom_call" | custom-call | tf_op jit(solution)/shard_map/gather_send/pallas_call | solution.py:49
  5.7 4.0 %collective-permute-start = (f32[16,2304]{1,0:T(8,128)}, f32[16,2304]{1,0:T(8,128)S(1)}, u32[]{:S(2)}, u32[]{:S(2)}) collective-permute-start(f32[16,2304]{1,0:T(8,128)} %get-tuple-element.16), channel_id=1, source_target_pairs={{0,16},{1,17},{2,18},{3,19},{4,20},{5,21},{6,22},{7,23},{8,24},{9,... | collective-permute-start | bytes 442376 | tf_op jit(solution)/shard_map/ppermute | solution.py:160
  9.7 0.0 collective-permute-start.1
  9.7 0.7 %collective-permute-start.2 = (f32[16,2304]{1,0:T(8,128)}, f32[16,2304]{1,0:T(8,128)S(1)}, u32[]{:S(2)}, u32[]{:S(2)}) collective-permute-start(f32[16,2304]{1,0:T(8,128)} %get-tuple-element.18), channel_id=1, source_target_pairs={{1,2},{2,1},{3,4},{4,3},{5,6},{6,5},{7,8},{8,7},{9,10},{10,9},{11,... | collective-permute-start | bytes 442376 | tf_op jit(solution)/shard_map/ppermute | solution.py:160
  10.4 3.4 %collective-permute-start.3 = (f32[16,2304]{1,0:T(8,128)}, f32[16,2304]{1,0:T(8,128)S(1)}, u32[]{:S(2)}, u32[]{:S(2)}) collective-permute-start(f32[16,2304]{1,0:T(8,128)} %get-tuple-element.19), channel_id=1, source_target_pairs={{0,2},{1,3},{2,0},{3,1},{4,6},{5,7},{6,4},{7,5},{8,10},{9,11},{10,... | collective-permute-start | bytes 442376 | tf_op jit(solution)/shard_map/ppermute | solution.py:160
  13.8 0.7 %collective-permute-start.4 = (f32[16,2304]{1,0:T(8,128)}, f32[16,2304]{1,0:T(8,128)S(1)}, u32[]{:S(2)}, u32[]{:S(2)}) collective-permute-start(f32[16,2304]{1,0:T(8,128)} %get-tuple-element.20), channel_id=1, source_target_pairs={{2,4},{3,5},{4,2},{5,3},{6,8},{7,9},{8,6},{9,7},{10,12},{11,13},{1... | collective-permute-start | bytes 442376 | tf_op jit(solution)/shard_map/ppermute | solution.py:160
  14.5 0.0 copy-done.10
  14.6 0.6 %add_add_fusion.weight_sum_ref = f32[9,128]{1,0:T(8,128)} fusion(f32[1,9,128]{2,0,1:T(1,128)S(1)} %get-tuple-element.43, f32[1,9,128]{2,0,1:T(1,128)S(1)} %get-tuple-element.49, f32[1,9,128]{2,0,1:T(1,128)S(1)} %get-tuple-element.48, f32[1,9,128]{2,0,1:T(1,128)S(1)} %get-tuple-element.47, f32[1,9,128]{2,0,1:T(1,128)S(1)} %get-tuple-element.46, ...), kind=kLoop, calls=%fused_computation.33 | loop fusion | flops 8064 | bytes 41472 | tf_op jit(solution)/shard_map/add | solution.py:153
  15.2 0.0 copy-done.12
  15.4 0.0 copy-start.11
  15.4 1.0 %multiply_add_fusion.1.refs_6_ = f32[9,80,128]{2,1,0:T(8,128)} fusion(f32[80,128]{1,0:T(8,128)S(1)} %get-tuple-element.36, f32[9,128]{1,0:T(8,128)S(1)} %get-tuple-element.53, f32[80,128]{1,0:T(8,128)S(1)} %get-tuple-element.37, f32[9,128]{1,0:T(8,128)S(1)} %get-tuple-element.54, f32[80,128]{1,0:T(8,128)S(1)} %get-tuple-element.38, ...), kind=kLoop, calls=%fused_computation.4 | loop fusion | flops 1382400 | bytes 733184 | tf_op jit(solution)/shard_map/add | solution.py:152
  16.4 1.1 %multiply_add_fusion.local_ref = f32[9,128,128]{2,1,0:T(8,128)} fusion(f32[128,128]{1,0:T(8,128)S(1)} %get-tuple-element.28, f32[9,128]{1,0:T(8,128)S(1)} %get-tuple-element.53, f32[128,128]{1,0:T(8,128)S(1)} %get-tuple-element.29, f32[9,128]{1,0:T(8,128)S(1)} %get-tuple-element.54, f32[128,128]{1,0:T(8,128)S(1)} %get-tuple-element.30, ...), kind=kLoop, calls=%fused_computation.1 | loop fusion | flops 2211840 | bytes 1150976 | tf_op jit(solution)/shard_map/add | solution.py:151
  17.5 0.0 copy-done.11
  17.5 0.6 %broadcast_subtract_fusion.refs_7_ = f32[9,128]{1,0:T(8,128)} fusion(f32[9,128]{1,0:T(8,128)S(1)} %copy-done.11), kind=kLoop, calls=%fused_computation.42 | loop fusion | flops 1152 | bytes 9216 | tf_op jit(solution)/shard_map/sub | solution.py:156
  18.7 3.7 %local_part.2.refs_0_ = f32[9,256,128]{2,1,0:T(8,128)} custom-call(f32[9,256,128]{2,1,0:T(8,128)} %values_ref.3, f32[9,128,128]{2,1,0:T(8,128)} %multiply_add_fusion.local_ref, f32[9,128]{1,0:T(8,128)} %add_add_fusion.weight_sum_ref, f32[8,128]{1,0:T(8,128)} %mixing_ref.3), custom_call_target="tpu_custom_call" | custom-call | tf_op jit(solution)/shard_map/local_part/pallas_call | solution.py:73
  22.5 0.6 %compare_convert_fusion.refs_8_ = f32[1,128]{1,0:T(1,128)} fusion(s32[]{:T(128)} %bitcast.73), kind=kLoop, calls=%fused_computation.48 | loop fusion | flops 256 | bytes 516 | tf_op jit(solution)/shard_map/convert_element_type | solution.py:155
  23.1 0.0 collective-permute-done.refs_1_
  23.1 0.0 collective-permute-done.1.refs_2_
  23.1 0.0 collective-permute-done.2.refs_3_
  23.1 0.0 copy-start.2
  23.1 0.0 collective-permute-done.3.refs_4_
  23.1 0.0 collective-permute-done.4.refs_5_
  23.1 0.6 %copy-done = f32[16,2304]{1,0:T(8,128)} copy-done((f32[16,2304]{1,0:T(8,128)}, f32[16,2304]{1,0:T(8,128)S(1)}, u32[]{:S(2)}) %copy-start) | copy-done | bytes 147480
  23.7 0.1 copy-done.1
  23.8 0.0 copy-done.2
  23.8 0.1 copy-done.3
  23.9 0.7 %copy-done.4 = f32[16,2304]{1,0:T(8,128)} copy-done((f32[16,2304]{1,0:T(8,128)}, f32[16,2304]{1,0:T(8,128)S(1)}, u32[]{:S(2)}) %copy-start.4) | copy-done | bytes 147480
  24.6 5.0 %finish_send.1 = (f32[9,256,128]{2,1,0:T(8,128)}, f32[16,2304]{1,0:T(8,128)}, f32[16,2304]{1,0:T(8,128)}, f32[16,2304]{1,0:T(8,128)}, f32[16,2304]{1,0:T(8,128)}, /*index=5*/f32[16,2304]{1,0:T(8,128)}) custom-call(f32[9,256,128]{2,1,0:T(8,128)} %local_part.2.refs_0_, f32[16,2304]{1,0:T(8,128)} %copy-done, f32[16,2304]{1,0:T(8,128)} %copy-done.1, ...), custom_call_target="tpu_custom_call" | custom-call | tf_op jit(solution)/shard_map/finish_send/pallas_call | solution.py:112
  29.6 6.1 %collective-permute-start.5 = (f32[16,2304]{1,0:T(8,128)}, f32[16,2304]{1,0:T(8,128)S(1)}, u32[]{:S(2)}, u32[]{:S(2)}) collective-permute-start(f32[16,2304]{1,0:T(8,128)} %get-tuple-element.22), channel_id=1, source_target_pairs={{0,16},{1,17},{2,18},{3,19},{4,20},{5,21},{6,22},{7,23},{8,24},{9,... | collective-permute-start | bytes 442376 | tf_op jit(solution)/shard_map/ppermute | solution.py:160
  35.7 0.0 collective-permute-start.6
  35.7 0.7 %collective-permute-start.7 = (f32[16,2304]{1,0:T(8,128)}, f32[16,2304]{1,0:T(8,128)S(1)}, u32[]{:S(2)}, u32[]{:S(2)}) collective-permute-start(f32[16,2304]{1,0:T(8,128)} %get-tuple-element.24), channel_id=1, source_target_pairs={{1,2},{2,1},{3,4},{4,3},{5,6},{6,5},{7,8},{8,7},{9,10},{10,9},{11,... | collective-permute-start | bytes 442376 | tf_op jit(solution)/shard_map/ppermute | solution.py:160
  36.4 3.4 %collective-permute-start.8 = (f32[16,2304]{1,0:T(8,128)}, f32[16,2304]{1,0:T(8,128)S(1)}, u32[]{:S(2)}, u32[]{:S(2)}) collective-permute-start(f32[16,2304]{1,0:T(8,128)} %get-tuple-element.25), channel_id=1, source_target_pairs={{0,2},{1,3},{2,0},{3,1},{4,6},{5,7},{6,4},{7,5},{8,10},{9,11},{10,... | collective-permute-start | bytes 442376 | tf_op jit(solution)/shard_map/ppermute | solution.py:160
  39.8 0.7 %collective-permute-start.9 = (f32[16,2304]{1,0:T(8,128)}, f32[16,2304]{1,0:T(8,128)S(1)}, u32[]{:S(2)}, u32[]{:S(2)}) collective-permute-start(f32[16,2304]{1,0:T(8,128)} %get-tuple-element.26), channel_id=1, source_target_pairs={{2,4},{3,5},{4,2},{5,3},{6,8},{7,9},{8,6},{9,7},{10,12},{11,13},{1... | collective-permute-start | bytes 442376 | tf_op jit(solution)/shard_map/ppermute | solution.py:160
  40.5 3.7 %local_part.3.refs_0_ = f32[9,256,128]{2,1,0:T(8,128)} custom-call(f32[9,256,128]{2,1,0:T(8,128)} %get-tuple-element.21.values_ref, f32[9,128,128]{2,1,0:T(8,128)} %multiply_add_fusion.local_ref, f32[9,128]{1,0:T(8,128)} %add_add_fusion.weight_sum_ref, f32[8,128]{1,0:T(8,128)} %mixing_ref.3), custom_call_target="tpu_custom_call" | custom-call | tf_op jit(solution)/shard_map/local_part/pallas_call | solution.py:73
  44.2 0.0 collective-permute-done.5.refs_1_
  44.2 0.0 collective-permute-done.6.refs_2_
  44.2 0.0 collective-permute-done.7.refs_3_
  44.3 4.8 %collective-permute-done.8.refs_4_ = f32[16,2304]{1,0:T(8,128)S(1)} collective-permute-done((f32[16,2304]{1,0:T(8,128)}, f32[16,2304]{1,0:T(8,128)S(1)}, u32[]{:S(2)}, u32[]{:S(2)}) %collective-permute-start.8) | collective-permute-done | bytes 147488 | tf_op jit(solution)/shard_map/ppermute | solution.py:160
  49.0 0.0 collective-permute-done.9.refs_5_
  49.0 0.0 copy-done.6
  49.0 0.6 %copy-done.8 = f32[16,2304]{1,0:T(8,128)} copy-done((f32[16,2304]{1,0:T(8,128)}, f32[16,2304]{1,0:T(8,128)S(1)}, u32[]{:S(2)}) %copy-start.8) | copy-done | bytes 147480
  49.7 0.6 %copy-done.9 = f32[16,2304]{1,0:T(8,128)} copy-done((f32[16,2304]{1,0:T(8,128)}, f32[16,2304]{1,0:T(8,128)S(1)}, u32[]{:S(2)}) %copy-start.9) | copy-done | bytes 147480
  50.3 3.9 %finish.1 = f32[9,256,128]{2,1,0:T(8,128)} custom-call(f32[9,256,128]{2,1,0:T(8,128)} %local_part.3.refs_0_, f32[16,2304]{1,0:T(8,128)} %copy-done.5, f32[16,2304]{1,0:T(8,128)} %copy-done.6, f32[16,2304]{1,0:T(8,128)} %copy-done.7, f32[16,2304]{1,0:T(8,128)} %copy-done.8, f32[16,2304]{1,0:T(8,128)} %copy-done.9, f32[9,80,128]{2,1,0:T(8,128)} %multiply_add_fusion.1.refs_6_, ...), custom_call_target="tpu_custom_call" | custom-call | tf_op jit(solution)/shard_map/finish/pallas_call | solution.py:112
  (25 shorter events, 0.2 us)
Async XLA Ops:
  0.0 14.5 %copy-start.10 = (f32[8,9,128]{2,0,1:T(8,128)S(1)}, f32[8,9,128]{2,0,1:T(8,128)}, u32[]{:S(2)}) copy-start(f32[8,9,128]{2,0,1:T(8,128)} %param.8) | copy-start | bytes 110596
  0.0 15.2 %copy-start.12 = (s32[8,128]{1,0:T(8,128)S(1)}, s32[8,128]{1,0:T(8,128)}, u32[]{:S(2)}) copy-start(s32[8,128]{1,0:T(8,128)} %param.11) | copy-start | bytes 12292
  5.7 17.4 %collective-permute-start = (f32[16,2304]{1,0:T(8,128)}, f32[16,2304]{1,0:T(8,128)S(1)}, u32[]{:S(2)}, u32[]{:S(2)}) collective-permute-start(f32[16,2304]{1,0:T(8,128)} %get-tuple-element.16), channel_id=1, source_target_pairs={{0,16},{1,17},{2,18},{3,19},{4,20},{5,21},{6,22},{7,23},{8,24},{9,... | collective-permute-start | bytes 442376 | tf_op jit(solution)/shard_map/ppermute | solution.py:160
  9.7 13.3 %collective-permute-start.1 = (f32[16,2304]{1,0:T(8,128)}, f32[16,2304]{1,0:T(8,128)S(1)}, u32[]{:S(2)}, u32[]{:S(2)}) collective-permute-start(f32[16,2304]{1,0:T(8,128)} %get-tuple-element.17), channel_id=1, source_target_pairs={{0,1},{1,0},{2,3},{3,2},{4,5},{5,4},{6,7},{7,6},{8,9},{9,8},{10,11... | collective-permute-start | bytes 442376 | tf_op jit(solution)/shard_map/ppermute | solution.py:160
  9.7 13.4 %collective-permute-start.2 = (f32[16,2304]{1,0:T(8,128)}, f32[16,2304]{1,0:T(8,128)S(1)}, u32[]{:S(2)}, u32[]{:S(2)}) collective-permute-start(f32[16,2304]{1,0:T(8,128)} %get-tuple-element.18), channel_id=1, source_target_pairs={{1,2},{2,1},{3,4},{4,3},{5,6},{6,5},{7,8},{8,7},{9,10},{10,9},{11,... | collective-permute-start | bytes 442376 | tf_op jit(solution)/shard_map/ppermute | solution.py:160
  10.4 12.7 %collective-permute-start.3 = (f32[16,2304]{1,0:T(8,128)}, f32[16,2304]{1,0:T(8,128)S(1)}, u32[]{:S(2)}, u32[]{:S(2)}) collective-permute-start(f32[16,2304]{1,0:T(8,128)} %get-tuple-element.19), channel_id=1, source_target_pairs={{0,2},{1,3},{2,0},{3,1},{4,6},{5,7},{6,4},{7,5},{8,10},{9,11},{10,... | collective-permute-start | bytes 442376 | tf_op jit(solution)/shard_map/ppermute | solution.py:160
  13.8 9.3 %collective-permute-start.4 = (f32[16,2304]{1,0:T(8,128)}, f32[16,2304]{1,0:T(8,128)S(1)}, u32[]{:S(2)}, u32[]{:S(2)}) collective-permute-start(f32[16,2304]{1,0:T(8,128)} %get-tuple-element.20), channel_id=1, source_target_pairs={{2,4},{3,5},{4,2},{5,3},{6,8},{7,9},{8,6},{9,7},{10,12},{11,13},{1... | collective-permute-start | bytes 442376 | tf_op jit(solution)/shard_map/ppermute | solution.py:160
  15.4 2.1 %copy-start.11 = (f32[9,128]{1,0:T(8,128)S(1)}, f32[9,128]{1,0:T(8,128)}, u32[]{:S(2)}) copy-start(f32[9,128]{1,0:T(8,128)} %param.10) | copy-start | bytes 13828
  23.1 0.6 %copy-start = (f32[16,2304]{1,0:T(8,128)}, f32[16,2304]{1,0:T(8,128)S(1)}, u32[]{:S(2)}) copy-start(f32[16,2304]{1,0:T(8,128)S(1)} %collective-permute-done.refs_1_) | copy-start | bytes 442372
  23.1 0.7 %copy-start.1 = (f32[16,2304]{1,0:T(8,128)}, f32[16,2304]{1,0:T(8,128)S(1)}, u32[]{:S(2)}) copy-start(f32[16,2304]{1,0:T(8,128)S(1)} %collective-permute-done.1.refs_2_) | copy-start | bytes 442372
  23.1 0.7 %copy-start.2 = (f32[16,2304]{1,0:T(8,128)}, f32[16,2304]{1,0:T(8,128)S(1)}, u32[]{:S(2)}) copy-start(f32[16,2304]{1,0:T(8,128)S(1)} %collective-permute-done.2.refs_3_) | copy-start | bytes 442372
  23.1 0.8 %copy-start.3 = (f32[16,2304]{1,0:T(8,128)}, f32[16,2304]{1,0:T(8,128)S(1)}, u32[]{:S(2)}) copy-start(f32[16,2304]{1,0:T(8,128)S(1)} %collective-permute-done.3.refs_4_) | copy-start | bytes 442372
  23.9 0.7 %copy-start.4 = (f32[16,2304]{1,0:T(8,128)}, f32[16,2304]{1,0:T(8,128)S(1)}, u32[]{:S(2)}) copy-start(f32[16,2304]{1,0:T(8,128)S(1)} %collective-permute-done.4.refs_5_) | copy-start | bytes 442372
  29.6 14.6 %collective-permute-start.5 = (f32[16,2304]{1,0:T(8,128)}, f32[16,2304]{1,0:T(8,128)S(1)}, u32[]{:S(2)}, u32[]{:S(2)}) collective-permute-start(f32[16,2304]{1,0:T(8,128)} %get-tuple-element.22), channel_id=1, source_target_pairs={{0,16},{1,17},{2,18},{3,19},{4,20},{5,21},{6,22},{7,23},{8,24},{9,... | collective-permute-start | bytes 442376 | tf_op jit(solution)/shard_map/ppermute | solution.py:160
  35.7 8.5 %collective-permute-start.6 = (f32[16,2304]{1,0:T(8,128)}, f32[16,2304]{1,0:T(8,128)S(1)}, u32[]{:S(2)}, u32[]{:S(2)}) collective-permute-start(f32[16,2304]{1,0:T(8,128)} %get-tuple-element.23), channel_id=1, source_target_pairs={{0,1},{1,0},{2,3},{3,2},{4,5},{5,4},{6,7},{7,6},{8,9},{9,8},{10,11... | collective-permute-start | bytes 442376 | tf_op jit(solution)/shard_map/ppermute | solution.py:160
  35.7 8.5 %collective-permute-start.7 = (f32[16,2304]{1,0:T(8,128)}, f32[16,2304]{1,0:T(8,128)S(1)}, u32[]{:S(2)}, u32[]{:S(2)}) collective-permute-start(f32[16,2304]{1,0:T(8,128)} %get-tuple-element.24), channel_id=1, source_target_pairs={{1,2},{2,1},{3,4},{4,3},{5,6},{6,5},{7,8},{8,7},{9,10},{10,9},{11,... | collective-permute-start | bytes 442376 | tf_op jit(solution)/shard_map/ppermute | solution.py:160
  36.4 12.6 %collective-permute-start.8 = (f32[16,2304]{1,0:T(8,128)}, f32[16,2304]{1,0:T(8,128)S(1)}, u32[]{:S(2)}, u32[]{:S(2)}) collective-permute-start(f32[16,2304]{1,0:T(8,128)} %get-tuple-element.25), channel_id=1, source_target_pairs={{0,2},{1,3},{2,0},{3,1},{4,6},{5,7},{6,4},{7,5},{8,10},{9,11},{10,... | collective-permute-start | bytes 442376 | tf_op jit(solution)/shard_map/ppermute | solution.py:160
  39.8 9.2 %collective-permute-start.9 = (f32[16,2304]{1,0:T(8,128)}, f32[16,2304]{1,0:T(8,128)S(1)}, u32[]{:S(2)}, u32[]{:S(2)}) collective-permute-start(f32[16,2304]{1,0:T(8,128)} %get-tuple-element.26), channel_id=1, source_target_pairs={{2,4},{3,5},{4,2},{5,3},{6,8},{7,9},{8,6},{9,7},{10,12},{11,13},{1... | collective-permute-start | bytes 442376 | tf_op jit(solution)/shard_map/ppermute | solution.py:160
  44.2 4.8 %copy-start.5 = (f32[16,2304]{1,0:T(8,128)}, f32[16,2304]{1,0:T(8,128)S(1)}, u32[]{:S(2)}) copy-start(f32[16,2304]{1,0:T(8,128)S(1)} %collective-permute-done.5.refs_1_) | copy-start | bytes 442372
  44.2 4.8 %copy-start.6 = (f32[16,2304]{1,0:T(8,128)}, f32[16,2304]{1,0:T(8,128)S(1)}, u32[]{:S(2)}) copy-start(f32[16,2304]{1,0:T(8,128)S(1)} %collective-permute-done.6.refs_2_) | copy-start | bytes 442372
  44.2 4.8 %copy-start.7 = (f32[16,2304]{1,0:T(8,128)}, f32[16,2304]{1,0:T(8,128)S(1)}, u32[]{:S(2)}) copy-start(f32[16,2304]{1,0:T(8,128)S(1)} %collective-permute-done.7.refs_3_) | copy-start | bytes 442372
  49.0 0.7 %copy-start.8 = (f32[16,2304]{1,0:T(8,128)}, f32[16,2304]{1,0:T(8,128)S(1)}, u32[]{:S(2)}) copy-start(f32[16,2304]{1,0:T(8,128)S(1)} %collective-permute-done.8.refs_4_) | copy-start | bytes 442372
  49.7 0.7 %copy-start.9 = (f32[16,2304]{1,0:T(8,128)}, f32[16,2304]{1,0:T(8,128)S(1)}, u32[]{:S(2)}) copy-start(f32[16,2304]{1,0:T(8,128)S(1)} %collective-permute-done.9.refs_5_) | copy-start | bytes 442372

commit v4 on v3

--- a/solution.py
+++ b/solution.py
@@ -34,21 +34,38 @@
     return pairs
 
 
-def select_kernel(groups, hslot, pulses, values_ref, select_ref, *out_refs):
+LEVEL_BLOCKS = 3
+PULSE_BLOCKS = 2
+
+
+def level_block(levels):
+    return levels // LEVEL_BLOCKS if levels % LEVEL_BLOCKS == 0 else levels
+
+
+def full_spec(shape):
+    return pl.BlockSpec(shape, lambda i: (0,) * len(shape))
+
+
+def select_kernel(groups, hslot, values_ref, select_ref, *out_refs):
     select = select_ref[...]
     for level in range(values_ref.shape[0]):
         block = lax.dot_general(
             select, values_ref[level], NT, precision=HIGHEST, preferred_element_type=jnp.float32
         )
         for g in range(groups):
-            out_refs[g][:, level * pulses : (level + 1) * pulses] = block[g * hslot : (g + 1) * hslot]
+            out_refs[g][level] = block[g * hslot : (g + 1) * hslot]
 
 
 def gather_send(values, select, groups, hslot):
     levels, pulses, capacity = values.shape
+    lb = level_block(levels)
+    send_spec = pl.BlockSpec((lb, hslot, pulses), lambda i: (i, 0, 0))
     return pl.pallas_call(
-        functools.partial(select_kernel, groups, hslot, pulses),
-        out_shape=[jax.ShapeDtypeStruct((hslot, levels * pulses), jnp.float32)] * groups,
+        functools.partial(select_kernel, groups, hslot),
+        out_shape=[jax.ShapeDtypeStruct((levels, hslot, pulses), jnp.float32)] * groups,
+        grid=(levels // lb,),
+        in_specs=[pl.BlockSpec((lb, pulses, capacity), lambda i: (i, 0, 0)), full_spec(select.shape)],
+        out_specs=[send_spec] * groups,
         interpret=INTERPRET,
         name="gather_send",
     )(values, select)
@@ -70,15 +87,26 @@
 
 
 def local_part(values, local_matrix, weight_sum, mixing):
+    levels, pulses, capacity = values.shape
+    pb = pulses // PULSE_BLOCKS if pulses % (8 * PULSE_BLOCKS) == 0 else pulses
+    value_spec = pl.BlockSpec((levels, pb, capacity), lambda i: (0, i, 0))
     return pl.pallas_call(
         local_kernel,
         out_shape=jax.ShapeDtypeStruct(values.shape, jnp.float32),
+        grid=(pulses // pb,),
+        in_specs=[
+            value_spec,
+            full_spec(local_matrix.shape),
+            full_spec(weight_sum.shape),
+            full_spec(mixing.shape),
+        ],
+        out_specs=value_spec,
         interpret=INTERPRET,
         name="local_part",
     )(values, local_matrix, weight_sum, mixing)
 
 
-def finish_kernel(groups, hslot, pulses, send, *refs):
+def finish_kernel(groups, hslot, send, *refs):
     partial_ref = refs[0]
     incoming = refs[1 : 1 + groups]
     remote_ref, keep_ref, living_ref, select_ref = refs[1 + groups : 5 + groups]
@@ -86,12 +114,11 @@
     send_refs = refs[6 + groups :]
     living = living_ref[...] > 0.5
     for level in range(partial_ref.shape[0]):
-        columns = slice(level * pulses, (level + 1) * pulses)
-        received = jnp.concatenate([incoming[g][:, columns] for g in range(groups)], axis=0)
+        received = jnp.concatenate([incoming[g][level] for g in range(groups)], axis=0)
         far = lax.dot_general(
             received, remote_ref[level], TN, precision=HIGHEST, preferred_element_type=jnp.float32
         )
-        x = (partial_ref[level] + far) * keep_ref[level : level + 1, :]
+        x = (partial_ref[level] + far) * keep_ref[level]
         x = jnp.where(living, x, 0.0)
         out_ref[level] = x
         if send:
@@ -99,19 +126,37 @@
                 select_ref[...], x, NT, precision=HIGHEST, preferred_element_type=jnp.float32
             )
             for g in range(groups):
-                send_refs[g][:, columns] = block[g * hslot : (g + 1) * hslot]
+                send_refs[g][level] = block[g * hslot : (g + 1) * hslot]
 
 
 def finish(partial, incoming, remote_matrix, keep, living, select, send):
     levels, pulses, capacity = partial.shape
     groups = len(incoming)
-    hslot = incoming[0].shape[0]
+    hslot = incoming[0].shape[1]
+    lb = level_block(levels)
+    value_spec = pl.BlockSpec((lb, pulses, capacity), lambda i: (i, 0, 0))
+    send_spec = pl.BlockSpec((lb, hslot, pulses), lambda i: (i, 0, 0))
     shapes = [jax.ShapeDtypeStruct(partial.shape, jnp.float32)]
+    out_specs = [value_spec]
     if send:
-        shapes += [jax.ShapeDtypeStruct((hslot, levels * pulses), jnp.float32)] * groups
+        shapes += [jax.ShapeDtypeStruct((levels, hslot, pulses), jnp.float32)] * groups
+        out_specs += [send_spec] * groups
+    in_specs = (
+        [value_spec]
+        + [send_spec] * groups
+        + [
+            pl.BlockSpec((lb,) + remote_matrix.shape[1:], lambda i: (i, 0, 0)),
+            pl.BlockSpec((lb,) + keep.shape[1:], lambda i: (i, 0, 0)),
+            full_spec(living.shape),
+            full_spec(select.shape),
+        ]
+    )
     outs = pl.pallas_call(
-        functools.partial(finish_kernel, groups, hslot, pulses, send),
+        functools.partial(finish_kernel, groups, hslot, send),
         out_shape=shapes,
+        grid=(levels // lb,),
+        in_specs=in_specs,
+        out_specs=out_specs,
         interpret=INTERPRET,
         name="finish_send" if send else "finish",
     )(partial, *incoming, remote_matrix, keep, living, select)
@@ -153,7 +198,7 @@
     weight_sum = sum(flux_weight[k] for k in range(nbr))
 
     living = (jnp.arange(capacity, dtype=jnp.int32) < live_count[0]).astype(f32)[None, :]
-    keep = 1.0 - deposition
+    keep = (1.0 - deposition)[:, None, :]
 
     for sweep in range(STEPS):
         incoming = [

time: 54.6 us -> 55.7 us (1.020)
  Pallas kernels: 19.8 us -> 20.7 us
  other arithmetic: 4.69 us -> 4.1 us
    pallas_call x3, Pallas kernels: 12.4 us -> 13.5 us  [the longest x2 9.67 us: finish(): pl.pallas_call(functools.partial(finish_kernel, groups, hslot, send), out...]
    broadcast_in_dim x0 -> x1, local copies, waits for them, and re-layouts: none -> 0.6 us  [per_device(): keep = (1.0 - deposition)[:, None, :]]
    sub x1, other arithmetic: 0.6 us -> 0.01 us  [per_device(): keep = (1.0 - deposition)[:, None, :]]
  transfers between devices with their start and end apart: 10 -> 10, of which waited for: 1 -> 2; matrix products, arithmetic and copies ran while one was open for 8% -> 7% of each run, Pallas kernels for 14% -> 13%
where the time goes in v4:
time: 55.7 us; the launch traced here: 55.2 us
  Pallas kernels  20.7 us (37%)
  starting transfers between devices  19.7 us (35%)
  waiting for transfers between devices  4.95 us (9%)
  local copies, waits for them, and re-layouts  4.9 us (9%)
  other arithmetic  4.1 us (7%)
  between operations  0.86 us (2%)
    ppermute x10, starting transfers between devices, per_device(): lax.ppermute(outgoing[g], 'cells', perm=pair_list(n, partner))  19.7 us
    pallas_call x2, Pallas kernels, finish(): pl.pallas_call(functools.partial(finish_kernel, groups, hslot, send), out...  9.67 us
    pallas_call x2, Pallas kernels, local_part(): pl.pallas_call(local_kernel, out_shape=jax.ShapeDtypeStruct(values.shape,...  7.2 us
    ppermute x10, waiting for transfers between devices, per_device(): lax.ppermute(outgoing[g], 'cells', perm=pair_list(n, partner))  4.95 us
    pallas_call x1, Pallas kernels, gather_send(): pl.pallas_call(functools.partial(select_kernel, groups, hslot), out_shape...  3.83 us
    unnamed x27, local copies, waits for them, and re-layouts  3.46 us
    add x1, other arithmetic, per_device(): sum((flux_weight[k][:, None, :] * onehot_local[k][None] for k in range(nb...  1.14 us
  transfers between devices with their start and end apart: 10, of which 2 were waited for; matrix products, arithmetic and copies ran while one was open for 7% of the time, Pallas kernels for 13%

profile of v4, /device:TPU:0, one launch (start us, length us, event | category | flops | bytes accessed | tf_op | source)
XLA Modules:
  0.0 55.2 jit_solution(14350798839704580274)
XLA Ops:
  0.0 0.1 stack.23
  0.1 0.8 %copy.16 = s32[1,32,16]{2,1,0:T(8,128)S(1)} copy(s32[1,32,16]{1,2,0:T(8,128)} %param.12) | data formatting | bytes 4096 | tf_op args[5]
  0.9 0.6 %gather_fusion = s32[5,16]{1,0:T(8,128)S(1)} fusion(s32[32,16]{1,0:T(8,128)S(1)} %bitcast.74, s32[1024]{0:T(1024)S(1)} %pad_clamp_fusion), kind=kCustom, calls=%fused_computation | custom fusion | bytes 660 | tf_op jit(solution)/shard_map/gather | solution.py:178
  1.5 0.1 eq.90
  1.5 0.7 %fusion.2.select_ref.refs_9_ = f32[80,128]{1,0:T(8,128)} fusion(s32[80]{0:T(128)S(1)} %eq.90), kind=kLoop, calls=%fused_computation.24 | loop fusion | flops 20480 | bytes 41280 | tf_op jit(solution)/shard_map/convert_element_type | solution.py:179
  2.2 3.8 %gather_send.1 = (f32[9,16,256]{2,1,0:T(8,128)}, f32[9,16,256]{2,1,0:T(8,128)}, f32[9,16,256]{2,1,0:T(8,128)}, f32[9,16,256]{2,1,0:T(8,128)}, f32[9,16,256]{2,1,0:T(8,128)}) custom-call(f32[9,256,128]{2,1,0:T(8,128)} %values_ref.3, f32[80,128]{1,0:T(8,128)} %fusion.2.select_ref.refs_9_), custom_call_target="tpu_custom_call" | custom-call | tf_op jit(solution)/shard_map/gather_send/pallas_call | solution.py:63
  6.1 4.0 %collective-permute-start = (f32[9,16,256]{2,1,0:T(8,128)}, f32[9,16,256]{2,1,0:T(8,128)S(1)}, u32[]{:S(2)}, u32[]{:S(2)}) collective-permute-start(f32[9,16,256]{2,1,0:T(8,128)} %get-tuple-element.16), channel_id=1, source_target_pairs={{0,16},{1,17},{2,18},{3,19},{4,20},{5,21},{6,22},{7,23},{8,24},{9,... | collective-permute-start | bytes 442376 | tf_op jit(solution)/shard_map/ppermute | solution.py:205
  10.1 0.0 collective-permute-start.1
  10.1 0.7 %collective-permute-start.2 = (f32[9,16,256]{2,1,0:T(8,128)}, f32[9,16,256]{2,1,0:T(8,128)S(1)}, u32[]{:S(2)}, u32[]{:S(2)}) collective-permute-start(f32[9,16,256]{2,1,0:T(8,128)} %get-tuple-element.18), channel_id=1, source_target_pairs={{1,2},{2,1},{3,4},{4,3},{5,6},{6,5},{7,8},{8,7},{9,10},{10,9},{11,... | collective-permute-start | bytes 442376 | tf_op jit(solution)/shard_map/ppermute | solution.py:205
  10.8 3.4 %collective-permute-start.3 = (f32[9,16,256]{2,1,0:T(8,128)}, f32[9,16,256]{2,1,0:T(8,128)S(1)}, u32[]{:S(2)}, u32[]{:S(2)}) collective-permute-start(f32[9,16,256]{2,1,0:T(8,128)} %get-tuple-element.19), channel_id=1, source_target_pairs={{0,2},{1,3},{2,0},{3,1},{4,6},{5,7},{6,4},{7,5},{8,10},{9,11},{10,... | collective-permute-start | bytes 442376 | tf_op jit(solution)/shard_map/ppermute | solution.py:205
  14.2 0.7 %collective-permute-start.4 = (f32[9,16,256]{2,1,0:T(8,128)}, f32[9,16,256]{2,1,0:T(8,128)S(1)}, u32[]{:S(2)}, u32[]{:S(2)}) collective-permute-start(f32[9,16,256]{2,1,0:T(8,128)} %get-tuple-element.20), channel_id=1, source_target_pairs={{2,4},{3,5},{4,2},{5,3},{6,8},{7,9},{8,6},{9,7},{10,12},{11,13},{1... | collective-permute-start | bytes 442376 | tf_op jit(solution)/shard_map/ppermute | solution.py:205
  14.9 0.0 copy-done.10
  15.0 0.6 %add_add_fusion.weight_sum_ref = f32[9,128]{1,0:T(8,128)} fusion(f32[1,9,128]{2,0,1:T(1,128)S(1)} %get-tuple-element.43, f32[1,9,128]{2,0,1:T(1,128)S(1)} %get-tuple-element.49, f32[1,9,128]{2,0,1:T(1,128)S(1)} %get-tuple-element.48, f32[1,9,128]{2,0,1:T(1,128)S(1)} %get-tuple-element.47, f32[1,9,128]{2,0,1:T(1,128)S(1)} %get-tuple-element.46, ...), kind=kLoop, calls=%fused_computation.33 | loop fusion | flops 8064 | bytes 41472 | tf_op jit(solution)/shard_map/add | solution.py:198
  15.6 0.0 copy-done.12
  15.8 0.0 copy-start.11
  15.8 1.0 %multiply_add_fusion.1.refs_6_ = f32[9,80,128]{2,1,0:T(8,128)} fusion(f32[80,128]{1,0:T(8,128)S(1)} %get-tuple-element.36, f32[9,128]{1,0:T(8,128)S(1)} %get-tuple-element.53, f32[80,128]{1,0:T(8,128)S(1)} %get-tuple-element.37, f32[9,128]{1,0:T(8,128)S(1)} %get-tuple-element.54, f32[80,128]{1,0:T(8,128)S(1)} %get-tuple-element.38, ...), kind=kLoop, calls=%fused_computation.4 | loop fusion | flops 1382400 | bytes 733184 | tf_op jit(solution)/shard_map/add | solution.py:197
  16.7 1.1 %multiply_add_fusion.local_ref = f32[9,128,128]{2,1,0:T(8,128)} fusion(f32[128,128]{1,0:T(8,128)S(1)} %get-tuple-element.28, f32[9,128]{1,0:T(8,128)S(1)} %get-tuple-element.53, f32[128,128]{1,0:T(8,128)S(1)} %get-tuple-element.29, f32[9,128]{1,0:T(8,128)S(1)} %get-tuple-element.54, f32[128,128]{1,0:T(8,128)S(1)} %get-tuple-element.30, ...), kind=kLoop, calls=%fused_computation.1 | loop fusion | flops 2211840 | bytes 1150976 | tf_op jit(solution)/shard_map/add | solution.py:196
  17.9 0.0 copy-done.11
  18.5 0.6 %broadcast_in_dim.29.refs_7_ = f32[9,1,128]{2,1,0:T(1,128)} reshape(f32[9,128]{1,0:T(8,128)S(1)} %broadcast_subtract_fusion) | data formatting | bytes 9216 | tf_op jit(solution)/shard_map/broadcast_in_dim | solution.py:201
  19.1 3.6 %local_part.2.refs_0_ = f32[9,256,128]{2,1,0:T(8,128)} custom-call(f32[9,256,128]{2,1,0:T(8,128)} %values_ref.3, f32[9,128,128]{2,1,0:T(8,128)} %multiply_add_fusion.local_ref, f32[9,128]{1,0:T(8,128)} %add_add_fusion.weight_sum_ref, f32[8,128]{1,0:T(8,128)} %mixing_ref.3), custom_call_target="tpu_custom_call" | custom-call | tf_op jit(solution)/shard_map/local_part/pallas_call | solution.py:93
  22.7 0.6 %compare_convert_fusion.refs_8_ = f32[1,128]{1,0:T(1,128)} fusion(s32[]{:T(128)} %bitcast.73), kind=kLoop, calls=%fused_computation.48 | loop fusion | flops 256 | bytes 516 | tf_op jit(solution)/shard_map/convert_element_type | solution.py:200
  23.3 0.0 collective-permute-done.refs_1_
  23.3 0.0 collective-permute-done.1.refs_2_
  23.3 0.0 copy-start.1
  23.3 0.0 collective-permute-done.2.refs_3_
  23.3 0.1 collective-permute-done.3.refs_4_
  23.4 0.0 collective-permute-done.4.refs_5_
  23.4 0.5 copy-done
  23.9 0.1 copy-done.1
  24.0 0.0 copy-done.2
  24.1 0.1 copy-done.3
  24.1 0.7 %copy-done.4 = f32[9,16,256]{2,1,0:T(8,128)} copy-done((f32[9,16,256]{2,1,0:T(8,128)}, f32[9,16,256]{2,1,0:T(8,128)S(1)}, u32[]{:S(2)}) %copy-start.4) | copy-done | bytes 147480
  24.8 5.5 %finish_send.1 = (f32[9,256,128]{2,1,0:T(8,128)}, f32[9,16,256]{2,1,0:T(8,128)}, f32[9,16,256]{2,1,0:T(8,128)}, f32[9,16,256]{2,1,0:T(8,128)}, f32[9,16,256]{2,1,0:T(8,128)}, /*index=5*/f32[9,16,256]{2,1,0:T(8,128)}) custom-call(f32[9,256,128]{2,1,0:T(8,128)} %local_part.2.refs_0_, f32[9,16,256]{2,1,0:T(8,128)} %copy-done, f32[9,16,256]{2,1,0:T(8,128)} %copy-done.1, ...), custom_call_target="tpu_custom_call" | custom-call | tf_op jit(solution)/shard_map/finish_send/pallas_call | solution.py:154
  30.3 6.2 %collective-permute-start.5 = (f32[9,16,256]{2,1,0:T(8,128)}, f32[9,16,256]{2,1,0:T(8,128)S(1)}, u32[]{:S(2)}, u32[]{:S(2)}) collective-permute-start(f32[9,16,256]{2,1,0:T(8,128)} %get-tuple-element.22), channel_id=1, source_target_pairs={{0,16},{1,17},{2,18},{3,19},{4,20},{5,21},{6,22},{7,23},{8,24},{9,... | collective-permute-start | bytes 442376 | tf_op jit(solution)/shard_map/ppermute | solution.py:205
  36.4 0.0 collective-permute-start.6
  36.4 0.7 %collective-permute-start.7 = (f32[9,16,256]{2,1,0:T(8,128)}, f32[9,16,256]{2,1,0:T(8,128)S(1)}, u32[]{:S(2)}, u32[]{:S(2)}) collective-permute-start(f32[9,16,256]{2,1,0:T(8,128)} %get-tuple-element.24), channel_id=1, source_target_pairs={{1,2},{2,1},{3,4},{4,3},{5,6},{6,5},{7,8},{8,7},{9,10},{10,9},{11,... | collective-permute-start | bytes 442376 | tf_op jit(solution)/shard_map/ppermute | solution.py:205
  37.1 3.4 %collective-permute-start.8 = (f32[9,16,256]{2,1,0:T(8,128)}, f32[9,16,256]{2,1,0:T(8,128)S(1)}, u32[]{:S(2)}, u32[]{:S(2)}) collective-permute-start(f32[9,16,256]{2,1,0:T(8,128)} %get-tuple-element.25), channel_id=1, source_target_pairs={{0,2},{1,3},{2,0},{3,1},{4,6},{5,7},{6,4},{7,5},{8,10},{9,11},{10,... | collective-permute-start | bytes 442376 | tf_op jit(solution)/shard_map/ppermute | solution.py:205
  40.5 0.7 %collective-permute-start.9 = (f32[9,16,256]{2,1,0:T(8,128)}, f32[9,16,256]{2,1,0:T(8,128)S(1)}, u32[]{:S(2)}, u32[]{:S(2)}) collective-permute-start(f32[9,16,256]{2,1,0:T(8,128)} %get-tuple-element.26), channel_id=1, source_target_pairs={{2,4},{3,5},{4,2},{5,3},{6,8},{7,9},{8,6},{9,7},{10,12},{11,13},{1... | collective-permute-start | bytes 442376 | tf_op jit(solution)/shard_map/ppermute | solution.py:205
  41.2 3.6 %local_part.3.refs_0_ = f32[9,256,128]{2,1,0:T(8,128)} custom-call(f32[9,256,128]{2,1,0:T(8,128)} %get-tuple-element.21.values_ref, f32[9,128,128]{2,1,0:T(8,128)} %multiply_add_fusion.local_ref, f32[9,128]{1,0:T(8,128)} %add_add_fusion.weight_sum_ref, f32[8,128]{1,0:T(8,128)} %mixing_ref.3), custom_call_target="tpu_custom_call" | custom-call | tf_op jit(solution)/shard_map/local_part/pallas_call | solution.py:93
  44.8 0.0 collective-permute-done.5.refs_1_
  44.8 0.0 collective-permute-done.6.refs_2_
  44.8 0.0 collective-permute-done.7.refs_3_
  44.9 0.0 copy-start.7
  44.9 4.8 %collective-permute-done.8.refs_4_ = f32[9,16,256]{2,1,0:T(8,128)S(1)} collective-permute-done((f32[9,16,256]{2,1,0:T(8,128)}, f32[9,16,256]{2,1,0:T(8,128)S(1)}, u32[]{:S(2)}, u32[]{:S(2)}) %collective-permute-start.8) | collective-permute-done | bytes 147488 | tf_op jit(solution)/shard_map/ppermute | solution.py:205
  49.7 0.0 collective-permute-done.9.refs_5_
  49.7 0.6 %copy-done.8 = f32[9,16,256]{2,1,0:T(8,128)} copy-done((f32[9,16,256]{2,1,0:T(8,128)}, f32[9,16,256]{2,1,0:T(8,128)S(1)}, u32[]{:S(2)}) %copy-start.8) | copy-done | bytes 147480
  50.4 0.6 %copy-done.9 = f32[9,16,256]{2,1,0:T(8,128)} copy-done((f32[9,16,256]{2,1,0:T(8,128)}, f32[9,16,256]{2,1,0:T(8,128)S(1)}, u32[]{:S(2)}) %copy-start.9) | copy-done | bytes 147480
  51.0 4.2 %finish.1 = f32[9,256,128]{2,1,0:T(8,128)} custom-call(f32[9,256,128]{2,1,0:T(8,128)} %local_part.3.refs_0_, f32[9,16,256]{2,1,0:T(8,128)} %copy-done.5, f32[9,16,256]{2,1,0:T(8,128)} %copy-done.6, f32[9,16,256]{2,1,0:T(8,128)} %copy-done.7, f32[9,16,256]{2,1,0:T(8,128)} %copy-done.8, f32[9,16,256]{2,1,0:T(8,128)} %copy-done.9, ...), custom_call_target="tpu_custom_call" | custom-call | tf_op jit(solution)/shard_map/finish/pallas_call | solution.py:154
  (26 shorter events, 0.2 us)
Async XLA Ops:
  0.0 14.9 %copy-start.10 = (f32[8,9,128]{2,0,1:T(8,128)S(1)}, f32[8,9,128]{2,0,1:T(8,128)}, u32[]{:S(2)}) copy-start(f32[8,9,128]{2,0,1:T(8,128)} %param.8) | copy-start | bytes 110596
  0.0 15.6 %copy-start.12 = (s32[8,128]{1,0:T(8,128)S(1)}, s32[8,128]{1,0:T(8,128)}, u32[]{:S(2)}) copy-start(s32[8,128]{1,0:T(8,128)} %param.11) | copy-start | bytes 12292
  6.1 17.2 %collective-permute-start = (f32[9,16,256]{2,1,0:T(8,128)}, f32[9,16,256]{2,1,0:T(8,128)S(1)}, u32[]{:S(2)}, u32[]{:S(2)}) collective-permute-start(f32[9,16,256]{2,1,0:T(8,128)} %get-tuple-element.16), channel_id=1, source_target_pairs={{0,16},{1,17},{2,18},{3,19},{4,20},{5,21},{6,22},{7,23},{8,24},{9,... | collective-permute-start | bytes 442376 | tf_op jit(solution)/shard_map/ppermute | solution.py:205
  10.1 13.2 %collective-permute-start.1 = (f32[9,16,256]{2,1,0:T(8,128)}, f32[9,16,256]{2,1,0:T(8,128)S(1)}, u32[]{:S(2)}, u32[]{:S(2)}) collective-permute-start(f32[9,16,256]{2,1,0:T(8,128)} %get-tuple-element.17), channel_id=1, source_target_pairs={{0,1},{1,0},{2,3},{3,2},{4,5},{5,4},{6,7},{7,6},{8,9},{9,8},{10,11... | collective-permute-start | bytes 442376 | tf_op jit(solution)/shard_map/ppermute | solution.py:205
  10.1 13.2 %collective-permute-start.2 = (f32[9,16,256]{2,1,0:T(8,128)}, f32[9,16,256]{2,1,0:T(8,128)S(1)}, u32[]{:S(2)}, u32[]{:S(2)}) collective-permute-start(f32[9,16,256]{2,1,0:T(8,128)} %get-tuple-element.18), channel_id=1, source_target_pairs={{1,2},{2,1},{3,4},{4,3},{5,6},{6,5},{7,8},{8,7},{9,10},{10,9},{11,... | collective-permute-start | bytes 442376 | tf_op jit(solution)/shard_map/ppermute | solution.py:205
  10.8 12.6 %collective-permute-start.3 = (f32[9,16,256]{2,1,0:T(8,128)}, f32[9,16,256]{2,1,0:T(8,128)S(1)}, u32[]{:S(2)}, u32[]{:S(2)}) collective-permute-start(f32[9,16,256]{2,1,0:T(8,128)} %get-tuple-element.19), channel_id=1, source_target_pairs={{0,2},{1,3},{2,0},{3,1},{4,6},{5,7},{6,4},{7,5},{8,10},{9,11},{10,... | collective-permute-start | bytes 442376 | tf_op jit(solution)/shard_map/ppermute | solution.py:205
  14.2 9.2 %collective-permute-start.4 = (f32[9,16,256]{2,1,0:T(8,128)}, f32[9,16,256]{2,1,0:T(8,128)S(1)}, u32[]{:S(2)}, u32[]{:S(2)}) collective-permute-start(f32[9,16,256]{2,1,0:T(8,128)} %get-tuple-element.20), channel_id=1, source_target_pairs={{2,4},{3,5},{4,2},{5,3},{6,8},{7,9},{8,6},{9,7},{10,12},{11,13},{1... | collective-permute-start | bytes 442376 | tf_op jit(solution)/shard_map/ppermute | solution.py:205
  15.8 2.1 %copy-start.11 = (f32[9,128]{1,0:T(8,128)S(1)}, f32[9,128]{1,0:T(8,128)}, u32[]{:S(2)}) copy-start(f32[9,128]{1,0:T(8,128)} %param.10) | copy-start | bytes 13828
  23.3 0.6 %copy-start = (f32[9,16,256]{2,1,0:T(8,128)}, f32[9,16,256]{2,1,0:T(8,128)S(1)}, u32[]{:S(2)}) copy-start(f32[9,16,256]{2,1,0:T(8,128)S(1)} %collective-permute-done.refs_1_) | copy-start | bytes 442372
  23.3 0.7 %copy-start.1 = (f32[9,16,256]{2,1,0:T(8,128)}, f32[9,16,256]{2,1,0:T(8,128)S(1)}, u32[]{:S(2)}) copy-start(f32[9,16,256]{2,1,0:T(8,128)S(1)} %collective-permute-done.1.refs_2_) | copy-start | bytes 442372
  23.3 0.7 %copy-start.2 = (f32[9,16,256]{2,1,0:T(8,128)}, f32[9,16,256]{2,1,0:T(8,128)S(1)}, u32[]{:S(2)}) copy-start(f32[9,16,256]{2,1,0:T(8,128)S(1)} %collective-permute-done.2.refs_3_) | copy-start | bytes 442372
  23.4 0.7 %copy-start.3 = (f32[9,16,256]{2,1,0:T(8,128)}, f32[9,16,256]{2,1,0:T(8,128)S(1)}, u32[]{:S(2)}) copy-start(f32[9,16,256]{2,1,0:T(8,128)S(1)} %collective-permute-done.3.refs_4_) | copy-start | bytes 442372
  24.1 0.7 %copy-start.4 = (f32[9,16,256]{2,1,0:T(8,128)}, f32[9,16,256]{2,1,0:T(8,128)S(1)}, u32[]{:S(2)}) copy-start(f32[9,16,256]{2,1,0:T(8,128)S(1)} %collective-permute-done.4.refs_5_) | copy-start | bytes 442372
  30.3 14.6 %collective-permute-start.5 = (f32[9,16,256]{2,1,0:T(8,128)}, f32[9,16,256]{2,1,0:T(8,128)S(1)}, u32[]{:S(2)}, u32[]{:S(2)}) collective-permute-start(f32[9,16,256]{2,1,0:T(8,128)} %get-tuple-element.22), channel_id=1, source_target_pairs={{0,16},{1,17},{2,18},{3,19},{4,20},{5,21},{6,22},{7,23},{8,24},{9,... | collective-permute-start | bytes 442376 | tf_op jit(solution)/shard_map/ppermute | solution.py:205
  36.4 8.4 %collective-permute-start.6 = (f32[9,16,256]{2,1,0:T(8,128)}, f32[9,16,256]{2,1,0:T(8,128)S(1)}, u32[]{:S(2)}, u32[]{:S(2)}) collective-permute-start(f32[9,16,256]{2,1,0:T(8,128)} %get-tuple-element.23), channel_id=1, source_target_pairs={{0,1},{1,0},{2,3},{3,2},{4,5},{5,4},{6,7},{7,6},{8,9},{9,8},{10,11... | collective-permute-start | bytes 442376 | tf_op jit(solution)/shard_map/ppermute | solution.py:205
  36.4 8.4 %collective-permute-start.7 = (f32[9,16,256]{2,1,0:T(8,128)}, f32[9,16,256]{2,1,0:T(8,128)S(1)}, u32[]{:S(2)}, u32[]{:S(2)}) collective-permute-start(f32[9,16,256]{2,1,0:T(8,128)} %get-tuple-element.24), channel_id=1, source_target_pairs={{1,2},{2,1},{3,4},{4,3},{5,6},{6,5},{7,8},{8,7},{9,10},{10,9},{11,... | collective-permute-start | bytes 442376 | tf_op jit(solution)/shard_map/ppermute | solution.py:205
  37.1 12.6 %collective-permute-start.8 = (f32[9,16,256]{2,1,0:T(8,128)}, f32[9,16,256]{2,1,0:T(8,128)S(1)}, u32[]{:S(2)}, u32[]{:S(2)}) collective-permute-start(f32[9,16,256]{2,1,0:T(8,128)} %get-tuple-element.25), channel_id=1, source_target_pairs={{0,2},{1,3},{2,0},{3,1},{4,6},{5,7},{6,4},{7,5},{8,10},{9,11},{10,... | collective-permute-start | bytes 442376 | tf_op jit(solution)/shard_map/ppermute | solution.py:205
  40.5 9.2 %collective-permute-start.9 = (f32[9,16,256]{2,1,0:T(8,128)}, f32[9,16,256]{2,1,0:T(8,128)S(1)}, u32[]{:S(2)}, u32[]{:S(2)}) collective-permute-start(f32[9,16,256]{2,1,0:T(8,128)} %get-tuple-element.26), channel_id=1, source_target_pairs={{2,4},{3,5},{4,2},{5,3},{6,8},{7,9},{8,6},{9,7},{10,12},{11,13},{1... | collective-permute-start | bytes 442376 | tf_op jit(solution)/shard_map/ppermute | solution.py:205
  44.8 4.9 %copy-start.5 = (f32[9,16,256]{2,1,0:T(8,128)}, f32[9,16,256]{2,1,0:T(8,128)S(1)}, u32[]{:S(2)}) copy-start(f32[9,16,256]{2,1,0:T(8,128)S(1)} %collective-permute-done.5.refs_1_) | copy-start | bytes 442372
  44.8 4.9 %copy-start.6 = (f32[9,16,256]{2,1,0:T(8,128)}, f32[9,16,256]{2,1,0:T(8,128)S(1)}, u32[]{:S(2)}) copy-start(f32[9,16,256]{2,1,0:T(8,128)S(1)} %collective-permute-done.6.refs_2_) | copy-start | bytes 442372
  44.9 4.9 %copy-start.7 = (f32[9,16,256]{2,1,0:T(8,128)}, f32[9,16,256]{2,1,0:T(8,128)S(1)}, u32[]{:S(2)}) copy-start(f32[9,16,256]{2,1,0:T(8,128)S(1)} %collective-permute-done.7.refs_3_) | copy-start | bytes 442372
  49.7 0.7 %copy-start.8 = (f32[9,16,256]{2,1,0:T(8,128)}, f32[9,16,256]{2,1,0:T(8,128)S(1)}, u32[]{:S(2)}) copy-start(f32[9,16,256]{2,1,0:T(8,128)S(1)} %collective-permute-done.8.refs_4_) | copy-start | bytes 442372
  50.4 0.7 %copy-start.9 = (f32[9,16,256]{2,1,0:T(8,128)}, f32[9,16,256]{2,1,0:T(8,128)S(1)}, u32[]{:S(2)}) copy-start(f32[9,16,256]{2,1,0:T(8,128)S(1)} %collective-permute-done.9.refs_5_) | copy-start | bytes 442372

commit v5 on v4

--- a/solution.py
+++ b/solution.py
@@ -71,12 +71,11 @@
     )(values, select)
 
 
-def local_kernel(values_ref, local_ref, weight_sum_ref, mixing_ref, out_ref):
+def local_kernel(values_ref, local_ref, mixing_ref, out_ref):
     levels = values_ref.shape[0]
     for level in range(levels):
         v = values_ref[level]
-        x = v - weight_sum_ref[level : level + 1, :] * v
-        x = x + jnp.dot(
+        x = v + jnp.dot(
             v, local_ref[level], precision=HIGHEST, preferred_element_type=jnp.float32
         )
         if level + 1 < levels:
@@ -86,7 +85,7 @@
         out_ref[level] = x
 
 
-def local_part(values, local_matrix, weight_sum, mixing):
+def local_part(values, matrix, mixing):
     levels, pulses, capacity = values.shape
     pb = pulses // PULSE_BLOCKS if pulses % (8 * PULSE_BLOCKS) == 0 else pulses
     value_spec = pl.BlockSpec((levels, pb, capacity), lambda i: (0, i, 0))
@@ -96,29 +95,37 @@
         grid=(pulses // pb,),
         in_specs=[
             value_spec,
-            full_spec(local_matrix.shape),
-            full_spec(weight_sum.shape),
+            pl.BlockSpec((levels, capacity, capacity), lambda i: (0, 1, 0)),
             full_spec(mixing.shape),
         ],
         out_specs=value_spec,
         interpret=INTERPRET,
         name="local_part",
-    )(values, local_matrix, weight_sum, mixing)
+    )(values, matrix, mixing)
 
 
 def finish_kernel(groups, hslot, send, *refs):
     partial_ref = refs[0]
     incoming = refs[1 : 1 + groups]
-    remote_ref, keep_ref, living_ref, select_ref = refs[1 + groups : 5 + groups]
+    remote_ref, deposition_ref, count_ref, select_ref = refs[1 + groups : 5 + groups]
     out_ref = refs[5 + groups]
     send_refs = refs[6 + groups :]
-    living = living_ref[...] > 0.5
-    for level in range(partial_ref.shape[0]):
+    rows = groups * hslot
+    lb = partial_ref.shape[0]
+    first = pl.program_id(0) * lb
+    capacity = partial_ref.shape[2]
+    living = lax.broadcasted_iota(jnp.int32, (1, capacity), 1) < count_ref[...]
+    for level in range(lb):
         received = jnp.concatenate([incoming[g][level] for g in range(groups)], axis=0)
         far = lax.dot_general(
-            received, remote_ref[level], TN, precision=HIGHEST, preferred_element_type=jnp.float32
-        )
-        x = (partial_ref[level] + far) * keep_ref[level]
+            received,
+            remote_ref[level, :rows, :],
+            TN,
+            precision=HIGHEST,
+            preferred_element_type=jnp.float32,
+        )
+        keep = 1.0 - deposition_ref[pl.ds(first + level, 1), :]
+        x = (partial_ref[level] + far) * keep
         x = jnp.where(living, x, 0.0)
         out_ref[level] = x
         if send:
@@ -129,7 +136,7 @@
                 send_refs[g][level] = block[g * hslot : (g + 1) * hslot]
 
 
-def finish(partial, incoming, remote_matrix, keep, living, select, send):
+def finish(partial, incoming, matrix, deposition, count, select, send):
     levels, pulses, capacity = partial.shape
     groups = len(incoming)
     hslot = incoming[0].shape[1]
@@ -145,9 +152,9 @@
         [value_spec]
         + [send_spec] * groups
         + [
-            pl.BlockSpec((lb,) + remote_matrix.shape[1:], lambda i: (i, 0, 0)),
-            pl.BlockSpec((lb,) + keep.shape[1:], lambda i: (i, 0, 0)),
-            full_spec(living.shape),
+            pl.BlockSpec((lb, capacity, capacity), lambda i: (i, 0, 0)),
+            full_spec(deposition.shape),
+            full_spec(count.shape),
             full_spec(select.shape),
         ]
     )
@@ -159,7 +166,7 @@
         out_specs=out_specs,
         interpret=INTERPRET,
         name="finish_send" if send else "finish",
-    )(partial, *incoming, remote_matrix, keep, living, select)
+    )(partial, *incoming, matrix, deposition, count, select)
     return outs[0], outs[1:]
 
 
@@ -174,9 +181,11 @@
     me = lax.axis_index("cells")
     f32 = jnp.float32
 
-    peers = jnp.clip(jnp.stack([partner(me, jnp) for partner in partners]), 0, n - 1)
-    picked = send_cells[0][peers].reshape(groups * hslot)
-    select = (picked[:, None] == jnp.arange(capacity, dtype=jnp.int32)[None, :]).astype(f32)
+    peers = jnp.stack([partner(me, jnp) for partner in partners])
+    is_peer = peers[:, None] == jnp.arange(n, dtype=jnp.int32)[None, :]
+    lanes = jnp.arange(capacity, dtype=jnp.int32)
+    hit = is_peer[:, :, None, None] & (send_cells[0][None, :, :, None] == lanes)
+    select = jnp.sum(hit.astype(f32), axis=1).reshape(groups * hslot, capacity)
 
     values = concentration
     outgoing = gather_send(values, select, groups, hslot)
@@ -184,30 +193,25 @@
     beyond = halo_index - capacity
     sender = beyond // hslot
     place = beyond % hslot
-    group = jnp.full(halo_index.shape, -1, dtype=jnp.int32)
+    row = jnp.where(beyond < 0, capacity + halo_index, -1)
     for g, partner in enumerate(partners):
-        group = jnp.where(sender == partner(me, jnp), g, group)
-    local_col = jnp.where(beyond < 0, halo_index, -1)
-    remote_col = jnp.where((beyond >= 0) & (group >= 0), group * hslot + place, -1)
-    onehot_local = (local_col[:, None, :] == jnp.arange(capacity)[None, :, None]).astype(f32)
-    onehot_remote = (
-        remote_col[:, None, :] == jnp.arange(groups * hslot)[None, :, None]
-    ).astype(f32)
-    local_matrix = sum(flux_weight[k][:, None, :] * onehot_local[k][None] for k in range(nbr))
-    remote_matrix = sum(flux_weight[k][:, None, :] * onehot_remote[k][None] for k in range(nbr))
-    weight_sum = sum(flux_weight[k] for k in range(nbr))
-
-    living = (jnp.arange(capacity, dtype=jnp.int32) < live_count[0]).astype(f32)[None, :]
-    keep = (1.0 - deposition)[:, None, :]
+        row = jnp.where((beyond >= 0) & (sender == partner(me, jnp)), g * hslot + place, row)
+    slots = jnp.arange(2 * capacity, dtype=jnp.int32)[:, None]
+    diagonal = (slots == capacity + lanes[None, :]).astype(f32)
+    matrix = sum(
+        flux_weight[k][:, None, :] * ((row[k][None, :] == slots).astype(f32) - diagonal)[None]
+        for k in range(nbr)
+    )
+    count = live_count.reshape(1, 1)
 
     for sweep in range(STEPS):
         incoming = [
             lax.ppermute(outgoing[g], "cells", perm=pair_list(n, partner))
             for g, partner in enumerate(partners)
         ]
-        partial = local_part(values, local_matrix, weight_sum, vertical_mixing)
+        partial = local_part(values, matrix, vertical_mixing)
         values, outgoing = finish(
-            partial, incoming, remote_matrix, keep, living, select, sweep + 1 < STEPS
+            partial, incoming, matrix, deposition, count, select, sweep + 1 < STEPS
         )
     return values
 

time: 55.7 us -> 52.4 us (0.941)
  the two profiles are of different devices: /device:TPU:0 before, /device:TPU:5 now
where the time goes in v5:
time: 52.4 us; the launch traced here: 52 us
  Pallas kernels  20.7 us (40%)
  starting transfers between devices  18.5 us (35%)
  waiting for transfers between devices  6.78 us (13%)
  other arithmetic  2.9 us (6%)
  local copies, waits for them, and re-layouts  2.22 us (4%)
  between operations  0.91 us (2%)
    ppermute x10, starting transfers between devices, per_device(): lax.ppermute(outgoing[g], 'cells', perm=pair_list(n, partner))  18.5 us
    pallas_call x2, Pallas kernels, finish(): pl.pallas_call(functools.partial(finish_kernel, groups, hslot, send), out...  9.79 us
    pallas_call x2, Pallas kernels, local_part(): pl.pallas_call(local_kernel, out_shape=jax.ShapeDtypeStruct(values.shape,...  7.03 us
    ppermute x10, waiting for transfers between devices, per_device(): lax.ppermute(outgoing[g], 'cells', perm=pair_list(n, partner))  6.78 us
    pallas_call x1, Pallas kernels, gather_send(): pl.pallas_call(functools.partial(select_kernel, groups, hslot), out_shape...  3.86 us
    add x1, other arithmetic, per_device(): sum((flux_weight[k][:, None, :] * ((row[k][None, :] == slots).astype(f32)...  1.67 us
    unnamed x24, local copies, waits for them, and re-layouts  1.32 us
  transfers between devices with their start and end apart: 10, of which 2 were waited for; matrix products, arithmetic and copies ran while one was open for 4% of the time, Pallas kernels for 14%

profile of v5, /device:TPU:5, one launch (start us, length us, event | category | flops | bytes accessed | tf_op | source)
XLA Modules:
  0.0 52.0 jit_solution(9003718453751551799)
XLA Ops:
  0.0 0.1 stack.23
  0.1 0.1 iota_compare_fusion.10
  0.2 0.8 %copy.26 = s32[32,16]{1,0:T(8,128)S(1)} copy(s32[32,16]{0,1:T(8,128)} %bitcast.45) | data formatting | bytes 4096 | tf_op jit(solution)/shard_map/eq | solution.py:187
  0.9 0.1 iota_compare_fusion
  1.1 0.9 %convert_reduce_fusion = f32[5,16,128]{2,1,0:T(8,128)} fusion(pred[32,16,128]{2,1,0:T(8,128)(4,1)S(1)} %iota_compare_fusion, pred[5,32]{1,0:T(8,128)(4,1)S(1)} %iota_compare_fusion.10), kind=kLoop, calls=%fused_computation | loop fusion | flops 972800 | bytes 106656 | tf_op jit(solution)/shard_map/reduce_sum | solution.py:188
  1.9 3.9 %gather_send.1 = (f32[9,16,256]{2,1,0:T(8,128)}, f32[9,16,256]{2,1,0:T(8,128)}, f32[9,16,256]{2,1,0:T(8,128)}, f32[9,16,256]{2,1,0:T(8,128)}, f32[9,16,256]{2,1,0:T(8,128)}) custom-call(f32[9,256,128]{2,1,0:T(8,128)} %values_ref.3, f32[80,128]{1,0:T(8,128)} %bitcast.42), custom_call_target="tpu_custom_call" | custom-call | tf_op jit(solution)/shard_map/gather_send/pallas_call | solution.py:63
  5.8 2.3 %collective-permute-start = (f32[9,16,256]{2,1,0:T(8,128)}, f32[9,16,256]{2,1,0:T(8,128)S(1)}, u32[]{:S(2)}, u32[]{:S(2)}) collective-permute-start(f32[9,16,256]{2,1,0:T(8,128)} %get-tuple-element.16), channel_id=1, source_target_pairs={{0,16},{1,17},{2,18},{3,19},{4,20},{5,21},{6,22},{7,23},{8,24},{9,... | collective-permute-start | bytes 442376 | tf_op jit(solution)/shard_map/ppermute | solution.py:209
  8.1 1.0 %collective-permute-start.1 = (f32[9,16,256]{2,1,0:T(8,128)}, f32[9,16,256]{2,1,0:T(8,128)S(1)}, u32[]{:S(2)}, u32[]{:S(2)}) collective-permute-start(f32[9,16,256]{2,1,0:T(8,128)} %get-tuple-element.17), channel_id=1, source_target_pairs={{0,1},{1,0},{2,3},{3,2},{4,5},{5,4},{6,7},{7,6},{8,9},{9,8},{10,11... | collective-permute-start | bytes 442376 | tf_op jit(solution)/shard_map/ppermute | solution.py:209
  9.1 3.0 %collective-permute-start.2 = (f32[9,16,256]{2,1,0:T(8,128)}, f32[9,16,256]{2,1,0:T(8,128)S(1)}, u32[]{:S(2)}, u32[]{:S(2)}) collective-permute-start(f32[9,16,256]{2,1,0:T(8,128)} %get-tuple-element.18), channel_id=1, source_target_pairs={{1,2},{2,1},{3,4},{4,3},{5,6},{6,5},{7,8},{8,7},{9,10},{10,9},{11,... | collective-permute-start | bytes 442376 | tf_op jit(solution)/shard_map/ppermute | solution.py:209
  12.1 1.3 %collective-permute-start.3 = (f32[9,16,256]{2,1,0:T(8,128)}, f32[9,16,256]{2,1,0:T(8,128)S(1)}, u32[]{:S(2)}, u32[]{:S(2)}) collective-permute-start(f32[9,16,256]{2,1,0:T(8,128)} %get-tuple-element.19), channel_id=1, source_target_pairs={{0,2},{1,3},{2,0},{3,1},{4,6},{5,7},{6,4},{7,5},{8,10},{9,11},{10,... | collective-permute-start | bytes 442376 | tf_op jit(solution)/shard_map/ppermute | solution.py:209
  13.3 2.1 %collective-permute-start.4 = (f32[9,16,256]{2,1,0:T(8,128)}, f32[9,16,256]{2,1,0:T(8,128)S(1)}, u32[]{:S(2)}, u32[]{:S(2)}) collective-permute-start(f32[9,16,256]{2,1,0:T(8,128)} %get-tuple-element.20), channel_id=1, source_target_pairs={{2,4},{3,5},{4,2},{5,3},{6,8},{7,9},{8,6},{9,7},{10,12},{11,13},{1... | collective-permute-start | bytes 442376 | tf_op jit(solution)/shard_map/ppermute | solution.py:209
  16.1 0.0 copy-done.11
  16.2 0.0 copy-done.10
  16.2 0.1 convert_subtract_fusion.7
  16.4 1.7 %multiply_add_fusion.local_ref.refs_6_ = f32[9,256,128]{2,1,0:T(8,128)} fusion(f32[256,128]{1,0:T(8,128)S(1)} %get-tuple-element.50, f32[9,128]{1,0:T(8,128)S(1)} %get-tuple-element.51, f32[256,128]{1,0:T(8,128)S(1)} %get-tuple-element.49, f32[9,128]{1,0:T(8,128)S(1)} %get-tuple-element.52, f32[256,128]{1,0:T(8,128)S(1)} %get-tuple-element.48, ...), kind=kLoop, calls=%fused_computation.1 | loop fusion | flops 4423680 | bytes 2265088 | tf_op jit(solution)/shard_map/add | solution.py:201
  18.1 3.5 %local_part.2.refs_0_ = f32[9,256,128]{2,1,0:T(8,128)} custom-call(f32[9,256,128]{2,1,0:T(8,128)} %values_ref.3, f32[9,256,128]{2,1,0:T(8,128)} %multiply_add_fusion.local_ref.refs_6_, f32[8,128]{1,0:T(8,128)} %mixing_ref.3), custom_call_target="tpu_custom_call" | custom-call | tf_op jit(solution)/shard_map/local_part/pallas_call | solution.py:92
  21.6 0.0 collective-permute-done.refs_1_
  21.6 0.0 collective-permute-done.1.refs_2_
  21.6 0.0 copy-start.6
  21.6 0.0 collective-permute-done.2.refs_3_
  21.6 0.0 copy-start.7
  21.6 0.0 collective-permute-done.3.refs_4_
  21.6 0.0 copy-start.8
  21.6 2.0 %collective-permute-done.4.refs_5_ = f32[9,16,256]{2,1,0:T(8,128)S(1)} collective-permute-done((f32[9,16,256]{2,1,0:T(8,128)}, f32[9,16,256]{2,1,0:T(8,128)S(1)}, u32[]{:S(2)}, u32[]{:S(2)}) %collective-permute-start.4) | collective-permute-done | bytes 147488 | tf_op jit(solution)/shard_map/ppermute | solution.py:209
  23.6 0.0 copy-done.5
  23.6 0.0 copy-done.6
  23.6 0.0 copy-done.7
  23.6 0.0 copy-done.8
  23.6 0.6 %copy-done.9 = f32[9,16,256]{2,1,0:T(8,128)} copy-done((f32[9,16,256]{2,1,0:T(8,128)}, f32[9,16,256]{2,1,0:T(8,128)S(1)}, u32[]{:S(2)}) %copy-start.9) | copy-done | bytes 147480
  24.2 5.5 %finish_send.1 = (f32[9,256,128]{2,1,0:T(8,128)}, f32[9,16,256]{2,1,0:T(8,128)}, f32[9,16,256]{2,1,0:T(8,128)}, f32[9,16,256]{2,1,0:T(8,128)}, f32[9,16,256]{2,1,0:T(8,128)}, /*index=5*/f32[9,16,256]{2,1,0:T(8,128)}) custom-call(f32[9,256,128]{2,1,0:T(8,128)} %local_part.2.refs_0_, f32[9,16,256]{2,1,0:T(8,128)} %copy-done.5, f32[9,16,256]{2,1,0:T(8,128)} %copy-done.6, ...), custom_call_target="tpu_custom_call" | custom-call | tf_op jit(solution)/shard_map/finish_send/pallas_call | solution.py:161
  29.8 0.1 collective-permute-start.5
  29.8 2.7 %collective-permute-start.6 = (f32[9,16,256]{2,1,0:T(8,128)}, f32[9,16,256]{2,1,0:T(8,128)S(1)}, u32[]{:S(2)}, u32[]{:S(2)}) collective-permute-start(f32[9,16,256]{2,1,0:T(8,128)} %get-tuple-element.23), channel_id=1, source_target_pairs={{0,1},{1,0},{2,3},{3,2},{4,5},{5,4},{6,7},{7,6},{8,9},{9,8},{10,11... | collective-permute-start | bytes 442376 | tf_op jit(solution)/shard_map/ppermute | solution.py:209
  32.5 1.9 %collective-permute-start.7 = (f32[9,16,256]{2,1,0:T(8,128)}, f32[9,16,256]{2,1,0:T(8,128)S(1)}, u32[]{:S(2)}, u32[]{:S(2)}) collective-permute-start(f32[9,16,256]{2,1,0:T(8,128)} %get-tuple-element.24), channel_id=1, source_target_pairs={{1,2},{2,1},{3,4},{4,3},{5,6},{6,5},{7,8},{8,7},{9,10},{10,9},{11,... | collective-permute-start | bytes 442376 | tf_op jit(solution)/shard_map/ppermute | solution.py:209
  34.4 0.3 collective-permute-start.8
  34.7 3.9 %collective-permute-start.9 = (f32[9,16,256]{2,1,0:T(8,128)}, f32[9,16,256]{2,1,0:T(8,128)S(1)}, u32[]{:S(2)}, u32[]{:S(2)}) collective-permute-start(f32[9,16,256]{2,1,0:T(8,128)} %get-tuple-element.26), channel_id=1, source_target_pairs={{2,4},{3,5},{4,2},{5,3},{6,8},{7,9},{8,6},{9,7},{10,12},{11,13},{1... | collective-permute-start | bytes 442376 | tf_op jit(solution)/shard_map/ppermute | solution.py:209
  38.7 3.5 %local_part.3.refs_0_ = f32[9,256,128]{2,1,0:T(8,128)} custom-call(f32[9,256,128]{2,1,0:T(8,128)} %get-tuple-element.21.values_ref, f32[9,256,128]{2,1,0:T(8,128)} %multiply_add_fusion.local_ref.refs_6_, f32[8,128]{1,0:T(8,128)} %mixing_ref.3), custom_call_target="tpu_custom_call" | custom-call | tf_op jit(solution)/shard_map/local_part/pallas_call | solution.py:92
  42.2 0.0 collective-permute-done.5.refs_1_
  42.2 0.0 collective-permute-done.6.refs_2_
  42.2 0.0 copy-start.1
  42.2 0.0 collective-permute-done.7.refs_3_
  42.2 0.0 copy-start.2
  42.2 0.0 collective-permute-done.8.refs_4_
  42.3 0.0 copy-start.3
  42.3 4.8 %collective-permute-done.9.refs_5_ = f32[9,16,256]{2,1,0:T(8,128)S(1)} collective-permute-done((f32[9,16,256]{2,1,0:T(8,128)}, f32[9,16,256]{2,1,0:T(8,128)S(1)}, u32[]{:S(2)}, u32[]{:S(2)}) %collective-permute-start.9) | collective-permute-done | bytes 147488 | tf_op jit(solution)/shard_map/ppermute | solution.py:209
  47.1 0.0 copy-done
  47.1 0.0 copy-done.1
  47.1 0.6 %copy-done.4 = f32[9,16,256]{2,1,0:T(8,128)} copy-done((f32[9,16,256]{2,1,0:T(8,128)}, f32[9,16,256]{2,1,0:T(8,128)S(1)}, u32[]{:S(2)}) %copy-start.4) | copy-done | bytes 147480
  47.7 4.3 %finish.1 = f32[9,256,128]{2,1,0:T(8,128)} custom-call(f32[9,256,128]{2,1,0:T(8,128)} %local_part.3.refs_0_, f32[9,16,256]{2,1,0:T(8,128)} %copy-done, f32[9,16,256]{2,1,0:T(8,128)} %copy-done.1, f32[9,16,256]{2,1,0:T(8,128)} %copy-done.2, f32[9,16,256]{2,1,0:T(8,128)} %copy-done.3, f32[9,16,256]{2,1,0:T(8,128)} %copy-done.4, ...), custom_call_target="tpu_custom_call" | custom-call | tf_op jit(solution)/shard_map/finish/pallas_call | solution.py:161
  (16 shorter events, 0.1 us)
Async XLA Ops:
  0.0 16.1 %copy-start.11 = (s32[8,128]{1,0:T(8,128)S(1)}, s32[8,128]{1,0:T(8,128)}, u32[]{:S(2)}) copy-start(s32[8,128]{1,0:T(8,128)} %param.11) | copy-start | bytes 12292
  0.0 16.2 %copy-start.10 = (f32[8,9,128]{2,0,1:T(8,128)S(1)}, f32[8,9,128]{2,0,1:T(8,128)}, u32[]{:S(2)}) copy-start(f32[8,9,128]{2,0,1:T(8,128)} %param.8) | copy-start | bytes 110596
  5.8 15.8 %collective-permute-start = (f32[9,16,256]{2,1,0:T(8,128)}, f32[9,16,256]{2,1,0:T(8,128)S(1)}, u32[]{:S(2)}, u32[]{:S(2)}) collective-permute-start(f32[9,16,256]{2,1,0:T(8,128)} %get-tuple-element.16), channel_id=1, source_target_pairs={{0,16},{1,17},{2,18},{3,19},{4,20},{5,21},{6,22},{7,23},{8,24},{9,... | collective-permute-start | bytes 442376 | tf_op jit(solution)/shard_map/ppermute | solution.py:209
  8.1 13.5 %collective-permute-start.1 = (f32[9,16,256]{2,1,0:T(8,128)}, f32[9,16,256]{2,1,0:T(8,128)S(1)}, u32[]{:S(2)}, u32[]{:S(2)}) collective-permute-start(f32[9,16,256]{2,1,0:T(8,128)} %get-tuple-element.17), channel_id=1, source_target_pairs={{0,1},{1,0},{2,3},{3,2},{4,5},{5,4},{6,7},{7,6},{8,9},{9,8},{10,11... | collective-permute-start | bytes 442376 | tf_op jit(solution)/shard_map/ppermute | solution.py:209
  9.1 12.5 %collective-permute-start.2 = (f32[9,16,256]{2,1,0:T(8,128)}, f32[9,16,256]{2,1,0:T(8,128)S(1)}, u32[]{:S(2)}, u32[]{:S(2)}) collective-permute-start(f32[9,16,256]{2,1,0:T(8,128)} %get-tuple-element.18), channel_id=1, source_target_pairs={{1,2},{2,1},{3,4},{4,3},{5,6},{6,5},{7,8},{8,7},{9,10},{10,9},{11,... | collective-permute-start | bytes 442376 | tf_op jit(solution)/shard_map/ppermute | solution.py:209
  12.1 9.5 %collective-permute-start.3 = (f32[9,16,256]{2,1,0:T(8,128)}, f32[9,16,256]{2,1,0:T(8,128)S(1)}, u32[]{:S(2)}, u32[]{:S(2)}) collective-permute-start(f32[9,16,256]{2,1,0:T(8,128)} %get-tuple-element.19), channel_id=1, source_target_pairs={{0,2},{1,3},{2,0},{3,1},{4,6},{5,7},{6,4},{7,5},{8,10},{9,11},{10,... | collective-permute-start | bytes 442376 | tf_op jit(solution)/shard_map/ppermute | solution.py:209
  13.3 10.2 %collective-permute-start.4 = (f32[9,16,256]{2,1,0:T(8,128)}, f32[9,16,256]{2,1,0:T(8,128)S(1)}, u32[]{:S(2)}, u32[]{:S(2)}) collective-permute-start(f32[9,16,256]{2,1,0:T(8,128)} %get-tuple-element.20), channel_id=1, source_target_pairs={{2,4},{3,5},{4,2},{5,3},{6,8},{7,9},{8,6},{9,7},{10,12},{11,13},{1... | collective-permute-start | bytes 442376 | tf_op jit(solution)/shard_map/ppermute | solution.py:209
  21.6 2.0 %copy-start.5 = (f32[9,16,256]{2,1,0:T(8,128)}, f32[9,16,256]{2,1,0:T(8,128)S(1)}, u32[]{:S(2)}) copy-start(f32[9,16,256]{2,1,0:T(8,128)S(1)} %collective-permute-done.refs_1_) | copy-start | bytes 442372
  21.6 2.0 %copy-start.6 = (f32[9,16,256]{2,1,0:T(8,128)}, f32[9,16,256]{2,1,0:T(8,128)S(1)}, u32[]{:S(2)}) copy-start(f32[9,16,256]{2,1,0:T(8,128)S(1)} %collective-permute-done.1.refs_2_) | copy-start | bytes 442372
  21.6 2.0 %copy-start.7 = (f32[9,16,256]{2,1,0:T(8,128)}, f32[9,16,256]{2,1,0:T(8,128)S(1)}, u32[]{:S(2)}) copy-start(f32[9,16,256]{2,1,0:T(8,128)S(1)} %collective-permute-done.2.refs_3_) | copy-start | bytes 442372
  21.6 2.0 %copy-start.8 = (f32[9,16,256]{2,1,0:T(8,128)}, f32[9,16,256]{2,1,0:T(8,128)S(1)}, u32[]{:S(2)}) copy-start(f32[9,16,256]{2,1,0:T(8,128)S(1)} %collective-permute-done.3.refs_4_) | copy-start | bytes 442372
  23.6 0.7 %copy-start.9 = (f32[9,16,256]{2,1,0:T(8,128)}, f32[9,16,256]{2,1,0:T(8,128)S(1)}, u32[]{:S(2)}) copy-start(f32[9,16,256]{2,1,0:T(8,128)S(1)} %collective-permute-done.4.refs_5_) | copy-start | bytes 442372
  29.8 12.5 %collective-permute-start.5 = (f32[9,16,256]{2,1,0:T(8,128)}, f32[9,16,256]{2,1,0:T(8,128)S(1)}, u32[]{:S(2)}, u32[]{:S(2)}) collective-permute-start(f32[9,16,256]{2,1,0:T(8,128)} %get-tuple-element.22), channel_id=1, source_target_pairs={{0,16},{1,17},{2,18},{3,19},{4,20},{5,21},{6,22},{7,23},{8,24},{9,... | collective-permute-start | bytes 442376 | tf_op jit(solution)/shard_map/ppermute | solution.py:209
  29.8 12.4 %collective-permute-start.6 = (f32[9,16,256]{2,1,0:T(8,128)}, f32[9,16,256]{2,1,0:T(8,128)S(1)}, u32[]{:S(2)}, u32[]{:S(2)}) collective-permute-start(f32[9,16,256]{2,1,0:T(8,128)} %get-tuple-element.23), channel_id=1, source_target_pairs={{0,1},{1,0},{2,3},{3,2},{4,5},{5,4},{6,7},{7,6},{8,9},{9,8},{10,11... | collective-permute-start | bytes 442376 | tf_op jit(solution)/shard_map/ppermute | solution.py:209
  32.5 9.7 %collective-permute-start.7 = (f32[9,16,256]{2,1,0:T(8,128)}, f32[9,16,256]{2,1,0:T(8,128)S(1)}, u32[]{:S(2)}, u32[]{:S(2)}) collective-permute-start(f32[9,16,256]{2,1,0:T(8,128)} %get-tuple-element.24), channel_id=1, source_target_pairs={{1,2},{2,1},{3,4},{4,3},{5,6},{6,5},{7,8},{8,7},{9,10},{10,9},{11,... | collective-permute-start | bytes 442376 | tf_op jit(solution)/shard_map/ppermute | solution.py:209
  34.4 7.8 %collective-permute-start.8 = (f32[9,16,256]{2,1,0:T(8,128)}, f32[9,16,256]{2,1,0:T(8,128)S(1)}, u32[]{:S(2)}, u32[]{:S(2)}) collective-permute-start(f32[9,16,256]{2,1,0:T(8,128)} %get-tuple-element.25), channel_id=1, source_target_pairs={{0,2},{1,3},{2,0},{3,1},{4,6},{5,7},{6,4},{7,5},{8,10},{9,11},{10,... | collective-permute-start | bytes 442376 | tf_op jit(solution)/shard_map/ppermute | solution.py:209
  34.7 12.3 %collective-permute-start.9 = (f32[9,16,256]{2,1,0:T(8,128)}, f32[9,16,256]{2,1,0:T(8,128)S(1)}, u32[]{:S(2)}, u32[]{:S(2)}) collective-permute-start(f32[9,16,256]{2,1,0:T(8,128)} %get-tuple-element.26), channel_id=1, source_target_pairs={{2,4},{3,5},{4,2},{5,3},{6,8},{7,9},{8,6},{9,7},{10,12},{11,13},{1... | collective-permute-start | bytes 442376 | tf_op jit(solution)/shard_map/ppermute | solution.py:209
  42.2 4.8 %copy-start = (f32[9,16,256]{2,1,0:T(8,128)}, f32[9,16,256]{2,1,0:T(8,128)S(1)}, u32[]{:S(2)}) copy-start(f32[9,16,256]{2,1,0:T(8,128)S(1)} %collective-permute-done.5.refs_1_) | copy-start | bytes 442372
  42.2 4.8 %copy-start.1 = (f32[9,16,256]{2,1,0:T(8,128)}, f32[9,16,256]{2,1,0:T(8,128)S(1)}, u32[]{:S(2)}) copy-start(f32[9,16,256]{2,1,0:T(8,128)S(1)} %collective-permute-done.6.refs_2_) | copy-start | bytes 442372
  42.2 4.8 %copy-start.2 = (f32[9,16,256]{2,1,0:T(8,128)}, f32[9,16,256]{2,1,0:T(8,128)S(1)}, u32[]{:S(2)}) copy-start(f32[9,16,256]{2,1,0:T(8,128)S(1)} %collective-permute-done.7.refs_3_) | copy-start | bytes 442372
  42.3 4.8 %copy-start.3 = (f32[9,16,256]{2,1,0:T(8,128)}, f32[9,16,256]{2,1,0:T(8,128)S(1)}, u32[]{:S(2)}) copy-start(f32[9,16,256]{2,1,0:T(8,128)S(1)} %collective-permute-done.8.refs_4_) | copy-start | bytes 442372
  47.1 0.7 %copy-start.4 = (f32[9,16,256]{2,1,0:T(8,128)}, f32[9,16,256]{2,1,0:T(8,128)S(1)}, u32[]{:S(2)}) copy-start(f32[9,16,256]{2,1,0:T(8,128)S(1)} %collective-permute-done.9.refs_5_) | copy-start | bytes 442372

commit v6 on v5

--- a/solution.py
+++ b/solution.py
@@ -17,10 +17,10 @@
 def pairings(n):
     half = n // 2
     return (
+        lambda d, xp: d ^ 1,
+        lambda d, xp: xp.where(d % 4 < 2, d + 2, d - 2),
         lambda d, xp: (d + half) % n,
-        lambda d, xp: d ^ 1,
         lambda d, xp: xp.where(d % 2 == 1, d + 1, d - 1),
-        lambda d, xp: xp.where(d % 4 < 2, d + 2, d - 2),
         lambda d, xp: xp.where(d % 4 < 2, d - 2, d + 2),
     )
 

time: 52.4 us -> 49.5 us (0.945)
  the two profiles are of different devices: /device:TPU:5 before, /device:TPU:25 now
where the time goes in v6:
time: 49.5 us; the launch traced here: 49.1 us
  Pallas kernels  20.7 us (42%)
  starting transfers between devices  18.9 us (38%)
  waiting for transfers between devices  3.44 us (7%)
  other arithmetic  2.9 us (6%)
  local copies, waits for them, and re-layouts  2.22 us (4%)
  between operations  0.91 us (2%)
    ppermute x10, starting transfers between devices, per_device(): lax.ppermute(outgoing[g], 'cells', perm=pair_list(n, partner))  18.9 us
    pallas_call x2, Pallas kernels, finish(): pl.pallas_call(functools.partial(finish_kernel, groups, hslot, send), out...  9.8 us
    pallas_call x2, Pallas kernels, local_part(): pl.pallas_call(local_kernel, out_shape=jax.ShapeDtypeStruct(values.shape,...  7.03 us
    pallas_call x1, Pallas kernels, gather_send(): pl.pallas_call(functools.partial(select_kernel, groups, hslot), out_shape...  3.86 us
    ppermute x10, waiting for transfers between devices, per_device(): lax.ppermute(outgoing[g], 'cells', perm=pair_list(n, partner))  3.44 us
    add x1, other arithmetic, per_device(): sum((flux_weight[k][:, None, :] * ((row[k][None, :] == slots).astype(f32)...  1.67 us
    unnamed x24, local copies, waits for them, and re-layouts  1.32 us
  transfers between devices with their start and end apart: 10, of which 2 were waited for; matrix products, arithmetic and copies ran while one was open for 4% of the time, Pallas kernels for 14%

profile of v6, /device:TPU:25, one launch (start us, length us, event | category | flops | bytes accessed | tf_op | source)
XLA Modules:
  0.0 49.1 jit_solution(18361267029632918517)
XLA Ops:
  0.0 0.1 stack.23
  0.1 0.1 iota_compare_fusion.10
  0.2 0.8 %copy.26 = s32[32,16]{1,0:T(8,128)S(1)} copy(s32[32,16]{0,1:T(8,128)} %bitcast.45) | data formatting | bytes 4096 | tf_op jit(solution)/shard_map/eq | solution.py:187
  0.9 0.1 iota_compare_fusion
  1.1 0.9 %convert_reduce_fusion = f32[5,16,128]{2,1,0:T(8,128)} fusion(pred[32,16,128]{2,1,0:T(8,128)(4,1)S(1)} %iota_compare_fusion, pred[5,32]{1,0:T(8,128)(4,1)S(1)} %iota_compare_fusion.10), kind=kLoop, calls=%fused_computation | loop fusion | flops 972800 | bytes 106656 | tf_op jit(solution)/shard_map/reduce_sum | solution.py:188
  1.9 3.9 %gather_send.1 = (f32[9,16,256]{2,1,0:T(8,128)}, f32[9,16,256]{2,1,0:T(8,128)}, f32[9,16,256]{2,1,0:T(8,128)}, f32[9,16,256]{2,1,0:T(8,128)}, f32[9,16,256]{2,1,0:T(8,128)}) custom-call(f32[9,256,128]{2,1,0:T(8,128)} %values_ref.3, f32[80,128]{1,0:T(8,128)} %bitcast.42), custom_call_target="tpu_custom_call" | custom-call | tf_op jit(solution)/shard_map/gather_send/pallas_call | solution.py:63
  5.8 0.7 %collective-permute-start = (f32[9,16,256]{2,1,0:T(8,128)}, f32[9,16,256]{2,1,0:T(8,128)S(1)}, u32[]{:S(2)}, u32[]{:S(2)}) collective-permute-start(f32[9,16,256]{2,1,0:T(8,128)} %get-tuple-element.16), channel_id=1, source_target_pairs={{0,1},{1,0},{2,3},{3,2},{4,5},{5,4},{6,7},{7,6},{8,9},{9,8},{10,11... | collective-permute-start | bytes 442376 | tf_op jit(solution)/shard_map/ppermute | solution.py:209
  6.5 1.2 %collective-permute-start.1 = (f32[9,16,256]{2,1,0:T(8,128)}, f32[9,16,256]{2,1,0:T(8,128)S(1)}, u32[]{:S(2)}, u32[]{:S(2)}) collective-permute-start(f32[9,16,256]{2,1,0:T(8,128)} %get-tuple-element.17), channel_id=1, source_target_pairs={{0,2},{1,3},{2,0},{3,1},{4,6},{5,7},{6,4},{7,5},{8,10},{9,11},{10,... | collective-permute-start | bytes 442376 | tf_op jit(solution)/shard_map/ppermute | solution.py:209
  7.7 0.1 collective-permute-start.2
  7.7 2.7 %collective-permute-start.3 = (f32[9,16,256]{2,1,0:T(8,128)}, f32[9,16,256]{2,1,0:T(8,128)S(1)}, u32[]{:S(2)}, u32[]{:S(2)}) collective-permute-start(f32[9,16,256]{2,1,0:T(8,128)} %get-tuple-element.19), channel_id=1, source_target_pairs={{1,2},{2,1},{3,4},{4,3},{5,6},{6,5},{7,8},{8,7},{9,10},{10,9},{11,... | collective-permute-start | bytes 442376 | tf_op jit(solution)/shard_map/ppermute | solution.py:209
  10.4 4.9 %collective-permute-start.4 = (f32[9,16,256]{2,1,0:T(8,128)}, f32[9,16,256]{2,1,0:T(8,128)S(1)}, u32[]{:S(2)}, u32[]{:S(2)}) collective-permute-start(f32[9,16,256]{2,1,0:T(8,128)} %get-tuple-element.20), channel_id=1, source_target_pairs={{2,4},{3,5},{4,2},{5,3},{6,8},{7,9},{8,6},{9,7},{10,12},{11,13},{1... | collective-permute-start | bytes 442376 | tf_op jit(solution)/shard_map/ppermute | solution.py:209
  16.0 0.0 copy-done.11
  16.0 0.0 copy-done.10
  16.1 0.1 convert_subtract_fusion.7
  16.3 1.7 %multiply_add_fusion.local_ref.refs_6_ = f32[9,256,128]{2,1,0:T(8,128)} fusion(f32[256,128]{1,0:T(8,128)S(1)} %get-tuple-element.50, f32[9,128]{1,0:T(8,128)S(1)} %get-tuple-element.51, f32[256,128]{1,0:T(8,128)S(1)} %get-tuple-element.49, f32[9,128]{1,0:T(8,128)S(1)} %get-tuple-element.52, f32[256,128]{1,0:T(8,128)S(1)} %get-tuple-element.48, ...), kind=kLoop, calls=%fused_computation.1 | loop fusion | flops 4423680 | bytes 2265088 | tf_op jit(solution)/shard_map/add | solution.py:201
  17.9 3.5 %local_part.2.refs_0_ = f32[9,256,128]{2,1,0:T(8,128)} custom-call(f32[9,256,128]{2,1,0:T(8,128)} %values_ref.3, f32[9,256,128]{2,1,0:T(8,128)} %multiply_add_fusion.local_ref.refs_6_, f32[8,128]{1,0:T(8,128)} %mixing_ref.3), custom_call_target="tpu_custom_call" | custom-call | tf_op jit(solution)/shard_map/local_part/pallas_call | solution.py:92
  21.4 0.0 collective-permute-done.refs_1_
  21.4 0.0 collective-permute-done.1.refs_2_
  21.5 0.0 copy-start.6
  21.5 0.0 collective-permute-done.2.refs_3_
  21.5 0.0 copy-start.7
  21.5 0.0 collective-permute-done.3.refs_4_
  21.5 0.0 copy-start.8
  21.5 0.8 %collective-permute-done.4.refs_5_ = f32[9,16,256]{2,1,0:T(8,128)S(1)} collective-permute-done((f32[9,16,256]{2,1,0:T(8,128)}, f32[9,16,256]{2,1,0:T(8,128)S(1)}, u32[]{:S(2)}, u32[]{:S(2)}) %collective-permute-start.4) | collective-permute-done | bytes 147488 | tf_op jit(solution)/shard_map/ppermute | solution.py:209
  22.3 0.0 copy-done.5
  22.4 0.0 copy-done.6
  22.4 0.0 copy-done.7
  22.4 0.0 copy-done.8
  22.4 0.6 %copy-done.9 = f32[9,16,256]{2,1,0:T(8,128)} copy-done((f32[9,16,256]{2,1,0:T(8,128)}, f32[9,16,256]{2,1,0:T(8,128)S(1)}, u32[]{:S(2)}) %copy-start.9) | copy-done | bytes 147480
  23.0 5.5 %finish_send.1 = (f32[9,256,128]{2,1,0:T(8,128)}, f32[9,16,256]{2,1,0:T(8,128)}, f32[9,16,256]{2,1,0:T(8,128)}, f32[9,16,256]{2,1,0:T(8,128)}, f32[9,16,256]{2,1,0:T(8,128)}, /*index=5*/f32[9,16,256]{2,1,0:T(8,128)}) custom-call(f32[9,256,128]{2,1,0:T(8,128)} %local_part.2.refs_0_, f32[9,16,256]{2,1,0:T(8,128)} %copy-done.5, f32[9,16,256]{2,1,0:T(8,128)} %copy-done.6, ...), custom_call_target="tpu_custom_call" | custom-call | tf_op jit(solution)/shard_map/finish_send/pallas_call | solution.py:161
  28.5 0.1 collective-permute-start.5
  28.6 0.1 collective-permute-start.6
  28.7 1.7 %collective-permute-start.7 = (f32[9,16,256]{2,1,0:T(8,128)}, f32[9,16,256]{2,1,0:T(8,128)S(1)}, u32[]{:S(2)}, u32[]{:S(2)}) collective-permute-start(f32[9,16,256]{2,1,0:T(8,128)} %get-tuple-element.24), channel_id=1, source_target_pairs={{0,16},{1,17},{2,18},{3,19},{4,20},{5,21},{6,22},{7,23},{8,24},{9,... | collective-permute-start | bytes 442376 | tf_op jit(solution)/shard_map/ppermute | solution.py:209
  30.4 4.2 %collective-permute-start.8 = (f32[9,16,256]{2,1,0:T(8,128)}, f32[9,16,256]{2,1,0:T(8,128)S(1)}, u32[]{:S(2)}, u32[]{:S(2)}) collective-permute-start(f32[9,16,256]{2,1,0:T(8,128)} %get-tuple-element.25), channel_id=1, source_target_pairs={{1,2},{2,1},{3,4},{4,3},{5,6},{6,5},{7,8},{8,7},{9,10},{10,9},{11,... | collective-permute-start | bytes 442376 | tf_op jit(solution)/shard_map/ppermute | solution.py:209
  34.5 3.4 %collective-permute-start.9 = (f32[9,16,256]{2,1,0:T(8,128)}, f32[9,16,256]{2,1,0:T(8,128)S(1)}, u32[]{:S(2)}, u32[]{:S(2)}) collective-permute-start(f32[9,16,256]{2,1,0:T(8,128)} %get-tuple-element.26), channel_id=1, source_target_pairs={{2,4},{3,5},{4,2},{5,3},{6,8},{7,9},{8,6},{9,7},{10,12},{11,13},{1... | collective-permute-start | bytes 442376 | tf_op jit(solution)/shard_map/ppermute | solution.py:209
  38.0 3.5 %local_part.3.refs_0_ = f32[9,256,128]{2,1,0:T(8,128)} custom-call(f32[9,256,128]{2,1,0:T(8,128)} %get-tuple-element.21.values_ref, f32[9,256,128]{2,1,0:T(8,128)} %multiply_add_fusion.local_ref.refs_6_, f32[8,128]{1,0:T(8,128)} %mixing_ref.3), custom_call_target="tpu_custom_call" | custom-call | tf_op jit(solution)/shard_map/local_part/pallas_call | solution.py:92
  41.5 0.0 collective-permute-done.5.refs_1_
  41.5 0.0 collective-permute-done.6.refs_2_
  41.5 0.0 copy-start.1
  41.5 0.0 collective-permute-done.7.refs_3_
  41.5 0.0 copy-start.2
  41.6 0.0 collective-permute-done.8.refs_4_
  41.6 0.0 copy-start.3
  41.6 2.6 %collective-permute-done.9.refs_5_ = f32[9,16,256]{2,1,0:T(8,128)S(1)} collective-permute-done((f32[9,16,256]{2,1,0:T(8,128)}, f32[9,16,256]{2,1,0:T(8,128)S(1)}, u32[]{:S(2)}, u32[]{:S(2)}) %collective-permute-start.9) | collective-permute-done | bytes 147488 | tf_op jit(solution)/shard_map/ppermute | solution.py:209
  44.2 0.0 copy-done
  44.2 0.0 copy-done.3
  44.2 0.6 %copy-done.4 = f32[9,16,256]{2,1,0:T(8,128)} copy-done((f32[9,16,256]{2,1,0:T(8,128)}, f32[9,16,256]{2,1,0:T(8,128)S(1)}, u32[]{:S(2)}) %copy-start.4) | copy-done | bytes 147480
  44.8 4.3 %finish.1 = f32[9,256,128]{2,1,0:T(8,128)} custom-call(f32[9,256,128]{2,1,0:T(8,128)} %local_part.3.refs_0_, f32[9,16,256]{2,1,0:T(8,128)} %copy-done, f32[9,16,256]{2,1,0:T(8,128)} %copy-done.1, f32[9,16,256]{2,1,0:T(8,128)} %copy-done.2, f32[9,16,256]{2,1,0:T(8,128)} %copy-done.3, f32[9,16,256]{2,1,0:T(8,128)} %copy-done.4, ...), custom_call_target="tpu_custom_call" | custom-call | tf_op jit(solution)/shard_map/finish/pallas_call | solution.py:161
  (16 shorter events, 0.1 us)
Async XLA Ops:
  0.0 16.0 %copy-start.11 = (s32[8,128]{1,0:T(8,128)S(1)}, s32[8,128]{1,0:T(8,128)}, u32[]{:S(2)}) copy-start(s32[8,128]{1,0:T(8,128)} %param.11) | copy-start | bytes 12292
  0.0 16.0 %copy-start.10 = (f32[8,9,128]{2,0,1:T(8,128)S(1)}, f32[8,9,128]{2,0,1:T(8,128)}, u32[]{:S(2)}) copy-start(f32[8,9,128]{2,0,1:T(8,128)} %param.8) | copy-start | bytes 110596
  5.8 15.6 %collective-permute-start = (f32[9,16,256]{2,1,0:T(8,128)}, f32[9,16,256]{2,1,0:T(8,128)S(1)}, u32[]{:S(2)}, u32[]{:S(2)}) collective-permute-start(f32[9,16,256]{2,1,0:T(8,128)} %get-tuple-element.16), channel_id=1, source_target_pairs={{0,1},{1,0},{2,3},{3,2},{4,5},{5,4},{6,7},{7,6},{8,9},{9,8},{10,11... | collective-permute-start | bytes 442376 | tf_op jit(solution)/shard_map/ppermute | solution.py:209
  6.5 15.0 %collective-permute-start.1 = (f32[9,16,256]{2,1,0:T(8,128)}, f32[9,16,256]{2,1,0:T(8,128)S(1)}, u32[]{:S(2)}, u32[]{:S(2)}) collective-permute-start(f32[9,16,256]{2,1,0:T(8,128)} %get-tuple-element.17), channel_id=1, source_target_pairs={{0,2},{1,3},{2,0},{3,1},{4,6},{5,7},{6,4},{7,5},{8,10},{9,11},{10,... | collective-permute-start | bytes 442376 | tf_op jit(solution)/shard_map/ppermute | solution.py:209
  7.7 13.8 %collective-permute-start.2 = (f32[9,16,256]{2,1,0:T(8,128)}, f32[9,16,256]{2,1,0:T(8,128)S(1)}, u32[]{:S(2)}, u32[]{:S(2)}) collective-permute-start(f32[9,16,256]{2,1,0:T(8,128)} %get-tuple-element.18), channel_id=1, source_target_pairs={{0,16},{1,17},{2,18},{3,19},{4,20},{5,21},{6,22},{7,23},{8,24},{9,... | collective-permute-start | bytes 442376 | tf_op jit(solution)/shard_map/ppermute | solution.py:209
  7.7 13.7 %collective-permute-start.3 = (f32[9,16,256]{2,1,0:T(8,128)}, f32[9,16,256]{2,1,0:T(8,128)S(1)}, u32[]{:S(2)}, u32[]{:S(2)}) collective-permute-start(f32[9,16,256]{2,1,0:T(8,128)} %get-tuple-element.19), channel_id=1, source_target_pairs={{1,2},{2,1},{3,4},{4,3},{5,6},{6,5},{7,8},{8,7},{9,10},{10,9},{11,... | collective-permute-start | bytes 442376 | tf_op jit(solution)/shard_map/ppermute | solution.py:209
  10.4 11.9 %collective-permute-start.4 = (f32[9,16,256]{2,1,0:T(8,128)}, f32[9,16,256]{2,1,0:T(8,128)S(1)}, u32[]{:S(2)}, u32[]{:S(2)}) collective-permute-start(f32[9,16,256]{2,1,0:T(8,128)} %get-tuple-element.20), channel_id=1, source_target_pairs={{2,4},{3,5},{4,2},{5,3},{6,8},{7,9},{8,6},{9,7},{10,12},{11,13},{1... | collective-permute-start | bytes 442376 | tf_op jit(solution)/shard_map/ppermute | solution.py:209
  21.4 0.9 %copy-start.5 = (f32[9,16,256]{2,1,0:T(8,128)}, f32[9,16,256]{2,1,0:T(8,128)S(1)}, u32[]{:S(2)}) copy-start(f32[9,16,256]{2,1,0:T(8,128)S(1)} %collective-permute-done.refs_1_) | copy-start | bytes 442372
  21.5 0.9 %copy-start.6 = (f32[9,16,256]{2,1,0:T(8,128)}, f32[9,16,256]{2,1,0:T(8,128)S(1)}, u32[]{:S(2)}) copy-start(f32[9,16,256]{2,1,0:T(8,128)S(1)} %collective-permute-done.1.refs_2_) | copy-start | bytes 442372
  21.5 0.9 %copy-start.7 = (f32[9,16,256]{2,1,0:T(8,128)}, f32[9,16,256]{2,1,0:T(8,128)S(1)}, u32[]{:S(2)}) copy-start(f32[9,16,256]{2,1,0:T(8,128)S(1)} %collective-permute-done.2.refs_3_) | copy-start | bytes 442372
  21.5 0.9 %copy-start.8 = (f32[9,16,256]{2,1,0:T(8,128)}, f32[9,16,256]{2,1,0:T(8,128)S(1)}, u32[]{:S(2)}) copy-start(f32[9,16,256]{2,1,0:T(8,128)S(1)} %collective-permute-done.3.refs_4_) | copy-start | bytes 442372
  22.3 0.7 %copy-start.9 = (f32[9,16,256]{2,1,0:T(8,128)}, f32[9,16,256]{2,1,0:T(8,128)S(1)}, u32[]{:S(2)}) copy-start(f32[9,16,256]{2,1,0:T(8,128)S(1)} %collective-permute-done.4.refs_5_) | copy-start | bytes 442372
  28.5 13.0 %collective-permute-start.5 = (f32[9,16,256]{2,1,0:T(8,128)}, f32[9,16,256]{2,1,0:T(8,128)S(1)}, u32[]{:S(2)}, u32[]{:S(2)}) collective-permute-start(f32[9,16,256]{2,1,0:T(8,128)} %get-tuple-element.22), channel_id=1, source_target_pairs={{0,1},{1,0},{2,3},{3,2},{4,5},{5,4},{6,7},{7,6},{8,9},{9,8},{10,11... | collective-permute-start | bytes 442376 | tf_op jit(solution)/shard_map/ppermute | solution.py:209
  28.6 12.9 %collective-permute-start.6 = (f32[9,16,256]{2,1,0:T(8,128)}, f32[9,16,256]{2,1,0:T(8,128)S(1)}, u32[]{:S(2)}, u32[]{:S(2)}) collective-permute-start(f32[9,16,256]{2,1,0:T(8,128)} %get-tuple-element.23), channel_id=1, source_target_pairs={{0,2},{1,3},{2,0},{3,1},{4,6},{5,7},{6,4},{7,5},{8,10},{9,11},{10,... | collective-permute-start | bytes 442376 | tf_op jit(solution)/shard_map/ppermute | solution.py:209
  28.7 12.9 %collective-permute-start.7 = (f32[9,16,256]{2,1,0:T(8,128)}, f32[9,16,256]{2,1,0:T(8,128)S(1)}, u32[]{:S(2)}, u32[]{:S(2)}) collective-permute-start(f32[9,16,256]{2,1,0:T(8,128)} %get-tuple-element.24), channel_id=1, source_target_pairs={{0,16},{1,17},{2,18},{3,19},{4,20},{5,21},{6,22},{7,23},{8,24},{9,... | collective-permute-start | bytes 442376 | tf_op jit(solution)/shard_map/ppermute | solution.py:209
  30.4 11.2 %collective-permute-start.8 = (f32[9,16,256]{2,1,0:T(8,128)}, f32[9,16,256]{2,1,0:T(8,128)S(1)}, u32[]{:S(2)}, u32[]{:S(2)}) collective-permute-start(f32[9,16,256]{2,1,0:T(8,128)} %get-tuple-element.25), channel_id=1, source_target_pairs={{1,2},{2,1},{3,4},{4,3},{5,6},{6,5},{7,8},{8,7},{9,10},{10,9},{11,... | collective-permute-start | bytes 442376 | tf_op jit(solution)/shard_map/ppermute | solution.py:209
  34.5 9.6 %collective-permute-start.9 = (f32[9,16,256]{2,1,0:T(8,128)}, f32[9,16,256]{2,1,0:T(8,128)S(1)}, u32[]{:S(2)}, u32[]{:S(2)}) collective-permute-start(f32[9,16,256]{2,1,0:T(8,128)} %get-tuple-element.26), channel_id=1, source_target_pairs={{2,4},{3,5},{4,2},{5,3},{6,8},{7,9},{8,6},{9,7},{10,12},{11,13},{1... | collective-permute-start | bytes 442376 | tf_op jit(solution)/shard_map/ppermute | solution.py:209
  41.5 2.6 %copy-start = (f32[9,16,256]{2,1,0:T(8,128)}, f32[9,16,256]{2,1,0:T(8,128)S(1)}, u32[]{:S(2)}) copy-start(f32[9,16,256]{2,1,0:T(8,128)S(1)} %collective-permute-done.5.refs_1_) | copy-start | bytes 442372
  41.5 2.6 %copy-start.1 = (f32[9,16,256]{2,1,0:T(8,128)}, f32[9,16,256]{2,1,0:T(8,128)S(1)}, u32[]{:S(2)}) copy-start(f32[9,16,256]{2,1,0:T(8,128)S(1)} %collective-permute-done.6.refs_2_) | copy-start | bytes 442372
  41.5 2.6 %copy-start.2 = (f32[9,16,256]{2,1,0:T(8,128)}, f32[9,16,256]{2,1,0:T(8,128)S(1)}, u32[]{:S(2)}) copy-start(f32[9,16,256]{2,1,0:T(8,128)S(1)} %collective-permute-done.7.refs_3_) | copy-start | bytes 442372
  41.6 2.6 %copy-start.3 = (f32[9,16,256]{2,1,0:T(8,128)}, f32[9,16,256]{2,1,0:T(8,128)S(1)}, u32[]{:S(2)}) copy-start(f32[9,16,256]{2,1,0:T(8,128)S(1)} %collective-permute-done.8.refs_4_) | copy-start | bytes 442372
  44.1 0.7 %copy-start.4 = (f32[9,16,256]{2,1,0:T(8,128)}, f32[9,16,256]{2,1,0:T(8,128)S(1)}, u32[]{:S(2)}) copy-start(f32[9,16,256]{2,1,0:T(8,128)S(1)} %collective-permute-done.9.refs_5_) | copy-start | bytes 442372

commit v7 on v6

--- a/solution.py
+++ b/solution.py
@@ -5,6 +5,7 @@
 import jax.numpy as jnp
 from jax import lax
 from jax.experimental import pallas as pl
+from jax.experimental.pallas import tpu as pltpu
 from jax.sharding import PartitionSpec as P
 
 STEPS = 2
@@ -46,29 +47,39 @@
     return pl.BlockSpec(shape, lambda i: (0,) * len(shape))
 
 
-def select_kernel(groups, hslot, values_ref, select_ref, *out_refs):
-    select = select_ref[...]
+def copy_rows(partners, n, hslot, me_ref, cells_ref, flipped_ref, send_refs, level):
+    me = me_ref[0]
+    capacity = flipped_ref.shape[0]
+    for g, partner in enumerate(partners):
+        peer = jnp.clip(partner(me, jnp), 0, n - 1)
+        for h in range(hslot):
+            row = jnp.clip(cells_ref[peer, h], 0, capacity - 1)
+            send_refs[g][level, pl.ds(h, 1), :] = flipped_ref[pl.ds(row, 1), :]
+
+
+def select_kernel(partners, n, hslot, me_ref, cells_ref, values_ref, *refs):
+    send_refs, flipped_ref = refs[:-1], refs[-1]
     for level in range(values_ref.shape[0]):
-        block = lax.dot_general(
-            select, values_ref[level], NT, precision=HIGHEST, preferred_element_type=jnp.float32
-        )
-        for g in range(groups):
-            out_refs[g][level] = block[g * hslot : (g + 1) * hslot]
-
-
-def gather_send(values, select, groups, hslot):
+        flipped_ref[...] = values_ref[level].T
+        copy_rows(partners, n, hslot, me_ref, cells_ref, flipped_ref, send_refs, level)
+
+
+def gather_send(values, me, cells, partners, n, hslot):
     levels, pulses, capacity = values.shape
+    groups = len(partners)
     lb = level_block(levels)
     send_spec = pl.BlockSpec((lb, hslot, pulses), lambda i: (i, 0, 0))
+    smem = pl.BlockSpec(memory_space=pltpu.SMEM)
     return pl.pallas_call(
-        functools.partial(select_kernel, groups, hslot),
+        functools.partial(select_kernel, partners, n, hslot),
         out_shape=[jax.ShapeDtypeStruct((levels, hslot, pulses), jnp.float32)] * groups,
         grid=(levels // lb,),
-        in_specs=[pl.BlockSpec((lb, pulses, capacity), lambda i: (i, 0, 0)), full_spec(select.shape)],
+        in_specs=[smem, smem, pl.BlockSpec((lb, pulses, capacity), lambda i: (i, 0, 0))],
         out_specs=[send_spec] * groups,
+        scratch_shapes=[pltpu.VMEM((capacity, pulses), jnp.float32)],
         interpret=INTERPRET,
         name="gather_send",
-    )(values, select)
+    )(me, cells, values)
 
 
 def local_kernel(values_ref, local_ref, mixing_ref, out_ref):
@@ -104,12 +115,14 @@
     )(values, matrix, mixing)
 
 
-def finish_kernel(groups, hslot, send, *refs):
+def finish_kernel(partners, n, hslot, send, me_ref, cells_ref, *refs):
+    groups = len(partners)
     partial_ref = refs[0]
     incoming = refs[1 : 1 + groups]
-    remote_ref, deposition_ref, count_ref, select_ref = refs[1 + groups : 5 + groups]
-    out_ref = refs[5 + groups]
-    send_refs = refs[6 + groups :]
+    remote_ref, deposition_ref, count_ref = refs[1 + groups : 4 + groups]
+    out_ref = refs[4 + groups]
+    send_refs = refs[5 + groups : 5 + 2 * groups] if send else ()
+    flipped_ref = refs[-1]
     rows = groups * hslot
     lb = partial_ref.shape[0]
     first = pl.program_id(0) * lb
@@ -129,17 +142,15 @@
         x = jnp.where(living, x, 0.0)
         out_ref[level] = x
         if send:
-            block = lax.dot_general(
-                select_ref[...], x, NT, precision=HIGHEST, preferred_element_type=jnp.float32
-            )
-            for g in range(groups):
-                send_refs[g][level] = block[g * hslot : (g + 1) * hslot]
-
-
-def finish(partial, incoming, matrix, deposition, count, select, send):
+            flipped_ref[...] = x.T
+            copy_rows(partners, n, hslot, me_ref, cells_ref, flipped_ref, send_refs, level)
+
+
+def finish(partial, incoming, matrix, deposition, count, me, cells, partners, n, send):
     levels, pulses, capacity = partial.shape
     groups = len(incoming)
     hslot = incoming[0].shape[1]
+    smem = pl.BlockSpec(memory_space=pltpu.SMEM)
     lb = level_block(levels)
     value_spec = pl.BlockSpec((lb, pulses, capacity), lambda i: (i, 0, 0))
     send_spec = pl.BlockSpec((lb, hslot, pulses), lambda i: (i, 0, 0))
@@ -149,24 +160,24 @@
         shapes += [jax.ShapeDtypeStruct((levels, hslot, pulses), jnp.float32)] * groups
         out_specs += [send_spec] * groups
     in_specs = (
-        [value_spec]
+        [smem, smem, value_spec]
         + [send_spec] * groups
         + [
             pl.BlockSpec((lb, capacity, capacity), lambda i: (i, 0, 0)),
             full_spec(deposition.shape),
             full_spec(count.shape),
-            full_spec(select.shape),
         ]
     )
     outs = pl.pallas_call(
-        functools.partial(finish_kernel, groups, hslot, send),
+        functools.partial(finish_kernel, partners, n, hslot, send),
         out_shape=shapes,
         grid=(levels // lb,),
         in_specs=in_specs,
         out_specs=out_specs,
+        scratch_shapes=[pltpu.VMEM((capacity, pulses), jnp.float32)],
         interpret=INTERPRET,
         name="finish_send" if send else "finish",
-    )(partial, *incoming, matrix, deposition, count, select)
+    )(me, cells, partial, *incoming, matrix, deposition, count)
     return outs[0], outs[1:]
 
 
@@ -181,14 +192,12 @@
     me = lax.axis_index("cells")
     f32 = jnp.float32
 
-    peers = jnp.stack([partner(me, jnp) for partner in partners])
-    is_peer = peers[:, None] == jnp.arange(n, dtype=jnp.int32)[None, :]
+    me_array = jnp.reshape(me, (1,)).astype(jnp.int32)
+    cells = send_cells[0]
     lanes = jnp.arange(capacity, dtype=jnp.int32)
-    hit = is_peer[:, :, None, None] & (send_cells[0][None, :, :, None] == lanes)
-    select = jnp.sum(hit.astype(f32), axis=1).reshape(groups * hslot, capacity)
 
     values = concentration
-    outgoing = gather_send(values, select, groups, hslot)
+    outgoing = gather_send(values, me_array, cells, partners, n, hslot)
 
     beyond = halo_index - capacity
     sender = beyond // hslot
@@ -211,7 +220,16 @@
         ]
         partial = local_part(values, matrix, vertical_mixing)
         values, outgoing = finish(
-            partial, incoming, matrix, deposition, count, select, sweep + 1 < STEPS
+            partial,
+            incoming,
+            matrix,
+            deposition,
+            count,
+            me_array,
+            cells,
+            partners,
+            n,
+            sweep + 1 < STEPS,
         )
     return values
 

time: 49.5 us -> 50.2 us (1.014)
  Pallas kernels: 20.7 us -> 21.8 us
  other arithmetic: 2.9 us -> 1.8 us
  local copies, waits for them, and re-layouts: 2.22 us -> 2.77 us
    unnamed x24 -> x25, local copies, waits for them, and re-layouts: 1.32 us -> 2.72 us
    pallas_call x3, Pallas kernels: 13.7 us -> 14.8 us  [the longest x2 10.3 us: finish(): pl.pallas_call(functools.partial(finish_kernel, partners, n, hslot, send)...]
    reduce_sum x1 -> x0, other arithmetic: 0.86 us -> none  [per_device(): select = jnp.sum(hit.astype(f32), axis=1).reshape(groups * hslot, capacity)]
    eq x1 -> x0, local copies, waits for them, and re-layouts: 0.77 us -> none  [per_device(): hit = is_peer[:, :, None, None] & (send_cells[0][None, :, :, None] == lanes)]
where the time goes in v7:
time: 50.2 us; the launch traced here: 49.7 us
  Pallas kernels  21.8 us (43%)
  starting transfers between devices  19 us (38%)
  waiting for transfers between devices  3.38 us (7%)
  local copies, waits for them, and re-layouts  2.77 us (6%)
  other arithmetic  1.8 us (4%)
  between operations  0.96 us (2%)
    ppermute x10, starting transfers between devices, per_device(): lax.ppermute(outgoing[g], 'cells', perm=pair_list(n, partner))  19 us
    pallas_call x2, Pallas kernels, finish(): pl.pallas_call(functools.partial(finish_kernel, partners, n, hslot, send)...  10.3 us
    pallas_call x2, Pallas kernels, local_part(): pl.pallas_call(local_kernel, out_shape=jax.ShapeDtypeStruct(values.shape,...  7.06 us
    pallas_call x1, Pallas kernels, gather_send(): pl.pallas_call(functools.partial(select_kernel, partners, n, hslot), out_...  4.53 us
    ppermute x10, waiting for transfers between devices, per_device(): lax.ppermute(outgoing[g], 'cells', perm=pair_list(n, partner))  3.38 us
    unnamed x25, local copies, waits for them, and re-layouts  2.72 us
    add x1, other arithmetic, per_device(): sum((flux_weight[k][:, None, :] * ((row[k][None, :] == slots).astype(f32)...  1.65 us
  transfers between devices with their start and end apart: 10, of which 2 were waited for; matrix products, arithmetic and copies ran while one was open for 4% of the time, Pallas kernels for 14%

profile of v7, /device:TPU:25, one launch (start us, length us, event | category | flops | bytes accessed | tf_op | source)
XLA Modules:
  0.0 49.7 jit_solution(11417770201785986613)
XLA Ops:
  0.0 0.0 copy-start.11
  0.0 0.0 copy-start.10
  0.0 1.4 %copy.9 = s32[1,32,16]{2,1,0:T(8,128)} copy(s32[1,32,16]{1,2,0:T(8,128)} %param.12) | data formatting | bytes 4096 | tf_op args[5]
  1.4 4.5 %gather_send.1 = (f32[9,16,256]{2,1,0:T(8,128)}, f32[9,16,256]{2,1,0:T(8,128)}, f32[9,16,256]{2,1,0:T(8,128)}, f32[9,16,256]{2,1,0:T(8,128)}, f32[9,16,256]{2,1,0:T(8,128)}) custom-call(s32[1]{0:T(128)} %bitcast.me_ref, s32[32,16]{1,0:T(8,128)} %bitcast.37, f32[9,256,128]{2,1,0:T(8,128)} %values_ref.3), custom_call_target="tpu_custom_call" | custom-call | tf_op jit(solution)/shard_map/gather_send/pallas_call | solution.py:73
  5.9 0.7 %collective-permute-start = (f32[9,16,256]{2,1,0:T(8,128)}, f32[9,16,256]{2,1,0:T(8,128)S(1)}, u32[]{:S(2)}, u32[]{:S(2)}) collective-permute-start(f32[9,16,256]{2,1,0:T(8,128)} %get-tuple-element.16), channel_id=1, source_target_pairs={{0,1},{1,0},{2,3},{3,2},{4,5},{5,4},{6,7},{7,6},{8,9},{9,8},{10,11... | collective-permute-start | bytes 442376 | tf_op jit(solution)/shard_map/ppermute | solution.py:218
  6.6 1.2 %collective-permute-start.1 = (f32[9,16,256]{2,1,0:T(8,128)}, f32[9,16,256]{2,1,0:T(8,128)S(1)}, u32[]{:S(2)}, u32[]{:S(2)}) collective-permute-start(f32[9,16,256]{2,1,0:T(8,128)} %get-tuple-element.17), channel_id=1, source_target_pairs={{0,2},{1,3},{2,0},{3,1},{4,6},{5,7},{6,4},{7,5},{8,10},{9,11},{10,... | collective-permute-start | bytes 442376 | tf_op jit(solution)/shard_map/ppermute | solution.py:218
  7.8 0.1 collective-permute-start.2
  7.9 2.7 %collective-permute-start.3 = (f32[9,16,256]{2,1,0:T(8,128)}, f32[9,16,256]{2,1,0:T(8,128)S(1)}, u32[]{:S(2)}, u32[]{:S(2)}) collective-permute-start(f32[9,16,256]{2,1,0:T(8,128)} %get-tuple-element.19), channel_id=1, source_target_pairs={{1,2},{2,1},{3,4},{4,3},{5,6},{6,5},{7,8},{8,7},{9,10},{10,9},{11,... | collective-permute-start | bytes 442376 | tf_op jit(solution)/shard_map/ppermute | solution.py:218
  10.5 4.9 %collective-permute-start.4 = (f32[9,16,256]{2,1,0:T(8,128)}, f32[9,16,256]{2,1,0:T(8,128)S(1)}, u32[]{:S(2)}, u32[]{:S(2)}) collective-permute-start(f32[9,16,256]{2,1,0:T(8,128)} %get-tuple-element.20), channel_id=1, source_target_pairs={{2,4},{3,5},{4,2},{5,3},{6,8},{7,9},{8,6},{9,7},{10,12},{11,13},{1... | collective-permute-start | bytes 442376 | tf_op jit(solution)/shard_map/ppermute | solution.py:218
  16.2 0.0 copy-done.11
  16.2 0.0 copy-done.10
  16.3 0.1 convert_subtract_fusion.7
  16.4 1.7 %multiply_add_fusion.local_ref.refs_6_ = f32[9,256,128]{2,1,0:T(8,128)} fusion(f32[256,128]{1,0:T(8,128)S(1)} %get-tuple-element.50, f32[9,128]{1,0:T(8,128)S(1)} %get-tuple-element.51, f32[256,128]{1,0:T(8,128)S(1)} %get-tuple-element.49, f32[9,128]{1,0:T(8,128)S(1)} %get-tuple-element.52, f32[256,128]{1,0:T(8,128)S(1)} %get-tuple-element.48, ...), kind=kLoop, calls=%fused_computation | loop fusion | flops 4423680 | bytes 2265088 | tf_op jit(solution)/shard_map/add | solution.py:210
  18.1 3.5 %local_part.2.refs_0_ = f32[9,256,128]{2,1,0:T(8,128)} custom-call(f32[9,256,128]{2,1,0:T(8,128)} %values_ref.3, f32[9,256,128]{2,1,0:T(8,128)} %multiply_add_fusion.local_ref.refs_6_, f32[8,128]{1,0:T(8,128)} %mixing_ref.3), custom_call_target="tpu_custom_call" | custom-call | tf_op jit(solution)/shard_map/local_part/pallas_call | solution.py:103
  21.6 0.0 collective-permute-done.refs_1_
  21.6 0.0 collective-permute-done.1.refs_2_
  21.6 0.0 copy-start.1
  21.6 0.0 collective-permute-done.2.refs_3_
  21.6 0.0 copy-start.2
  21.6 0.0 collective-permute-done.3.refs_4_
  21.7 0.0 copy-start.3
  21.7 0.8 %collective-permute-done.4.refs_5_ = f32[9,16,256]{2,1,0:T(8,128)S(1)} collective-permute-done((f32[9,16,256]{2,1,0:T(8,128)}, f32[9,16,256]{2,1,0:T(8,128)S(1)}, u32[]{:S(2)}, u32[]{:S(2)}) %collective-permute-start.4) | collective-permute-done | bytes 147488 | tf_op jit(solution)/shard_map/ppermute | solution.py:218
  22.5 0.0 copy-done
  22.5 0.0 copy-done.1
  22.5 0.0 copy-done.2
  22.5 0.0 copy-done.3
  22.5 0.6 %copy-done.4 = f32[9,16,256]{2,1,0:T(8,128)} copy-done((f32[9,16,256]{2,1,0:T(8,128)}, f32[9,16,256]{2,1,0:T(8,128)S(1)}, u32[]{:S(2)}) %copy-start.4) | copy-done | bytes 147480
  23.1 6.0 %finish_send.1 = (f32[9,256,128]{2,1,0:T(8,128)}, f32[9,16,256]{2,1,0:T(8,128)}, f32[9,16,256]{2,1,0:T(8,128)}, f32[9,16,256]{2,1,0:T(8,128)}, f32[9,16,256]{2,1,0:T(8,128)}, /*index=5*/f32[9,16,256]{2,1,0:T(8,128)}) custom-call(s32[1]{0:T(128)} %bitcast.me_ref, s32[32,16]{1,0:T(8,128)} %bitcast.38, f32[9,256,128]{2,1,0:T(8,128)} %local_part.2.refs_0_, ...), custom_call_target="tpu_custom_call" | custom-call | tf_op jit(solution)/shard_map/finish_send/pallas_call | solution.py:171
  29.1 0.1 collective-permute-start.5
  29.2 0.1 collective-permute-start.6
  29.2 1.7 %collective-permute-start.7 = (f32[9,16,256]{2,1,0:T(8,128)}, f32[9,16,256]{2,1,0:T(8,128)S(1)}, u32[]{:S(2)}, u32[]{:S(2)}) collective-permute-start(f32[9,16,256]{2,1,0:T(8,128)} %get-tuple-element.24), channel_id=1, source_target_pairs={{0,16},{1,17},{2,18},{3,19},{4,20},{5,21},{6,22},{7,23},{8,24},{9,... | collective-permute-start | bytes 442376 | tf_op jit(solution)/shard_map/ppermute | solution.py:218
  31.0 4.2 %collective-permute-start.8 = (f32[9,16,256]{2,1,0:T(8,128)}, f32[9,16,256]{2,1,0:T(8,128)S(1)}, u32[]{:S(2)}, u32[]{:S(2)}) collective-permute-start(f32[9,16,256]{2,1,0:T(8,128)} %get-tuple-element.25), channel_id=1, source_target_pairs={{1,2},{2,1},{3,4},{4,3},{5,6},{6,5},{7,8},{8,7},{9,10},{10,9},{11,... | collective-permute-start | bytes 442376 | tf_op jit(solution)/shard_map/ppermute | solution.py:218
  35.2 3.4 %collective-permute-start.9 = (f32[9,16,256]{2,1,0:T(8,128)}, f32[9,16,256]{2,1,0:T(8,128)S(1)}, u32[]{:S(2)}, u32[]{:S(2)}) collective-permute-start(f32[9,16,256]{2,1,0:T(8,128)} %get-tuple-element.26), channel_id=1, source_target_pairs={{2,4},{3,5},{4,2},{5,3},{6,8},{7,9},{8,6},{9,7},{10,12},{11,13},{1... | collective-permute-start | bytes 442376 | tf_op jit(solution)/shard_map/ppermute | solution.py:218
  38.6 3.6 %local_part.3.refs_0_ = f32[9,256,128]{2,1,0:T(8,128)} custom-call(f32[9,256,128]{2,1,0:T(8,128)} %get-tuple-element.21.values_ref, f32[9,256,128]{2,1,0:T(8,128)} %multiply_add_fusion.local_ref.refs_6_, f32[8,128]{1,0:T(8,128)} %mixing_ref.3), custom_call_target="tpu_custom_call" | custom-call | tf_op jit(solution)/shard_map/local_part/pallas_call | solution.py:103
  42.2 0.0 collective-permute-done.5.refs_1_
  42.2 0.0 collective-permute-done.6.refs_2_
  42.2 0.0 copy-start.6
  42.2 0.0 collective-permute-done.7.refs_3_
  42.2 0.0 copy-start.7
  42.2 0.0 collective-permute-done.8.refs_4_
  42.2 0.0 copy-start.8
  42.2 2.6 %collective-permute-done.9.refs_5_ = f32[9,16,256]{2,1,0:T(8,128)S(1)} collective-permute-done((f32[9,16,256]{2,1,0:T(8,128)}, f32[9,16,256]{2,1,0:T(8,128)S(1)}, u32[]{:S(2)}, u32[]{:S(2)}) %collective-permute-start.9) | collective-permute-done | bytes 147488 | tf_op jit(solution)/shard_map/ppermute | solution.py:218
  44.8 0.0 copy-done.5
  44.8 0.0 copy-done.6
  44.8 0.0 copy-done.7
  44.8 0.0 copy-done.8
  44.8 0.7 %copy-done.9 = f32[9,16,256]{2,1,0:T(8,128)} copy-done((f32[9,16,256]{2,1,0:T(8,128)}, f32[9,16,256]{2,1,0:T(8,128)S(1)}, u32[]{:S(2)}) %copy-start.9) | copy-done | bytes 147480
  45.4 4.3 %finish.1 = f32[9,256,128]{2,1,0:T(8,128)} custom-call(s32[1]{0:T(128)} %bitcast.me_ref, s32[32,16]{1,0:T(8,128)} %bitcast.39, f32[9,256,128]{2,1,0:T(8,128)} %local_part.3.refs_0_, f32[9,16,256]{2,1,0:T(8,128)} %copy-done.5, f32[9,16,256]{2,1,0:T(8,128)} %copy-done.6, f32[9,16,256]{2,1,0:T(8,128)} %copy-done.7, f32[9,16,256]{2,1,0:T(8,128)} %copy-done.8, ...), custom_call_target="tpu_custom_call" | custom-call | tf_op jit(solution)/shard_map/finish/pallas_call | solution.py:171
  (12 shorter events, 0.1 us)
Async XLA Ops:
  0.0 16.2 %copy-start.11 = (s32[8,128]{1,0:T(8,128)S(1)}, s32[8,128]{1,0:T(8,128)}, u32[]{:S(2)}) copy-start(s32[8,128]{1,0:T(8,128)} %param.11) | copy-start | bytes 12292
  0.0 16.2 %copy-start.10 = (f32[8,9,128]{2,0,1:T(8,128)S(1)}, f32[8,9,128]{2,0,1:T(8,128)}, u32[]{:S(2)}) copy-start(f32[8,9,128]{2,0,1:T(8,128)} %param.8) | copy-start | bytes 110596
  5.9 15.7 %collective-permute-start = (f32[9,16,256]{2,1,0:T(8,128)}, f32[9,16,256]{2,1,0:T(8,128)S(1)}, u32[]{:S(2)}, u32[]{:S(2)}) collective-permute-start(f32[9,16,256]{2,1,0:T(8,128)} %get-tuple-element.16), channel_id=1, source_target_pairs={{0,1},{1,0},{2,3},{3,2},{4,5},{5,4},{6,7},{7,6},{8,9},{9,8},{10,11... | collective-permute-start | bytes 442376 | tf_op jit(solution)/shard_map/ppermute | solution.py:218
  6.6 15.0 %collective-permute-start.1 = (f32[9,16,256]{2,1,0:T(8,128)}, f32[9,16,256]{2,1,0:T(8,128)S(1)}, u32[]{:S(2)}, u32[]{:S(2)}) collective-permute-start(f32[9,16,256]{2,1,0:T(8,128)} %get-tuple-element.17), channel_id=1, source_target_pairs={{0,2},{1,3},{2,0},{3,1},{4,6},{5,7},{6,4},{7,5},{8,10},{9,11},{10,... | collective-permute-start | bytes 442376 | tf_op jit(solution)/shard_map/ppermute | solution.py:218
  7.8 13.8 %collective-permute-start.2 = (f32[9,16,256]{2,1,0:T(8,128)}, f32[9,16,256]{2,1,0:T(8,128)S(1)}, u32[]{:S(2)}, u32[]{:S(2)}) collective-permute-start(f32[9,16,256]{2,1,0:T(8,128)} %get-tuple-element.18), channel_id=1, source_target_pairs={{0,16},{1,17},{2,18},{3,19},{4,20},{5,21},{6,22},{7,23},{8,24},{9,... | collective-permute-start | bytes 442376 | tf_op jit(solution)/shard_map/ppermute | solution.py:218
  7.9 13.8 %collective-permute-start.3 = (f32[9,16,256]{2,1,0:T(8,128)}, f32[9,16,256]{2,1,0:T(8,128)S(1)}, u32[]{:S(2)}, u32[]{:S(2)}) collective-permute-start(f32[9,16,256]{2,1,0:T(8,128)} %get-tuple-element.19), channel_id=1, source_target_pairs={{1,2},{2,1},{3,4},{4,3},{5,6},{6,5},{7,8},{8,7},{9,10},{10,9},{11,... | collective-permute-start | bytes 442376 | tf_op jit(solution)/shard_map/ppermute | solution.py:218
  10.5 11.9 %collective-permute-start.4 = (f32[9,16,256]{2,1,0:T(8,128)}, f32[9,16,256]{2,1,0:T(8,128)S(1)}, u32[]{:S(2)}, u32[]{:S(2)}) collective-permute-start(f32[9,16,256]{2,1,0:T(8,128)} %get-tuple-element.20), channel_id=1, source_target_pairs={{2,4},{3,5},{4,2},{5,3},{6,8},{7,9},{8,6},{9,7},{10,12},{11,13},{1... | collective-permute-start | bytes 442376 | tf_op jit(solution)/shard_map/ppermute | solution.py:218
  21.6 0.9 %copy-start = (f32[9,16,256]{2,1,0:T(8,128)}, f32[9,16,256]{2,1,0:T(8,128)S(1)}, u32[]{:S(2)}) copy-start(f32[9,16,256]{2,1,0:T(8,128)S(1)} %collective-permute-done.refs_1_) | copy-start | bytes 442372
  21.6 0.9 %copy-start.1 = (f32[9,16,256]{2,1,0:T(8,128)}, f32[9,16,256]{2,1,0:T(8,128)S(1)}, u32[]{:S(2)}) copy-start(f32[9,16,256]{2,1,0:T(8,128)S(1)} %collective-permute-done.1.refs_2_) | copy-start | bytes 442372
  21.6 0.9 %copy-start.2 = (f32[9,16,256]{2,1,0:T(8,128)}, f32[9,16,256]{2,1,0:T(8,128)S(1)}, u32[]{:S(2)}) copy-start(f32[9,16,256]{2,1,0:T(8,128)S(1)} %collective-permute-done.2.refs_3_) | copy-start | bytes 442372
  21.7 0.8 %copy-start.3 = (f32[9,16,256]{2,1,0:T(8,128)}, f32[9,16,256]{2,1,0:T(8,128)S(1)}, u32[]{:S(2)}) copy-start(f32[9,16,256]{2,1,0:T(8,128)S(1)} %collective-permute-done.3.refs_4_) | copy-start | bytes 442372
  22.5 0.7 %copy-start.4 = (f32[9,16,256]{2,1,0:T(8,128)}, f32[9,16,256]{2,1,0:T(8,128)S(1)}, u32[]{:S(2)}) copy-start(f32[9,16,256]{2,1,0:T(8,128)S(1)} %collective-permute-done.4.refs_5_) | copy-start | bytes 442372
  29.1 13.1 %collective-permute-start.5 = (f32[9,16,256]{2,1,0:T(8,128)}, f32[9,16,256]{2,1,0:T(8,128)S(1)}, u32[]{:S(2)}, u32[]{:S(2)}) collective-permute-start(f32[9,16,256]{2,1,0:T(8,128)} %get-tuple-element.22), channel_id=1, source_target_pairs={{0,1},{1,0},{2,3},{3,2},{4,5},{5,4},{6,7},{7,6},{8,9},{9,8},{10,11... | collective-permute-start | bytes 442376 | tf_op jit(solution)/shard_map/ppermute | solution.py:218
  29.2 13.0 %collective-permute-start.6 = (f32[9,16,256]{2,1,0:T(8,128)}, f32[9,16,256]{2,1,0:T(8,128)S(1)}, u32[]{:S(2)}, u32[]{:S(2)}) collective-permute-start(f32[9,16,256]{2,1,0:T(8,128)} %get-tuple-element.23), channel_id=1, source_target_pairs={{0,2},{1,3},{2,0},{3,1},{4,6},{5,7},{6,4},{7,5},{8,10},{9,11},{10,... | collective-permute-start | bytes 442376 | tf_op jit(solution)/shard_map/ppermute | solution.py:218
  29.2 12.9 %collective-permute-start.7 = (f32[9,16,256]{2,1,0:T(8,128)}, f32[9,16,256]{2,1,0:T(8,128)S(1)}, u32[]{:S(2)}, u32[]{:S(2)}) collective-permute-start(f32[9,16,256]{2,1,0:T(8,128)} %get-tuple-element.24), channel_id=1, source_target_pairs={{0,16},{1,17},{2,18},{3,19},{4,20},{5,21},{6,22},{7,23},{8,24},{9,... | collective-permute-start | bytes 442376 | tf_op jit(solution)/shard_map/ppermute | solution.py:218
  31.0 11.2 %collective-permute-start.8 = (f32[9,16,256]{2,1,0:T(8,128)}, f32[9,16,256]{2,1,0:T(8,128)S(1)}, u32[]{:S(2)}, u32[]{:S(2)}) collective-permute-start(f32[9,16,256]{2,1,0:T(8,128)} %get-tuple-element.25), channel_id=1, source_target_pairs={{1,2},{2,1},{3,4},{4,3},{5,6},{6,5},{7,8},{8,7},{9,10},{10,9},{11,... | collective-permute-start | bytes 442376 | tf_op jit(solution)/shard_map/ppermute | solution.py:218
  35.2 9.6 %collective-permute-start.9 = (f32[9,16,256]{2,1,0:T(8,128)}, f32[9,16,256]{2,1,0:T(8,128)S(1)}, u32[]{:S(2)}, u32[]{:S(2)}) collective-permute-start(f32[9,16,256]{2,1,0:T(8,128)} %get-tuple-element.26), channel_id=1, source_target_pairs={{2,4},{3,5},{4,2},{5,3},{6,8},{7,9},{8,6},{9,7},{10,12},{11,13},{1... | collective-permute-start | bytes 442376 | tf_op jit(solution)/shard_map/ppermute | solution.py:218
  42.2 2.6 %copy-start.5 = (f32[9,16,256]{2,1,0:T(8,128)}, f32[9,16,256]{2,1,0:T(8,128)S(1)}, u32[]{:S(2)}) copy-start(f32[9,16,256]{2,1,0:T(8,128)S(1)} %collective-permute-done.5.refs_1_) | copy-start | bytes 442372
  42.2 2.6 %copy-start.6 = (f32[9,16,256]{2,1,0:T(8,128)}, f32[9,16,256]{2,1,0:T(8,128)S(1)}, u32[]{:S(2)}) copy-start(f32[9,16,256]{2,1,0:T(8,128)S(1)} %collective-permute-done.6.refs_2_) | copy-start | bytes 442372
  42.2 2.6 %copy-start.7 = (f32[9,16,256]{2,1,0:T(8,128)}, f32[9,16,256]{2,1,0:T(8,128)S(1)}, u32[]{:S(2)}) copy-start(f32[9,16,256]{2,1,0:T(8,128)S(1)} %collective-permute-done.7.refs_3_) | copy-start | bytes 442372
  42.2 2.6 %copy-start.8 = (f32[9,16,256]{2,1,0:T(8,128)}, f32[9,16,256]{2,1,0:T(8,128)S(1)}, u32[]{:S(2)}) copy-start(f32[9,16,256]{2,1,0:T(8,128)S(1)} %collective-permute-done.8.refs_4_) | copy-start | bytes 442372
  44.8 0.7 %copy-start.9 = (f32[9,16,256]{2,1,0:T(8,128)}, f32[9,16,256]{2,1,0:T(8,128)S(1)}, u32[]{:S(2)}) copy-start(f32[9,16,256]{2,1,0:T(8,128)S(1)} %collective-permute-done.9.refs_5_) | copy-start | bytes 442372

commit v8 on v6

--- a/solution.py
+++ b/solution.py
@@ -58,14 +58,9 @@
 
 def gather_send(values, select, groups, hslot):
     levels, pulses, capacity = values.shape
-    lb = level_block(levels)
-    send_spec = pl.BlockSpec((lb, hslot, pulses), lambda i: (i, 0, 0))
     return pl.pallas_call(
         functools.partial(select_kernel, groups, hslot),
         out_shape=[jax.ShapeDtypeStruct((levels, hslot, pulses), jnp.float32)] * groups,
-        grid=(levels // lb,),
-        in_specs=[pl.BlockSpec((lb, pulses, capacity), lambda i: (i, 0, 0)), full_spec(select.shape)],
-        out_specs=[send_spec] * groups,
         interpret=INTERPRET,
         name="gather_send",
     )(values, select)
@@ -95,7 +90,7 @@
         grid=(pulses // pb,),
         in_specs=[
             value_spec,
-            pl.BlockSpec((levels, capacity, capacity), lambda i: (0, 1, 0)),
+            pl.BlockSpec((levels, capacity, capacity), lambda i: (0, 0, 0)),
             full_spec(mixing.shape),
         ],
         out_specs=value_spec,
@@ -107,24 +102,25 @@
 def finish_kernel(groups, hslot, send, *refs):
     partial_ref = refs[0]
     incoming = refs[1 : 1 + groups]
-    remote_ref, deposition_ref, count_ref, select_ref = refs[1 + groups : 5 + groups]
-    out_ref = refs[5 + groups]
-    send_refs = refs[6 + groups :]
-    rows = groups * hslot
+    remote_refs = refs[1 + groups : 1 + 2 * groups]
+    deposition_ref, count_ref, select_ref = refs[1 + 2 * groups : 4 + 2 * groups]
+    out_ref = refs[4 + 2 * groups]
+    send_refs = refs[5 + 2 * groups :]
     lb = partial_ref.shape[0]
-    first = pl.program_id(0) * lb
+    first = 0
     capacity = partial_ref.shape[2]
     living = lax.broadcasted_iota(jnp.int32, (1, capacity), 1) < count_ref[...]
     for level in range(lb):
         received = jnp.concatenate([incoming[g][level] for g in range(groups)], axis=0)
+        weights = jnp.concatenate([remote_refs[g][level] for g in range(groups)], axis=0)
         far = lax.dot_general(
             received,
-            remote_ref[level, :rows, :],
+            weights,
             TN,
             precision=HIGHEST,
             preferred_element_type=jnp.float32,
         )
-        keep = 1.0 - deposition_ref[pl.ds(first + level, 1), :]
+        keep = 1.0 - deposition_ref[first + level : first + level + 1, :]
         x = (partial_ref[level] + far) * keep
         x = jnp.where(living, x, 0.0)
         out_ref[level] = x
@@ -140,33 +136,25 @@
     levels, pulses, capacity = partial.shape
     groups = len(incoming)
     hslot = incoming[0].shape[1]
-    lb = level_block(levels)
-    value_spec = pl.BlockSpec((lb, pulses, capacity), lambda i: (i, 0, 0))
-    send_spec = pl.BlockSpec((lb, hslot, pulses), lambda i: (i, 0, 0))
     shapes = [jax.ShapeDtypeStruct(partial.shape, jnp.float32)]
-    out_specs = [value_spec]
     if send:
         shapes += [jax.ShapeDtypeStruct((levels, hslot, pulses), jnp.float32)] * groups
-        out_specs += [send_spec] * groups
-    in_specs = (
-        [value_spec]
-        + [send_spec] * groups
-        + [
-            pl.BlockSpec((lb, capacity, capacity), lambda i: (i, 0, 0)),
-            full_spec(deposition.shape),
-            full_spec(count.shape),
-            full_spec(select.shape),
-        ]
-    )
+    operands = [partial, *incoming, *([matrix] * groups), deposition, count, select]
+    specs = [full_spec(x.shape) for x in operands]
+    for g in range(groups):
+        block = capacity // hslot + g
+        specs[1 + groups + g] = pl.BlockSpec(
+            (levels, hslot, capacity), lambda i, block=block: (0, block, 0)
+        )
     outs = pl.pallas_call(
         functools.partial(finish_kernel, groups, hslot, send),
         out_shape=shapes,
-        grid=(levels // lb,),
-        in_specs=in_specs,
-        out_specs=out_specs,
+        grid=(1,),
+        in_specs=specs,
+        out_specs=[full_spec(x.shape) for x in shapes],
         interpret=INTERPRET,
         name="finish_send" if send else "finish",
-    )(partial, *incoming, matrix, deposition, count, select)
+    )(*operands)
     return outs[0], outs[1:]
 
 
@@ -193,11 +181,13 @@
     beyond = halo_index - capacity
     sender = beyond // hslot
     place = beyond % hslot
-    row = jnp.where(beyond < 0, capacity + halo_index, -1)
+    row = jnp.where(beyond < 0, halo_index, -1)
     for g, partner in enumerate(partners):
-        row = jnp.where((beyond >= 0) & (sender == partner(me, jnp)), g * hslot + place, row)
-    slots = jnp.arange(2 * capacity, dtype=jnp.int32)[:, None]
-    diagonal = (slots == capacity + lanes[None, :]).astype(f32)
+        row = jnp.where(
+            (beyond >= 0) & (sender == partner(me, jnp)), capacity + g * hslot + place, row
+        )
+    slots = jnp.arange(capacity + groups * hslot, dtype=jnp.int32)[:, None]
+    diagonal = (slots == lanes[None, :]).astype(f32)
     matrix = sum(
         flux_weight[k][:, None, :] * ((row[k][None, :] == slots).astype(f32) - diagonal)[None]
         for k in range(nbr)

time: 49.5 us -> 47.8 us (0.966)
  Pallas kernels: 20.7 us -> 19.4 us
    pallas_call x2, Pallas kernels: 9.8 us -> 8.89 us  [finish(): pl.pallas_call(functools.partial(finish_kernel, groups, hslot, send), out...]
  transfers between devices with their start and end apart: 10 -> 10, of which waited for: 2 -> 2; matrix products, arithmetic and copies ran while one was open for 4% -> 3% of each run, Pallas kernels for 14% -> 15%
where the time goes in v8:
time: 47.8 us; the launch traced here: 47.5 us
  Pallas kernels  19.4 us (41%)
  starting transfers between devices  18.6 us (39%)
  waiting for transfers between devices  3.62 us (8%)
  other arithmetic  2.68 us (6%)
  local copies, waits for them, and re-layouts  2.22 us (5%)
  between operations  0.92 us (2%)
    ppermute x10, starting transfers between devices, per_device(): lax.ppermute(outgoing[g], 'cells', perm=pair_list(n, partner))  18.6 us
    pallas_call x2, Pallas kernels, finish(): pl.pallas_call(functools.partial(finish_kernel, groups, hslot, send), out...  8.89 us
    pallas_call x2, Pallas kernels, local_part(): pl.pallas_call(local_kernel, out_shape=jax.ShapeDtypeStruct(values.shape,...  7.04 us
    ppermute x10, waiting for transfers between devices, per_device(): lax.ppermute(outgoing[g], 'cells', perm=pair_list(n, partner))  3.62 us
    pallas_call x1, Pallas kernels, gather_send(): pl.pallas_call(functools.partial(select_kernel, groups, hslot), out_shape...  3.47 us
    add x1, other arithmetic, per_device(): sum((flux_weight[k][:, None, :] * ((row[k][None, :] == slots).astype(f32)...  1.46 us
    unnamed x24, local copies, waits for them, and re-layouts  1.32 us
  transfers between devices with their start and end apart: 10, of which 2 were waited for; matrix products, arithmetic and copies ran while one was open for 3% of the time, Pallas kernels for 15%

profile of v8, /device:TPU:25, one launch (start us, length us, event | category | flops | bytes accessed | tf_op | source)
XLA Modules:
  0.0 47.5 jit_solution(7283407016745107334)
XLA Ops:
  0.0 0.1 stack.23
  0.1 0.1 iota_compare_fusion.10
  0.2 0.8 %copy.26 = s32[32,16]{1,0:T(8,128)S(1)} copy(s32[32,16]{0,1:T(8,128)} %bitcast.45) | data formatting | bytes 4096 | tf_op jit(solution)/shard_map/eq | solution.py:175
  0.9 0.1 iota_compare_fusion
  1.1 0.9 %convert_reduce_fusion = f32[5,16,128]{2,1,0:T(8,128)} fusion(pred[32,16,128]{2,1,0:T(8,128)(4,1)S(1)} %iota_compare_fusion, pred[5,32]{1,0:T(8,128)(4,1)S(1)} %iota_compare_fusion.10), kind=kLoop, calls=%fused_computation | loop fusion | flops 972800 | bytes 106656 | tf_op jit(solution)/shard_map/reduce_sum | solution.py:176
  1.9 3.5 %gather_send.1 = (f32[9,16,256]{2,1,0:T(8,128)}, f32[9,16,256]{2,1,0:T(8,128)}, f32[9,16,256]{2,1,0:T(8,128)}, f32[9,16,256]{2,1,0:T(8,128)}, f32[9,16,256]{2,1,0:T(8,128)}) custom-call(f32[9,256,128]{2,1,0:T(8,128)} %values_ref.3, f32[80,128]{1,0:T(8,128)} %bitcast.42), custom_call_target="tpu_custom_call" | custom-call | tf_op jit(solution)/shard_map/gather_send/pallas_call | solution.py:61
  5.4 0.7 %collective-permute-start = (f32[9,16,256]{2,1,0:T(8,128)}, f32[9,16,256]{2,1,0:T(8,128)S(1)}, u32[]{:S(2)}, u32[]{:S(2)}) collective-permute-start(f32[9,16,256]{2,1,0:T(8,128)} %get-tuple-element.16), channel_id=1, source_target_pairs={{0,1},{1,0},{2,3},{3,2},{4,5},{5,4},{6,7},{7,6},{8,9},{9,8},{10,11... | collective-permute-start | bytes 442376 | tf_op jit(solution)/shard_map/ppermute | solution.py:199
  6.1 1.2 %collective-permute-start.1 = (f32[9,16,256]{2,1,0:T(8,128)}, f32[9,16,256]{2,1,0:T(8,128)S(1)}, u32[]{:S(2)}, u32[]{:S(2)}) collective-permute-start(f32[9,16,256]{2,1,0:T(8,128)} %get-tuple-element.17), channel_id=1, source_target_pairs={{0,2},{1,3},{2,0},{3,1},{4,6},{5,7},{6,4},{7,5},{8,10},{9,11},{10,... | collective-permute-start | bytes 442376 | tf_op jit(solution)/shard_map/ppermute | solution.py:199
  7.3 0.1 collective-permute-start.2
  7.3 2.6 %collective-permute-start.3 = (f32[9,16,256]{2,1,0:T(8,128)}, f32[9,16,256]{2,1,0:T(8,128)S(1)}, u32[]{:S(2)}, u32[]{:S(2)}) collective-permute-start(f32[9,16,256]{2,1,0:T(8,128)} %get-tuple-element.19), channel_id=1, source_target_pairs={{1,2},{2,1},{3,4},{4,3},{5,6},{6,5},{7,8},{8,7},{9,10},{10,9},{11,... | collective-permute-start | bytes 442376 | tf_op jit(solution)/shard_map/ppermute | solution.py:199
  9.9 4.9 %collective-permute-start.4 = (f32[9,16,256]{2,1,0:T(8,128)}, f32[9,16,256]{2,1,0:T(8,128)S(1)}, u32[]{:S(2)}, u32[]{:S(2)}) collective-permute-start(f32[9,16,256]{2,1,0:T(8,128)} %get-tuple-element.20), channel_id=1, source_target_pairs={{2,4},{3,5},{4,2},{5,3},{6,8},{7,9},{8,6},{9,7},{10,12},{11,13},{1... | collective-permute-start | bytes 442376 | tf_op jit(solution)/shard_map/ppermute | solution.py:199
  15.5 0.0 copy-done.11
  15.6 0.0 copy-done.10
  15.8 1.5 %multiply_add_fusion.local_ref.refs_6_.refs_7_.refs_8_.refs_9_.refs_10_ = f32[9,208,128]{2,1,0:T(8,128)} fusion(f32[208,128]{1,0:T(8,128)S(1)} %get-tuple-element.43, f32[9,128]{1,0:T(8,128)S(1)} %get-tuple-element.51, f32[208,128]{1,0:T(8,128)S(1)} %get-tuple-element.44, f32[9,128]{1,0:T(8,128)S(1)} %get-tuple-element.52, ...), kind=kLoop, calls=%fused_computation.1 | loop fusion | flops 3594240 | bytes 1847296 | tf_op jit(solution)/shard_map/add | solution.py:191
  17.3 3.5 %local_part.2.refs_0_ = f32[9,256,128]{2,1,0:T(8,128)} custom-call(f32[9,256,128]{2,1,0:T(8,128)} %values_ref.3, f32[9,208,128]{2,1,0:T(8,128)} %multiply_add_fusion.local_ref.refs_6_.refs_7_.refs_8_.refs_9_.refs_10_, f32[8,128]{1,0:T(8,128)} %mixing_ref.3), custom_call_target="tpu_custom_call" | custom-call | tf_op jit(solution)/shard_map/local_part/pallas_call | solution.py:87
  20.8 0.0 collective-permute-done.refs_1_
  20.8 0.0 collective-permute-done.1.refs_2_
  20.8 0.0 copy-start.1
  20.8 0.0 collective-permute-done.2.refs_3_
  20.8 0.0 copy-start.2
  20.8 0.0 collective-permute-done.3.refs_4_
  20.8 0.0 copy-start.3
  20.9 1.0 %collective-permute-done.4.refs_5_ = f32[9,16,256]{2,1,0:T(8,128)S(1)} collective-permute-done((f32[9,16,256]{2,1,0:T(8,128)}, f32[9,16,256]{2,1,0:T(8,128)S(1)}, u32[]{:S(2)}, u32[]{:S(2)}) %collective-permute-start.4) | collective-permute-done | bytes 147488 | tf_op jit(solution)/shard_map/ppermute | solution.py:199
  21.9 0.0 copy-done
  21.9 0.0 copy-done.1
  21.9 0.0 copy-done.2
  21.9 0.0 copy-done.3
  21.9 0.6 %copy-done.4 = f32[9,16,256]{2,1,0:T(8,128)} copy-done((f32[9,16,256]{2,1,0:T(8,128)}, f32[9,16,256]{2,1,0:T(8,128)S(1)}, u32[]{:S(2)}) %copy-start.4) | copy-done | bytes 147480
  22.6 5.0 %finish_send.1 = (f32[9,256,128]{2,1,0:T(8,128)}, f32[9,16,256]{2,1,0:T(8,128)}, f32[9,16,256]{2,1,0:T(8,128)}, f32[9,16,256]{2,1,0:T(8,128)}, f32[9,16,256]{2,1,0:T(8,128)}, /*index=5*/f32[9,16,256]{2,1,0:T(8,128)}) custom-call(f32[9,256,128]{2,1,0:T(8,128)} %local_part.2.refs_0_, f32[9,16,256]{2,1,0:T(8,128)} %copy-done, f32[9,16,256]{2,1,0:T(8,128)} %copy-done.1, ...), custom_call_target="tpu_custom_call" | custom-call | tf_op jit(solution)/shard_map/finish_send/pallas_call | solution.py:149
  27.6 0.1 collective-permute-start.5
  27.7 0.0 collective-permute-start.6
  27.7 1.5 %collective-permute-start.7 = (f32[9,16,256]{2,1,0:T(8,128)}, f32[9,16,256]{2,1,0:T(8,128)S(1)}, u32[]{:S(2)}, u32[]{:S(2)}) collective-permute-start(f32[9,16,256]{2,1,0:T(8,128)} %get-tuple-element.24), channel_id=1, source_target_pairs={{0,16},{1,17},{2,18},{3,19},{4,20},{5,21},{6,22},{7,23},{8,24},{9,... | collective-permute-start | bytes 442376 | tf_op jit(solution)/shard_map/ppermute | solution.py:199
  29.2 4.2 %collective-permute-start.8 = (f32[9,16,256]{2,1,0:T(8,128)}, f32[9,16,256]{2,1,0:T(8,128)S(1)}, u32[]{:S(2)}, u32[]{:S(2)}) collective-permute-start(f32[9,16,256]{2,1,0:T(8,128)} %get-tuple-element.25), channel_id=1, source_target_pairs={{1,2},{2,1},{3,4},{4,3},{5,6},{6,5},{7,8},{8,7},{9,10},{10,9},{11,... | collective-permute-start | bytes 442376 | tf_op jit(solution)/shard_map/ppermute | solution.py:199
  33.4 3.4 %collective-permute-start.9 = (f32[9,16,256]{2,1,0:T(8,128)}, f32[9,16,256]{2,1,0:T(8,128)S(1)}, u32[]{:S(2)}, u32[]{:S(2)}) collective-permute-start(f32[9,16,256]{2,1,0:T(8,128)} %get-tuple-element.26), channel_id=1, source_target_pairs={{2,4},{3,5},{4,2},{5,3},{6,8},{7,9},{8,6},{9,7},{10,12},{11,13},{1... | collective-permute-start | bytes 442376 | tf_op jit(solution)/shard_map/ppermute | solution.py:199
  36.8 3.5 %local_part.3.refs_0_ = f32[9,256,128]{2,1,0:T(8,128)} custom-call(f32[9,256,128]{2,1,0:T(8,128)} %get-tuple-element.21.values_ref, f32[9,208,128]{2,1,0:T(8,128)} %multiply_add_fusion.local_ref.refs_6_.refs_7_.refs_8_.refs_9_.refs_10_, f32[8,128]{1,0:T(8,128)} %mixing_ref.3), custom_call_target="tpu_custom_call" | custom-call | tf_op jit(solution)/shard_map/local_part/pallas_call | solution.py:87
  40.3 0.0 collective-permute-done.5.refs_1_
  40.3 0.0 collective-permute-done.6.refs_2_
  40.3 0.0 copy-start.6
  40.4 0.0 collective-permute-done.7.refs_3_
  40.4 0.0 copy-start.7
  40.4 0.0 collective-permute-done.8.refs_4_
  40.4 0.0 copy-start.8
  40.4 2.6 %collective-permute-done.9.refs_5_ = f32[9,16,256]{2,1,0:T(8,128)S(1)} collective-permute-done((f32[9,16,256]{2,1,0:T(8,128)}, f32[9,16,256]{2,1,0:T(8,128)S(1)}, u32[]{:S(2)}, u32[]{:S(2)}) %collective-permute-start.9) | collective-permute-done | bytes 147488 | tf_op jit(solution)/shard_map/ppermute | solution.py:199
  43.0 0.0 copy-done.5
  43.0 0.0 copy-done.6
  43.0 0.0 copy-done.7
  43.0 0.6 %copy-done.9 = f32[9,16,256]{2,1,0:T(8,128)} copy-done((f32[9,16,256]{2,1,0:T(8,128)}, f32[9,16,256]{2,1,0:T(8,128)S(1)}, u32[]{:S(2)}) %copy-start.9) | copy-done | bytes 147480
  43.6 3.8 %finish.1 = f32[9,256,128]{2,1,0:T(8,128)} custom-call(f32[9,256,128]{2,1,0:T(8,128)} %local_part.3.refs_0_, f32[9,16,256]{2,1,0:T(8,128)} %copy-done.5, f32[9,16,256]{2,1,0:T(8,128)} %copy-done.6, f32[9,16,256]{2,1,0:T(8,128)} %copy-done.7, f32[9,16,256]{2,1,0:T(8,128)} %copy-done.8, f32[9,16,256]{2,1,0:T(8,128)} %copy-done.9, ...), custom_call_target="tpu_custom_call" | custom-call | tf_op jit(solution)/shard_map/finish/pallas_call | solution.py:149
  (18 shorter events, 0.2 us)
Async XLA Ops:
  0.0 15.5 %copy-start.11 = (s32[8,128]{1,0:T(8,128)S(1)}, s32[8,128]{1,0:T(8,128)}, u32[]{:S(2)}) copy-start(s32[8,128]{1,0:T(8,128)} %param.11) | copy-start | bytes 12292
  0.0 15.6 %copy-start.10 = (f32[8,9,128]{2,0,1:T(8,128)S(1)}, f32[8,9,128]{2,0,1:T(8,128)}, u32[]{:S(2)}) copy-start(f32[8,9,128]{2,0,1:T(8,128)} %param.8) | copy-start | bytes 110596
  5.4 15.4 %collective-permute-start = (f32[9,16,256]{2,1,0:T(8,128)}, f32[9,16,256]{2,1,0:T(8,128)S(1)}, u32[]{:S(2)}, u32[]{:S(2)}) collective-permute-start(f32[9,16,256]{2,1,0:T(8,128)} %get-tuple-element.16), channel_id=1, source_target_pairs={{0,1},{1,0},{2,3},{3,2},{4,5},{5,4},{6,7},{7,6},{8,9},{9,8},{10,11... | collective-permute-start | bytes 442376 | tf_op jit(solution)/shard_map/ppermute | solution.py:199
  6.1 14.7 %collective-permute-start.1 = (f32[9,16,256]{2,1,0:T(8,128)}, f32[9,16,256]{2,1,0:T(8,128)S(1)}, u32[]{:S(2)}, u32[]{:S(2)}) collective-permute-start(f32[9,16,256]{2,1,0:T(8,128)} %get-tuple-element.17), channel_id=1, source_target_pairs={{0,2},{1,3},{2,0},{3,1},{4,6},{5,7},{6,4},{7,5},{8,10},{9,11},{10,... | collective-permute-start | bytes 442376 | tf_op jit(solution)/shard_map/ppermute | solution.py:199
  7.3 13.5 %collective-permute-start.2 = (f32[9,16,256]{2,1,0:T(8,128)}, f32[9,16,256]{2,1,0:T(8,128)S(1)}, u32[]{:S(2)}, u32[]{:S(2)}) collective-permute-start(f32[9,16,256]{2,1,0:T(8,128)} %get-tuple-element.18), channel_id=1, source_target_pairs={{0,16},{1,17},{2,18},{3,19},{4,20},{5,21},{6,22},{7,23},{8,24},{9,... | collective-permute-start | bytes 442376 | tf_op jit(solution)/shard_map/ppermute | solution.py:199
  7.3 13.5 %collective-permute-start.3 = (f32[9,16,256]{2,1,0:T(8,128)}, f32[9,16,256]{2,1,0:T(8,128)S(1)}, u32[]{:S(2)}, u32[]{:S(2)}) collective-permute-start(f32[9,16,256]{2,1,0:T(8,128)} %get-tuple-element.19), channel_id=1, source_target_pairs={{1,2},{2,1},{3,4},{4,3},{5,6},{6,5},{7,8},{8,7},{9,10},{10,9},{11,... | collective-permute-start | bytes 442376 | tf_op jit(solution)/shard_map/ppermute | solution.py:199
  9.9 11.9 %collective-permute-start.4 = (f32[9,16,256]{2,1,0:T(8,128)}, f32[9,16,256]{2,1,0:T(8,128)S(1)}, u32[]{:S(2)}, u32[]{:S(2)}) collective-permute-start(f32[9,16,256]{2,1,0:T(8,128)} %get-tuple-element.20), channel_id=1, source_target_pairs={{2,4},{3,5},{4,2},{5,3},{6,8},{7,9},{8,6},{9,7},{10,12},{11,13},{1... | collective-permute-start | bytes 442376 | tf_op jit(solution)/shard_map/ppermute | solution.py:199
  20.8 1.1 %copy-start = (f32[9,16,256]{2,1,0:T(8,128)}, f32[9,16,256]{2,1,0:T(8,128)S(1)}, u32[]{:S(2)}) copy-start(f32[9,16,256]{2,1,0:T(8,128)S(1)} %collective-permute-done.refs_1_) | copy-start | bytes 442372
  20.8 1.1 %copy-start.1 = (f32[9,16,256]{2,1,0:T(8,128)}, f32[9,16,256]{2,1,0:T(8,128)S(1)}, u32[]{:S(2)}) copy-start(f32[9,16,256]{2,1,0:T(8,128)S(1)} %collective-permute-done.1.refs_2_) | copy-start | bytes 442372
  20.8 1.1 %copy-start.2 = (f32[9,16,256]{2,1,0:T(8,128)}, f32[9,16,256]{2,1,0:T(8,128)S(1)}, u32[]{:S(2)}) copy-start(f32[9,16,256]{2,1,0:T(8,128)S(1)} %collective-permute-done.2.refs_3_) | copy-start | bytes 442372
  20.8 1.1 %copy-start.3 = (f32[9,16,256]{2,1,0:T(8,128)}, f32[9,16,256]{2,1,0:T(8,128)S(1)}, u32[]{:S(2)}) copy-start(f32[9,16,256]{2,1,0:T(8,128)S(1)} %collective-permute-done.3.refs_4_) | copy-start | bytes 442372
  21.9 0.7 %copy-start.4 = (f32[9,16,256]{2,1,0:T(8,128)}, f32[9,16,256]{2,1,0:T(8,128)S(1)}, u32[]{:S(2)}) copy-start(f32[9,16,256]{2,1,0:T(8,128)S(1)} %collective-permute-done.4.refs_5_) | copy-start | bytes 442372
  27.6 12.7 %collective-permute-start.5 = (f32[9,16,256]{2,1,0:T(8,128)}, f32[9,16,256]{2,1,0:T(8,128)S(1)}, u32[]{:S(2)}, u32[]{:S(2)}) collective-permute-start(f32[9,16,256]{2,1,0:T(8,128)} %get-tuple-element.22), channel_id=1, source_target_pairs={{0,1},{1,0},{2,3},{3,2},{4,5},{5,4},{6,7},{7,6},{8,9},{9,8},{10,11... | collective-permute-start | bytes 442376 | tf_op jit(solution)/shard_map/ppermute | solution.py:199
  27.7 12.7 %collective-permute-start.6 = (f32[9,16,256]{2,1,0:T(8,128)}, f32[9,16,256]{2,1,0:T(8,128)S(1)}, u32[]{:S(2)}, u32[]{:S(2)}) collective-permute-start(f32[9,16,256]{2,1,0:T(8,128)} %get-tuple-element.23), channel_id=1, source_target_pairs={{0,2},{1,3},{2,0},{3,1},{4,6},{5,7},{6,4},{7,5},{8,10},{9,11},{10,... | collective-permute-start | bytes 442376 | tf_op jit(solution)/shard_map/ppermute | solution.py:199
  27.7 12.7 %collective-permute-start.7 = (f32[9,16,256]{2,1,0:T(8,128)}, f32[9,16,256]{2,1,0:T(8,128)S(1)}, u32[]{:S(2)}, u32[]{:S(2)}) collective-permute-start(f32[9,16,256]{2,1,0:T(8,128)} %get-tuple-element.24), channel_id=1, source_target_pairs={{0,16},{1,17},{2,18},{3,19},{4,20},{5,21},{6,22},{7,23},{8,24},{9,... | collective-permute-start | bytes 442376 | tf_op jit(solution)/shard_map/ppermute | solution.py:199
  29.2 11.2 %collective-permute-start.8 = (f32[9,16,256]{2,1,0:T(8,128)}, f32[9,16,256]{2,1,0:T(8,128)S(1)}, u32[]{:S(2)}, u32[]{:S(2)}) collective-permute-start(f32[9,16,256]{2,1,0:T(8,128)} %get-tuple-element.25), channel_id=1, source_target_pairs={{1,2},{2,1},{3,4},{4,3},{5,6},{6,5},{7,8},{8,7},{9,10},{10,9},{11,... | collective-permute-start | bytes 442376 | tf_op jit(solution)/shard_map/ppermute | solution.py:199
  33.4 9.6 %collective-permute-start.9 = (f32[9,16,256]{2,1,0:T(8,128)}, f32[9,16,256]{2,1,0:T(8,128)S(1)}, u32[]{:S(2)}, u32[]{:S(2)}) collective-permute-start(f32[9,16,256]{2,1,0:T(8,128)} %get-tuple-element.26), channel_id=1, source_target_pairs={{2,4},{3,5},{4,2},{5,3},{6,8},{7,9},{8,6},{9,7},{10,12},{11,13},{1... | collective-permute-start | bytes 442376 | tf_op jit(solution)/shard_map/ppermute | solution.py:199
  40.3 2.6 %copy-start.5 = (f32[9,16,256]{2,1,0:T(8,128)}, f32[9,16,256]{2,1,0:T(8,128)S(1)}, u32[]{:S(2)}) copy-start(f32[9,16,256]{2,1,0:T(8,128)S(1)} %collective-permute-done.5.refs_1_) | copy-start | bytes 442372
  40.3 2.6 %copy-start.6 = (f32[9,16,256]{2,1,0:T(8,128)}, f32[9,16,256]{2,1,0:T(8,128)S(1)}, u32[]{:S(2)}) copy-start(f32[9,16,256]{2,1,0:T(8,128)S(1)} %collective-permute-done.6.refs_2_) | copy-start | bytes 442372
  40.4 2.6 %copy-start.7 = (f32[9,16,256]{2,1,0:T(8,128)}, f32[9,16,256]{2,1,0:T(8,128)S(1)}, u32[]{:S(2)}) copy-start(f32[9,16,256]{2,1,0:T(8,128)S(1)} %collective-permute-done.7.refs_3_) | copy-start | bytes 442372
  40.4 2.6 %copy-start.8 = (f32[9,16,256]{2,1,0:T(8,128)}, f32[9,16,256]{2,1,0:T(8,128)S(1)}, u32[]{:S(2)}) copy-start(f32[9,16,256]{2,1,0:T(8,128)S(1)} %collective-permute-done.8.refs_4_) | copy-start | bytes 442372
  43.0 0.7 %copy-start.9 = (f32[9,16,256]{2,1,0:T(8,128)}, f32[9,16,256]{2,1,0:T(8,128)S(1)}, u32[]{:S(2)}) copy-start(f32[9,16,256]{2,1,0:T(8,128)S(1)} %collective-permute-done.9.refs_5_) | copy-start | bytes 442372

commit v9 on v8

--- a/solution.py
+++ b/solution.py
@@ -172,8 +172,9 @@
     peers = jnp.stack([partner(me, jnp) for partner in partners])
     is_peer = peers[:, None] == jnp.arange(n, dtype=jnp.int32)[None, :]
     lanes = jnp.arange(capacity, dtype=jnp.int32)
-    hit = is_peer[:, :, None, None] & (send_cells[0][None, :, :, None] == lanes)
-    select = jnp.sum(hit.astype(f32), axis=1).reshape(groups * hslot, capacity)
+    slots_by_peer = send_cells[0].T
+    hit = is_peer[:, None, :, None] & (slots_by_peer[None, :, :, None] == lanes)
+    select = jnp.sum(hit.astype(f32), axis=2).reshape(groups * hslot, capacity)
 
     values = concentration
     outgoing = gather_send(values, select, groups, hslot)

time: 47.8 us -> 47.8 us (level)
  local copies, waits for them, and re-layouts: 2.22 us -> 1.45 us
  other arithmetic: 2.68 us -> 3.41 us
    eq x1 -> x0, local copies, waits for them, and re-layouts: 0.77 us -> none  [per_device(): hit = is_peer[:, :, None, None] & (send_cells[0][None, :, :, None] == lanes)]
    eq x1, other arithmetic: 0.13 us -> 0.83 us  [per_device(): hit = is_peer[:, None, :, None] & (slots_by_peer[None, :, :, None] == lanes)]
  transfers between devices with their start and end apart: 10 -> 10, of which waited for: 2 -> 2; matrix products, arithmetic and copies ran while one was open for 3% -> 4% of each run, Pallas kernels for 15% -> 15%
where the time goes in v9:
time: 47.8 us; the launch traced here: 47.4 us
  Pallas kernels  19.4 us (41%)
  starting transfers between devices  18.6 us (39%)
  waiting for transfers between devices  3.64 us (8%)
  other arithmetic  3.41 us (7%)
  local copies, waits for them, and re-layouts  1.45 us (3%)
  between operations  0.92 us (2%)
    ppermute x10, starting transfers between devices, per_device(): lax.ppermute(outgoing[g], 'cells', perm=pair_list(n, partner))  18.6 us
    pallas_call x2, Pallas kernels, finish(): pl.pallas_call(functools.partial(finish_kernel, groups, hslot, send), out...  8.88 us
    pallas_call x2, Pallas kernels, local_part(): pl.pallas_call(local_kernel, out_shape=jax.ShapeDtypeStruct(values.shape,...  7.04 us
    ppermute x10, waiting for transfers between devices, per_device(): lax.ppermute(outgoing[g], 'cells', perm=pair_list(n, partner))  3.64 us
    pallas_call x1, Pallas kernels, gather_send(): pl.pallas_call(functools.partial(select_kernel, groups, hslot), out_shape...  3.47 us
    add x1, other arithmetic, per_device(): sum((flux_weight[k][:, None, :] * ((row[k][None, :] == slots).astype(f32)...  1.46 us
    unnamed x24, local copies, waits for them, and re-layouts  1.32 us
  transfers between devices with their start and end apart: 10, of which 2 were waited for; matrix products, arithmetic and copies ran while one was open for 4% of the time, Pallas kernels for 15%

profile of v9, /device:TPU:25, one launch (start us, length us, event | category | flops | bytes accessed | tf_op | source)
XLA Modules:
  0.0 47.4 jit_solution(10116252795503290206)
XLA Ops:
  0.0 0.1 stack.23
  0.1 0.1 iota_compare_fusion.10
  0.2 0.8 %iota_compare_fusion = pred[16,32,128]{2,1,0:T(8,128)(4,1)S(1)} fusion(s32[16,32]{1,0:T(8,128)} %bitcast.47), kind=kLoop, calls=%fused_computation.10 | loop fusion | flops 65536 | bytes 67584 | tf_op jit(solution)/shard_map/eq | solution.py:176
  1.0 0.9 %convert_reduce_fusion = f32[5,16,128]{2,1,0:T(8,128)} fusion(pred[16,32,128]{2,1,0:T(8,128)(4,1)S(1)} %iota_compare_fusion, pred[5,32]{1,0:T(8,128)(4,1)S(1)} %iota_compare_fusion.10), kind=kLoop, calls=%fused_computation | loop fusion | flops 972800 | bytes 106656 | tf_op jit(solution)/shard_map/reduce_sum | solution.py:177
  1.9 3.5 %gather_send.1 = (f32[9,16,256]{2,1,0:T(8,128)}, f32[9,16,256]{2,1,0:T(8,128)}, f32[9,16,256]{2,1,0:T(8,128)}, f32[9,16,256]{2,1,0:T(8,128)}, f32[9,16,256]{2,1,0:T(8,128)}) custom-call(f32[9,256,128]{2,1,0:T(8,128)} %values_ref.3, f32[80,128]{1,0:T(8,128)} %bitcast.44), custom_call_target="tpu_custom_call" | custom-call | tf_op jit(solution)/shard_map/gather_send/pallas_call | solution.py:61
  5.4 0.7 %collective-permute-start = (f32[9,16,256]{2,1,0:T(8,128)}, f32[9,16,256]{2,1,0:T(8,128)S(1)}, u32[]{:S(2)}, u32[]{:S(2)}) collective-permute-start(f32[9,16,256]{2,1,0:T(8,128)} %get-tuple-element.16), channel_id=1, source_target_pairs={{0,1},{1,0},{2,3},{3,2},{4,5},{5,4},{6,7},{7,6},{8,9},{9,8},{10,11... | collective-permute-start | bytes 442376 | tf_op jit(solution)/shard_map/ppermute | solution.py:200
  6.0 1.2 %collective-permute-start.1 = (f32[9,16,256]{2,1,0:T(8,128)}, f32[9,16,256]{2,1,0:T(8,128)S(1)}, u32[]{:S(2)}, u32[]{:S(2)}) collective-permute-start(f32[9,16,256]{2,1,0:T(8,128)} %get-tuple-element.17), channel_id=1, source_target_pairs={{0,2},{1,3},{2,0},{3,1},{4,6},{5,7},{6,4},{7,5},{8,10},{9,11},{10,... | collective-permute-start | bytes 442376 | tf_op jit(solution)/shard_map/ppermute | solution.py:200
  7.2 0.1 collective-permute-start.2
  7.3 2.6 %collective-permute-start.3 = (f32[9,16,256]{2,1,0:T(8,128)}, f32[9,16,256]{2,1,0:T(8,128)S(1)}, u32[]{:S(2)}, u32[]{:S(2)}) collective-permute-start(f32[9,16,256]{2,1,0:T(8,128)} %get-tuple-element.19), channel_id=1, source_target_pairs={{1,2},{2,1},{3,4},{4,3},{5,6},{6,5},{7,8},{8,7},{9,10},{10,9},{11,... | collective-permute-start | bytes 442376 | tf_op jit(solution)/shard_map/ppermute | solution.py:200
  9.9 4.9 %collective-permute-start.4 = (f32[9,16,256]{2,1,0:T(8,128)}, f32[9,16,256]{2,1,0:T(8,128)S(1)}, u32[]{:S(2)}, u32[]{:S(2)}) collective-permute-start(f32[9,16,256]{2,1,0:T(8,128)} %get-tuple-element.20), channel_id=1, source_target_pairs={{2,4},{3,5},{4,2},{5,3},{6,8},{7,9},{8,6},{9,7},{10,12},{11,13},{1... | collective-permute-start | bytes 442376 | tf_op jit(solution)/shard_map/ppermute | solution.py:200
  15.5 0.0 copy-done.11
  15.5 0.0 copy-done.10
  15.8 1.5 %multiply_add_fusion.local_ref.refs_6_.refs_7_.refs_8_.refs_9_.refs_10_ = f32[9,208,128]{2,1,0:T(8,128)} fusion(f32[208,128]{1,0:T(8,128)S(1)} %get-tuple-element.43, f32[9,128]{1,0:T(8,128)S(1)} %get-tuple-element.51, f32[208,128]{1,0:T(8,128)S(1)} %get-tuple-element.44, f32[9,128]{1,0:T(8,128)S(1)} %get-tuple-element.52, ...), kind=kLoop, calls=%fused_computation.1 | loop fusion | flops 3594240 | bytes 1847296 | tf_op jit(solution)/shard_map/add | solution.py:192
  17.2 3.5 %local_part.2.refs_0_ = f32[9,256,128]{2,1,0:T(8,128)} custom-call(f32[9,256,128]{2,1,0:T(8,128)} %values_ref.3, f32[9,208,128]{2,1,0:T(8,128)} %multiply_add_fusion.local_ref.refs_6_.refs_7_.refs_8_.refs_9_.refs_10_, f32[8,128]{1,0:T(8,128)} %mixing_ref.3), custom_call_target="tpu_custom_call" | custom-call | tf_op jit(solution)/shard_map/local_part/pallas_call | solution.py:87
  20.8 0.0 collective-permute-done.refs_1_
  20.8 0.0 collective-permute-done.1.refs_2_
  20.8 0.0 copy-start.1
  20.8 0.0 collective-permute-done.2.refs_3_
  20.8 0.0 copy-start.2
  20.8 0.0 collective-permute-done.3.refs_4_
  20.8 0.0 copy-start.3
  20.8 1.0 %collective-permute-done.4.refs_5_ = f32[9,16,256]{2,1,0:T(8,128)S(1)} collective-permute-done((f32[9,16,256]{2,1,0:T(8,128)}, f32[9,16,256]{2,1,0:T(8,128)S(1)}, u32[]{:S(2)}, u32[]{:S(2)}) %collective-permute-start.4) | collective-permute-done | bytes 147488 | tf_op jit(solution)/shard_map/ppermute | solution.py:200
  21.9 0.0 copy-done
  21.9 0.0 copy-done.1
  21.9 0.0 copy-done.2
  21.9 0.0 copy-done.3
  21.9 0.6 %copy-done.4 = f32[9,16,256]{2,1,0:T(8,128)} copy-done((f32[9,16,256]{2,1,0:T(8,128)}, f32[9,16,256]{2,1,0:T(8,128)S(1)}, u32[]{:S(2)}) %copy-start.4) | copy-done | bytes 147480
  22.5 5.0 %finish_send.1 = (f32[9,256,128]{2,1,0:T(8,128)}, f32[9,16,256]{2,1,0:T(8,128)}, f32[9,16,256]{2,1,0:T(8,128)}, f32[9,16,256]{2,1,0:T(8,128)}, f32[9,16,256]{2,1,0:T(8,128)}, /*index=5*/f32[9,16,256]{2,1,0:T(8,128)}) custom-call(f32[9,256,128]{2,1,0:T(8,128)} %local_part.2.refs_0_, f32[9,16,256]{2,1,0:T(8,128)} %copy-done, f32[9,16,256]{2,1,0:T(8,128)} %copy-done.1, ...), custom_call_target="tpu_custom_call" | custom-call | tf_op jit(solution)/shard_map/finish_send/pallas_call | solution.py:149
  27.6 0.0 collective-permute-start.5
  27.6 0.1 collective-permute-start.6
  27.7 1.5 %collective-permute-start.7 = (f32[9,16,256]{2,1,0:T(8,128)}, f32[9,16,256]{2,1,0:T(8,128)S(1)}, u32[]{:S(2)}, u32[]{:S(2)}) collective-permute-start(f32[9,16,256]{2,1,0:T(8,128)} %get-tuple-element.24), channel_id=1, source_target_pairs={{0,16},{1,17},{2,18},{3,19},{4,20},{5,21},{6,22},{7,23},{8,24},{9,... | collective-permute-start | bytes 442376 | tf_op jit(solution)/shard_map/ppermute | solution.py:200
  29.1 4.2 %collective-permute-start.8 = (f32[9,16,256]{2,1,0:T(8,128)}, f32[9,16,256]{2,1,0:T(8,128)S(1)}, u32[]{:S(2)}, u32[]{:S(2)}) collective-permute-start(f32[9,16,256]{2,1,0:T(8,128)} %get-tuple-element.25), channel_id=1, source_target_pairs={{1,2},{2,1},{3,4},{4,3},{5,6},{6,5},{7,8},{8,7},{9,10},{10,9},{11,... | collective-permute-start | bytes 442376 | tf_op jit(solution)/shard_map/ppermute | solution.py:200
  33.3 3.4 %collective-permute-start.9 = (f32[9,16,256]{2,1,0:T(8,128)}, f32[9,16,256]{2,1,0:T(8,128)S(1)}, u32[]{:S(2)}, u32[]{:S(2)}) collective-permute-start(f32[9,16,256]{2,1,0:T(8,128)} %get-tuple-element.26), channel_id=1, source_target_pairs={{2,4},{3,5},{4,2},{5,3},{6,8},{7,9},{8,6},{9,7},{10,12},{11,13},{1... | collective-permute-start | bytes 442376 | tf_op jit(solution)/shard_map/ppermute | solution.py:200
  36.8 3.5 %local_part.3.refs_0_ = f32[9,256,128]{2,1,0:T(8,128)} custom-call(f32[9,256,128]{2,1,0:T(8,128)} %get-tuple-element.21.values_ref, f32[9,208,128]{2,1,0:T(8,128)} %multiply_add_fusion.local_ref.refs_6_.refs_7_.refs_8_.refs_9_.refs_10_, f32[8,128]{1,0:T(8,128)} %mixing_ref.3), custom_call_target="tpu_custom_call" | custom-call | tf_op jit(solution)/shard_map/local_part/pallas_call | solution.py:87
  40.3 0.0 collective-permute-done.5.refs_1_
  40.3 0.0 collective-permute-done.6.refs_2_
  40.3 0.0 copy-start.6
  40.3 0.0 collective-permute-done.7.refs_3_
  40.3 0.0 copy-start.7
  40.3 0.0 collective-permute-done.8.refs_4_
  40.3 0.0 copy-start.8
  40.4 2.6 %collective-permute-done.9.refs_5_ = f32[9,16,256]{2,1,0:T(8,128)S(1)} collective-permute-done((f32[9,16,256]{2,1,0:T(8,128)}, f32[9,16,256]{2,1,0:T(8,128)S(1)}, u32[]{:S(2)}, u32[]{:S(2)}) %collective-permute-start.9) | collective-permute-done | bytes 147488 | tf_op jit(solution)/shard_map/ppermute | solution.py:200
  42.9 0.0 copy-done.5
  42.9 0.0 copy-done.6
  42.9 0.0 copy-done.7
  42.9 0.0 copy-done.8
  43.0 0.6 %copy-done.9 = f32[9,16,256]{2,1,0:T(8,128)} copy-done((f32[9,16,256]{2,1,0:T(8,128)}, f32[9,16,256]{2,1,0:T(8,128)S(1)}, u32[]{:S(2)}) %copy-start.9) | copy-done | bytes 147480
  43.6 3.8 %finish.1 = f32[9,256,128]{2,1,0:T(8,128)} custom-call(f32[9,256,128]{2,1,0:T(8,128)} %local_part.3.refs_0_, f32[9,16,256]{2,1,0:T(8,128)} %copy-done.5, f32[9,16,256]{2,1,0:T(8,128)} %copy-done.6, f32[9,16,256]{2,1,0:T(8,128)} %copy-done.7, f32[9,16,256]{2,1,0:T(8,128)} %copy-done.8, f32[9,16,256]{2,1,0:T(8,128)} %copy-done.9, ...), custom_call_target="tpu_custom_call" | custom-call | tf_op jit(solution)/shard_map/finish/pallas_call | solution.py:149
  (17 shorter events, 0.2 us)
Async XLA Ops:
  0.0 15.5 %copy-start.11 = (s32[8,128]{1,0:T(8,128)S(1)}, s32[8,128]{1,0:T(8,128)}, u32[]{:S(2)}) copy-start(s32[8,128]{1,0:T(8,128)} %param.11) | copy-start | bytes 12292
  0.0 15.5 %copy-start.10 = (f32[8,9,128]{2,0,1:T(8,128)S(1)}, f32[8,9,128]{2,0,1:T(8,128)}, u32[]{:S(2)}) copy-start(f32[8,9,128]{2,0,1:T(8,128)} %param.8) | copy-start | bytes 110596
  5.4 15.4 %collective-permute-start = (f32[9,16,256]{2,1,0:T(8,128)}, f32[9,16,256]{2,1,0:T(8,128)S(1)}, u32[]{:S(2)}, u32[]{:S(2)}) collective-permute-start(f32[9,16,256]{2,1,0:T(8,128)} %get-tuple-element.16), channel_id=1, source_target_pairs={{0,1},{1,0},{2,3},{3,2},{4,5},{5,4},{6,7},{7,6},{8,9},{9,8},{10,11... | collective-permute-start | bytes 442376 | tf_op jit(solution)/shard_map/ppermute | solution.py:200
  6.0 14.7 %collective-permute-start.1 = (f32[9,16,256]{2,1,0:T(8,128)}, f32[9,16,256]{2,1,0:T(8,128)S(1)}, u32[]{:S(2)}, u32[]{:S(2)}) collective-permute-start(f32[9,16,256]{2,1,0:T(8,128)} %get-tuple-element.17), channel_id=1, source_target_pairs={{0,2},{1,3},{2,0},{3,1},{4,6},{5,7},{6,4},{7,5},{8,10},{9,11},{10,... | collective-permute-start | bytes 442376 | tf_op jit(solution)/shard_map/ppermute | solution.py:200
  7.2 13.5 %collective-permute-start.2 = (f32[9,16,256]{2,1,0:T(8,128)}, f32[9,16,256]{2,1,0:T(8,128)S(1)}, u32[]{:S(2)}, u32[]{:S(2)}) collective-permute-start(f32[9,16,256]{2,1,0:T(8,128)} %get-tuple-element.18), channel_id=1, source_target_pairs={{0,16},{1,17},{2,18},{3,19},{4,20},{5,21},{6,22},{7,23},{8,24},{9,... | collective-permute-start | bytes 442376 | tf_op jit(solution)/shard_map/ppermute | solution.py:200
  7.3 13.5 %collective-permute-start.3 = (f32[9,16,256]{2,1,0:T(8,128)}, f32[9,16,256]{2,1,0:T(8,128)S(1)}, u32[]{:S(2)}, u32[]{:S(2)}) collective-permute-start(f32[9,16,256]{2,1,0:T(8,128)} %get-tuple-element.19), channel_id=1, source_target_pairs={{1,2},{2,1},{3,4},{4,3},{5,6},{6,5},{7,8},{8,7},{9,10},{10,9},{11,... | collective-permute-start | bytes 442376 | tf_op jit(solution)/shard_map/ppermute | solution.py:200
  9.9 12.0 %collective-permute-start.4 = (f32[9,16,256]{2,1,0:T(8,128)}, f32[9,16,256]{2,1,0:T(8,128)S(1)}, u32[]{:S(2)}, u32[]{:S(2)}) collective-permute-start(f32[9,16,256]{2,1,0:T(8,128)} %get-tuple-element.20), channel_id=1, source_target_pairs={{2,4},{3,5},{4,2},{5,3},{6,8},{7,9},{8,6},{9,7},{10,12},{11,13},{1... | collective-permute-start | bytes 442376 | tf_op jit(solution)/shard_map/ppermute | solution.py:200
  20.8 1.1 %copy-start = (f32[9,16,256]{2,1,0:T(8,128)}, f32[9,16,256]{2,1,0:T(8,128)S(1)}, u32[]{:S(2)}) copy-start(f32[9,16,256]{2,1,0:T(8,128)S(1)} %collective-permute-done.refs_1_) | copy-start | bytes 442372
  20.8 1.1 %copy-start.1 = (f32[9,16,256]{2,1,0:T(8,128)}, f32[9,16,256]{2,1,0:T(8,128)S(1)}, u32[]{:S(2)}) copy-start(f32[9,16,256]{2,1,0:T(8,128)S(1)} %collective-permute-done.1.refs_2_) | copy-start | bytes 442372
  20.8 1.1 %copy-start.2 = (f32[9,16,256]{2,1,0:T(8,128)}, f32[9,16,256]{2,1,0:T(8,128)S(1)}, u32[]{:S(2)}) copy-start(f32[9,16,256]{2,1,0:T(8,128)S(1)} %collective-permute-done.2.refs_3_) | copy-start | bytes 442372
  20.8 1.1 %copy-start.3 = (f32[9,16,256]{2,1,0:T(8,128)}, f32[9,16,256]{2,1,0:T(8,128)S(1)}, u32[]{:S(2)}) copy-start(f32[9,16,256]{2,1,0:T(8,128)S(1)} %collective-permute-done.3.refs_4_) | copy-start | bytes 442372
  21.9 0.7 %copy-start.4 = (f32[9,16,256]{2,1,0:T(8,128)}, f32[9,16,256]{2,1,0:T(8,128)S(1)}, u32[]{:S(2)}) copy-start(f32[9,16,256]{2,1,0:T(8,128)S(1)} %collective-permute-done.4.refs_5_) | copy-start | bytes 442372
  27.6 12.7 %collective-permute-start.5 = (f32[9,16,256]{2,1,0:T(8,128)}, f32[9,16,256]{2,1,0:T(8,128)S(1)}, u32[]{:S(2)}, u32[]{:S(2)}) collective-permute-start(f32[9,16,256]{2,1,0:T(8,128)} %get-tuple-element.22), channel_id=1, source_target_pairs={{0,1},{1,0},{2,3},{3,2},{4,5},{5,4},{6,7},{7,6},{8,9},{9,8},{10,11... | collective-permute-start | bytes 442376 | tf_op jit(solution)/shard_map/ppermute | solution.py:200
  27.6 12.7 %collective-permute-start.6 = (f32[9,16,256]{2,1,0:T(8,128)}, f32[9,16,256]{2,1,0:T(8,128)S(1)}, u32[]{:S(2)}, u32[]{:S(2)}) collective-permute-start(f32[9,16,256]{2,1,0:T(8,128)} %get-tuple-element.23), channel_id=1, source_target_pairs={{0,2},{1,3},{2,0},{3,1},{4,6},{5,7},{6,4},{7,5},{8,10},{9,11},{10,... | collective-permute-start | bytes 442376 | tf_op jit(solution)/shard_map/ppermute | solution.py:200
  27.7 12.7 %collective-permute-start.7 = (f32[9,16,256]{2,1,0:T(8,128)}, f32[9,16,256]{2,1,0:T(8,128)S(1)}, u32[]{:S(2)}, u32[]{:S(2)}) collective-permute-start(f32[9,16,256]{2,1,0:T(8,128)} %get-tuple-element.24), channel_id=1, source_target_pairs={{0,16},{1,17},{2,18},{3,19},{4,20},{5,21},{6,22},{7,23},{8,24},{9,... | collective-permute-start | bytes 442376 | tf_op jit(solution)/shard_map/ppermute | solution.py:200
  29.1 11.2 %collective-permute-start.8 = (f32[9,16,256]{2,1,0:T(8,128)}, f32[9,16,256]{2,1,0:T(8,128)S(1)}, u32[]{:S(2)}, u32[]{:S(2)}) collective-permute-start(f32[9,16,256]{2,1,0:T(8,128)} %get-tuple-element.25), channel_id=1, source_target_pairs={{1,2},{2,1},{3,4},{4,3},{5,6},{6,5},{7,8},{8,7},{9,10},{10,9},{11,... | collective-permute-start | bytes 442376 | tf_op jit(solution)/shard_map/ppermute | solution.py:200
  33.3 9.6 %collective-permute-start.9 = (f32[9,16,256]{2,1,0:T(8,128)}, f32[9,16,256]{2,1,0:T(8,128)S(1)}, u32[]{:S(2)}, u32[]{:S(2)}) collective-permute-start(f32[9,16,256]{2,1,0:T(8,128)} %get-tuple-element.26), channel_id=1, source_target_pairs={{2,4},{3,5},{4,2},{5,3},{6,8},{7,9},{8,6},{9,7},{10,12},{11,13},{1... | collective-permute-start | bytes 442376 | tf_op jit(solution)/shard_map/ppermute | solution.py:200
  40.3 2.6 %copy-start.5 = (f32[9,16,256]{2,1,0:T(8,128)}, f32[9,16,256]{2,1,0:T(8,128)S(1)}, u32[]{:S(2)}) copy-start(f32[9,16,256]{2,1,0:T(8,128)S(1)} %collective-permute-done.5.refs_1_) | copy-start | bytes 442372
  40.3 2.6 %copy-start.6 = (f32[9,16,256]{2,1,0:T(8,128)}, f32[9,16,256]{2,1,0:T(8,128)S(1)}, u32[]{:S(2)}) copy-start(f32[9,16,256]{2,1,0:T(8,128)S(1)} %collective-permute-done.6.refs_2_) | copy-start | bytes 442372
  40.3 2.6 %copy-start.7 = (f32[9,16,256]{2,1,0:T(8,128)}, f32[9,16,256]{2,1,0:T(8,128)S(1)}, u32[]{:S(2)}) copy-start(f32[9,16,256]{2,1,0:T(8,128)S(1)} %collective-permute-done.7.refs_3_) | copy-start | bytes 442372
  40.3 2.6 %copy-start.8 = (f32[9,16,256]{2,1,0:T(8,128)}, f32[9,16,256]{2,1,0:T(8,128)S(1)}, u32[]{:S(2)}) copy-start(f32[9,16,256]{2,1,0:T(8,128)S(1)} %collective-permute-done.8.refs_4_) | copy-start | bytes 442372
  42.9 0.7 %copy-start.9 = (f32[9,16,256]{2,1,0:T(8,128)}, f32[9,16,256]{2,1,0:T(8,128)S(1)}, u32[]{:S(2)}) copy-start(f32[9,16,256]{2,1,0:T(8,128)S(1)} %collective-permute-done.9.refs_5_) | copy-start | bytes 442372

commit v10 on v9

--- a/solution.py
+++ b/solution.py
@@ -19,9 +19,9 @@
     return (
         lambda d, xp: d ^ 1,
         lambda d, xp: xp.where(d % 4 < 2, d + 2, d - 2),
-        lambda d, xp: (d + half) % n,
         lambda d, xp: xp.where(d % 2 == 1, d + 1, d - 1),
         lambda d, xp: xp.where(d % 4 < 2, d - 2, d + 2),
+        lambda d, xp: (d + half) % n,
     )
 
 

time: 47.8 us -> 56.3 us (1.18)
  the two profiles are of different devices: /device:TPU:25 before, /device:TPU:0 now
where the time goes in v10:
time: 56.3 us; the launch traced here: 56 us
  Pallas kernels  19.4 us (34%)
  starting transfers between devices  18.6 us (33%)
  waiting for transfers between devices  12.2 us (22%)
  other arithmetic  3.41 us (6%)
  local copies, waits for them, and re-layouts  1.45 us (3%)
  between operations  0.91 us (2%)
    ppermute x10, starting transfers between devices, per_device(): lax.ppermute(outgoing[g], 'cells', perm=pair_list(n, partner))  18.6 us
    ppermute x10, waiting for transfers between devices, per_device(): lax.ppermute(outgoing[g], 'cells', perm=pair_list(n, partner))  12.2 us
    pallas_call x2, Pallas kernels, finish(): pl.pallas_call(functools.partial(finish_kernel, groups, hslot, send), out...  8.89 us
    pallas_call x2, Pallas kernels, local_part(): pl.pallas_call(local_kernel, out_shape=jax.ShapeDtypeStruct(values.shape,...  7.02 us
    pallas_call x1, Pallas kernels, gather_send(): pl.pallas_call(functools.partial(select_kernel, groups, hslot), out_shape...  3.47 us
    add x1, other arithmetic, per_device(): sum((flux_weight[k][:, None, :] * ((row[k][None, :] == slots).astype(f32)...  1.46 us
    unnamed x24, local copies, waits for them, and re-layouts  1.32 us
  transfers between devices with their start and end apart: 10, of which 2 were waited for; matrix products, arithmetic and copies ran while one was open for 3% of the time, Pallas kernels for 13%

profile of v10, /device:TPU:0, one launch (start us, length us, event | category | flops | bytes accessed | tf_op | source)
XLA Modules:
  0.0 56.0 jit_solution(14945464849198271957)
XLA Ops:
  0.0 0.1 stack.23
  0.1 0.1 iota_compare_fusion.10
  0.2 0.8 %iota_compare_fusion = pred[16,32,128]{2,1,0:T(8,128)(4,1)S(1)} fusion(s32[16,32]{1,0:T(8,128)} %bitcast.47), kind=kLoop, calls=%fused_computation.10 | loop fusion | flops 65536 | bytes 67584 | tf_op jit(solution)/shard_map/eq | solution.py:176
  1.0 0.9 %convert_reduce_fusion = f32[5,16,128]{2,1,0:T(8,128)} fusion(pred[16,32,128]{2,1,0:T(8,128)(4,1)S(1)} %iota_compare_fusion, pred[5,32]{1,0:T(8,128)(4,1)S(1)} %iota_compare_fusion.10), kind=kLoop, calls=%fused_computation | loop fusion | flops 972800 | bytes 106656 | tf_op jit(solution)/shard_map/reduce_sum | solution.py:177
  1.9 3.5 %gather_send.1 = (f32[9,16,256]{2,1,0:T(8,128)}, f32[9,16,256]{2,1,0:T(8,128)}, f32[9,16,256]{2,1,0:T(8,128)}, f32[9,16,256]{2,1,0:T(8,128)}, f32[9,16,256]{2,1,0:T(8,128)}) custom-call(f32[9,256,128]{2,1,0:T(8,128)} %values_ref.3, f32[80,128]{1,0:T(8,128)} %bitcast.44), custom_call_target="tpu_custom_call" | custom-call | tf_op jit(solution)/shard_map/gather_send/pallas_call | solution.py:61
  5.4 0.4 collective-permute-start
  5.8 2.5 %collective-permute-start.1 = (f32[9,16,256]{2,1,0:T(8,128)}, f32[9,16,256]{2,1,0:T(8,128)S(1)}, u32[]{:S(2)}, u32[]{:S(2)}) collective-permute-start(f32[9,16,256]{2,1,0:T(8,128)} %get-tuple-element.17), channel_id=1, source_target_pairs={{0,2},{1,3},{2,0},{3,1},{4,6},{5,7},{6,4},{7,5},{8,10},{9,11},{10,... | collective-permute-start | bytes 442376 | tf_op jit(solution)/shard_map/ppermute | solution.py:200
  8.3 0.7 %collective-permute-start.2 = (f32[9,16,256]{2,1,0:T(8,128)}, f32[9,16,256]{2,1,0:T(8,128)S(1)}, u32[]{:S(2)}, u32[]{:S(2)}) collective-permute-start(f32[9,16,256]{2,1,0:T(8,128)} %get-tuple-element.18), channel_id=1, source_target_pairs={{1,2},{2,1},{3,4},{4,3},{5,6},{6,5},{7,8},{8,7},{9,10},{10,9},{11,... | collective-permute-start | bytes 442376 | tf_op jit(solution)/shard_map/ppermute | solution.py:200
  9.0 0.7 %collective-permute-start.3 = (f32[9,16,256]{2,1,0:T(8,128)}, f32[9,16,256]{2,1,0:T(8,128)S(1)}, u32[]{:S(2)}, u32[]{:S(2)}) collective-permute-start(f32[9,16,256]{2,1,0:T(8,128)} %get-tuple-element.19), channel_id=1, source_target_pairs={{2,4},{3,5},{4,2},{5,3},{6,8},{7,9},{8,6},{9,7},{10,12},{11,13},{1... | collective-permute-start | bytes 442376 | tf_op jit(solution)/shard_map/ppermute | solution.py:200
  9.6 7.8 %collective-permute-start.4 = (f32[9,16,256]{2,1,0:T(8,128)}, f32[9,16,256]{2,1,0:T(8,128)S(1)}, u32[]{:S(2)}, u32[]{:S(2)}) collective-permute-start(f32[9,16,256]{2,1,0:T(8,128)} %get-tuple-element.20), channel_id=1, source_target_pairs={{0,16},{1,17},{2,18},{3,19},{4,20},{5,21},{6,22},{7,23},{8,24},{9,... | collective-permute-start | bytes 442376 | tf_op jit(solution)/shard_map/ppermute | solution.py:200
  18.1 0.0 copy-done.11
  18.2 0.0 copy-done.10
  18.4 1.5 %multiply_add_fusion.local_ref.refs_6_.refs_7_.refs_8_.refs_9_.refs_10_ = f32[9,208,128]{2,1,0:T(8,128)} fusion(f32[208,128]{1,0:T(8,128)S(1)} %get-tuple-element.43, f32[9,128]{1,0:T(8,128)S(1)} %get-tuple-element.51, f32[208,128]{1,0:T(8,128)S(1)} %get-tuple-element.44, f32[9,128]{1,0:T(8,128)S(1)} %get-tuple-element.52, ...), kind=kLoop, calls=%fused_computation.1 | loop fusion | flops 3594240 | bytes 1847296 | tf_op jit(solution)/shard_map/add | solution.py:192
  19.9 3.5 %local_part.2.refs_0_ = f32[9,256,128]{2,1,0:T(8,128)} custom-call(f32[9,256,128]{2,1,0:T(8,128)} %values_ref.3, f32[9,208,128]{2,1,0:T(8,128)} %multiply_add_fusion.local_ref.refs_6_.refs_7_.refs_8_.refs_9_.refs_10_, f32[8,128]{1,0:T(8,128)} %mixing_ref.3), custom_call_target="tpu_custom_call" | custom-call | tf_op jit(solution)/shard_map/local_part/pallas_call | solution.py:87
  23.4 0.0 collective-permute-done.refs_1_
  23.4 0.0 collective-permute-done.1.refs_2_
  23.4 0.0 copy-start.1
  23.4 0.0 collective-permute-done.2.refs_3_
  23.4 0.0 copy-start.2
  23.4 0.0 collective-permute-done.3.refs_4_
  23.5 0.0 copy-start.3
  23.5 4.9 %collective-permute-done.4.refs_5_ = f32[9,16,256]{2,1,0:T(8,128)S(1)} collective-permute-done((f32[9,16,256]{2,1,0:T(8,128)}, f32[9,16,256]{2,1,0:T(8,128)S(1)}, u32[]{:S(2)}, u32[]{:S(2)}) %collective-permute-start.4) | collective-permute-done | bytes 147488 | tf_op jit(solution)/shard_map/ppermute | solution.py:200
  28.3 0.0 copy-done
  28.4 0.0 copy-done.1
  28.4 0.0 copy-done.2
  28.4 0.0 copy-done.3
  28.4 0.6 %copy-done.4 = f32[9,16,256]{2,1,0:T(8,128)} copy-done((f32[9,16,256]{2,1,0:T(8,128)}, f32[9,16,256]{2,1,0:T(8,128)S(1)}, u32[]{:S(2)}) %copy-start.4) | copy-done | bytes 147480
  29.0 5.0 %finish_send.1 = (f32[9,256,128]{2,1,0:T(8,128)}, f32[9,16,256]{2,1,0:T(8,128)}, f32[9,16,256]{2,1,0:T(8,128)}, f32[9,16,256]{2,1,0:T(8,128)}, f32[9,16,256]{2,1,0:T(8,128)}, /*index=5*/f32[9,16,256]{2,1,0:T(8,128)}) custom-call(f32[9,256,128]{2,1,0:T(8,128)} %local_part.2.refs_0_, f32[9,16,256]{2,1,0:T(8,128)} %copy-done, f32[9,16,256]{2,1,0:T(8,128)} %copy-done.1, ...), custom_call_target="tpu_custom_call" | custom-call | tf_op jit(solution)/shard_map/finish_send/pallas_call | solution.py:149
  34.1 0.1 collective-permute-start.5
  34.2 0.0 collective-permute-start.6
  34.2 0.7 %collective-permute-start.7 = (f32[9,16,256]{2,1,0:T(8,128)}, f32[9,16,256]{2,1,0:T(8,128)S(1)}, u32[]{:S(2)}, u32[]{:S(2)}) collective-permute-start(f32[9,16,256]{2,1,0:T(8,128)} %get-tuple-element.24), channel_id=1, source_target_pairs={{1,2},{2,1},{3,4},{4,3},{5,6},{6,5},{7,8},{8,7},{9,10},{10,9},{11,... | collective-permute-start | bytes 442376 | tf_op jit(solution)/shard_map/ppermute | solution.py:200
  34.8 0.7 %collective-permute-start.8 = (f32[9,16,256]{2,1,0:T(8,128)}, f32[9,16,256]{2,1,0:T(8,128)S(1)}, u32[]{:S(2)}, u32[]{:S(2)}) collective-permute-start(f32[9,16,256]{2,1,0:T(8,128)} %get-tuple-element.25), channel_id=1, source_target_pairs={{2,4},{3,5},{4,2},{5,3},{6,8},{7,9},{8,6},{9,7},{10,12},{11,13},{1... | collective-permute-start | bytes 442376 | tf_op jit(solution)/shard_map/ppermute | solution.py:200
  35.5 5.1 %collective-permute-start.9 = (f32[9,16,256]{2,1,0:T(8,128)}, f32[9,16,256]{2,1,0:T(8,128)S(1)}, u32[]{:S(2)}, u32[]{:S(2)}) collective-permute-start(f32[9,16,256]{2,1,0:T(8,128)} %get-tuple-element.26), channel_id=1, source_target_pairs={{0,16},{1,17},{2,18},{3,19},{4,20},{5,21},{6,22},{7,23},{8,24},{9,... | collective-permute-start | bytes 442376 | tf_op jit(solution)/shard_map/ppermute | solution.py:200
  40.6 3.5 %local_part.3.refs_0_ = f32[9,256,128]{2,1,0:T(8,128)} custom-call(f32[9,256,128]{2,1,0:T(8,128)} %get-tuple-element.21.values_ref, f32[9,208,128]{2,1,0:T(8,128)} %multiply_add_fusion.local_ref.refs_6_.refs_7_.refs_8_.refs_9_.refs_10_, f32[8,128]{1,0:T(8,128)} %mixing_ref.3), custom_call_target="tpu_custom_call" | custom-call | tf_op jit(solution)/shard_map/local_part/pallas_call | solution.py:87
  44.1 0.0 collective-permute-done.5.refs_1_
  44.1 0.0 collective-permute-done.6.refs_2_
  44.1 0.0 copy-start.6
  44.1 0.0 collective-permute-done.7.refs_3_
  44.1 0.0 copy-start.7
  44.1 0.0 collective-permute-done.8.refs_4_
  44.1 0.0 copy-start.8
  44.2 7.3 %collective-permute-done.9.refs_5_ = f32[9,16,256]{2,1,0:T(8,128)S(1)} collective-permute-done((f32[9,16,256]{2,1,0:T(8,128)}, f32[9,16,256]{2,1,0:T(8,128)S(1)}, u32[]{:S(2)}, u32[]{:S(2)}) %collective-permute-start.9) | collective-permute-done | bytes 147488 | tf_op jit(solution)/shard_map/ppermute | solution.py:200
  51.5 0.0 copy-done.5
  51.5 0.0 copy-done.6
  51.5 0.0 copy-done.7
  51.5 0.0 copy-done.8
  51.5 0.6 %copy-done.9 = f32[9,16,256]{2,1,0:T(8,128)} copy-done((f32[9,16,256]{2,1,0:T(8,128)}, f32[9,16,256]{2,1,0:T(8,128)S(1)}, u32[]{:S(2)}) %copy-start.9) | copy-done | bytes 147480
  52.1 3.8 %finish.1 = f32[9,256,128]{2,1,0:T(8,128)} custom-call(f32[9,256,128]{2,1,0:T(8,128)} %local_part.3.refs_0_, f32[9,16,256]{2,1,0:T(8,128)} %copy-done.5, f32[9,16,256]{2,1,0:T(8,128)} %copy-done.6, f32[9,16,256]{2,1,0:T(8,128)} %copy-done.7, f32[9,16,256]{2,1,0:T(8,128)} %copy-done.8, f32[9,16,256]{2,1,0:T(8,128)} %copy-done.9, ...), custom_call_target="tpu_custom_call" | custom-call | tf_op jit(solution)/shard_map/finish/pallas_call | solution.py:149
  (17 shorter events, 0.2 us)
Async XLA Ops:
  0.0 18.1 %copy-start.11 = (s32[8,128]{1,0:T(8,128)S(1)}, s32[8,128]{1,0:T(8,128)}, u32[]{:S(2)}) copy-start(s32[8,128]{1,0:T(8,128)} %param.11) | copy-start | bytes 12292
  0.0 18.2 %copy-start.10 = (f32[8,9,128]{2,0,1:T(8,128)S(1)}, f32[8,9,128]{2,0,1:T(8,128)}, u32[]{:S(2)}) copy-start(f32[8,9,128]{2,0,1:T(8,128)} %param.8) | copy-start | bytes 110596
  5.4 18.0 %collective-permute-start = (f32[9,16,256]{2,1,0:T(8,128)}, f32[9,16,256]{2,1,0:T(8,128)S(1)}, u32[]{:S(2)}, u32[]{:S(2)}) collective-permute-start(f32[9,16,256]{2,1,0:T(8,128)} %get-tuple-element.16), channel_id=1, source_target_pairs={{0,1},{1,0},{2,3},{3,2},{4,5},{5,4},{6,7},{7,6},{8,9},{9,8},{10,11... | collective-permute-start | bytes 442376 | tf_op jit(solution)/shard_map/ppermute | solution.py:200
  5.8 17.6 %collective-permute-start.1 = (f32[9,16,256]{2,1,0:T(8,128)}, f32[9,16,256]{2,1,0:T(8,128)S(1)}, u32[]{:S(2)}, u32[]{:S(2)}) collective-permute-start(f32[9,16,256]{2,1,0:T(8,128)} %get-tuple-element.17), channel_id=1, source_target_pairs={{0,2},{1,3},{2,0},{3,1},{4,6},{5,7},{6,4},{7,5},{8,10},{9,11},{10,... | collective-permute-start | bytes 442376 | tf_op jit(solution)/shard_map/ppermute | solution.py:200
  8.3 15.1 %collective-permute-start.2 = (f32[9,16,256]{2,1,0:T(8,128)}, f32[9,16,256]{2,1,0:T(8,128)S(1)}, u32[]{:S(2)}, u32[]{:S(2)}) collective-permute-start(f32[9,16,256]{2,1,0:T(8,128)} %get-tuple-element.18), channel_id=1, source_target_pairs={{1,2},{2,1},{3,4},{4,3},{5,6},{6,5},{7,8},{8,7},{9,10},{10,9},{11,... | collective-permute-start | bytes 442376 | tf_op jit(solution)/shard_map/ppermute | solution.py:200
  9.0 14.5 %collective-permute-start.3 = (f32[9,16,256]{2,1,0:T(8,128)}, f32[9,16,256]{2,1,0:T(8,128)S(1)}, u32[]{:S(2)}, u32[]{:S(2)}) collective-permute-start(f32[9,16,256]{2,1,0:T(8,128)} %get-tuple-element.19), channel_id=1, source_target_pairs={{2,4},{3,5},{4,2},{5,3},{6,8},{7,9},{8,6},{9,7},{10,12},{11,13},{1... | collective-permute-start | bytes 442376 | tf_op jit(solution)/shard_map/ppermute | solution.py:200
  9.6 18.7 %collective-permute-start.4 = (f32[9,16,256]{2,1,0:T(8,128)}, f32[9,16,256]{2,1,0:T(8,128)S(1)}, u32[]{:S(2)}, u32[]{:S(2)}) collective-permute-start(f32[9,16,256]{2,1,0:T(8,128)} %get-tuple-element.20), channel_id=1, source_target_pairs={{0,16},{1,17},{2,18},{3,19},{4,20},{5,21},{6,22},{7,23},{8,24},{9,... | collective-permute-start | bytes 442376 | tf_op jit(solution)/shard_map/ppermute | solution.py:200
  23.4 4.9 %copy-start = (f32[9,16,256]{2,1,0:T(8,128)}, f32[9,16,256]{2,1,0:T(8,128)S(1)}, u32[]{:S(2)}) copy-start(f32[9,16,256]{2,1,0:T(8,128)S(1)} %collective-permute-done.refs_1_) | copy-start | bytes 442372
  23.4 4.9 %copy-start.1 = (f32[9,16,256]{2,1,0:T(8,128)}, f32[9,16,256]{2,1,0:T(8,128)S(1)}, u32[]{:S(2)}) copy-start(f32[9,16,256]{2,1,0:T(8,128)S(1)} %collective-permute-done.1.refs_2_) | copy-start | bytes 442372
  23.4 4.9 %copy-start.2 = (f32[9,16,256]{2,1,0:T(8,128)}, f32[9,16,256]{2,1,0:T(8,128)S(1)}, u32[]{:S(2)}) copy-start(f32[9,16,256]{2,1,0:T(8,128)S(1)} %collective-permute-done.2.refs_3_) | copy-start | bytes 442372
  23.5 4.9 %copy-start.3 = (f32[9,16,256]{2,1,0:T(8,128)}, f32[9,16,256]{2,1,0:T(8,128)S(1)}, u32[]{:S(2)}) copy-start(f32[9,16,256]{2,1,0:T(8,128)S(1)} %collective-permute-done.3.refs_4_) | copy-start | bytes 442372
  28.3 0.7 %copy-start.4 = (f32[9,16,256]{2,1,0:T(8,128)}, f32[9,16,256]{2,1,0:T(8,128)S(1)}, u32[]{:S(2)}) copy-start(f32[9,16,256]{2,1,0:T(8,128)S(1)} %collective-permute-done.4.refs_5_) | copy-start | bytes 442372
  34.1 10.0 %collective-permute-start.5 = (f32[9,16,256]{2,1,0:T(8,128)}, f32[9,16,256]{2,1,0:T(8,128)S(1)}, u32[]{:S(2)}, u32[]{:S(2)}) collective-permute-start(f32[9,16,256]{2,1,0:T(8,128)} %get-tuple-element.22), channel_id=1, source_target_pairs={{0,1},{1,0},{2,3},{3,2},{4,5},{5,4},{6,7},{7,6},{8,9},{9,8},{10,11... | collective-permute-start | bytes 442376 | tf_op jit(solution)/shard_map/ppermute | solution.py:200
  34.2 9.9 %collective-permute-start.6 = (f32[9,16,256]{2,1,0:T(8,128)}, f32[9,16,256]{2,1,0:T(8,128)S(1)}, u32[]{:S(2)}, u32[]{:S(2)}) collective-permute-start(f32[9,16,256]{2,1,0:T(8,128)} %get-tuple-element.23), channel_id=1, source_target_pairs={{0,2},{1,3},{2,0},{3,1},{4,6},{5,7},{6,4},{7,5},{8,10},{9,11},{10,... | collective-permute-start | bytes 442376 | tf_op jit(solution)/shard_map/ppermute | solution.py:200
  34.2 9.9 %collective-permute-start.7 = (f32[9,16,256]{2,1,0:T(8,128)}, f32[9,16,256]{2,1,0:T(8,128)S(1)}, u32[]{:S(2)}, u32[]{:S(2)}) collective-permute-start(f32[9,16,256]{2,1,0:T(8,128)} %get-tuple-element.24), channel_id=1, source_target_pairs={{1,2},{2,1},{3,4},{4,3},{5,6},{6,5},{7,8},{8,7},{9,10},{10,9},{11,... | collective-permute-start | bytes 442376 | tf_op jit(solution)/shard_map/ppermute | solution.py:200
  34.8 9.3 %collective-permute-start.8 = (f32[9,16,256]{2,1,0:T(8,128)}, f32[9,16,256]{2,1,0:T(8,128)S(1)}, u32[]{:S(2)}, u32[]{:S(2)}) collective-permute-start(f32[9,16,256]{2,1,0:T(8,128)} %get-tuple-element.25), channel_id=1, source_target_pairs={{2,4},{3,5},{4,2},{5,3},{6,8},{7,9},{8,6},{9,7},{10,12},{11,13},{1... | collective-permute-start | bytes 442376 | tf_op jit(solution)/shard_map/ppermute | solution.py:200
  35.5 15.9 %collective-permute-start.9 = (f32[9,16,256]{2,1,0:T(8,128)}, f32[9,16,256]{2,1,0:T(8,128)S(1)}, u32[]{:S(2)}, u32[]{:S(2)}) collective-permute-start(f32[9,16,256]{2,1,0:T(8,128)} %get-tuple-element.26), channel_id=1, source_target_pairs={{0,16},{1,17},{2,18},{3,19},{4,20},{5,21},{6,22},{7,23},{8,24},{9,... | collective-permute-start | bytes 442376 | tf_op jit(solution)/shard_map/ppermute | solution.py:200
  44.1 7.4 %copy-start.5 = (f32[9,16,256]{2,1,0:T(8,128)}, f32[9,16,256]{2,1,0:T(8,128)S(1)}, u32[]{:S(2)}) copy-start(f32[9,16,256]{2,1,0:T(8,128)S(1)} %collective-permute-done.5.refs_1_) | copy-start | bytes 442372
  44.1 7.4 %copy-start.6 = (f32[9,16,256]{2,1,0:T(8,128)}, f32[9,16,256]{2,1,0:T(8,128)S(1)}, u32[]{:S(2)}) copy-start(f32[9,16,256]{2,1,0:T(8,128)S(1)} %collective-permute-done.6.refs_2_) | copy-start | bytes 442372
  44.1 7.3 %copy-start.7 = (f32[9,16,256]{2,1,0:T(8,128)}, f32[9,16,256]{2,1,0:T(8,128)S(1)}, u32[]{:S(2)}) copy-start(f32[9,16,256]{2,1,0:T(8,128)S(1)} %collective-permute-done.7.refs_3_) | copy-start | bytes 442372
  44.1 7.3 %copy-start.8 = (f32[9,16,256]{2,1,0:T(8,128)}, f32[9,16,256]{2,1,0:T(8,128)S(1)}, u32[]{:S(2)}) copy-start(f32[9,16,256]{2,1,0:T(8,128)S(1)} %collective-permute-done.8.refs_4_) | copy-start | bytes 442372
  51.5 0.7 %copy-start.9 = (f32[9,16,256]{2,1,0:T(8,128)}, f32[9,16,256]{2,1,0:T(8,128)S(1)}, u32[]{:S(2)}) copy-start(f32[9,16,256]{2,1,0:T(8,128)S(1)} %collective-permute-done.9.refs_5_) | copy-start | bytes 442372

commit v11 on v10

--- a/solution.py
+++ b/solution.py
@@ -18,10 +18,10 @@
     half = n // 2
     return (
         lambda d, xp: d ^ 1,
+        lambda d, xp: (d + half) % n,
         lambda d, xp: xp.where(d % 4 < 2, d + 2, d - 2),
         lambda d, xp: xp.where(d % 2 == 1, d + 1, d - 1),
         lambda d, xp: xp.where(d % 4 < 2, d - 2, d + 2),
-        lambda d, xp: (d + half) % n,
     )
 
 

time: 56.3 us -> 48.2 us (0.86)
  the two profiles are of different devices: /device:TPU:0 before, /device:TPU:25 now
where the time goes in v11:
time: 48.2 us; the launch traced here: 47.4 us
  Pallas kernels  19.4 us (40%)
  starting transfers between devices  18.6 us (39%)
  waiting for transfers between devices  3.64 us (8%)
  other arithmetic  3.41 us (7%)
  local copies, waits for them, and re-layouts  1.45 us (3%)
  between operations  0.91 us (2%)
    ppermute x10, starting transfers between devices, per_device(): lax.ppermute(outgoing[g], 'cells', perm=pair_list(n, partner))  18.6 us
    pallas_call x2, Pallas kernels, finish(): pl.pallas_call(functools.partial(finish_kernel, groups, hslot, send), out...  8.88 us
    pallas_call x2, Pallas kernels, local_part(): pl.pallas_call(local_kernel, out_shape=jax.ShapeDtypeStruct(values.shape,...  7.04 us
    ppermute x10, waiting for transfers between devices, per_device(): lax.ppermute(outgoing[g], 'cells', perm=pair_list(n, partner))  3.64 us
    pallas_call x1, Pallas kernels, gather_send(): pl.pallas_call(functools.partial(select_kernel, groups, hslot), out_shape...  3.47 us
    add x1, other arithmetic, per_device(): sum((flux_weight[k][:, None, :] * ((row[k][None, :] == slots).astype(f32)...  1.46 us
    unnamed x24, local copies, waits for them, and re-layouts  1.32 us
  transfers between devices with their start and end apart: 10, of which 2 were waited for; matrix products, arithmetic and copies ran while one was open for 4% of the time, Pallas kernels for 15%

profile of v11, /device:TPU:25, one launch (start us, length us, event | category | flops | bytes accessed | tf_op | source)
XLA Modules:
  0.0 47.4 jit_solution(3764646332458836166)
XLA Ops:
  0.0 0.1 stack.23
  0.1 0.1 iota_compare_fusion.10
  0.2 0.8 %iota_compare_fusion = pred[16,32,128]{2,1,0:T(8,128)(4,1)S(1)} fusion(s32[16,32]{1,0:T(8,128)} %bitcast.47), kind=kLoop, calls=%fused_computation.10 | loop fusion | flops 65536 | bytes 67584 | tf_op jit(solution)/shard_map/eq | solution.py:176
  1.0 0.9 %convert_reduce_fusion = f32[5,16,128]{2,1,0:T(8,128)} fusion(pred[16,32,128]{2,1,0:T(8,128)(4,1)S(1)} %iota_compare_fusion, pred[5,32]{1,0:T(8,128)(4,1)S(1)} %iota_compare_fusion.10), kind=kLoop, calls=%fused_computation | loop fusion | flops 972800 | bytes 106656 | tf_op jit(solution)/shard_map/reduce_sum | solution.py:177
  1.9 3.5 %gather_send.1 = (f32[9,16,256]{2,1,0:T(8,128)}, f32[9,16,256]{2,1,0:T(8,128)}, f32[9,16,256]{2,1,0:T(8,128)}, f32[9,16,256]{2,1,0:T(8,128)}, f32[9,16,256]{2,1,0:T(8,128)}) custom-call(f32[9,256,128]{2,1,0:T(8,128)} %values_ref.3, f32[80,128]{1,0:T(8,128)} %bitcast.44), custom_call_target="tpu_custom_call" | custom-call | tf_op jit(solution)/shard_map/gather_send/pallas_call | solution.py:61
  5.4 0.7 %collective-permute-start = (f32[9,16,256]{2,1,0:T(8,128)}, f32[9,16,256]{2,1,0:T(8,128)S(1)}, u32[]{:S(2)}, u32[]{:S(2)}) collective-permute-start(f32[9,16,256]{2,1,0:T(8,128)} %get-tuple-element.16), channel_id=1, source_target_pairs={{0,1},{1,0},{2,3},{3,2},{4,5},{5,4},{6,7},{7,6},{8,9},{9,8},{10,11... | collective-permute-start | bytes 442376 | tf_op jit(solution)/shard_map/ppermute | solution.py:200
  6.0 0.1 collective-permute-start.1
  6.1 1.2 %collective-permute-start.2 = (f32[9,16,256]{2,1,0:T(8,128)}, f32[9,16,256]{2,1,0:T(8,128)S(1)}, u32[]{:S(2)}, u32[]{:S(2)}) collective-permute-start(f32[9,16,256]{2,1,0:T(8,128)} %get-tuple-element.18), channel_id=1, source_target_pairs={{0,2},{1,3},{2,0},{3,1},{4,6},{5,7},{6,4},{7,5},{8,10},{9,11},{10,... | collective-permute-start | bytes 442376 | tf_op jit(solution)/shard_map/ppermute | solution.py:200
  7.3 2.6 %collective-permute-start.3 = (f32[9,16,256]{2,1,0:T(8,128)}, f32[9,16,256]{2,1,0:T(8,128)S(1)}, u32[]{:S(2)}, u32[]{:S(2)}) collective-permute-start(f32[9,16,256]{2,1,0:T(8,128)} %get-tuple-element.19), channel_id=1, source_target_pairs={{1,2},{2,1},{3,4},{4,3},{5,6},{6,5},{7,8},{8,7},{9,10},{10,9},{11,... | collective-permute-start | bytes 442376 | tf_op jit(solution)/shard_map/ppermute | solution.py:200
  9.9 4.9 %collective-permute-start.4 = (f32[9,16,256]{2,1,0:T(8,128)}, f32[9,16,256]{2,1,0:T(8,128)S(1)}, u32[]{:S(2)}, u32[]{:S(2)}) collective-permute-start(f32[9,16,256]{2,1,0:T(8,128)} %get-tuple-element.20), channel_id=1, source_target_pairs={{2,4},{3,5},{4,2},{5,3},{6,8},{7,9},{8,6},{9,7},{10,12},{11,13},{1... | collective-permute-start | bytes 442376 | tf_op jit(solution)/shard_map/ppermute | solution.py:200
  15.5 0.0 copy-done.11
  15.5 0.0 copy-done.10
  15.8 1.5 %multiply_add_fusion.local_ref.refs_6_.refs_7_.refs_8_.refs_9_.refs_10_ = f32[9,208,128]{2,1,0:T(8,128)} fusion(f32[208,128]{1,0:T(8,128)S(1)} %get-tuple-element.43, f32[9,128]{1,0:T(8,128)S(1)} %get-tuple-element.51, f32[208,128]{1,0:T(8,128)S(1)} %get-tuple-element.44, f32[9,128]{1,0:T(8,128)S(1)} %get-tuple-element.52, ...), kind=kLoop, calls=%fused_computation.1 | loop fusion | flops 3594240 | bytes 1847296 | tf_op jit(solution)/shard_map/add | solution.py:192
  17.2 3.5 %local_part.2.refs_0_ = f32[9,256,128]{2,1,0:T(8,128)} custom-call(f32[9,256,128]{2,1,0:T(8,128)} %values_ref.3, f32[9,208,128]{2,1,0:T(8,128)} %multiply_add_fusion.local_ref.refs_6_.refs_7_.refs_8_.refs_9_.refs_10_, f32[8,128]{1,0:T(8,128)} %mixing_ref.3), custom_call_target="tpu_custom_call" | custom-call | tf_op jit(solution)/shard_map/local_part/pallas_call | solution.py:87
  20.8 0.0 collective-permute-done.refs_1_
  20.8 0.0 collective-permute-done.1.refs_2_
  20.8 0.0 copy-start.1
  20.8 0.0 collective-permute-done.2.refs_3_
  20.8 0.0 copy-start.2
  20.8 0.0 collective-permute-done.3.refs_4_
  20.8 0.0 copy-start.3
  20.8 1.0 %collective-permute-done.4.refs_5_ = f32[9,16,256]{2,1,0:T(8,128)S(1)} collective-permute-done((f32[9,16,256]{2,1,0:T(8,128)}, f32[9,16,256]{2,1,0:T(8,128)S(1)}, u32[]{:S(2)}, u32[]{:S(2)}) %collective-permute-start.4) | collective-permute-done | bytes 147488 | tf_op jit(solution)/shard_map/ppermute | solution.py:200
  21.9 0.0 copy-done
  21.9 0.0 copy-done.1
  21.9 0.0 copy-done.2
  21.9 0.0 copy-done.3
  21.9 0.6 %copy-done.4 = f32[9,16,256]{2,1,0:T(8,128)} copy-done((f32[9,16,256]{2,1,0:T(8,128)}, f32[9,16,256]{2,1,0:T(8,128)S(1)}, u32[]{:S(2)}) %copy-start.4) | copy-done | bytes 147480
  22.5 5.0 %finish_send.1 = (f32[9,256,128]{2,1,0:T(8,128)}, f32[9,16,256]{2,1,0:T(8,128)}, f32[9,16,256]{2,1,0:T(8,128)}, f32[9,16,256]{2,1,0:T(8,128)}, f32[9,16,256]{2,1,0:T(8,128)}, /*index=5*/f32[9,16,256]{2,1,0:T(8,128)}) custom-call(f32[9,256,128]{2,1,0:T(8,128)} %local_part.2.refs_0_, f32[9,16,256]{2,1,0:T(8,128)} %copy-done, f32[9,16,256]{2,1,0:T(8,128)} %copy-done.1, ...), custom_call_target="tpu_custom_call" | custom-call | tf_op jit(solution)/shard_map/finish_send/pallas_call | solution.py:149
  27.6 0.0 collective-permute-start.5
  27.6 1.5 %collective-permute-start.6 = (f32[9,16,256]{2,1,0:T(8,128)}, f32[9,16,256]{2,1,0:T(8,128)S(1)}, u32[]{:S(2)}, u32[]{:S(2)}) collective-permute-start(f32[9,16,256]{2,1,0:T(8,128)} %get-tuple-element.23), channel_id=1, source_target_pairs={{0,16},{1,17},{2,18},{3,19},{4,20},{5,21},{6,22},{7,23},{8,24},{9,... | collective-permute-start | bytes 442376 | tf_op jit(solution)/shard_map/ppermute | solution.py:200
  29.1 0.0 collective-permute-start.7
  29.1 4.2 %collective-permute-start.8 = (f32[9,16,256]{2,1,0:T(8,128)}, f32[9,16,256]{2,1,0:T(8,128)S(1)}, u32[]{:S(2)}, u32[]{:S(2)}) collective-permute-start(f32[9,16,256]{2,1,0:T(8,128)} %get-tuple-element.25), channel_id=1, source_target_pairs={{1,2},{2,1},{3,4},{4,3},{5,6},{6,5},{7,8},{8,7},{9,10},{10,9},{11,... | collective-permute-start | bytes 442376 | tf_op jit(solution)/shard_map/ppermute | solution.py:200
  33.3 3.4 %collective-permute-start.9 = (f32[9,16,256]{2,1,0:T(8,128)}, f32[9,16,256]{2,1,0:T(8,128)S(1)}, u32[]{:S(2)}, u32[]{:S(2)}) collective-permute-start(f32[9,16,256]{2,1,0:T(8,128)} %get-tuple-element.26), channel_id=1, source_target_pairs={{2,4},{3,5},{4,2},{5,3},{6,8},{7,9},{8,6},{9,7},{10,12},{11,13},{1... | collective-permute-start | bytes 442376 | tf_op jit(solution)/shard_map/ppermute | solution.py:200
  36.8 3.5 %local_part.3.refs_0_ = f32[9,256,128]{2,1,0:T(8,128)} custom-call(f32[9,256,128]{2,1,0:T(8,128)} %get-tuple-element.21.values_ref, f32[9,208,128]{2,1,0:T(8,128)} %multiply_add_fusion.local_ref.refs_6_.refs_7_.refs_8_.refs_9_.refs_10_, f32[8,128]{1,0:T(8,128)} %mixing_ref.3), custom_call_target="tpu_custom_call" | custom-call | tf_op jit(solution)/shard_map/local_part/pallas_call | solution.py:87
  40.3 0.0 collective-permute-done.5.refs_1_
  40.3 0.0 collective-permute-done.6.refs_2_
  40.3 0.0 copy-start.6
  40.3 0.0 collective-permute-done.7.refs_3_
  40.3 0.0 copy-start.7
  40.3 0.0 collective-permute-done.8.refs_4_
  40.3 0.0 copy-start.8
  40.4 2.6 %collective-permute-done.9.refs_5_ = f32[9,16,256]{2,1,0:T(8,128)S(1)} collective-permute-done((f32[9,16,256]{2,1,0:T(8,128)}, f32[9,16,256]{2,1,0:T(8,128)S(1)}, u32[]{:S(2)}, u32[]{:S(2)}) %collective-permute-start.9) | collective-permute-done | bytes 147488 | tf_op jit(solution)/shard_map/ppermute | solution.py:200
  42.9 0.0 copy-done.5
  42.9 0.0 copy-done.6
  42.9 0.0 copy-done.7
  42.9 0.0 copy-done.8
  43.0 0.6 %copy-done.9 = f32[9,16,256]{2,1,0:T(8,128)} copy-done((f32[9,16,256]{2,1,0:T(8,128)}, f32[9,16,256]{2,1,0:T(8,128)S(1)}, u32[]{:S(2)}) %copy-start.9) | copy-done | bytes 147480
  43.6 3.8 %finish.1 = f32[9,256,128]{2,1,0:T(8,128)} custom-call(f32[9,256,128]{2,1,0:T(8,128)} %local_part.3.refs_0_, f32[9,16,256]{2,1,0:T(8,128)} %copy-done.5, f32[9,16,256]{2,1,0:T(8,128)} %copy-done.6, f32[9,16,256]{2,1,0:T(8,128)} %copy-done.7, f32[9,16,256]{2,1,0:T(8,128)} %copy-done.8, f32[9,16,256]{2,1,0:T(8,128)} %copy-done.9, ...), custom_call_target="tpu_custom_call" | custom-call | tf_op jit(solution)/shard_map/finish/pallas_call | solution.py:149
  (17 shorter events, 0.2 us)
Async XLA Ops:
  0.0 15.5 %copy-start.11 = (s32[8,128]{1,0:T(8,128)S(1)}, s32[8,128]{1,0:T(8,128)}, u32[]{:S(2)}) copy-start(s32[8,128]{1,0:T(8,128)} %param.11) | copy-start | bytes 12292
  0.0 15.5 %copy-start.10 = (f32[8,9,128]{2,0,1:T(8,128)S(1)}, f32[8,9,128]{2,0,1:T(8,128)}, u32[]{:S(2)}) copy-start(f32[8,9,128]{2,0,1:T(8,128)} %param.8) | copy-start | bytes 110596
  5.4 15.4 %collective-permute-start = (f32[9,16,256]{2,1,0:T(8,128)}, f32[9,16,256]{2,1,0:T(8,128)S(1)}, u32[]{:S(2)}, u32[]{:S(2)}) collective-permute-start(f32[9,16,256]{2,1,0:T(8,128)} %get-tuple-element.16), channel_id=1, source_target_pairs={{0,1},{1,0},{2,3},{3,2},{4,5},{5,4},{6,7},{7,6},{8,9},{9,8},{10,11... | collective-permute-start | bytes 442376 | tf_op jit(solution)/shard_map/ppermute | solution.py:200
  6.0 14.7 %collective-permute-start.1 = (f32[9,16,256]{2,1,0:T(8,128)}, f32[9,16,256]{2,1,0:T(8,128)S(1)}, u32[]{:S(2)}, u32[]{:S(2)}) collective-permute-start(f32[9,16,256]{2,1,0:T(8,128)} %get-tuple-element.17), channel_id=1, source_target_pairs={{0,16},{1,17},{2,18},{3,19},{4,20},{5,21},{6,22},{7,23},{8,24},{9,... | collective-permute-start | bytes 442376 | tf_op jit(solution)/shard_map/ppermute | solution.py:200
  6.1 14.7 %collective-permute-start.2 = (f32[9,16,256]{2,1,0:T(8,128)}, f32[9,16,256]{2,1,0:T(8,128)S(1)}, u32[]{:S(2)}, u32[]{:S(2)}) collective-permute-start(f32[9,16,256]{2,1,0:T(8,128)} %get-tuple-element.18), channel_id=1, source_target_pairs={{0,2},{1,3},{2,0},{3,1},{4,6},{5,7},{6,4},{7,5},{8,10},{9,11},{10,... | collective-permute-start | bytes 442376 | tf_op jit(solution)/shard_map/ppermute | solution.py:200
  7.3 13.5 %collective-permute-start.3 = (f32[9,16,256]{2,1,0:T(8,128)}, f32[9,16,256]{2,1,0:T(8,128)S(1)}, u32[]{:S(2)}, u32[]{:S(2)}) collective-permute-start(f32[9,16,256]{2,1,0:T(8,128)} %get-tuple-element.19), channel_id=1, source_target_pairs={{1,2},{2,1},{3,4},{4,3},{5,6},{6,5},{7,8},{8,7},{9,10},{10,9},{11,... | collective-permute-start | bytes 442376 | tf_op jit(solution)/shard_map/ppermute | solution.py:200
  9.9 12.0 %collective-permute-start.4 = (f32[9,16,256]{2,1,0:T(8,128)}, f32[9,16,256]{2,1,0:T(8,128)S(1)}, u32[]{:S(2)}, u32[]{:S(2)}) collective-permute-start(f32[9,16,256]{2,1,0:T(8,128)} %get-tuple-element.20), channel_id=1, source_target_pairs={{2,4},{3,5},{4,2},{5,3},{6,8},{7,9},{8,6},{9,7},{10,12},{11,13},{1... | collective-permute-start | bytes 442376 | tf_op jit(solution)/shard_map/ppermute | solution.py:200
  20.8 1.1 %copy-start = (f32[9,16,256]{2,1,0:T(8,128)}, f32[9,16,256]{2,1,0:T(8,128)S(1)}, u32[]{:S(2)}) copy-start(f32[9,16,256]{2,1,0:T(8,128)S(1)} %collective-permute-done.refs_1_) | copy-start | bytes 442372
  20.8 1.1 %copy-start.1 = (f32[9,16,256]{2,1,0:T(8,128)}, f32[9,16,256]{2,1,0:T(8,128)S(1)}, u32[]{:S(2)}) copy-start(f32[9,16,256]{2,1,0:T(8,128)S(1)} %collective-permute-done.1.refs_2_) | copy-start | bytes 442372
  20.8 1.1 %copy-start.2 = (f32[9,16,256]{2,1,0:T(8,128)}, f32[9,16,256]{2,1,0:T(8,128)S(1)}, u32[]{:S(2)}) copy-start(f32[9,16,256]{2,1,0:T(8,128)S(1)} %collective-permute-done.2.refs_3_) | copy-start | bytes 442372
  20.8 1.1 %copy-start.3 = (f32[9,16,256]{2,1,0:T(8,128)}, f32[9,16,256]{2,1,0:T(8,128)S(1)}, u32[]{:S(2)}) copy-start(f32[9,16,256]{2,1,0:T(8,128)S(1)} %collective-permute-done.3.refs_4_) | copy-start | bytes 442372
  21.9 0.7 %copy-start.4 = (f32[9,16,256]{2,1,0:T(8,128)}, f32[9,16,256]{2,1,0:T(8,128)S(1)}, u32[]{:S(2)}) copy-start(f32[9,16,256]{2,1,0:T(8,128)S(1)} %collective-permute-done.4.refs_5_) | copy-start | bytes 442372
  27.6 12.7 %collective-permute-start.5 = (f32[9,16,256]{2,1,0:T(8,128)}, f32[9,16,256]{2,1,0:T(8,128)S(1)}, u32[]{:S(2)}, u32[]{:S(2)}) collective-permute-start(f32[9,16,256]{2,1,0:T(8,128)} %get-tuple-element.22), channel_id=1, source_target_pairs={{0,1},{1,0},{2,3},{3,2},{4,5},{5,4},{6,7},{7,6},{8,9},{9,8},{10,11... | collective-permute-start | bytes 442376 | tf_op jit(solution)/shard_map/ppermute | solution.py:200
  27.6 12.7 %collective-permute-start.6 = (f32[9,16,256]{2,1,0:T(8,128)}, f32[9,16,256]{2,1,0:T(8,128)S(1)}, u32[]{:S(2)}, u32[]{:S(2)}) collective-permute-start(f32[9,16,256]{2,1,0:T(8,128)} %get-tuple-element.23), channel_id=1, source_target_pairs={{0,16},{1,17},{2,18},{3,19},{4,20},{5,21},{6,22},{7,23},{8,24},{9,... | collective-permute-start | bytes 442376 | tf_op jit(solution)/shard_map/ppermute | solution.py:200
  29.1 11.3 %collective-permute-start.7 = (f32[9,16,256]{2,1,0:T(8,128)}, f32[9,16,256]{2,1,0:T(8,128)S(1)}, u32[]{:S(2)}, u32[]{:S(2)}) collective-permute-start(f32[9,16,256]{2,1,0:T(8,128)} %get-tuple-element.24), channel_id=1, source_target_pairs={{0,2},{1,3},{2,0},{3,1},{4,6},{5,7},{6,4},{7,5},{8,10},{9,11},{10,... | collective-permute-start | bytes 442376 | tf_op jit(solution)/shard_map/ppermute | solution.py:200
  29.1 11.3 %collective-permute-start.8 = (f32[9,16,256]{2,1,0:T(8,128)}, f32[9,16,256]{2,1,0:T(8,128)S(1)}, u32[]{:S(2)}, u32[]{:S(2)}) collective-permute-start(f32[9,16,256]{2,1,0:T(8,128)} %get-tuple-element.25), channel_id=1, source_target_pairs={{1,2},{2,1},{3,4},{4,3},{5,6},{6,5},{7,8},{8,7},{9,10},{10,9},{11,... | collective-permute-start | bytes 442376 | tf_op jit(solution)/shard_map/ppermute | solution.py:200
  33.3 9.6 %collective-permute-start.9 = (f32[9,16,256]{2,1,0:T(8,128)}, f32[9,16,256]{2,1,0:T(8,128)S(1)}, u32[]{:S(2)}, u32[]{:S(2)}) collective-permute-start(f32[9,16,256]{2,1,0:T(8,128)} %get-tuple-element.26), channel_id=1, source_target_pairs={{2,4},{3,5},{4,2},{5,3},{6,8},{7,9},{8,6},{9,7},{10,12},{11,13},{1... | collective-permute-start | bytes 442376 | tf_op jit(solution)/shard_map/ppermute | solution.py:200
  40.3 2.6 %copy-start.5 = (f32[9,16,256]{2,1,0:T(8,128)}, f32[9,16,256]{2,1,0:T(8,128)S(1)}, u32[]{:S(2)}) copy-start(f32[9,16,256]{2,1,0:T(8,128)S(1)} %collective-permute-done.5.refs_1_) | copy-start | bytes 442372
  40.3 2.6 %copy-start.6 = (f32[9,16,256]{2,1,0:T(8,128)}, f32[9,16,256]{2,1,0:T(8,128)S(1)}, u32[]{:S(2)}) copy-start(f32[9,16,256]{2,1,0:T(8,128)S(1)} %collective-permute-done.6.refs_2_) | copy-start | bytes 442372
  40.3 2.6 %copy-start.7 = (f32[9,16,256]{2,1,0:T(8,128)}, f32[9,16,256]{2,1,0:T(8,128)S(1)}, u32[]{:S(2)}) copy-start(f32[9,16,256]{2,1,0:T(8,128)S(1)} %collective-permute-done.7.refs_3_) | copy-start | bytes 442372
  40.3 2.6 %copy-start.8 = (f32[9,16,256]{2,1,0:T(8,128)}, f32[9,16,256]{2,1,0:T(8,128)S(1)}, u32[]{:S(2)}) copy-start(f32[9,16,256]{2,1,0:T(8,128)S(1)} %collective-permute-done.8.refs_4_) | copy-start | bytes 442372
  42.9 0.7 %copy-start.9 = (f32[9,16,256]{2,1,0:T(8,128)}, f32[9,16,256]{2,1,0:T(8,128)S(1)}, u32[]{:S(2)}) copy-start(f32[9,16,256]{2,1,0:T(8,128)S(1)} %collective-permute-done.9.refs_5_) | copy-start | bytes 442372

commit v12 on v8

--- a/solution.py
+++ b/solution.py
@@ -46,7 +46,18 @@
     return pl.BlockSpec(shape, lambda i: (0,) * len(shape))
 
 
-def select_kernel(groups, hslot, values_ref, select_ref, *out_refs):
+def select_kernel(partners, hslot, slots_ref, values_ref, *refs):
+    groups = len(partners)
+    out_refs, select_ref = refs[:groups], refs[groups]
+    me = lax.axis_index("cells")
+    capacity = values_ref.shape[2]
+    slots = slots_ref[...].astype(jnp.float32)
+    peer_index = lax.broadcasted_iota(jnp.int32, slots.shape, 1)
+    lanes = lax.broadcasted_iota(jnp.int32, (hslot, capacity), 1).astype(jnp.float32)
+    for g, partner in enumerate(partners):
+        peer = partner(me, jnp)
+        column = jnp.sum(jnp.where(peer_index == peer, slots, 0.0), axis=1, keepdims=True)
+        select_ref[g * hslot : (g + 1) * hslot, :] = (lanes == column).astype(jnp.float32)
     select = select_ref[...]
     for level in range(values_ref.shape[0]):
         block = lax.dot_general(
@@ -56,14 +67,18 @@
             out_refs[g][level] = block[g * hslot : (g + 1) * hslot]
 
 
-def gather_send(values, select, groups, hslot):
+def gather_send(values, slots, partners, hslot):
     levels, pulses, capacity = values.shape
-    return pl.pallas_call(
-        functools.partial(select_kernel, groups, hslot),
-        out_shape=[jax.ShapeDtypeStruct((levels, hslot, pulses), jnp.float32)] * groups,
+    groups = len(partners)
+    shapes = [jax.ShapeDtypeStruct((levels, hslot, pulses), jnp.float32)] * groups
+    shapes.append(jax.ShapeDtypeStruct((groups * hslot, capacity), jnp.float32))
+    outs = pl.pallas_call(
+        functools.partial(select_kernel, partners, hslot),
+        out_shape=shapes,
         interpret=INTERPRET,
         name="gather_send",
-    )(values, select)
+    )(slots, values)
+    return outs[:groups], outs[groups]
 
 
 def local_kernel(values_ref, local_ref, mixing_ref, out_ref):
@@ -169,14 +184,9 @@
     me = lax.axis_index("cells")
     f32 = jnp.float32
 
-    peers = jnp.stack([partner(me, jnp) for partner in partners])
-    is_peer = peers[:, None] == jnp.arange(n, dtype=jnp.int32)[None, :]
     lanes = jnp.arange(capacity, dtype=jnp.int32)
-    hit = is_peer[:, :, None, None] & (send_cells[0][None, :, :, None] == lanes)
-    select = jnp.sum(hit.astype(f32), axis=1).reshape(groups * hslot, capacity)
-
     values = concentration
-    outgoing = gather_send(values, select, groups, hslot)
+    outgoing, select = gather_send(values, send_cells[0].T, partners, hslot)
 
     beyond = halo_index - capacity
     sender = beyond // hslot

time: 47.8 us -> 46 us (0.962)
  other arithmetic: 2.68 us -> 1.61 us
  local copies, waits for them, and re-layouts: 2.22 us -> 1.36 us
    reduce_sum x1 -> x0, other arithmetic: 0.86 us -> none  [per_device(): select = jnp.sum(hit.astype(f32), axis=1).reshape(groups * hslot, capacity)]
    eq x1 -> x0, local copies, waits for them, and re-layouts: 0.77 us -> none  [per_device(): hit = is_peer[:, :, None, None] & (send_cells[0][None, :, :, None] == lanes)]
  transfers between devices with their start and end apart: 10 -> 10, of which waited for: 2 -> 2; matrix products, arithmetic and copies ran while one was open for 3% -> 4% of each run, Pallas kernels for 15% -> 15%
where the time goes in v12:
time: 46 us; the launch traced here: 45.7 us
  Pallas kernels  19.4 us (42%)
  starting transfers between devices  18.7 us (41%)
  waiting for transfers between devices  3.6 us (8%)
  other arithmetic  1.61 us (4%)
  local copies, waits for them, and re-layouts  1.36 us (3%)
  between operations  0.95 us (2%)
    ppermute x10, starting transfers between devices, per_device(): lax.ppermute(outgoing[g], 'cells', perm=pair_list(n, partner))  18.7 us
    pallas_call x2, Pallas kernels, finish(): pl.pallas_call(functools.partial(finish_kernel, groups, hslot, send), out...  8.84 us
    pallas_call x2, Pallas kernels, local_part(): pl.pallas_call(local_kernel, out_shape=jax.ShapeDtypeStruct(values.shape,...  7.04 us
    ppermute x10, waiting for transfers between devices, per_device(): lax.ppermute(outgoing[g], 'cells', perm=pair_list(n, partner))  3.6 us
    pallas_call x1, Pallas kernels, gather_send(): pl.pallas_call(functools.partial(select_kernel, partners, hslot), out_sha...  3.56 us
    add x1, other arithmetic, per_device(): sum((flux_weight[k][:, None, :] * ((row[k][None, :] == slots).astype(f32)...  1.47 us
    unnamed x24, local copies, waits for them, and re-layouts  1.3 us
  transfers between devices with their start and end apart: 10, of which 2 were waited for; matrix products, arithmetic and copies ran while one was open for 4% of the time, Pallas kernels for 15%

profile of v12, /device:TPU:25, one launch (start us, length us, event | category | flops | bytes accessed | tf_op | source)
XLA Modules:
  0.0 45.7 jit_solution(9263702685932290898)
XLA Ops:
  0.0 0.0 copy-start.11
  0.0 0.0 copy-start.10
  0.0 3.6 %gather_send.1 = (f32[9,16,256]{2,1,0:T(8,128)}, f32[9,16,256]{2,1,0:T(8,128)}, f32[9,16,256]{2,1,0:T(8,128)}, f32[9,16,256]{2,1,0:T(8,128)}, f32[9,16,256]{2,1,0:T(8,128)}, /*index=5*/f32[80,128]{1,0:T(8,128)}) custom-call(s32[16,32]{1,0:T(8,128)} %bitcast.38, f32[9,256,128]{2,1,0:T(8,128)} %values_ref.3), custom_call_target="tpu_custom_call" | custom-call | tf_op jit(solution)/shard_map/gather_send/pallas_call | solution.py:75
  3.6 0.7 %collective-permute-start = (f32[9,16,256]{2,1,0:T(8,128)}, f32[9,16,256]{2,1,0:T(8,128)S(1)}, u32[]{:S(2)}, u32[]{:S(2)}) collective-permute-start(f32[9,16,256]{2,1,0:T(8,128)} %get-tuple-element.17), channel_id=1, source_target_pairs={{0,1},{1,0},{2,3},{3,2},{4,5},{5,4},{6,7},{7,6},{8,9},{9,8},{10,11... | collective-permute-start | bytes 442376 | tf_op jit(solution)/shard_map/ppermute | solution.py:209
  4.2 1.2 %collective-permute-start.1 = (f32[9,16,256]{2,1,0:T(8,128)}, f32[9,16,256]{2,1,0:T(8,128)S(1)}, u32[]{:S(2)}, u32[]{:S(2)}) collective-permute-start(f32[9,16,256]{2,1,0:T(8,128)} %get-tuple-element.18), channel_id=1, source_target_pairs={{0,2},{1,3},{2,0},{3,1},{4,6},{5,7},{6,4},{7,5},{8,10},{9,11},{10,... | collective-permute-start | bytes 442376 | tf_op jit(solution)/shard_map/ppermute | solution.py:209
  5.5 0.1 collective-permute-start.2
  5.5 2.6 %collective-permute-start.3 = (f32[9,16,256]{2,1,0:T(8,128)}, f32[9,16,256]{2,1,0:T(8,128)S(1)}, u32[]{:S(2)}, u32[]{:S(2)}) collective-permute-start(f32[9,16,256]{2,1,0:T(8,128)} %get-tuple-element.20), channel_id=1, source_target_pairs={{1,2},{2,1},{3,4},{4,3},{5,6},{6,5},{7,8},{8,7},{9,10},{10,9},{11,... | collective-permute-start | bytes 442376 | tf_op jit(solution)/shard_map/ppermute | solution.py:209
  8.1 4.9 %collective-permute-start.4 = (f32[9,16,256]{2,1,0:T(8,128)}, f32[9,16,256]{2,1,0:T(8,128)S(1)}, u32[]{:S(2)}, u32[]{:S(2)}) collective-permute-start(f32[9,16,256]{2,1,0:T(8,128)} %get-tuple-element.21), channel_id=1, source_target_pairs={{2,4},{3,5},{4,2},{5,3},{6,8},{7,9},{8,6},{9,7},{10,12},{11,13},{1... | collective-permute-start | bytes 442376 | tf_op jit(solution)/shard_map/ppermute | solution.py:209
  13.7 0.0 copy-done.11
  13.8 0.0 copy-done.10
  14.0 1.5 %multiply_add_fusion.local_ref.refs_6_.refs_7_.refs_8_.refs_9_.refs_10_ = f32[9,208,128]{2,1,0:T(8,128)} fusion(f32[208,128]{1,0:T(8,128)S(1)} %get-tuple-element.45, f32[9,128]{1,0:T(8,128)S(1)} %get-tuple-element.53, f32[208,128]{1,0:T(8,128)S(1)} %get-tuple-element.46, f32[9,128]{1,0:T(8,128)S(1)} %get-tuple-element.54, ...), kind=kLoop, calls=%fused_computation | loop fusion | flops 3594240 | bytes 1847296 | tf_op jit(solution)/shard_map/add | solution.py:201
  15.5 3.5 %local_part.2.refs_0_ = f32[9,256,128]{2,1,0:T(8,128)} custom-call(f32[9,256,128]{2,1,0:T(8,128)} %values_ref.3, f32[9,208,128]{2,1,0:T(8,128)} %multiply_add_fusion.local_ref.refs_6_.refs_7_.refs_8_.refs_9_.refs_10_, f32[8,128]{1,0:T(8,128)} %mixing_ref.3), custom_call_target="tpu_custom_call" | custom-call | tf_op jit(solution)/shard_map/local_part/pallas_call | solution.py:102
  19.0 0.0 collective-permute-done.refs_1_
  19.0 0.0 copy-start
  19.0 0.0 collective-permute-done.1.refs_2_
  19.0 0.0 copy-start.1
  19.0 0.0 collective-permute-done.2.refs_3_
  19.0 0.0 copy-start.2
  19.0 0.0 collective-permute-done.3.refs_4_
  19.0 0.0 copy-start.3
  19.1 1.0 %collective-permute-done.4.refs_5_ = f32[9,16,256]{2,1,0:T(8,128)S(1)} collective-permute-done((f32[9,16,256]{2,1,0:T(8,128)}, f32[9,16,256]{2,1,0:T(8,128)S(1)}, u32[]{:S(2)}, u32[]{:S(2)}) %collective-permute-start.4) | collective-permute-done | bytes 147488 | tf_op jit(solution)/shard_map/ppermute | solution.py:209
  20.1 0.0 copy-start.4
  20.1 0.0 copy-done
  20.1 0.0 copy-done.1
  20.1 0.0 copy-done.2
  20.1 0.0 copy-done.3
  20.1 0.6 %copy-done.4 = f32[9,16,256]{2,1,0:T(8,128)} copy-done((f32[9,16,256]{2,1,0:T(8,128)}, f32[9,16,256]{2,1,0:T(8,128)S(1)}, u32[]{:S(2)}) %copy-start.4) | copy-done | bytes 147480
  20.7 5.0 %finish_send.1 = (f32[9,256,128]{2,1,0:T(8,128)}, f32[9,16,256]{2,1,0:T(8,128)}, f32[9,16,256]{2,1,0:T(8,128)}, f32[9,16,256]{2,1,0:T(8,128)}, f32[9,16,256]{2,1,0:T(8,128)}, /*index=5*/f32[9,16,256]{2,1,0:T(8,128)}) custom-call(f32[9,256,128]{2,1,0:T(8,128)} %local_part.2.refs_0_, f32[9,16,256]{2,1,0:T(8,128)} %copy-done, f32[9,16,256]{2,1,0:T(8,128)} %copy-done.1, ...), custom_call_target="tpu_custom_call" | custom-call | tf_op jit(solution)/shard_map/finish_send/pallas_call | solution.py:164
  25.7 0.1 collective-permute-start.5
  25.8 0.0 collective-permute-start.6
  25.8 1.6 %collective-permute-start.7 = (f32[9,16,256]{2,1,0:T(8,128)}, f32[9,16,256]{2,1,0:T(8,128)S(1)}, u32[]{:S(2)}, u32[]{:S(2)}) collective-permute-start(f32[9,16,256]{2,1,0:T(8,128)} %get-tuple-element.26), channel_id=1, source_target_pairs={{0,16},{1,17},{2,18},{3,19},{4,20},{5,21},{6,22},{7,23},{8,24},{9,... | collective-permute-start | bytes 442376 | tf_op jit(solution)/shard_map/ppermute | solution.py:209
  27.4 4.2 %collective-permute-start.8 = (f32[9,16,256]{2,1,0:T(8,128)}, f32[9,16,256]{2,1,0:T(8,128)S(1)}, u32[]{:S(2)}, u32[]{:S(2)}) collective-permute-start(f32[9,16,256]{2,1,0:T(8,128)} %get-tuple-element.27), channel_id=1, source_target_pairs={{1,2},{2,1},{3,4},{4,3},{5,6},{6,5},{7,8},{8,7},{9,10},{10,9},{11,... | collective-permute-start | bytes 442376 | tf_op jit(solution)/shard_map/ppermute | solution.py:209
  31.6 3.4 %collective-permute-start.9 = (f32[9,16,256]{2,1,0:T(8,128)}, f32[9,16,256]{2,1,0:T(8,128)S(1)}, u32[]{:S(2)}, u32[]{:S(2)}) collective-permute-start(f32[9,16,256]{2,1,0:T(8,128)} %get-tuple-element.28), channel_id=1, source_target_pairs={{2,4},{3,5},{4,2},{5,3},{6,8},{7,9},{8,6},{9,7},{10,12},{11,13},{1... | collective-permute-start | bytes 442376 | tf_op jit(solution)/shard_map/ppermute | solution.py:209
  35.0 3.5 %local_part.3.refs_0_ = f32[9,256,128]{2,1,0:T(8,128)} custom-call(f32[9,256,128]{2,1,0:T(8,128)} %get-tuple-element.23.values_ref, f32[9,208,128]{2,1,0:T(8,128)} %multiply_add_fusion.local_ref.refs_6_.refs_7_.refs_8_.refs_9_.refs_10_, f32[8,128]{1,0:T(8,128)} %mixing_ref.3), custom_call_target="tpu_custom_call" | custom-call | tf_op jit(solution)/shard_map/local_part/pallas_call | solution.py:102
  38.5 0.0 collective-permute-done.5.refs_1_
  38.5 0.0 collective-permute-done.6.refs_2_
  38.5 0.0 copy-start.6
  38.5 0.0 collective-permute-done.7.refs_3_
  38.6 0.0 copy-start.7
  38.6 0.0 collective-permute-done.8.refs_4_
  38.6 0.0 copy-start.8
  38.6 2.6 %collective-permute-done.9.refs_5_ = f32[9,16,256]{2,1,0:T(8,128)S(1)} collective-permute-done((f32[9,16,256]{2,1,0:T(8,128)}, f32[9,16,256]{2,1,0:T(8,128)S(1)}, u32[]{:S(2)}, u32[]{:S(2)}) %collective-permute-start.9) | collective-permute-done | bytes 147488 | tf_op jit(solution)/shard_map/ppermute | solution.py:209
  41.2 0.0 copy-done.5
  41.2 0.0 copy-done.6
  41.2 0.0 copy-done.7
  41.2 0.0 copy-done.8
  41.2 0.6 %copy-done.9 = f32[9,16,256]{2,1,0:T(8,128)} copy-done((f32[9,16,256]{2,1,0:T(8,128)}, f32[9,16,256]{2,1,0:T(8,128)S(1)}, u32[]{:S(2)}) %copy-start.9) | copy-done | bytes 147480
  41.8 3.8 %finish.1 = f32[9,256,128]{2,1,0:T(8,128)} custom-call(f32[9,256,128]{2,1,0:T(8,128)} %local_part.3.refs_0_, f32[9,16,256]{2,1,0:T(8,128)} %copy-done.5, f32[9,16,256]{2,1,0:T(8,128)} %copy-done.6, f32[9,16,256]{2,1,0:T(8,128)} %copy-done.7, f32[9,16,256]{2,1,0:T(8,128)} %copy-done.8, f32[9,16,256]{2,1,0:T(8,128)} %copy-done.9, ...), custom_call_target="tpu_custom_call" | custom-call | tf_op jit(solution)/shard_map/finish/pallas_call | solution.py:164
  (13 shorter events, 0.2 us)
Async XLA Ops:
  0.0 13.7 %copy-start.11 = (s32[8,128]{1,0:T(8,128)S(1)}, s32[8,128]{1,0:T(8,128)}, u32[]{:S(2)}) copy-start(s32[8,128]{1,0:T(8,128)} %param.11) | copy-start | bytes 12292
  0.0 13.8 %copy-start.10 = (f32[8,9,128]{2,0,1:T(8,128)S(1)}, f32[8,9,128]{2,0,1:T(8,128)}, u32[]{:S(2)}) copy-start(f32[8,9,128]{2,0,1:T(8,128)} %param.8) | copy-start | bytes 110596
  3.6 15.4 %collective-permute-start = (f32[9,16,256]{2,1,0:T(8,128)}, f32[9,16,256]{2,1,0:T(8,128)S(1)}, u32[]{:S(2)}, u32[]{:S(2)}) collective-permute-start(f32[9,16,256]{2,1,0:T(8,128)} %get-tuple-element.17), channel_id=1, source_target_pairs={{0,1},{1,0},{2,3},{3,2},{4,5},{5,4},{6,7},{7,6},{8,9},{9,8},{10,11... | collective-permute-start | bytes 442376 | tf_op jit(solution)/shard_map/ppermute | solution.py:209
  4.2 14.8 %collective-permute-start.1 = (f32[9,16,256]{2,1,0:T(8,128)}, f32[9,16,256]{2,1,0:T(8,128)S(1)}, u32[]{:S(2)}, u32[]{:S(2)}) collective-permute-start(f32[9,16,256]{2,1,0:T(8,128)} %get-tuple-element.18), channel_id=1, source_target_pairs={{0,2},{1,3},{2,0},{3,1},{4,6},{5,7},{6,4},{7,5},{8,10},{9,11},{10,... | collective-permute-start | bytes 442376 | tf_op jit(solution)/shard_map/ppermute | solution.py:209
  5.5 13.6 %collective-permute-start.2 = (f32[9,16,256]{2,1,0:T(8,128)}, f32[9,16,256]{2,1,0:T(8,128)S(1)}, u32[]{:S(2)}, u32[]{:S(2)}) collective-permute-start(f32[9,16,256]{2,1,0:T(8,128)} %get-tuple-element.19), channel_id=1, source_target_pairs={{0,16},{1,17},{2,18},{3,19},{4,20},{5,21},{6,22},{7,23},{8,24},{9,... | collective-permute-start | bytes 442376 | tf_op jit(solution)/shard_map/ppermute | solution.py:209
  5.5 13.5 %collective-permute-start.3 = (f32[9,16,256]{2,1,0:T(8,128)}, f32[9,16,256]{2,1,0:T(8,128)S(1)}, u32[]{:S(2)}, u32[]{:S(2)}) collective-permute-start(f32[9,16,256]{2,1,0:T(8,128)} %get-tuple-element.20), channel_id=1, source_target_pairs={{1,2},{2,1},{3,4},{4,3},{5,6},{6,5},{7,8},{8,7},{9,10},{10,9},{11,... | collective-permute-start | bytes 442376 | tf_op jit(solution)/shard_map/ppermute | solution.py:209
  8.1 11.9 %collective-permute-start.4 = (f32[9,16,256]{2,1,0:T(8,128)}, f32[9,16,256]{2,1,0:T(8,128)S(1)}, u32[]{:S(2)}, u32[]{:S(2)}) collective-permute-start(f32[9,16,256]{2,1,0:T(8,128)} %get-tuple-element.21), channel_id=1, source_target_pairs={{2,4},{3,5},{4,2},{5,3},{6,8},{7,9},{8,6},{9,7},{10,12},{11,13},{1... | collective-permute-start | bytes 442376 | tf_op jit(solution)/shard_map/ppermute | solution.py:209
  19.0 1.1 %copy-start = (f32[9,16,256]{2,1,0:T(8,128)}, f32[9,16,256]{2,1,0:T(8,128)S(1)}, u32[]{:S(2)}) copy-start(f32[9,16,256]{2,1,0:T(8,128)S(1)} %collective-permute-done.refs_1_) | copy-start | bytes 442372
  19.0 1.1 %copy-start.1 = (f32[9,16,256]{2,1,0:T(8,128)}, f32[9,16,256]{2,1,0:T(8,128)S(1)}, u32[]{:S(2)}) copy-start(f32[9,16,256]{2,1,0:T(8,128)S(1)} %collective-permute-done.1.refs_2_) | copy-start | bytes 442372
  19.0 1.0 %copy-start.2 = (f32[9,16,256]{2,1,0:T(8,128)}, f32[9,16,256]{2,1,0:T(8,128)S(1)}, u32[]{:S(2)}) copy-start(f32[9,16,256]{2,1,0:T(8,128)S(1)} %collective-permute-done.2.refs_3_) | copy-start | bytes 442372
  19.0 1.0 %copy-start.3 = (f32[9,16,256]{2,1,0:T(8,128)}, f32[9,16,256]{2,1,0:T(8,128)S(1)}, u32[]{:S(2)}) copy-start(f32[9,16,256]{2,1,0:T(8,128)S(1)} %collective-permute-done.3.refs_4_) | copy-start | bytes 442372
  20.1 0.7 %copy-start.4 = (f32[9,16,256]{2,1,0:T(8,128)}, f32[9,16,256]{2,1,0:T(8,128)S(1)}, u32[]{:S(2)}) copy-start(f32[9,16,256]{2,1,0:T(8,128)S(1)} %collective-permute-done.4.refs_5_) | copy-start | bytes 442372
  25.7 12.8 %collective-permute-start.5 = (f32[9,16,256]{2,1,0:T(8,128)}, f32[9,16,256]{2,1,0:T(8,128)S(1)}, u32[]{:S(2)}, u32[]{:S(2)}) collective-permute-start(f32[9,16,256]{2,1,0:T(8,128)} %get-tuple-element.24), channel_id=1, source_target_pairs={{0,1},{1,0},{2,3},{3,2},{4,5},{5,4},{6,7},{7,6},{8,9},{9,8},{10,11... | collective-permute-start | bytes 442376 | tf_op jit(solution)/shard_map/ppermute | solution.py:209
  25.8 12.8 %collective-permute-start.6 = (f32[9,16,256]{2,1,0:T(8,128)}, f32[9,16,256]{2,1,0:T(8,128)S(1)}, u32[]{:S(2)}, u32[]{:S(2)}) collective-permute-start(f32[9,16,256]{2,1,0:T(8,128)} %get-tuple-element.25), channel_id=1, source_target_pairs={{0,2},{1,3},{2,0},{3,1},{4,6},{5,7},{6,4},{7,5},{8,10},{9,11},{10,... | collective-permute-start | bytes 442376 | tf_op jit(solution)/shard_map/ppermute | solution.py:209
  25.8 12.7 %collective-permute-start.7 = (f32[9,16,256]{2,1,0:T(8,128)}, f32[9,16,256]{2,1,0:T(8,128)S(1)}, u32[]{:S(2)}, u32[]{:S(2)}) collective-permute-start(f32[9,16,256]{2,1,0:T(8,128)} %get-tuple-element.26), channel_id=1, source_target_pairs={{0,16},{1,17},{2,18},{3,19},{4,20},{5,21},{6,22},{7,23},{8,24},{9,... | collective-permute-start | bytes 442376 | tf_op jit(solution)/shard_map/ppermute | solution.py:209
  27.4 11.2 %collective-permute-start.8 = (f32[9,16,256]{2,1,0:T(8,128)}, f32[9,16,256]{2,1,0:T(8,128)S(1)}, u32[]{:S(2)}, u32[]{:S(2)}) collective-permute-start(f32[9,16,256]{2,1,0:T(8,128)} %get-tuple-element.27), channel_id=1, source_target_pairs={{1,2},{2,1},{3,4},{4,3},{5,6},{6,5},{7,8},{8,7},{9,10},{10,9},{11,... | collective-permute-start | bytes 442376 | tf_op jit(solution)/shard_map/ppermute | solution.py:209
  31.6 9.6 %collective-permute-start.9 = (f32[9,16,256]{2,1,0:T(8,128)}, f32[9,16,256]{2,1,0:T(8,128)S(1)}, u32[]{:S(2)}, u32[]{:S(2)}) collective-permute-start(f32[9,16,256]{2,1,0:T(8,128)} %get-tuple-element.28), channel_id=1, source_target_pairs={{2,4},{3,5},{4,2},{5,3},{6,8},{7,9},{8,6},{9,7},{10,12},{11,13},{1... | collective-permute-start | bytes 442376 | tf_op jit(solution)/shard_map/ppermute | solution.py:209
  38.5 2.6 %copy-start.5 = (f32[9,16,256]{2,1,0:T(8,128)}, f32[9,16,256]{2,1,0:T(8,128)S(1)}, u32[]{:S(2)}) copy-start(f32[9,16,256]{2,1,0:T(8,128)S(1)} %collective-permute-done.5.refs_1_) | copy-start | bytes 442372
  38.5 2.6 %copy-start.6 = (f32[9,16,256]{2,1,0:T(8,128)}, f32[9,16,256]{2,1,0:T(8,128)S(1)}, u32[]{:S(2)}) copy-start(f32[9,16,256]{2,1,0:T(8,128)S(1)} %collective-permute-done.6.refs_2_) | copy-start | bytes 442372
  38.6 2.6 %copy-start.7 = (f32[9,16,256]{2,1,0:T(8,128)}, f32[9,16,256]{2,1,0:T(8,128)S(1)}, u32[]{:S(2)}) copy-start(f32[9,16,256]{2,1,0:T(8,128)S(1)} %collective-permute-done.7.refs_3_) | copy-start | bytes 442372
  38.6 2.6 %copy-start.8 = (f32[9,16,256]{2,1,0:T(8,128)}, f32[9,16,256]{2,1,0:T(8,128)S(1)}, u32[]{:S(2)}) copy-start(f32[9,16,256]{2,1,0:T(8,128)S(1)} %collective-permute-done.8.refs_4_) | copy-start | bytes 442372
  41.2 0.6 %copy-start.9 = (f32[9,16,256]{2,1,0:T(8,128)}, f32[9,16,256]{2,1,0:T(8,128)S(1)}, u32[]{:S(2)}) copy-start(f32[9,16,256]{2,1,0:T(8,128)S(1)} %collective-permute-done.9.refs_5_) | copy-start | bytes 442372

commit v13 on v12

--- a/solution.py
+++ b/solution.py
@@ -5,6 +5,7 @@
 import jax.numpy as jnp
 from jax import lax
 from jax.experimental import pallas as pl
+from jax.experimental.pallas import tpu as pltpu
 from jax.sharding import PartitionSpec as P
 
 STEPS = 2
@@ -114,13 +115,19 @@
     )(values, matrix, mixing)
 
 
-def finish_kernel(groups, hslot, send, *refs):
+def finish_kernel(groups, hslot, mode, *refs):
+    send = mode == "send"
     partial_ref = refs[0]
     incoming = refs[1 : 1 + groups]
     remote_refs = refs[1 + groups : 1 + 2 * groups]
     deposition_ref, count_ref, select_ref = refs[1 + 2 * groups : 4 + 2 * groups]
-    out_ref = refs[4 + 2 * groups]
-    send_refs = refs[5 + 2 * groups :]
+    rest = refs[4 + 2 * groups :]
+    if mode == "local":
+        local_ref, mixing_ref, out_ref, values_ref = rest
+    elif send:
+        out_ref, send_refs = None, rest
+    else:
+        (out_ref,) = rest
     lb = partial_ref.shape[0]
     first = 0
     capacity = partial_ref.shape[2]
@@ -138,22 +145,28 @@
         keep = 1.0 - deposition_ref[first + level : first + level + 1, :]
         x = (partial_ref[level] + far) * keep
         x = jnp.where(living, x, 0.0)
-        out_ref[level] = x
+        if mode == "local":
+            values_ref[level] = x
+        elif not send:
+            out_ref[level] = x
         if send:
             block = lax.dot_general(
                 select_ref[...], x, NT, precision=HIGHEST, preferred_element_type=jnp.float32
             )
             for g in range(groups):
                 send_refs[g][level] = block[g * hslot : (g + 1) * hslot]
-
-
-def finish(partial, incoming, matrix, deposition, count, select, send):
+    if mode == "local":
+        local_kernel(values_ref, local_ref, mixing_ref, out_ref)
+
+
+def finish(partial, incoming, matrix, deposition, count, select, mode, mixing=None):
     levels, pulses, capacity = partial.shape
     groups = len(incoming)
     hslot = incoming[0].shape[1]
-    shapes = [jax.ShapeDtypeStruct(partial.shape, jnp.float32)]
-    if send:
-        shapes += [jax.ShapeDtypeStruct((levels, hslot, pulses), jnp.float32)] * groups
+    if mode == "send":
+        shapes = [jax.ShapeDtypeStruct((levels, hslot, pulses), jnp.float32)] * groups
+    else:
+        shapes = [jax.ShapeDtypeStruct(partial.shape, jnp.float32)]
     operands = [partial, *incoming, *([matrix] * groups), deposition, count, select]
     specs = [full_spec(x.shape) for x in operands]
     for g in range(groups):
@@ -161,16 +174,22 @@
         specs[1 + groups + g] = pl.BlockSpec(
             (levels, hslot, capacity), lambda i, block=block: (0, block, 0)
         )
+    scratch = []
+    if mode == "local":
+        operands += [matrix, mixing]
+        specs += [pl.BlockSpec((levels, capacity, capacity), lambda i: (0, 0, 0)), full_spec(mixing.shape)]
+        scratch = [pltpu.VMEM(partial.shape, jnp.float32)]
     outs = pl.pallas_call(
-        functools.partial(finish_kernel, groups, hslot, send),
+        functools.partial(finish_kernel, groups, hslot, mode),
         out_shape=shapes,
         grid=(1,),
         in_specs=specs,
         out_specs=[full_spec(x.shape) for x in shapes],
+        scratch_shapes=scratch,
         interpret=INTERPRET,
-        name="finish_send" if send else "finish",
+        name="finish_" + mode,
     )(*operands)
-    return outs[0], outs[1:]
+    return outs
 
 
 def per_device(
@@ -204,15 +223,18 @@
     )
     count = live_count.reshape(1, 1)
 
+    partial = local_part(values, matrix, vertical_mixing)
     for sweep in range(STEPS):
         incoming = [
             lax.ppermute(outgoing[g], "cells", perm=pair_list(n, partner))
             for g, partner in enumerate(partners)
         ]
-        partial = local_part(values, matrix, vertical_mixing)
-        values, outgoing = finish(
-            partial, incoming, matrix, deposition, count, select, sweep + 1 < STEPS
-        )
+        common = (partial, incoming, matrix, deposition, count, select)
+        if sweep + 1 < STEPS:
+            outgoing = finish(*common, "send")
+            partial = finish(*common, "local", vertical_mixing)[0]
+        else:
+            values = finish(*common, "final")[0]
     return values
 
 

time: 46 us -> 46.2 us (level)
  waiting for transfers between devices: 3.6 us -> 1.95 us
  Pallas kernels: 19.4 us -> 21 us
    pallas_call x2 -> x3, Pallas kernels: 8.84 us -> 13.9 us  [finish(): pl.pallas_call(functools.partial(finish_kernel, groups, hslot, mode), out...]
    pallas_call x2 -> x1, Pallas kernels: 7.04 us -> 3.5 us  [local_part(): pl.pallas_call(local_kernel, out_shape=jax.ShapeDtypeStruct(values.shape,...]
    ppermute x10, waiting for transfers between devices: 3.6 us -> 1.95 us  [per_device(): lax.ppermute(outgoing[g], 'cells', perm=pair_list(n, partner))]
  transfers between devices with their start and end apart: 10 -> 10, of which waited for: 2 -> 2; matrix products, arithmetic and copies ran while one was open for 4% -> 4% of each run, Pallas kernels for 15% -> 19%
where the time goes in v13:
time: 46.2 us; the launch traced here: 45.5 us
  Pallas kernels  21 us (45%)
  starting transfers between devices  18.6 us (40%)
  waiting for transfers between devices  1.95 us (4%)
  other arithmetic  1.59 us (3%)
  local copies, waits for them, and re-layouts  1.35 us (3%)
  between operations  0.95 us (2%)
    ppermute x10, starting transfers between devices, per_device(): lax.ppermute(outgoing[g], 'cells', perm=pair_list(n, partner))  18.6 us
    pallas_call x3, Pallas kernels, finish(): pl.pallas_call(functools.partial(finish_kernel, groups, hslot, mode), out...  13.9 us
    pallas_call x1, Pallas kernels, gather_send(): pl.pallas_call(functools.partial(select_kernel, partners, hslot), out_sha...  3.57 us
    pallas_call x1, Pallas kernels, local_part(): pl.pallas_call(local_kernel, out_shape=jax.ShapeDtypeStruct(values.shape,...  3.5 us
    ppermute x10, waiting for transfers between devices, per_device(): lax.ppermute(outgoing[g], 'cells', perm=pair_list(n, partner))  1.95 us
    add x1, other arithmetic, per_device(): sum((flux_weight[k][:, None, :] * ((row[k][None, :] == slots).astype(f32)...  1.45 us
    unnamed x24, local copies, waits for them, and re-layouts  1.3 us
  transfers between devices with their start and end apart: 10, of which 2 were waited for; matrix products, arithmetic and copies ran while one was open for 4% of the time, Pallas kernels for 19%

profile of v13, /device:TPU:25, one launch (start us, length us, event | category | flops | bytes accessed | tf_op | source)
XLA Modules:
  0.0 45.5 jit_solution(11630086702929923785)
XLA Ops:
  0.0 0.0 copy-start.11
  0.0 0.0 copy-start.10
  0.0 3.6 %gather_send.1 = (f32[9,16,256]{2,1,0:T(8,128)}, f32[9,16,256]{2,1,0:T(8,128)}, f32[9,16,256]{2,1,0:T(8,128)}, f32[9,16,256]{2,1,0:T(8,128)}, f32[9,16,256]{2,1,0:T(8,128)}, /*index=5*/f32[80,128]{1,0:T(8,128)}) custom-call(s32[16,32]{1,0:T(8,128)} %bitcast.39, f32[9,256,128]{2,1,0:T(8,128)} %values_ref.3), custom_call_target="tpu_custom_call" | custom-call | tf_op jit(solution)/shard_map/gather_send/pallas_call | solution.py:76
  3.6 0.7 %collective-permute-start = (f32[9,16,256]{2,1,0:T(8,128)}, f32[9,16,256]{2,1,0:T(8,128)S(1)}, u32[]{:S(2)}, u32[]{:S(2)}) collective-permute-start(f32[9,16,256]{2,1,0:T(8,128)} %get-tuple-element.16), channel_id=1, source_target_pairs={{0,1},{1,0},{2,3},{3,2},{4,5},{5,4},{6,7},{7,6},{8,9},{9,8},{10,11... | collective-permute-start | bytes 442376 | tf_op jit(solution)/shard_map/ppermute | solution.py:229
  4.2 1.2 %collective-permute-start.1 = (f32[9,16,256]{2,1,0:T(8,128)}, f32[9,16,256]{2,1,0:T(8,128)S(1)}, u32[]{:S(2)}, u32[]{:S(2)}) collective-permute-start(f32[9,16,256]{2,1,0:T(8,128)} %get-tuple-element.17), channel_id=1, source_target_pairs={{0,2},{1,3},{2,0},{3,1},{4,6},{5,7},{6,4},{7,5},{8,10},{9,11},{10,... | collective-permute-start | bytes 442376 | tf_op jit(solution)/shard_map/ppermute | solution.py:229
  5.5 0.1 collective-permute-start.2
  5.5 2.6 %collective-permute-start.3 = (f32[9,16,256]{2,1,0:T(8,128)}, f32[9,16,256]{2,1,0:T(8,128)S(1)}, u32[]{:S(2)}, u32[]{:S(2)}) collective-permute-start(f32[9,16,256]{2,1,0:T(8,128)} %get-tuple-element.19), channel_id=1, source_target_pairs={{1,2},{2,1},{3,4},{4,3},{5,6},{6,5},{7,8},{8,7},{9,10},{10,9},{11,... | collective-permute-start | bytes 442376 | tf_op jit(solution)/shard_map/ppermute | solution.py:229
  8.1 4.9 %collective-permute-start.4 = (f32[9,16,256]{2,1,0:T(8,128)}, f32[9,16,256]{2,1,0:T(8,128)S(1)}, u32[]{:S(2)}, u32[]{:S(2)}) collective-permute-start(f32[9,16,256]{2,1,0:T(8,128)} %get-tuple-element.20), channel_id=1, source_target_pairs={{2,4},{3,5},{4,2},{5,3},{6,8},{7,9},{8,6},{9,7},{10,12},{11,13},{1... | collective-permute-start | bytes 442376 | tf_op jit(solution)/shard_map/ppermute | solution.py:229
  13.1 0.0 copy-done.11
  13.1 0.0 copy-done.10
  14.0 1.4 %multiply_add_fusion.local_ref.refs_6_.refs_7_.refs_8_.refs_9_.refs_10_.refs_14_ = f32[9,208,128]{2,1,0:T(8,128)} fusion(f32[208,128]{1,0:T(8,128)S(1)} %get-tuple-element.43, f32[9,128]{1,0:T(8,128)S(1)} %get-tuple-element.51, f32[208,128]{1,0:T(8,128)S(1)} %get-tuple-element.44, f32[9,128]{1,0:T(8,128)S(1)} %get-tuple-element.52, ...), kind=kLoop, calls=%fused_computation | loop fusion | flops 3594240 | bytes 1847296 | tf_op jit(solution)/shard_map/add | solution.py:220
  15.5 3.5 %local_part.1.refs_0_ = f32[9,256,128]{2,1,0:T(8,128)} custom-call(f32[9,256,128]{2,1,0:T(8,128)} %values_ref.3, f32[9,208,128]{2,1,0:T(8,128)} %multiply_add_fusion.local_ref.refs_6_.refs_7_.refs_8_.refs_9_.refs_10_.refs_14_, f32[8,128]{1,0:T(8,128)} %refs_15_.1), custom_call_target="tpu_custom_call" | custom-call | tf_op jit(solution)/shard_map/local_part/pallas_call | solution.py:103
  19.0 0.0 collective-permute-done.refs_1_
  19.0 0.0 copy-start
  19.0 0.0 collective-permute-done.1.refs_2_
  19.0 0.0 copy-start.1
  19.0 0.0 collective-permute-done.2.refs_3_
  19.0 0.0 copy-start.2
  19.0 0.0 collective-permute-done.3.refs_4_
  19.0 0.0 copy-start.3
  19.0 1.0 %collective-permute-done.4.refs_5_ = f32[9,16,256]{2,1,0:T(8,128)S(1)} collective-permute-done((f32[9,16,256]{2,1,0:T(8,128)}, f32[9,16,256]{2,1,0:T(8,128)S(1)}, u32[]{:S(2)}, u32[]{:S(2)}) %collective-permute-start.4) | collective-permute-done | bytes 147488 | tf_op jit(solution)/shard_map/ppermute | solution.py:229
  20.1 0.0 copy-start.4
  20.1 0.0 copy-done
  20.1 0.0 copy-done.1
  20.1 0.0 copy-done.2
  20.1 0.0 copy-done.3
  20.1 0.6 %copy-done.4 = f32[9,16,256]{2,1,0:T(8,128)} copy-done((f32[9,16,256]{2,1,0:T(8,128)}, f32[9,16,256]{2,1,0:T(8,128)S(1)}, u32[]{:S(2)}) %copy-start.4) | copy-done | bytes 147480
  20.7 4.9 %finish_send.1 = (f32[9,16,256]{2,1,0:T(8,128)}, f32[9,16,256]{2,1,0:T(8,128)}, f32[9,16,256]{2,1,0:T(8,128)}, f32[9,16,256]{2,1,0:T(8,128)}, f32[9,16,256]{2,1,0:T(8,128)}) custom-call(f32[9,256,128]{2,1,0:T(8,128)} %local_part.1.refs_0_, f32[9,16,256]{2,1,0:T(8,128)} %copy-done, f32[9,16,256]{2,1,0:T(8,128)} %copy-done.1, f32[9,16,256]{2,1,0:T(8,128)} %copy-done.2, ...), custom_call_target="tpu_custom_call" | custom-call | tf_op jit(solution)/shard_map/finish_send/pallas_call | solution.py:182
  25.6 0.1 collective-permute-start.5
  25.7 0.0 collective-permute-start.6
  25.7 1.5 %collective-permute-start.7 = (f32[9,16,256]{2,1,0:T(8,128)}, f32[9,16,256]{2,1,0:T(8,128)S(1)}, u32[]{:S(2)}, u32[]{:S(2)}) collective-permute-start(f32[9,16,256]{2,1,0:T(8,128)} %get-tuple-element.24), channel_id=1, source_target_pairs={{0,16},{1,17},{2,18},{3,19},{4,20},{5,21},{6,22},{7,23},{8,24},{9,... | collective-permute-start | bytes 442376 | tf_op jit(solution)/shard_map/ppermute | solution.py:229
  27.2 4.2 %collective-permute-start.8 = (f32[9,16,256]{2,1,0:T(8,128)}, f32[9,16,256]{2,1,0:T(8,128)S(1)}, u32[]{:S(2)}, u32[]{:S(2)}) collective-permute-start(f32[9,16,256]{2,1,0:T(8,128)} %get-tuple-element.25), channel_id=1, source_target_pairs={{1,2},{2,1},{3,4},{4,3},{5,6},{6,5},{7,8},{8,7},{9,10},{10,9},{11,... | collective-permute-start | bytes 442376 | tf_op jit(solution)/shard_map/ppermute | solution.py:229
  31.4 3.4 %collective-permute-start.9 = (f32[9,16,256]{2,1,0:T(8,128)}, f32[9,16,256]{2,1,0:T(8,128)S(1)}, u32[]{:S(2)}, u32[]{:S(2)}) collective-permute-start(f32[9,16,256]{2,1,0:T(8,128)} %get-tuple-element.26), channel_id=1, source_target_pairs={{2,4},{3,5},{4,2},{5,3},{6,8},{7,9},{8,6},{9,7},{10,12},{11,13},{1... | collective-permute-start | bytes 442376 | tf_op jit(solution)/shard_map/ppermute | solution.py:229
  34.8 5.2 %finish_local.1.refs_0_ = f32[9,256,128]{2,1,0:T(8,128)} custom-call(f32[9,256,128]{2,1,0:T(8,128)} %local_part.1.refs_0_, f32[9,16,256]{2,1,0:T(8,128)} %copy-done, f32[9,16,256]{2,1,0:T(8,128)} %copy-done.1, f32[9,16,256]{2,1,0:T(8,128)} %copy-done.2, f32[9,16,256]{2,1,0:T(8,128)} %copy-done.3, f32[9,16,256]{2,1,0:T(8,128)} %copy-done.4, ...), custom_call_target="tpu_custom_call" | custom-call | tf_op jit(solution)/shard_map/finish_local/pallas_call | solution.py:182
  40.0 0.0 collective-permute-done.5.refs_1_
  40.0 0.0 collective-permute-done.6.refs_2_
  40.0 0.0 copy-start.6
  40.0 0.0 collective-permute-done.7.refs_3_
  40.0 0.0 copy-start.7
  40.0 0.0 collective-permute-done.8.refs_4_
  40.1 0.0 copy-start.8
  40.1 0.9 %collective-permute-done.9.refs_5_ = f32[9,16,256]{2,1,0:T(8,128)S(1)} collective-permute-done((f32[9,16,256]{2,1,0:T(8,128)}, f32[9,16,256]{2,1,0:T(8,128)S(1)}, u32[]{:S(2)}, u32[]{:S(2)}) %collective-permute-start.9) | collective-permute-done | bytes 147488 | tf_op jit(solution)/shard_map/ppermute | solution.py:229
  41.0 0.0 copy-done.5
  41.0 0.0 copy-done.6
  41.0 0.0 copy-done.7
  41.0 0.0 copy-done.8
  41.0 0.6 %copy-done.9 = f32[9,16,256]{2,1,0:T(8,128)} copy-done((f32[9,16,256]{2,1,0:T(8,128)}, f32[9,16,256]{2,1,0:T(8,128)S(1)}, u32[]{:S(2)}) %copy-start.9) | copy-done | bytes 147480
  41.6 3.8 %finish_final.1 = f32[9,256,128]{2,1,0:T(8,128)} custom-call(f32[9,256,128]{2,1,0:T(8,128)} %finish_local.1.refs_0_, f32[9,16,256]{2,1,0:T(8,128)} %copy-done.5, f32[9,16,256]{2,1,0:T(8,128)} %copy-done.6, f32[9,16,256]{2,1,0:T(8,128)} %copy-done.7, f32[9,16,256]{2,1,0:T(8,128)} %copy-done.8, f32[9,16,256]{2,1,0:T(8,128)} %copy-done.9, ...), custom_call_target="tpu_custom_call" | custom-call | tf_op jit(solution)/shard_map/finish_final/pallas_call | solution.py:182
  (13 shorter events, 0.2 us)
Async XLA Ops:
  0.0 13.1 %copy-start.11 = (s32[8,128]{1,0:T(8,128)S(1)}, s32[8,128]{1,0:T(8,128)}, u32[]{:S(2)}) copy-start(s32[8,128]{1,0:T(8,128)} %param.11) | copy-start | bytes 12292
  0.0 13.1 %copy-start.10 = (f32[8,9,128]{2,0,1:T(8,128)S(1)}, f32[8,9,128]{2,0,1:T(8,128)}, u32[]{:S(2)}) copy-start(f32[8,9,128]{2,0,1:T(8,128)} %param.8) | copy-start | bytes 110596
  3.6 15.4 %collective-permute-start = (f32[9,16,256]{2,1,0:T(8,128)}, f32[9,16,256]{2,1,0:T(8,128)S(1)}, u32[]{:S(2)}, u32[]{:S(2)}) collective-permute-start(f32[9,16,256]{2,1,0:T(8,128)} %get-tuple-element.16), channel_id=1, source_target_pairs={{0,1},{1,0},{2,3},{3,2},{4,5},{5,4},{6,7},{7,6},{8,9},{9,8},{10,11... | collective-permute-start | bytes 442376 | tf_op jit(solution)/shard_map/ppermute | solution.py:229
  4.2 14.7 %collective-permute-start.1 = (f32[9,16,256]{2,1,0:T(8,128)}, f32[9,16,256]{2,1,0:T(8,128)S(1)}, u32[]{:S(2)}, u32[]{:S(2)}) collective-permute-start(f32[9,16,256]{2,1,0:T(8,128)} %get-tuple-element.17), channel_id=1, source_target_pairs={{0,2},{1,3},{2,0},{3,1},{4,6},{5,7},{6,4},{7,5},{8,10},{9,11},{10,... | collective-permute-start | bytes 442376 | tf_op jit(solution)/shard_map/ppermute | solution.py:229
  5.5 13.5 %collective-permute-start.2 = (f32[9,16,256]{2,1,0:T(8,128)}, f32[9,16,256]{2,1,0:T(8,128)S(1)}, u32[]{:S(2)}, u32[]{:S(2)}) collective-permute-start(f32[9,16,256]{2,1,0:T(8,128)} %get-tuple-element.18), channel_id=1, source_target_pairs={{0,16},{1,17},{2,18},{3,19},{4,20},{5,21},{6,22},{7,23},{8,24},{9,... | collective-permute-start | bytes 442376 | tf_op jit(solution)/shard_map/ppermute | solution.py:229
  5.5 13.5 %collective-permute-start.3 = (f32[9,16,256]{2,1,0:T(8,128)}, f32[9,16,256]{2,1,0:T(8,128)S(1)}, u32[]{:S(2)}, u32[]{:S(2)}) collective-permute-start(f32[9,16,256]{2,1,0:T(8,128)} %get-tuple-element.19), channel_id=1, source_target_pairs={{1,2},{2,1},{3,4},{4,3},{5,6},{6,5},{7,8},{8,7},{9,10},{10,9},{11,... | collective-permute-start | bytes 442376 | tf_op jit(solution)/shard_map/ppermute | solution.py:229
  8.1 11.9 %collective-permute-start.4 = (f32[9,16,256]{2,1,0:T(8,128)}, f32[9,16,256]{2,1,0:T(8,128)S(1)}, u32[]{:S(2)}, u32[]{:S(2)}) collective-permute-start(f32[9,16,256]{2,1,0:T(8,128)} %get-tuple-element.20), channel_id=1, source_target_pairs={{2,4},{3,5},{4,2},{5,3},{6,8},{7,9},{8,6},{9,7},{10,12},{11,13},{1... | collective-permute-start | bytes 442376 | tf_op jit(solution)/shard_map/ppermute | solution.py:229
  19.0 1.1 %copy-start = (f32[9,16,256]{2,1,0:T(8,128)}, f32[9,16,256]{2,1,0:T(8,128)S(1)}, u32[]{:S(2)}) copy-start(f32[9,16,256]{2,1,0:T(8,128)S(1)} %collective-permute-done.refs_1_) | copy-start | bytes 442372
  19.0 1.1 %copy-start.1 = (f32[9,16,256]{2,1,0:T(8,128)}, f32[9,16,256]{2,1,0:T(8,128)S(1)}, u32[]{:S(2)}) copy-start(f32[9,16,256]{2,1,0:T(8,128)S(1)} %collective-permute-done.1.refs_2_) | copy-start | bytes 442372
  19.0 1.1 %copy-start.2 = (f32[9,16,256]{2,1,0:T(8,128)}, f32[9,16,256]{2,1,0:T(8,128)S(1)}, u32[]{:S(2)}) copy-start(f32[9,16,256]{2,1,0:T(8,128)S(1)} %collective-permute-done.2.refs_3_) | copy-start | bytes 442372
  19.0 1.1 %copy-start.3 = (f32[9,16,256]{2,1,0:T(8,128)}, f32[9,16,256]{2,1,0:T(8,128)S(1)}, u32[]{:S(2)}) copy-start(f32[9,16,256]{2,1,0:T(8,128)S(1)} %collective-permute-done.3.refs_4_) | copy-start | bytes 442372
  20.1 0.7 %copy-start.4 = (f32[9,16,256]{2,1,0:T(8,128)}, f32[9,16,256]{2,1,0:T(8,128)S(1)}, u32[]{:S(2)}) copy-start(f32[9,16,256]{2,1,0:T(8,128)S(1)} %collective-permute-done.4.refs_5_) | copy-start | bytes 442372
  25.6 14.4 %collective-permute-start.5 = (f32[9,16,256]{2,1,0:T(8,128)}, f32[9,16,256]{2,1,0:T(8,128)S(1)}, u32[]{:S(2)}, u32[]{:S(2)}) collective-permute-start(f32[9,16,256]{2,1,0:T(8,128)} %get-tuple-element.22), channel_id=1, source_target_pairs={{0,1},{1,0},{2,3},{3,2},{4,5},{5,4},{6,7},{7,6},{8,9},{9,8},{10,11... | collective-permute-start | bytes 442376 | tf_op jit(solution)/shard_map/ppermute | solution.py:229
  25.7 14.3 %collective-permute-start.6 = (f32[9,16,256]{2,1,0:T(8,128)}, f32[9,16,256]{2,1,0:T(8,128)S(1)}, u32[]{:S(2)}, u32[]{:S(2)}) collective-permute-start(f32[9,16,256]{2,1,0:T(8,128)} %get-tuple-element.23), channel_id=1, source_target_pairs={{0,2},{1,3},{2,0},{3,1},{4,6},{5,7},{6,4},{7,5},{8,10},{9,11},{10,... | collective-permute-start | bytes 442376 | tf_op jit(solution)/shard_map/ppermute | solution.py:229
  25.7 14.3 %collective-permute-start.7 = (f32[9,16,256]{2,1,0:T(8,128)}, f32[9,16,256]{2,1,0:T(8,128)S(1)}, u32[]{:S(2)}, u32[]{:S(2)}) collective-permute-start(f32[9,16,256]{2,1,0:T(8,128)} %get-tuple-element.24), channel_id=1, source_target_pairs={{0,16},{1,17},{2,18},{3,19},{4,20},{5,21},{6,22},{7,23},{8,24},{9,... | collective-permute-start | bytes 442376 | tf_op jit(solution)/shard_map/ppermute | solution.py:229
  27.2 12.8 %collective-permute-start.8 = (f32[9,16,256]{2,1,0:T(8,128)}, f32[9,16,256]{2,1,0:T(8,128)S(1)}, u32[]{:S(2)}, u32[]{:S(2)}) collective-permute-start(f32[9,16,256]{2,1,0:T(8,128)} %get-tuple-element.25), channel_id=1, source_target_pairs={{1,2},{2,1},{3,4},{4,3},{5,6},{6,5},{7,8},{8,7},{9,10},{10,9},{11,... | collective-permute-start | bytes 442376 | tf_op jit(solution)/shard_map/ppermute | solution.py:229
  31.4 9.6 %collective-permute-start.9 = (f32[9,16,256]{2,1,0:T(8,128)}, f32[9,16,256]{2,1,0:T(8,128)S(1)}, u32[]{:S(2)}, u32[]{:S(2)}) collective-permute-start(f32[9,16,256]{2,1,0:T(8,128)} %get-tuple-element.26), channel_id=1, source_target_pairs={{2,4},{3,5},{4,2},{5,3},{6,8},{7,9},{8,6},{9,7},{10,12},{11,13},{1... | collective-permute-start | bytes 442376 | tf_op jit(solution)/shard_map/ppermute | solution.py:229
  40.0 1.0 %copy-start.5 = (f32[9,16,256]{2,1,0:T(8,128)}, f32[9,16,256]{2,1,0:T(8,128)S(1)}, u32[]{:S(2)}) copy-start(f32[9,16,256]{2,1,0:T(8,128)S(1)} %collective-permute-done.5.refs_1_) | copy-start | bytes 442372
  40.0 1.0 %copy-start.6 = (f32[9,16,256]{2,1,0:T(8,128)}, f32[9,16,256]{2,1,0:T(8,128)S(1)}, u32[]{:S(2)}) copy-start(f32[9,16,256]{2,1,0:T(8,128)S(1)} %collective-permute-done.6.refs_2_) | copy-start | bytes 442372
  40.0 0.9 %copy-start.7 = (f32[9,16,256]{2,1,0:T(8,128)}, f32[9,16,256]{2,1,0:T(8,128)S(1)}, u32[]{:S(2)}) copy-start(f32[9,16,256]{2,1,0:T(8,128)S(1)} %collective-permute-done.7.refs_3_) | copy-start | bytes 442372
  40.1 0.9 %copy-start.8 = (f32[9,16,256]{2,1,0:T(8,128)}, f32[9,16,256]{2,1,0:T(8,128)S(1)}, u32[]{:S(2)}) copy-start(f32[9,16,256]{2,1,0:T(8,128)S(1)} %collective-permute-done.8.refs_4_) | copy-start | bytes 442372
  41.0 0.7 %copy-start.9 = (f32[9,16,256]{2,1,0:T(8,128)}, f32[9,16,256]{2,1,0:T(8,128)S(1)}, u32[]{:S(2)}) copy-start(f32[9,16,256]{2,1,0:T(8,128)S(1)} %collective-permute-done.9.refs_5_) | copy-start | bytes 442372

commit v14 on v12

--- a/solution.py
+++ b/solution.py
@@ -44,6 +44,18 @@
 
 def full_spec(shape):
     return pl.BlockSpec(shape, lambda i: (0,) * len(shape))
+
+
+def select_rows(select, values):
+    picker = select.astype(jnp.bfloat16)
+    high = values.astype(jnp.bfloat16)
+    rest = values - high.astype(jnp.float32)
+    middle = rest.astype(jnp.bfloat16)
+    low = (rest - middle.astype(jnp.float32)).astype(jnp.bfloat16)
+    return sum(
+        lax.dot_general(picker, part, NT, preferred_element_type=jnp.float32)
+        for part in (high, middle, low)
+    )
 
 
 def select_kernel(partners, hslot, slots_ref, values_ref, *refs):
@@ -60,9 +72,7 @@
         select_ref[g * hslot : (g + 1) * hslot, :] = (lanes == column).astype(jnp.float32)
     select = select_ref[...]
     for level in range(values_ref.shape[0]):
-        block = lax.dot_general(
-            select, values_ref[level], NT, precision=HIGHEST, preferred_element_type=jnp.float32
-        )
+        block = select_rows(select, values_ref[level])
         for g in range(groups):
             out_refs[g][level] = block[g * hslot : (g + 1) * hslot]
 
@@ -140,9 +150,7 @@
         x = jnp.where(living, x, 0.0)
         out_ref[level] = x
         if send:
-            block = lax.dot_general(
-                select_ref[...], x, NT, precision=HIGHEST, preferred_element_type=jnp.float32
-            )
+            block = select_rows(select_ref[...], x)
             for g in range(groups):
                 send_refs[g][level] = block[g * hslot : (g + 1) * hslot]
 

time: 46 us -> 47.2 us (1.026)
  Pallas kernels: 19.4 us -> 20.6 us
    pallas_call x2, Pallas kernels: 8.84 us -> 10.6 us  [finish(): pl.pallas_call(functools.partial(finish_kernel, groups, hslot, send), out...]
    pallas_call x1, Pallas kernels: 3.56 us -> 2.99 us  [gather_send(): pl.pallas_call(functools.partial(select_kernel, partners, hslot), out_sha...]
where the time goes in v14:
time: 47.2 us; the launch traced here: 46.8 us
  Pallas kernels  20.6 us (44%)
  starting transfers between devices  18.7 us (40%)
  waiting for transfers between devices  3.59 us (8%)
  other arithmetic  1.61 us (3%)
  local copies, waits for them, and re-layouts  1.36 us (3%)
  between operations  0.95 us (2%)
    ppermute x10, starting transfers between devices, per_device(): lax.ppermute(outgoing[g], 'cells', perm=pair_list(n, partner))  18.7 us
    pallas_call x2, Pallas kernels, finish(): pl.pallas_call(functools.partial(finish_kernel, groups, hslot, send), out...  10.6 us
    pallas_call x2, Pallas kernels, local_part(): pl.pallas_call(local_kernel, out_shape=jax.ShapeDtypeStruct(values.shape,...  7.04 us
    ppermute x10, waiting for transfers between devices, per_device(): lax.ppermute(outgoing[g], 'cells', perm=pair_list(n, partner))  3.59 us
    pallas_call x1, Pallas kernels, gather_send(): pl.pallas_call(functools.partial(select_kernel, partners, hslot), out_sha...  2.99 us
    add x1, other arithmetic, per_device(): sum((flux_weight[k][:, None, :] * ((row[k][None, :] == slots).astype(f32)...  1.47 us
    unnamed x24, local copies, waits for them, and re-layouts  1.3 us
  transfers between devices with their start and end apart: 10, of which 2 were waited for; matrix products, arithmetic and copies ran while one was open for 4% of the time, Pallas kernels for 15%

profile of v14, /device:TPU:25, one launch (start us, length us, event | category | flops | bytes accessed | tf_op | source)
XLA Modules:
  0.0 46.8 jit_solution(10977885545102462204)
XLA Ops:
  0.0 0.0 copy-start.11
  0.0 0.0 copy-start.10
  0.0 3.0 %gather_send.1 = (f32[9,16,256]{2,1,0:T(8,128)}, f32[9,16,256]{2,1,0:T(8,128)}, f32[9,16,256]{2,1,0:T(8,128)}, f32[9,16,256]{2,1,0:T(8,128)}, f32[9,16,256]{2,1,0:T(8,128)}, /*index=5*/f32[80,128]{1,0:T(8,128)}) custom-call(s32[16,32]{1,0:T(8,128)} %bitcast.38, f32[9,256,128]{2,1,0:T(8,128)} %values_ref.3), custom_call_target="tpu_custom_call" | custom-call | tf_op jit(solution)/shard_map/gather_send/pallas_call | solution.py:85
  3.0 0.7 %collective-permute-start = (f32[9,16,256]{2,1,0:T(8,128)}, f32[9,16,256]{2,1,0:T(8,128)S(1)}, u32[]{:S(2)}, u32[]{:S(2)}) collective-permute-start(f32[9,16,256]{2,1,0:T(8,128)} %get-tuple-element.17), channel_id=1, source_target_pairs={{0,1},{1,0},{2,3},{3,2},{4,5},{5,4},{6,7},{7,6},{8,9},{9,8},{10,11... | collective-permute-start | bytes 442376 | tf_op jit(solution)/shard_map/ppermute | solution.py:217
  3.7 1.2 %collective-permute-start.1 = (f32[9,16,256]{2,1,0:T(8,128)}, f32[9,16,256]{2,1,0:T(8,128)S(1)}, u32[]{:S(2)}, u32[]{:S(2)}) collective-permute-start(f32[9,16,256]{2,1,0:T(8,128)} %get-tuple-element.18), channel_id=1, source_target_pairs={{0,2},{1,3},{2,0},{3,1},{4,6},{5,7},{6,4},{7,5},{8,10},{9,11},{10,... | collective-permute-start | bytes 442376 | tf_op jit(solution)/shard_map/ppermute | solution.py:217
  4.9 0.1 collective-permute-start.2
  4.9 2.7 %collective-permute-start.3 = (f32[9,16,256]{2,1,0:T(8,128)}, f32[9,16,256]{2,1,0:T(8,128)S(1)}, u32[]{:S(2)}, u32[]{:S(2)}) collective-permute-start(f32[9,16,256]{2,1,0:T(8,128)} %get-tuple-element.20), channel_id=1, source_target_pairs={{1,2},{2,1},{3,4},{4,3},{5,6},{6,5},{7,8},{8,7},{9,10},{10,9},{11,... | collective-permute-start | bytes 442376 | tf_op jit(solution)/shard_map/ppermute | solution.py:217
  7.6 4.9 %collective-permute-start.4 = (f32[9,16,256]{2,1,0:T(8,128)}, f32[9,16,256]{2,1,0:T(8,128)S(1)}, u32[]{:S(2)}, u32[]{:S(2)}) collective-permute-start(f32[9,16,256]{2,1,0:T(8,128)} %get-tuple-element.21), channel_id=1, source_target_pairs={{2,4},{3,5},{4,2},{5,3},{6,8},{7,9},{8,6},{9,7},{10,12},{11,13},{1... | collective-permute-start | bytes 442376 | tf_op jit(solution)/shard_map/ppermute | solution.py:217
  13.2 0.0 copy-done.11
  13.3 0.0 copy-done.10
  13.5 1.5 %multiply_add_fusion.local_ref.refs_6_.refs_7_.refs_8_.refs_9_.refs_10_ = f32[9,208,128]{2,1,0:T(8,128)} fusion(f32[208,128]{1,0:T(8,128)S(1)} %get-tuple-element.45, f32[9,128]{1,0:T(8,128)S(1)} %get-tuple-element.53, f32[208,128]{1,0:T(8,128)S(1)} %get-tuple-element.46, f32[9,128]{1,0:T(8,128)S(1)} %get-tuple-element.54, ...), kind=kLoop, calls=%fused_computation | loop fusion | flops 3594240 | bytes 1847296 | tf_op jit(solution)/shard_map/add | solution.py:209
  15.0 3.5 %local_part.2.refs_0_ = f32[9,256,128]{2,1,0:T(8,128)} custom-call(f32[9,256,128]{2,1,0:T(8,128)} %values_ref.3, f32[9,208,128]{2,1,0:T(8,128)} %multiply_add_fusion.local_ref.refs_6_.refs_7_.refs_8_.refs_9_.refs_10_, f32[8,128]{1,0:T(8,128)} %mixing_ref.3), custom_call_target="tpu_custom_call" | custom-call | tf_op jit(solution)/shard_map/local_part/pallas_call | solution.py:112
  18.5 0.0 collective-permute-done.refs_1_
  18.5 0.0 copy-start
  18.5 0.0 collective-permute-done.1.refs_2_
  18.5 0.0 copy-start.1
  18.5 0.0 collective-permute-done.2.refs_3_
  18.5 0.0 copy-start.2
  18.5 0.0 collective-permute-done.3.refs_4_
  18.5 0.0 copy-start.3
  18.5 1.0 %collective-permute-done.4.refs_5_ = f32[9,16,256]{2,1,0:T(8,128)S(1)} collective-permute-done((f32[9,16,256]{2,1,0:T(8,128)}, f32[9,16,256]{2,1,0:T(8,128)S(1)}, u32[]{:S(2)}, u32[]{:S(2)}) %collective-permute-start.4) | collective-permute-done | bytes 147488 | tf_op jit(solution)/shard_map/ppermute | solution.py:217
  19.6 0.0 copy-start.4
  19.6 0.0 copy-done
  19.6 0.0 copy-done.1
  19.6 0.0 copy-done.2
  19.6 0.0 copy-done.3
  19.6 0.6 %copy-done.4 = f32[9,16,256]{2,1,0:T(8,128)} copy-done((f32[9,16,256]{2,1,0:T(8,128)}, f32[9,16,256]{2,1,0:T(8,128)S(1)}, u32[]{:S(2)}) %copy-start.4) | copy-done | bytes 147480
  20.2 6.7 %finish_send.1 = (f32[9,256,128]{2,1,0:T(8,128)}, f32[9,16,256]{2,1,0:T(8,128)}, f32[9,16,256]{2,1,0:T(8,128)}, f32[9,16,256]{2,1,0:T(8,128)}, f32[9,16,256]{2,1,0:T(8,128)}, /*index=5*/f32[9,16,256]{2,1,0:T(8,128)}) custom-call(f32[9,256,128]{2,1,0:T(8,128)} %local_part.2.refs_0_, f32[9,16,256]{2,1,0:T(8,128)} %copy-done, f32[9,16,256]{2,1,0:T(8,128)} %copy-done.1, ...), custom_call_target="tpu_custom_call" | custom-call | tf_op jit(solution)/shard_map/finish_send/pallas_call | solution.py:172
  26.9 0.0 collective-permute-start.5
  27.0 0.1 collective-permute-start.6
  27.0 1.5 %collective-permute-start.7 = (f32[9,16,256]{2,1,0:T(8,128)}, f32[9,16,256]{2,1,0:T(8,128)S(1)}, u32[]{:S(2)}, u32[]{:S(2)}) collective-permute-start(f32[9,16,256]{2,1,0:T(8,128)} %get-tuple-element.26), channel_id=1, source_target_pairs={{0,16},{1,17},{2,18},{3,19},{4,20},{5,21},{6,22},{7,23},{8,24},{9,... | collective-permute-start | bytes 442376 | tf_op jit(solution)/shard_map/ppermute | solution.py:217
  28.6 4.2 %collective-permute-start.8 = (f32[9,16,256]{2,1,0:T(8,128)}, f32[9,16,256]{2,1,0:T(8,128)S(1)}, u32[]{:S(2)}, u32[]{:S(2)}) collective-permute-start(f32[9,16,256]{2,1,0:T(8,128)} %get-tuple-element.27), channel_id=1, source_target_pairs={{1,2},{2,1},{3,4},{4,3},{5,6},{6,5},{7,8},{8,7},{9,10},{10,9},{11,... | collective-permute-start | bytes 442376 | tf_op jit(solution)/shard_map/ppermute | solution.py:217
  32.7 3.4 %collective-permute-start.9 = (f32[9,16,256]{2,1,0:T(8,128)}, f32[9,16,256]{2,1,0:T(8,128)S(1)}, u32[]{:S(2)}, u32[]{:S(2)}) collective-permute-start(f32[9,16,256]{2,1,0:T(8,128)} %get-tuple-element.28), channel_id=1, source_target_pairs={{2,4},{3,5},{4,2},{5,3},{6,8},{7,9},{8,6},{9,7},{10,12},{11,13},{1... | collective-permute-start | bytes 442376 | tf_op jit(solution)/shard_map/ppermute | solution.py:217
  36.2 3.5 %local_part.3.refs_0_ = f32[9,256,128]{2,1,0:T(8,128)} custom-call(f32[9,256,128]{2,1,0:T(8,128)} %get-tuple-element.23.values_ref, f32[9,208,128]{2,1,0:T(8,128)} %multiply_add_fusion.local_ref.refs_6_.refs_7_.refs_8_.refs_9_.refs_10_, f32[8,128]{1,0:T(8,128)} %mixing_ref.3), custom_call_target="tpu_custom_call" | custom-call | tf_op jit(solution)/shard_map/local_part/pallas_call | solution.py:112
  39.7 0.0 collective-permute-done.5.refs_1_
  39.7 0.0 collective-permute-done.6.refs_2_
  39.7 0.0 copy-start.6
  39.7 0.0 collective-permute-done.7.refs_3_
  39.7 0.0 copy-start.7
  39.8 0.0 collective-permute-done.8.refs_4_
  39.8 0.0 copy-start.8
  39.8 2.6 %collective-permute-done.9.refs_5_ = f32[9,16,256]{2,1,0:T(8,128)S(1)} collective-permute-done((f32[9,16,256]{2,1,0:T(8,128)}, f32[9,16,256]{2,1,0:T(8,128)S(1)}, u32[]{:S(2)}, u32[]{:S(2)}) %collective-permute-start.9) | collective-permute-done | bytes 147488 | tf_op jit(solution)/shard_map/ppermute | solution.py:217
  42.3 0.0 copy-done.5
  42.3 0.0 copy-done.6
  42.3 0.0 copy-done.7
  42.4 0.0 copy-done.8
  42.4 0.6 %copy-done.9 = f32[9,16,256]{2,1,0:T(8,128)} copy-done((f32[9,16,256]{2,1,0:T(8,128)}, f32[9,16,256]{2,1,0:T(8,128)S(1)}, u32[]{:S(2)}) %copy-start.9) | copy-done | bytes 147480
  43.0 3.8 %finish.1 = f32[9,256,128]{2,1,0:T(8,128)} custom-call(f32[9,256,128]{2,1,0:T(8,128)} %local_part.3.refs_0_, f32[9,16,256]{2,1,0:T(8,128)} %copy-done.5, f32[9,16,256]{2,1,0:T(8,128)} %copy-done.6, f32[9,16,256]{2,1,0:T(8,128)} %copy-done.7, f32[9,16,256]{2,1,0:T(8,128)} %copy-done.8, f32[9,16,256]{2,1,0:T(8,128)} %copy-done.9, ...), custom_call_target="tpu_custom_call" | custom-call | tf_op jit(solution)/shard_map/finish/pallas_call | solution.py:172
  (13 shorter events, 0.2 us)
Async XLA Ops:
  0.0 13.2 %copy-start.11 = (s32[8,128]{1,0:T(8,128)S(1)}, s32[8,128]{1,0:T(8,128)}, u32[]{:S(2)}) copy-start(s32[8,128]{1,0:T(8,128)} %param.11) | copy-start | bytes 12292
  0.0 13.3 %copy-start.10 = (f32[8,9,128]{2,0,1:T(8,128)S(1)}, f32[8,9,128]{2,0,1:T(8,128)}, u32[]{:S(2)}) copy-start(f32[8,9,128]{2,0,1:T(8,128)} %param.8) | copy-start | bytes 110596
  3.0 15.5 %collective-permute-start = (f32[9,16,256]{2,1,0:T(8,128)}, f32[9,16,256]{2,1,0:T(8,128)S(1)}, u32[]{:S(2)}, u32[]{:S(2)}) collective-permute-start(f32[9,16,256]{2,1,0:T(8,128)} %get-tuple-element.17), channel_id=1, source_target_pairs={{0,1},{1,0},{2,3},{3,2},{4,5},{5,4},{6,7},{7,6},{8,9},{9,8},{10,11... | collective-permute-start | bytes 442376 | tf_op jit(solution)/shard_map/ppermute | solution.py:217
  3.7 14.8 %collective-permute-start.1 = (f32[9,16,256]{2,1,0:T(8,128)}, f32[9,16,256]{2,1,0:T(8,128)S(1)}, u32[]{:S(2)}, u32[]{:S(2)}) collective-permute-start(f32[9,16,256]{2,1,0:T(8,128)} %get-tuple-element.18), channel_id=1, source_target_pairs={{0,2},{1,3},{2,0},{3,1},{4,6},{5,7},{6,4},{7,5},{8,10},{9,11},{10,... | collective-permute-start | bytes 442376 | tf_op jit(solution)/shard_map/ppermute | solution.py:217
  4.9 13.6 %collective-permute-start.2 = (f32[9,16,256]{2,1,0:T(8,128)}, f32[9,16,256]{2,1,0:T(8,128)S(1)}, u32[]{:S(2)}, u32[]{:S(2)}) collective-permute-start(f32[9,16,256]{2,1,0:T(8,128)} %get-tuple-element.19), channel_id=1, source_target_pairs={{0,16},{1,17},{2,18},{3,19},{4,20},{5,21},{6,22},{7,23},{8,24},{9,... | collective-permute-start | bytes 442376 | tf_op jit(solution)/shard_map/ppermute | solution.py:217
  4.9 13.6 %collective-permute-start.3 = (f32[9,16,256]{2,1,0:T(8,128)}, f32[9,16,256]{2,1,0:T(8,128)S(1)}, u32[]{:S(2)}, u32[]{:S(2)}) collective-permute-start(f32[9,16,256]{2,1,0:T(8,128)} %get-tuple-element.20), channel_id=1, source_target_pairs={{1,2},{2,1},{3,4},{4,3},{5,6},{6,5},{7,8},{8,7},{9,10},{10,9},{11,... | collective-permute-start | bytes 442376 | tf_op jit(solution)/shard_map/ppermute | solution.py:217
  7.6 11.9 %collective-permute-start.4 = (f32[9,16,256]{2,1,0:T(8,128)}, f32[9,16,256]{2,1,0:T(8,128)S(1)}, u32[]{:S(2)}, u32[]{:S(2)}) collective-permute-start(f32[9,16,256]{2,1,0:T(8,128)} %get-tuple-element.21), channel_id=1, source_target_pairs={{2,4},{3,5},{4,2},{5,3},{6,8},{7,9},{8,6},{9,7},{10,12},{11,13},{1... | collective-permute-start | bytes 442376 | tf_op jit(solution)/shard_map/ppermute | solution.py:217
  18.5 1.1 %copy-start = (f32[9,16,256]{2,1,0:T(8,128)}, f32[9,16,256]{2,1,0:T(8,128)S(1)}, u32[]{:S(2)}) copy-start(f32[9,16,256]{2,1,0:T(8,128)S(1)} %collective-permute-done.refs_1_) | copy-start | bytes 442372
  18.5 1.1 %copy-start.1 = (f32[9,16,256]{2,1,0:T(8,128)}, f32[9,16,256]{2,1,0:T(8,128)S(1)}, u32[]{:S(2)}) copy-start(f32[9,16,256]{2,1,0:T(8,128)S(1)} %collective-permute-done.1.refs_2_) | copy-start | bytes 442372
  18.5 1.0 %copy-start.2 = (f32[9,16,256]{2,1,0:T(8,128)}, f32[9,16,256]{2,1,0:T(8,128)S(1)}, u32[]{:S(2)}) copy-start(f32[9,16,256]{2,1,0:T(8,128)S(1)} %collective-permute-done.2.refs_3_) | copy-start | bytes 442372
  18.5 1.0 %copy-start.3 = (f32[9,16,256]{2,1,0:T(8,128)}, f32[9,16,256]{2,1,0:T(8,128)S(1)}, u32[]{:S(2)}) copy-start(f32[9,16,256]{2,1,0:T(8,128)S(1)} %collective-permute-done.3.refs_4_) | copy-start | bytes 442372
  19.6 0.7 %copy-start.4 = (f32[9,16,256]{2,1,0:T(8,128)}, f32[9,16,256]{2,1,0:T(8,128)S(1)}, u32[]{:S(2)}) copy-start(f32[9,16,256]{2,1,0:T(8,128)S(1)} %collective-permute-done.4.refs_5_) | copy-start | bytes 442372
  26.9 12.8 %collective-permute-start.5 = (f32[9,16,256]{2,1,0:T(8,128)}, f32[9,16,256]{2,1,0:T(8,128)S(1)}, u32[]{:S(2)}, u32[]{:S(2)}) collective-permute-start(f32[9,16,256]{2,1,0:T(8,128)} %get-tuple-element.24), channel_id=1, source_target_pairs={{0,1},{1,0},{2,3},{3,2},{4,5},{5,4},{6,7},{7,6},{8,9},{9,8},{10,11... | collective-permute-start | bytes 442376 | tf_op jit(solution)/shard_map/ppermute | solution.py:217
  27.0 12.8 %collective-permute-start.6 = (f32[9,16,256]{2,1,0:T(8,128)}, f32[9,16,256]{2,1,0:T(8,128)S(1)}, u32[]{:S(2)}, u32[]{:S(2)}) collective-permute-start(f32[9,16,256]{2,1,0:T(8,128)} %get-tuple-element.25), channel_id=1, source_target_pairs={{0,2},{1,3},{2,0},{3,1},{4,6},{5,7},{6,4},{7,5},{8,10},{9,11},{10,... | collective-permute-start | bytes 442376 | tf_op jit(solution)/shard_map/ppermute | solution.py:217
  27.0 12.7 %collective-permute-start.7 = (f32[9,16,256]{2,1,0:T(8,128)}, f32[9,16,256]{2,1,0:T(8,128)S(1)}, u32[]{:S(2)}, u32[]{:S(2)}) collective-permute-start(f32[9,16,256]{2,1,0:T(8,128)} %get-tuple-element.26), channel_id=1, source_target_pairs={{0,16},{1,17},{2,18},{3,19},{4,20},{5,21},{6,22},{7,23},{8,24},{9,... | collective-permute-start | bytes 442376 | tf_op jit(solution)/shard_map/ppermute | solution.py:217
  28.6 11.2 %collective-permute-start.8 = (f32[9,16,256]{2,1,0:T(8,128)}, f32[9,16,256]{2,1,0:T(8,128)S(1)}, u32[]{:S(2)}, u32[]{:S(2)}) collective-permute-start(f32[9,16,256]{2,1,0:T(8,128)} %get-tuple-element.27), channel_id=1, source_target_pairs={{1,2},{2,1},{3,4},{4,3},{5,6},{6,5},{7,8},{8,7},{9,10},{10,9},{11,... | collective-permute-start | bytes 442376 | tf_op jit(solution)/shard_map/ppermute | solution.py:217
  32.7 9.6 %collective-permute-start.9 = (f32[9,16,256]{2,1,0:T(8,128)}, f32[9,16,256]{2,1,0:T(8,128)S(1)}, u32[]{:S(2)}, u32[]{:S(2)}) collective-permute-start(f32[9,16,256]{2,1,0:T(8,128)} %get-tuple-element.28), channel_id=1, source_target_pairs={{2,4},{3,5},{4,2},{5,3},{6,8},{7,9},{8,6},{9,7},{10,12},{11,13},{1... | collective-permute-start | bytes 442376 | tf_op jit(solution)/shard_map/ppermute | solution.py:217
  39.7 2.6 %copy-start.5 = (f32[9,16,256]{2,1,0:T(8,128)}, f32[9,16,256]{2,1,0:T(8,128)S(1)}, u32[]{:S(2)}) copy-start(f32[9,16,256]{2,1,0:T(8,128)S(1)} %collective-permute-done.5.refs_1_) | copy-start | bytes 442372
  39.7 2.6 %copy-start.6 = (f32[9,16,256]{2,1,0:T(8,128)}, f32[9,16,256]{2,1,0:T(8,128)S(1)}, u32[]{:S(2)}) copy-start(f32[9,16,256]{2,1,0:T(8,128)S(1)} %collective-permute-done.6.refs_2_) | copy-start | bytes 442372
  39.7 2.6 %copy-start.7 = (f32[9,16,256]{2,1,0:T(8,128)}, f32[9,16,256]{2,1,0:T(8,128)S(1)}, u32[]{:S(2)}) copy-start(f32[9,16,256]{2,1,0:T(8,128)S(1)} %collective-permute-done.7.refs_3_) | copy-start | bytes 442372
  39.8 2.6 %copy-start.8 = (f32[9,16,256]{2,1,0:T(8,128)}, f32[9,16,256]{2,1,0:T(8,128)S(1)}, u32[]{:S(2)}) copy-start(f32[9,16,256]{2,1,0:T(8,128)S(1)} %collective-permute-done.8.refs_4_) | copy-start | bytes 442372
  42.3 0.6 %copy-start.9 = (f32[9,16,256]{2,1,0:T(8,128)}, f32[9,16,256]{2,1,0:T(8,128)S(1)}, u32[]{:S(2)}) copy-start(f32[9,16,256]{2,1,0:T(8,128)S(1)} %collective-permute-done.9.refs_5_) | copy-start | bytes 442372

commit v15 on v12

--- a/solution.py
+++ b/solution.py
@@ -117,24 +117,18 @@
 def finish_kernel(groups, hslot, send, *refs):
     partial_ref = refs[0]
     incoming = refs[1 : 1 + groups]
-    remote_refs = refs[1 + groups : 1 + 2 * groups]
-    deposition_ref, count_ref, select_ref = refs[1 + 2 * groups : 4 + 2 * groups]
-    out_ref = refs[4 + 2 * groups]
-    send_refs = refs[5 + 2 * groups :]
+    remote_ref, deposition_ref, count_ref, select_ref = refs[1 + groups : 5 + groups]
+    out_ref = refs[5 + groups]
+    send_refs = refs[6 + groups :]
     lb = partial_ref.shape[0]
     first = 0
     capacity = partial_ref.shape[2]
     living = lax.broadcasted_iota(jnp.int32, (1, capacity), 1) < count_ref[...]
     for level in range(lb):
         received = jnp.concatenate([incoming[g][level] for g in range(groups)], axis=0)
-        weights = jnp.concatenate([remote_refs[g][level] for g in range(groups)], axis=0)
-        far = lax.dot_general(
-            received,
-            weights,
-            TN,
-            precision=HIGHEST,
-            preferred_element_type=jnp.float32,
-        )
+        far = jnp.dot(
+            remote_ref[level], received, precision=HIGHEST, preferred_element_type=jnp.float32
+        ).T
         keep = 1.0 - deposition_ref[first + level : first + level + 1, :]
         x = (partial_ref[level] + far) * keep
         x = jnp.where(living, x, 0.0)
@@ -154,13 +148,8 @@
     shapes = [jax.ShapeDtypeStruct(partial.shape, jnp.float32)]
     if send:
         shapes += [jax.ShapeDtypeStruct((levels, hslot, pulses), jnp.float32)] * groups
-    operands = [partial, *incoming, *([matrix] * groups), deposition, count, select]
+    operands = [partial, *incoming, matrix, deposition, count, select]
     specs = [full_spec(x.shape) for x in operands]
-    for g in range(groups):
-        block = capacity // hslot + g
-        specs[1 + groups + g] = pl.BlockSpec(
-            (levels, hslot, capacity), lambda i, block=block: (0, block, 0)
-        )
     outs = pl.pallas_call(
         functools.partial(finish_kernel, groups, hslot, send),
         out_shape=shapes,
@@ -202,6 +191,11 @@
         flux_weight[k][:, None, :] * ((row[k][None, :] == slots).astype(f32) - diagonal)[None]
         for k in range(nbr)
     )
+    received_slots = jnp.arange(groups * hslot, dtype=jnp.int32)[None, :]
+    remote_t = sum(
+        flux_weight[k][:, :, None] * (row[k][:, None] - capacity == received_slots).astype(f32)[None]
+        for k in range(nbr)
+    )
     count = live_count.reshape(1, 1)
 
     for sweep in range(STEPS):
@@ -211,7 +205,7 @@
         ]
         partial = local_part(values, matrix, vertical_mixing)
         values, outgoing = finish(
-            partial, incoming, matrix, deposition, count, select, sweep + 1 < STEPS
+            partial, incoming, remote_t, deposition, count, select, sweep + 1 < STEPS
         )
     return values
 

time: 46 us -> 49.1 us (1.067)
  other arithmetic: 1.61 us -> 4.45 us
  waiting for transfers between devices: 3.6 us -> 2.44 us
  starting transfers between devices: 18.7 us -> 19.5 us
    add x0 -> x1, other arithmetic: none -> 2.44 us  [per_device(): sum((flux_weight[k][:, :, None] * (row[k][:, None] - capacity == received...]
    ppermute x10, waiting for transfers between devices: 3.6 us -> 2.44 us  [per_device(): lax.ppermute(outgoing[g], 'cells', perm=pair_list(n, partner))]
    ppermute x10, starting transfers between devices: 18.7 us -> 19.5 us  [per_device(): lax.ppermute(outgoing[g], 'cells', perm=pair_list(n, partner))]
  transfers between devices with their start and end apart: 10 -> 10, of which waited for: 2 -> 1; matrix products, arithmetic and copies ran while one was open for 4% -> 9% of each run, Pallas kernels for 15% -> 15%
where the time goes in v15:
time: 49.1 us; the launch traced here: 48.7 us
  Pallas kernels  19.8 us (40%)
  starting transfers between devices  19.5 us (40%)
  other arithmetic  4.45 us (9%)
  waiting for transfers between devices  2.44 us (5%)
  local copies, waits for them, and re-layouts  1.51 us (3%)
  between operations  0.99 us (2%)
    ppermute x10, starting transfers between devices, per_device(): lax.ppermute(outgoing[g], 'cells', perm=pair_list(n, partner))  19.5 us
    pallas_call x2, Pallas kernels, finish(): pl.pallas_call(functools.partial(finish_kernel, groups, hslot, send), out...  9.17 us
    pallas_call x2, Pallas kernels, local_part(): pl.pallas_call(local_kernel, out_shape=jax.ShapeDtypeStruct(values.shape,...  7.09 us
    pallas_call x1, Pallas kernels, gather_send(): pl.pallas_call(functools.partial(select_kernel, partners, hslot), out_sha...  3.55 us
    add x1, other arithmetic, per_device(): sum((flux_weight[k][:, :, None] * (row[k][:, None] - capacity == received...  2.44 us
    ppermute x10, waiting for transfers between devices, per_device(): lax.ppermute(outgoing[g], 'cells', perm=pair_list(n, partner))  2.44 us
    unnamed x24, local copies, waits for them, and re-layouts  1.46 us
    add x1, other arithmetic, per_device(): sum((flux_weight[k][:, None, :] * ((row[k][None, :] == slots).astype(f32)...  1.46 us
  transfers between devices with their start and end apart: 10, of which 1 were waited for; matrix products, arithmetic and copies ran while one was open for 9% of the time, Pallas kernels for 15%

profile of v15, /device:TPU:25, one launch (start us, length us, event | category | flops | bytes accessed | tf_op | source)
XLA Modules:
  0.0 48.7 jit_solution(6495235486544769928)
XLA Ops:
  0.0 3.6 %gather_send.1 = (f32[9,16,256]{2,1,0:T(8,128)}, f32[9,16,256]{2,1,0:T(8,128)}, f32[9,16,256]{2,1,0:T(8,128)}, f32[9,16,256]{2,1,0:T(8,128)}, f32[9,16,256]{2,1,0:T(8,128)}, /*index=5*/f32[80,128]{1,0:T(8,128)}) custom-call(s32[16,32]{1,0:T(8,128)} %bitcast.54, f32[9,256,128]{2,1,0:T(8,128)} %values_ref.3), custom_call_target="tpu_custom_call" | custom-call | tf_op jit(solution)/shard_map/gather_send/pallas_call | solution.py:75
  3.6 0.7 %collective-permute-start = (f32[9,16,256]{2,1,0:T(8,128)}, f32[9,16,256]{2,1,0:T(8,128)S(1)}, u32[]{:S(2)}, u32[]{:S(2)}) collective-permute-start(f32[9,16,256]{2,1,0:T(8,128)} %get-tuple-element.17), channel_id=1, source_target_pairs={{0,1},{1,0},{2,3},{3,2},{4,5},{5,4},{6,7},{7,6},{8,9},{9,8},{10,11... | collective-permute-start | bytes 442376 | tf_op jit(solution)/shard_map/ppermute | solution.py:203
  4.2 1.2 %collective-permute-start.1 = (f32[9,16,256]{2,1,0:T(8,128)}, f32[9,16,256]{2,1,0:T(8,128)S(1)}, u32[]{:S(2)}, u32[]{:S(2)}) collective-permute-start(f32[9,16,256]{2,1,0:T(8,128)} %get-tuple-element.18), channel_id=1, source_target_pairs={{0,2},{1,3},{2,0},{3,1},{4,6},{5,7},{6,4},{7,5},{8,10},{9,11},{10,... | collective-permute-start | bytes 442376 | tf_op jit(solution)/shard_map/ppermute | solution.py:203
  5.4 0.1 collective-permute-start.2
  5.5 2.6 %collective-permute-start.3 = (f32[9,16,256]{2,1,0:T(8,128)}, f32[9,16,256]{2,1,0:T(8,128)S(1)}, u32[]{:S(2)}, u32[]{:S(2)}) collective-permute-start(f32[9,16,256]{2,1,0:T(8,128)} %get-tuple-element.20), channel_id=1, source_target_pairs={{1,2},{2,1},{3,4},{4,3},{5,6},{6,5},{7,8},{8,7},{9,10},{10,9},{11,... | collective-permute-start | bytes 442376 | tf_op jit(solution)/shard_map/ppermute | solution.py:203
  8.1 4.9 %collective-permute-start.4 = (f32[9,16,256]{2,1,0:T(8,128)}, f32[9,16,256]{2,1,0:T(8,128)S(1)}, u32[]{:S(2)}, u32[]{:S(2)}) collective-permute-start(f32[9,16,256]{2,1,0:T(8,128)} %get-tuple-element.21), channel_id=1, source_target_pairs={{2,4},{3,5},{4,2},{5,3},{6,8},{7,9},{8,6},{9,7},{10,12},{11,13},{1... | collective-permute-start | bytes 442376 | tf_op jit(solution)/shard_map/ppermute | solution.py:203
  13.1 0.0 copy-done.11
  13.8 0.0 copy-done.10
  13.9 0.1 fusion
  14.0 0.1 fusion.6
  14.1 0.1 fusion.4
  14.2 0.1 fusion.2
  14.5 1.5 %multiply_add_fusion.local_ref = f32[9,208,128]{2,1,0:T(8,128)} fusion(f32[208,128]{1,0:T(8,128)S(1)} %get-tuple-element.53, f32[9,128]{1,0:T(8,128)S(1)} %get-tuple-element.61, f32[208,128]{1,0:T(8,128)S(1)} %get-tuple-element.54, f32[9,128]{1,0:T(8,128)S(1)} %get-tuple-element.62, f32[208,128]{1,0:T(8,128)S(1)} %get-tuple-element.55, ...), kind=kLoop, calls=%fused_computation | loop fusion | flops 3594240 | bytes 1847296 | tf_op jit(solution)/shard_map/add | solution.py:190
  15.9 3.5 %local_part.2.refs_0_ = f32[9,256,128]{2,1,0:T(8,128)} custom-call(f32[9,256,128]{2,1,0:T(8,128)} %values_ref.3, f32[9,208,128]{2,1,0:T(8,128)} %multiply_add_fusion.local_ref, f32[8,128]{1,0:T(8,128)} %mixing_ref.3), custom_call_target="tpu_custom_call" | custom-call | tf_op jit(solution)/shard_map/local_part/pallas_call | solution.py:102
  19.4 2.4 %multiply_add_fusion.1.refs_6_ = f32[9,128,80]{2,1,0:T(8,128)} fusion(f32[128,80]{1,0:T(8,128)S(1)} %get-tuple-element.76, f32[9,128]{1,0:T(8,128)S(1)} %get-tuple-element.61, f32[128,80]{1,0:T(8,128)S(1)} %get-tuple-element.75, f32[9,128]{1,0:T(8,128)S(1)} %get-tuple-element.62, f32[128,80]{1,0:T(8,128)S(1)} %get-tuple-element.74, ...), kind=kLoop, calls=%fused_computation.1 | loop fusion | flops 1382400 | bytes 733184 | tf_op jit(solution)/shard_map/add | solution.py:195
  21.9 0.0 collective-permute-done.refs_1_
  21.9 0.0 collective-permute-done.1.refs_2_
  21.9 0.0 copy-start.1
  21.9 0.0 collective-permute-done.2.refs_3_
  21.9 0.0 copy-start.2
  21.9 0.0 collective-permute-done.3.refs_4_
  21.9 0.0 copy-start.3
  21.9 0.0 collective-permute-done.4.refs_5_
  21.9 0.0 copy-start.4
  22.0 0.6 %copy-done = f32[9,16,256]{2,1,0:T(8,128)} copy-done((f32[9,16,256]{2,1,0:T(8,128)}, f32[9,16,256]{2,1,0:T(8,128)S(1)}, u32[]{:S(2)}) %copy-start) | copy-done | bytes 147480
  22.5 0.1 copy-done.1
  22.6 0.0 copy-done.2
  22.6 0.1 copy-done.3
  22.7 0.0 copy-done.4
  22.8 5.2 %finish_send.1 = (f32[9,256,128]{2,1,0:T(8,128)}, f32[9,16,256]{2,1,0:T(8,128)}, f32[9,16,256]{2,1,0:T(8,128)}, f32[9,16,256]{2,1,0:T(8,128)}, f32[9,16,256]{2,1,0:T(8,128)}, /*index=5*/f32[9,16,256]{2,1,0:T(8,128)}) custom-call(f32[9,256,128]{2,1,0:T(8,128)} %local_part.2.refs_0_, f32[9,16,256]{2,1,0:T(8,128)} %copy-done, f32[9,16,256]{2,1,0:T(8,128)} %copy-done.1, ...), custom_call_target="tpu_custom_call" | custom-call | tf_op jit(solution)/shard_map/finish_send/pallas_call | solution.py:153
  28.0 0.0 collective-permute-start.5
  28.0 0.1 collective-permute-start.6
  28.0 2.4 %collective-permute-start.7 = (f32[9,16,256]{2,1,0:T(8,128)}, f32[9,16,256]{2,1,0:T(8,128)S(1)}, u32[]{:S(2)}, u32[]{:S(2)}) collective-permute-start(f32[9,16,256]{2,1,0:T(8,128)} %get-tuple-element.26), channel_id=1, source_target_pairs={{0,16},{1,17},{2,18},{3,19},{4,20},{5,21},{6,22},{7,23},{8,24},{9,... | collective-permute-start | bytes 442376 | tf_op jit(solution)/shard_map/ppermute | solution.py:203
  30.4 4.2 %collective-permute-start.8 = (f32[9,16,256]{2,1,0:T(8,128)}, f32[9,16,256]{2,1,0:T(8,128)S(1)}, u32[]{:S(2)}, u32[]{:S(2)}) collective-permute-start(f32[9,16,256]{2,1,0:T(8,128)} %get-tuple-element.27), channel_id=1, source_target_pairs={{1,2},{2,1},{3,4},{4,3},{5,6},{6,5},{7,8},{8,7},{9,10},{10,9},{11,... | collective-permute-start | bytes 442376 | tf_op jit(solution)/shard_map/ppermute | solution.py:203
  34.6 3.4 %collective-permute-start.9 = (f32[9,16,256]{2,1,0:T(8,128)}, f32[9,16,256]{2,1,0:T(8,128)S(1)}, u32[]{:S(2)}, u32[]{:S(2)}) collective-permute-start(f32[9,16,256]{2,1,0:T(8,128)} %get-tuple-element.28), channel_id=1, source_target_pairs={{2,4},{3,5},{4,2},{5,3},{6,8},{7,9},{8,6},{9,7},{10,12},{11,13},{1... | collective-permute-start | bytes 442376 | tf_op jit(solution)/shard_map/ppermute | solution.py:203
  38.0 3.6 %local_part.3.refs_0_ = f32[9,256,128]{2,1,0:T(8,128)} custom-call(f32[9,256,128]{2,1,0:T(8,128)} %get-tuple-element.23.values_ref, f32[9,208,128]{2,1,0:T(8,128)} %multiply_add_fusion.local_ref, f32[8,128]{1,0:T(8,128)} %mixing_ref.3), custom_call_target="tpu_custom_call" | custom-call | tf_op jit(solution)/shard_map/local_part/pallas_call | solution.py:102
  41.6 0.0 collective-permute-done.5.refs_1_
  41.6 0.0 collective-permute-done.6.refs_2_
  41.6 0.0 copy-start.6
  41.6 0.0 collective-permute-done.7.refs_3_
  41.7 0.0 copy-start.7
  41.7 0.0 collective-permute-done.8.refs_4_
  41.7 0.0 copy-start.8
  41.7 2.4 %collective-permute-done.9.refs_5_ = f32[9,16,256]{2,1,0:T(8,128)S(1)} collective-permute-done((f32[9,16,256]{2,1,0:T(8,128)}, f32[9,16,256]{2,1,0:T(8,128)S(1)}, u32[]{:S(2)}, u32[]{:S(2)}) %collective-permute-start.9) | collective-permute-done | bytes 147488 | tf_op jit(solution)/shard_map/ppermute | solution.py:203
  44.1 0.0 copy-done.5
  44.1 0.0 copy-done.7
  44.1 0.6 %copy-done.9 = f32[9,16,256]{2,1,0:T(8,128)} copy-done((f32[9,16,256]{2,1,0:T(8,128)}, f32[9,16,256]{2,1,0:T(8,128)S(1)}, u32[]{:S(2)}) %copy-start.9) | copy-done | bytes 147480
  44.8 4.0 %finish.1 = f32[9,256,128]{2,1,0:T(8,128)} custom-call(f32[9,256,128]{2,1,0:T(8,128)} %local_part.3.refs_0_, f32[9,16,256]{2,1,0:T(8,128)} %copy-done.5, f32[9,16,256]{2,1,0:T(8,128)} %copy-done.6, f32[9,16,256]{2,1,0:T(8,128)} %copy-done.7, f32[9,16,256]{2,1,0:T(8,128)} %copy-done.8, f32[9,16,256]{2,1,0:T(8,128)} %copy-done.9, ...), custom_call_target="tpu_custom_call" | custom-call | tf_op jit(solution)/shard_map/finish/pallas_call | solution.py:153
  (19 shorter events, 0.2 us)
Async XLA Ops:
  0.0 13.1 %copy-start.11 = (s32[8,128]{1,0:T(8,128)S(1)}, s32[8,128]{1,0:T(8,128)}, u32[]{:S(2)}) copy-start(s32[8,128]{1,0:T(8,128)} %param.11) | copy-start | bytes 12292
  0.0 13.8 %copy-start.10 = (f32[8,9,128]{2,0,1:T(8,128)S(1)}, f32[8,9,128]{2,0,1:T(8,128)}, u32[]{:S(2)}) copy-start(f32[8,9,128]{2,0,1:T(8,128)} %param.8) | copy-start | bytes 110596
  3.6 18.3 %collective-permute-start = (f32[9,16,256]{2,1,0:T(8,128)}, f32[9,16,256]{2,1,0:T(8,128)S(1)}, u32[]{:S(2)}, u32[]{:S(2)}) collective-permute-start(f32[9,16,256]{2,1,0:T(8,128)} %get-tuple-element.17), channel_id=1, source_target_pairs={{0,1},{1,0},{2,3},{3,2},{4,5},{5,4},{6,7},{7,6},{8,9},{9,8},{10,11... | collective-permute-start | bytes 442376 | tf_op jit(solution)/shard_map/ppermute | solution.py:203
  4.2 17.6 %collective-permute-start.1 = (f32[9,16,256]{2,1,0:T(8,128)}, f32[9,16,256]{2,1,0:T(8,128)S(1)}, u32[]{:S(2)}, u32[]{:S(2)}) collective-permute-start(f32[9,16,256]{2,1,0:T(8,128)} %get-tuple-element.18), channel_id=1, source_target_pairs={{0,2},{1,3},{2,0},{3,1},{4,6},{5,7},{6,4},{7,5},{8,10},{9,11},{10,... | collective-permute-start | bytes 442376 | tf_op jit(solution)/shard_map/ppermute | solution.py:203
  5.4 16.4 %collective-permute-start.2 = (f32[9,16,256]{2,1,0:T(8,128)}, f32[9,16,256]{2,1,0:T(8,128)S(1)}, u32[]{:S(2)}, u32[]{:S(2)}) collective-permute-start(f32[9,16,256]{2,1,0:T(8,128)} %get-tuple-element.19), channel_id=1, source_target_pairs={{0,16},{1,17},{2,18},{3,19},{4,20},{5,21},{6,22},{7,23},{8,24},{9,... | collective-permute-start | bytes 442376 | tf_op jit(solution)/shard_map/ppermute | solution.py:203
  5.5 16.4 %collective-permute-start.3 = (f32[9,16,256]{2,1,0:T(8,128)}, f32[9,16,256]{2,1,0:T(8,128)S(1)}, u32[]{:S(2)}, u32[]{:S(2)}) collective-permute-start(f32[9,16,256]{2,1,0:T(8,128)} %get-tuple-element.20), channel_id=1, source_target_pairs={{1,2},{2,1},{3,4},{4,3},{5,6},{6,5},{7,8},{8,7},{9,10},{10,9},{11,... | collective-permute-start | bytes 442376 | tf_op jit(solution)/shard_map/ppermute | solution.py:203
  8.1 13.8 %collective-permute-start.4 = (f32[9,16,256]{2,1,0:T(8,128)}, f32[9,16,256]{2,1,0:T(8,128)S(1)}, u32[]{:S(2)}, u32[]{:S(2)}) collective-permute-start(f32[9,16,256]{2,1,0:T(8,128)} %get-tuple-element.21), channel_id=1, source_target_pairs={{2,4},{3,5},{4,2},{5,3},{6,8},{7,9},{8,6},{9,7},{10,12},{11,13},{1... | collective-permute-start | bytes 442376 | tf_op jit(solution)/shard_map/ppermute | solution.py:203
  21.9 0.6 %copy-start = (f32[9,16,256]{2,1,0:T(8,128)}, f32[9,16,256]{2,1,0:T(8,128)S(1)}, u32[]{:S(2)}) copy-start(f32[9,16,256]{2,1,0:T(8,128)S(1)} %collective-permute-done.refs_1_) | copy-start | bytes 442372
  21.9 0.7 %copy-start.1 = (f32[9,16,256]{2,1,0:T(8,128)}, f32[9,16,256]{2,1,0:T(8,128)S(1)}, u32[]{:S(2)}) copy-start(f32[9,16,256]{2,1,0:T(8,128)S(1)} %collective-permute-done.1.refs_2_) | copy-start | bytes 442372
  21.9 0.7 %copy-start.2 = (f32[9,16,256]{2,1,0:T(8,128)}, f32[9,16,256]{2,1,0:T(8,128)S(1)}, u32[]{:S(2)}) copy-start(f32[9,16,256]{2,1,0:T(8,128)S(1)} %collective-permute-done.2.refs_3_) | copy-start | bytes 442372
  21.9 0.8 %copy-start.3 = (f32[9,16,256]{2,1,0:T(8,128)}, f32[9,16,256]{2,1,0:T(8,128)S(1)}, u32[]{:S(2)}) copy-start(f32[9,16,256]{2,1,0:T(8,128)S(1)} %collective-permute-done.3.refs_4_) | copy-start | bytes 442372
  21.9 0.8 %copy-start.4 = (f32[9,16,256]{2,1,0:T(8,128)}, f32[9,16,256]{2,1,0:T(8,128)S(1)}, u32[]{:S(2)}) copy-start(f32[9,16,256]{2,1,0:T(8,128)S(1)} %collective-permute-done.4.refs_5_) | copy-start | bytes 442372
  28.0 13.7 %collective-permute-start.5 = (f32[9,16,256]{2,1,0:T(8,128)}, f32[9,16,256]{2,1,0:T(8,128)S(1)}, u32[]{:S(2)}, u32[]{:S(2)}) collective-permute-start(f32[9,16,256]{2,1,0:T(8,128)} %get-tuple-element.24), channel_id=1, source_target_pairs={{0,1},{1,0},{2,3},{3,2},{4,5},{5,4},{6,7},{7,6},{8,9},{9,8},{10,11... | collective-permute-start | bytes 442376 | tf_op jit(solution)/shard_map/ppermute | solution.py:203
  28.0 13.7 %collective-permute-start.6 = (f32[9,16,256]{2,1,0:T(8,128)}, f32[9,16,256]{2,1,0:T(8,128)S(1)}, u32[]{:S(2)}, u32[]{:S(2)}) collective-permute-start(f32[9,16,256]{2,1,0:T(8,128)} %get-tuple-element.25), channel_id=1, source_target_pairs={{0,2},{1,3},{2,0},{3,1},{4,6},{5,7},{6,4},{7,5},{8,10},{9,11},{10,... | collective-permute-start | bytes 442376 | tf_op jit(solution)/shard_map/ppermute | solution.py:203
  28.0 13.6 %collective-permute-start.7 = (f32[9,16,256]{2,1,0:T(8,128)}, f32[9,16,256]{2,1,0:T(8,128)S(1)}, u32[]{:S(2)}, u32[]{:S(2)}) collective-permute-start(f32[9,16,256]{2,1,0:T(8,128)} %get-tuple-element.26), channel_id=1, source_target_pairs={{0,16},{1,17},{2,18},{3,19},{4,20},{5,21},{6,22},{7,23},{8,24},{9,... | collective-permute-start | bytes 442376 | tf_op jit(solution)/shard_map/ppermute | solution.py:203
  30.4 11.3 %collective-permute-start.8 = (f32[9,16,256]{2,1,0:T(8,128)}, f32[9,16,256]{2,1,0:T(8,128)S(1)}, u32[]{:S(2)}, u32[]{:S(2)}) collective-permute-start(f32[9,16,256]{2,1,0:T(8,128)} %get-tuple-element.27), channel_id=1, source_target_pairs={{1,2},{2,1},{3,4},{4,3},{5,6},{6,5},{7,8},{8,7},{9,10},{10,9},{11,... | collective-permute-start | bytes 442376 | tf_op jit(solution)/shard_map/ppermute | solution.py:203
  34.6 9.5 %collective-permute-start.9 = (f32[9,16,256]{2,1,0:T(8,128)}, f32[9,16,256]{2,1,0:T(8,128)S(1)}, u32[]{:S(2)}, u32[]{:S(2)}) collective-permute-start(f32[9,16,256]{2,1,0:T(8,128)} %get-tuple-element.28), channel_id=1, source_target_pairs={{2,4},{3,5},{4,2},{5,3},{6,8},{7,9},{8,6},{9,7},{10,12},{11,13},{1... | collective-permute-start | bytes 442376 | tf_op jit(solution)/shard_map/ppermute | solution.py:203
  41.6 2.5 %copy-start.5 = (f32[9,16,256]{2,1,0:T(8,128)}, f32[9,16,256]{2,1,0:T(8,128)S(1)}, u32[]{:S(2)}) copy-start(f32[9,16,256]{2,1,0:T(8,128)S(1)} %collective-permute-done.5.refs_1_) | copy-start | bytes 442372
  41.6 2.5 %copy-start.6 = (f32[9,16,256]{2,1,0:T(8,128)}, f32[9,16,256]{2,1,0:T(8,128)S(1)}, u32[]{:S(2)}) copy-start(f32[9,16,256]{2,1,0:T(8,128)S(1)} %collective-permute-done.6.refs_2_) | copy-start | bytes 442372
  41.7 2.5 %copy-start.7 = (f32[9,16,256]{2,1,0:T(8,128)}, f32[9,16,256]{2,1,0:T(8,128)S(1)}, u32[]{:S(2)}) copy-start(f32[9,16,256]{2,1,0:T(8,128)S(1)} %collective-permute-done.7.refs_3_) | copy-start | bytes 442372
  41.7 2.4 %copy-start.8 = (f32[9,16,256]{2,1,0:T(8,128)}, f32[9,16,256]{2,1,0:T(8,128)S(1)}, u32[]{:S(2)}) copy-start(f32[9,16,256]{2,1,0:T(8,128)S(1)} %collective-permute-done.8.refs_4_) | copy-start | bytes 442372
  44.1 0.7 %copy-start.9 = (f32[9,16,256]{2,1,0:T(8,128)}, f32[9,16,256]{2,1,0:T(8,128)S(1)}, u32[]{:S(2)}) copy-start(f32[9,16,256]{2,1,0:T(8,128)S(1)} %collective-permute-done.9.refs_5_) | copy-start | bytes 442372

commit v16 on v12

--- a/solution.py
+++ b/solution.py
@@ -9,6 +9,7 @@
 
 STEPS = 2
 HIGHEST = lax.Precision.HIGHEST
+HIGH = lax.Precision.HIGH
 INTERPRET = False
 NT = (((1,), (1,)), ((), ()))
 TN = (((0,), (0,)), ((), ()))
@@ -61,7 +62,7 @@
     select = select_ref[...]
     for level in range(values_ref.shape[0]):
         block = lax.dot_general(
-            select, values_ref[level], NT, precision=HIGHEST, preferred_element_type=jnp.float32
+            select, values_ref[level], NT, precision=HIGH, preferred_element_type=jnp.float32
         )
         for g in range(groups):
             out_refs[g][level] = block[g * hslot : (g + 1) * hslot]
@@ -132,7 +133,7 @@
             received,
             weights,
             TN,
-            precision=HIGHEST,
+            precision=HIGH,
             preferred_element_type=jnp.float32,
         )
         keep = 1.0 - deposition_ref[first + level : first + level + 1, :]
@@ -141,7 +142,7 @@
         out_ref[level] = x
         if send:
             block = lax.dot_general(
-                select_ref[...], x, NT, precision=HIGHEST, preferred_element_type=jnp.float32
+                select_ref[...], x, NT, precision=HIGH, preferred_element_type=jnp.float32
             )
             for g in range(groups):
                 send_refs[g][level] = block[g * hslot : (g + 1) * hslot]

time: 46 us -> 44.1 us (0.959)
  Pallas kernels: 19.4 us -> 17.4 us
    pallas_call x2, Pallas kernels: 8.84 us -> 7.39 us  [finish(): pl.pallas_call(functools.partial(finish_kernel, groups, hslot, send), out...]
    pallas_call x1, Pallas kernels: 3.56 us -> 2.97 us  [gather_send(): pl.pallas_call(functools.partial(select_kernel, partners, hslot), out_sha...]
  transfers between devices with their start and end apart: 10 -> 10, of which waited for: 2 -> 2; matrix products, arithmetic and copies ran while one was open for 4% -> 4% of each run, Pallas kernels for 15% -> 16%
where the time goes in v16:
time: 44.1 us; the launch traced here: 43.7 us
  starting transfers between devices  18.7 us (42%)
  Pallas kernels  17.4 us (39%)
  waiting for transfers between devices  3.74 us (8%)
  other arithmetic  1.61 us (4%)
  local copies, waits for them, and re-layouts  1.36 us (3%)
  between operations  0.95 us (2%)
    ppermute x10, starting transfers between devices, per_device(): lax.ppermute(outgoing[g], 'cells', perm=pair_list(n, partner))  18.7 us
    pallas_call x2, Pallas kernels, finish(): pl.pallas_call(functools.partial(finish_kernel, groups, hslot, send), out...  7.39 us
    pallas_call x2, Pallas kernels, local_part(): pl.pallas_call(local_kernel, out_shape=jax.ShapeDtypeStruct(values.shape,...  7.04 us
    ppermute x10, waiting for transfers between devices, per_device(): lax.ppermute(outgoing[g], 'cells', perm=pair_list(n, partner))  3.74 us
    pallas_call x1, Pallas kernels, gather_send(): pl.pallas_call(functools.partial(select_kernel, partners, hslot), out_sha...  2.97 us
    add x1, other arithmetic, per_device(): sum((flux_weight[k][:, None, :] * ((row[k][None, :] == slots).astype(f32)...  1.47 us
    unnamed x24, local copies, waits for them, and re-layouts  1.3 us
  transfers between devices with their start and end apart: 10, of which 2 were waited for; matrix products, arithmetic and copies ran while one was open for 4% of the time, Pallas kernels for 16%

profile of v16, /device:TPU:25, one launch (start us, length us, event | category | flops | bytes accessed | tf_op | source)
XLA Modules:
  0.0 43.7 jit_solution(5265587434065201697)
XLA Ops:
  0.0 0.0 copy-start.11
  0.0 0.0 copy-start.10
  0.0 3.0 %gather_send.1 = (f32[9,16,256]{2,1,0:T(8,128)}, f32[9,16,256]{2,1,0:T(8,128)}, f32[9,16,256]{2,1,0:T(8,128)}, f32[9,16,256]{2,1,0:T(8,128)}, f32[9,16,256]{2,1,0:T(8,128)}, /*index=5*/f32[80,128]{1,0:T(8,128)}) custom-call(s32[16,32]{1,0:T(8,128)} %bitcast.38, f32[9,256,128]{2,1,0:T(8,128)} %values_ref.3), custom_call_target="tpu_custom_call" | custom-call | tf_op jit(solution)/shard_map/gather_send/pallas_call | solution.py:76
  3.0 0.7 %collective-permute-start = (f32[9,16,256]{2,1,0:T(8,128)}, f32[9,16,256]{2,1,0:T(8,128)S(1)}, u32[]{:S(2)}, u32[]{:S(2)}) collective-permute-start(f32[9,16,256]{2,1,0:T(8,128)} %get-tuple-element.17), channel_id=1, source_target_pairs={{0,1},{1,0},{2,3},{3,2},{4,5},{5,4},{6,7},{7,6},{8,9},{9,8},{10,11... | collective-permute-start | bytes 442376 | tf_op jit(solution)/shard_map/ppermute | solution.py:210
  3.7 1.2 %collective-permute-start.1 = (f32[9,16,256]{2,1,0:T(8,128)}, f32[9,16,256]{2,1,0:T(8,128)S(1)}, u32[]{:S(2)}, u32[]{:S(2)}) collective-permute-start(f32[9,16,256]{2,1,0:T(8,128)} %get-tuple-element.18), channel_id=1, source_target_pairs={{0,2},{1,3},{2,0},{3,1},{4,6},{5,7},{6,4},{7,5},{8,10},{9,11},{10,... | collective-permute-start | bytes 442376 | tf_op jit(solution)/shard_map/ppermute | solution.py:210
  4.9 0.1 collective-permute-start.2
  4.9 2.6 %collective-permute-start.3 = (f32[9,16,256]{2,1,0:T(8,128)}, f32[9,16,256]{2,1,0:T(8,128)S(1)}, u32[]{:S(2)}, u32[]{:S(2)}) collective-permute-start(f32[9,16,256]{2,1,0:T(8,128)} %get-tuple-element.20), channel_id=1, source_target_pairs={{1,2},{2,1},{3,4},{4,3},{5,6},{6,5},{7,8},{8,7},{9,10},{10,9},{11,... | collective-permute-start | bytes 442376 | tf_op jit(solution)/shard_map/ppermute | solution.py:210
  7.6 4.9 %collective-permute-start.4 = (f32[9,16,256]{2,1,0:T(8,128)}, f32[9,16,256]{2,1,0:T(8,128)S(1)}, u32[]{:S(2)}, u32[]{:S(2)}) collective-permute-start(f32[9,16,256]{2,1,0:T(8,128)} %get-tuple-element.21), channel_id=1, source_target_pairs={{2,4},{3,5},{4,2},{5,3},{6,8},{7,9},{8,6},{9,7},{10,12},{11,13},{1... | collective-permute-start | bytes 442376 | tf_op jit(solution)/shard_map/ppermute | solution.py:210
  13.2 0.0 copy-done.11
  13.2 0.0 copy-done.10
  13.5 1.5 %multiply_add_fusion.local_ref.refs_6_.refs_7_.refs_8_.refs_9_.refs_10_ = f32[9,208,128]{2,1,0:T(8,128)} fusion(f32[208,128]{1,0:T(8,128)S(1)} %get-tuple-element.45, f32[9,128]{1,0:T(8,128)S(1)} %get-tuple-element.53, f32[208,128]{1,0:T(8,128)S(1)} %get-tuple-element.46, f32[9,128]{1,0:T(8,128)S(1)} %get-tuple-element.54, ...), kind=kLoop, calls=%fused_computation | loop fusion | flops 3594240 | bytes 1847296 | tf_op jit(solution)/shard_map/add | solution.py:202
  14.9 3.5 %local_part.2.refs_0_ = f32[9,256,128]{2,1,0:T(8,128)} custom-call(f32[9,256,128]{2,1,0:T(8,128)} %values_ref.3, f32[9,208,128]{2,1,0:T(8,128)} %multiply_add_fusion.local_ref.refs_6_.refs_7_.refs_8_.refs_9_.refs_10_, f32[8,128]{1,0:T(8,128)} %mixing_ref.3), custom_call_target="tpu_custom_call" | custom-call | tf_op jit(solution)/shard_map/local_part/pallas_call | solution.py:103
  18.4 0.0 collective-permute-done.refs_1_
  18.4 0.0 copy-start
  18.4 0.0 collective-permute-done.1.refs_2_
  18.4 0.0 copy-start.1
  18.5 0.0 collective-permute-done.2.refs_3_
  18.5 0.0 copy-start.2
  18.5 0.0 collective-permute-done.3.refs_4_
  18.5 0.0 copy-start.3
  18.5 1.0 %collective-permute-done.4.refs_5_ = f32[9,16,256]{2,1,0:T(8,128)S(1)} collective-permute-done((f32[9,16,256]{2,1,0:T(8,128)}, f32[9,16,256]{2,1,0:T(8,128)S(1)}, u32[]{:S(2)}, u32[]{:S(2)}) %collective-permute-start.4) | collective-permute-done | bytes 147488 | tf_op jit(solution)/shard_map/ppermute | solution.py:210
  19.5 0.0 copy-start.4
  19.5 0.0 copy-done
  19.5 0.0 copy-done.1
  19.5 0.0 copy-done.2
  19.5 0.0 copy-done.3
  19.5 0.6 %copy-done.4 = f32[9,16,256]{2,1,0:T(8,128)} copy-done((f32[9,16,256]{2,1,0:T(8,128)}, f32[9,16,256]{2,1,0:T(8,128)S(1)}, u32[]{:S(2)}) %copy-start.4) | copy-done | bytes 147480
  20.2 4.0 %finish_send.1 = (f32[9,256,128]{2,1,0:T(8,128)}, f32[9,16,256]{2,1,0:T(8,128)}, f32[9,16,256]{2,1,0:T(8,128)}, f32[9,16,256]{2,1,0:T(8,128)}, f32[9,16,256]{2,1,0:T(8,128)}, /*index=5*/f32[9,16,256]{2,1,0:T(8,128)}) custom-call(f32[9,256,128]{2,1,0:T(8,128)} %local_part.2.refs_0_, f32[9,16,256]{2,1,0:T(8,128)} %copy-done, f32[9,16,256]{2,1,0:T(8,128)} %copy-done.1, ...), custom_call_target="tpu_custom_call" | custom-call | tf_op jit(solution)/shard_map/finish_send/pallas_call | solution.py:165
  24.2 0.0 collective-permute-start.5
  24.2 0.1 collective-permute-start.6
  24.3 1.5 %collective-permute-start.7 = (f32[9,16,256]{2,1,0:T(8,128)}, f32[9,16,256]{2,1,0:T(8,128)S(1)}, u32[]{:S(2)}, u32[]{:S(2)}) collective-permute-start(f32[9,16,256]{2,1,0:T(8,128)} %get-tuple-element.26), channel_id=1, source_target_pairs={{0,16},{1,17},{2,18},{3,19},{4,20},{5,21},{6,22},{7,23},{8,24},{9,... | collective-permute-start | bytes 442376 | tf_op jit(solution)/shard_map/ppermute | solution.py:210
  25.8 4.2 %collective-permute-start.8 = (f32[9,16,256]{2,1,0:T(8,128)}, f32[9,16,256]{2,1,0:T(8,128)S(1)}, u32[]{:S(2)}, u32[]{:S(2)}) collective-permute-start(f32[9,16,256]{2,1,0:T(8,128)} %get-tuple-element.27), channel_id=1, source_target_pairs={{1,2},{2,1},{3,4},{4,3},{5,6},{6,5},{7,8},{8,7},{9,10},{10,9},{11,... | collective-permute-start | bytes 442376 | tf_op jit(solution)/shard_map/ppermute | solution.py:210
  30.0 3.4 %collective-permute-start.9 = (f32[9,16,256]{2,1,0:T(8,128)}, f32[9,16,256]{2,1,0:T(8,128)S(1)}, u32[]{:S(2)}, u32[]{:S(2)}) collective-permute-start(f32[9,16,256]{2,1,0:T(8,128)} %get-tuple-element.28), channel_id=1, source_target_pairs={{2,4},{3,5},{4,2},{5,3},{6,8},{7,9},{8,6},{9,7},{10,12},{11,13},{1... | collective-permute-start | bytes 442376 | tf_op jit(solution)/shard_map/ppermute | solution.py:210
  33.4 3.5 %local_part.3.refs_0_ = f32[9,256,128]{2,1,0:T(8,128)} custom-call(f32[9,256,128]{2,1,0:T(8,128)} %get-tuple-element.23.values_ref, f32[9,208,128]{2,1,0:T(8,128)} %multiply_add_fusion.local_ref.refs_6_.refs_7_.refs_8_.refs_9_.refs_10_, f32[8,128]{1,0:T(8,128)} %mixing_ref.3), custom_call_target="tpu_custom_call" | custom-call | tf_op jit(solution)/shard_map/local_part/pallas_call | solution.py:103
  37.0 0.0 collective-permute-done.5.refs_1_
  37.0 0.0 collective-permute-done.6.refs_2_
  37.0 0.0 copy-start.6
  37.0 0.0 collective-permute-done.7.refs_3_
  37.0 0.0 copy-start.7
  37.0 0.0 collective-permute-done.8.refs_4_
  37.0 0.0 copy-start.8
  37.0 2.7 %collective-permute-done.9.refs_5_ = f32[9,16,256]{2,1,0:T(8,128)S(1)} collective-permute-done((f32[9,16,256]{2,1,0:T(8,128)}, f32[9,16,256]{2,1,0:T(8,128)S(1)}, u32[]{:S(2)}, u32[]{:S(2)}) %collective-permute-start.9) | collective-permute-done | bytes 147488 | tf_op jit(solution)/shard_map/ppermute | solution.py:210
  39.7 0.0 copy-done.5
  39.7 0.0 copy-done.6
  39.7 0.0 copy-done.7
  39.7 0.0 copy-done.8
  39.8 0.6 %copy-done.9 = f32[9,16,256]{2,1,0:T(8,128)} copy-done((f32[9,16,256]{2,1,0:T(8,128)}, f32[9,16,256]{2,1,0:T(8,128)S(1)}, u32[]{:S(2)}) %copy-start.9) | copy-done | bytes 147480
  40.4 3.4 %finish.1 = f32[9,256,128]{2,1,0:T(8,128)} custom-call(f32[9,256,128]{2,1,0:T(8,128)} %local_part.3.refs_0_, f32[9,16,256]{2,1,0:T(8,128)} %copy-done.5, f32[9,16,256]{2,1,0:T(8,128)} %copy-done.6, f32[9,16,256]{2,1,0:T(8,128)} %copy-done.7, f32[9,16,256]{2,1,0:T(8,128)} %copy-done.8, f32[9,16,256]{2,1,0:T(8,128)} %copy-done.9, ...), custom_call_target="tpu_custom_call" | custom-call | tf_op jit(solution)/shard_map/finish/pallas_call | solution.py:165
  (13 shorter events, 0.2 us)
Async XLA Ops:
  0.0 13.2 %copy-start.11 = (s32[8,128]{1,0:T(8,128)S(1)}, s32[8,128]{1,0:T(8,128)}, u32[]{:S(2)}) copy-start(s32[8,128]{1,0:T(8,128)} %param.11) | copy-start | bytes 12292
  0.0 13.2 %copy-start.10 = (f32[8,9,128]{2,0,1:T(8,128)S(1)}, f32[8,9,128]{2,0,1:T(8,128)}, u32[]{:S(2)}) copy-start(f32[8,9,128]{2,0,1:T(8,128)} %param.8) | copy-start | bytes 110596
  3.0 15.5 %collective-permute-start = (f32[9,16,256]{2,1,0:T(8,128)}, f32[9,16,256]{2,1,0:T(8,128)S(1)}, u32[]{:S(2)}, u32[]{:S(2)}) collective-permute-start(f32[9,16,256]{2,1,0:T(8,128)} %get-tuple-element.17), channel_id=1, source_target_pairs={{0,1},{1,0},{2,3},{3,2},{4,5},{5,4},{6,7},{7,6},{8,9},{9,8},{10,11... | collective-permute-start | bytes 442376 | tf_op jit(solution)/shard_map/ppermute | solution.py:210
  3.7 14.8 %collective-permute-start.1 = (f32[9,16,256]{2,1,0:T(8,128)}, f32[9,16,256]{2,1,0:T(8,128)S(1)}, u32[]{:S(2)}, u32[]{:S(2)}) collective-permute-start(f32[9,16,256]{2,1,0:T(8,128)} %get-tuple-element.18), channel_id=1, source_target_pairs={{0,2},{1,3},{2,0},{3,1},{4,6},{5,7},{6,4},{7,5},{8,10},{9,11},{10,... | collective-permute-start | bytes 442376 | tf_op jit(solution)/shard_map/ppermute | solution.py:210
  4.9 13.6 %collective-permute-start.2 = (f32[9,16,256]{2,1,0:T(8,128)}, f32[9,16,256]{2,1,0:T(8,128)S(1)}, u32[]{:S(2)}, u32[]{:S(2)}) collective-permute-start(f32[9,16,256]{2,1,0:T(8,128)} %get-tuple-element.19), channel_id=1, source_target_pairs={{0,16},{1,17},{2,18},{3,19},{4,20},{5,21},{6,22},{7,23},{8,24},{9,... | collective-permute-start | bytes 442376 | tf_op jit(solution)/shard_map/ppermute | solution.py:210
  4.9 13.6 %collective-permute-start.3 = (f32[9,16,256]{2,1,0:T(8,128)}, f32[9,16,256]{2,1,0:T(8,128)S(1)}, u32[]{:S(2)}, u32[]{:S(2)}) collective-permute-start(f32[9,16,256]{2,1,0:T(8,128)} %get-tuple-element.20), channel_id=1, source_target_pairs={{1,2},{2,1},{3,4},{4,3},{5,6},{6,5},{7,8},{8,7},{9,10},{10,9},{11,... | collective-permute-start | bytes 442376 | tf_op jit(solution)/shard_map/ppermute | solution.py:210
  7.6 11.9 %collective-permute-start.4 = (f32[9,16,256]{2,1,0:T(8,128)}, f32[9,16,256]{2,1,0:T(8,128)S(1)}, u32[]{:S(2)}, u32[]{:S(2)}) collective-permute-start(f32[9,16,256]{2,1,0:T(8,128)} %get-tuple-element.21), channel_id=1, source_target_pairs={{2,4},{3,5},{4,2},{5,3},{6,8},{7,9},{8,6},{9,7},{10,12},{11,13},{1... | collective-permute-start | bytes 442376 | tf_op jit(solution)/shard_map/ppermute | solution.py:210
  18.4 1.1 %copy-start = (f32[9,16,256]{2,1,0:T(8,128)}, f32[9,16,256]{2,1,0:T(8,128)S(1)}, u32[]{:S(2)}) copy-start(f32[9,16,256]{2,1,0:T(8,128)S(1)} %collective-permute-done.refs_1_) | copy-start | bytes 442372
  18.4 1.1 %copy-start.1 = (f32[9,16,256]{2,1,0:T(8,128)}, f32[9,16,256]{2,1,0:T(8,128)S(1)}, u32[]{:S(2)}) copy-start(f32[9,16,256]{2,1,0:T(8,128)S(1)} %collective-permute-done.1.refs_2_) | copy-start | bytes 442372
  18.5 1.0 %copy-start.2 = (f32[9,16,256]{2,1,0:T(8,128)}, f32[9,16,256]{2,1,0:T(8,128)S(1)}, u32[]{:S(2)}) copy-start(f32[9,16,256]{2,1,0:T(8,128)S(1)} %collective-permute-done.2.refs_3_) | copy-start | bytes 442372
  18.5 1.0 %copy-start.3 = (f32[9,16,256]{2,1,0:T(8,128)}, f32[9,16,256]{2,1,0:T(8,128)S(1)}, u32[]{:S(2)}) copy-start(f32[9,16,256]{2,1,0:T(8,128)S(1)} %collective-permute-done.3.refs_4_) | copy-start | bytes 442372
  19.5 0.7 %copy-start.4 = (f32[9,16,256]{2,1,0:T(8,128)}, f32[9,16,256]{2,1,0:T(8,128)S(1)}, u32[]{:S(2)}) copy-start(f32[9,16,256]{2,1,0:T(8,128)S(1)} %collective-permute-done.4.refs_5_) | copy-start | bytes 442372
  24.2 12.8 %collective-permute-start.5 = (f32[9,16,256]{2,1,0:T(8,128)}, f32[9,16,256]{2,1,0:T(8,128)S(1)}, u32[]{:S(2)}, u32[]{:S(2)}) collective-permute-start(f32[9,16,256]{2,1,0:T(8,128)} %get-tuple-element.24), channel_id=1, source_target_pairs={{0,1},{1,0},{2,3},{3,2},{4,5},{5,4},{6,7},{7,6},{8,9},{9,8},{10,11... | collective-permute-start | bytes 442376 | tf_op jit(solution)/shard_map/ppermute | solution.py:210
  24.2 12.7 %collective-permute-start.6 = (f32[9,16,256]{2,1,0:T(8,128)}, f32[9,16,256]{2,1,0:T(8,128)S(1)}, u32[]{:S(2)}, u32[]{:S(2)}) collective-permute-start(f32[9,16,256]{2,1,0:T(8,128)} %get-tuple-element.25), channel_id=1, source_target_pairs={{0,2},{1,3},{2,0},{3,1},{4,6},{5,7},{6,4},{7,5},{8,10},{9,11},{10,... | collective-permute-start | bytes 442376 | tf_op jit(solution)/shard_map/ppermute | solution.py:210
  24.3 12.7 %collective-permute-start.7 = (f32[9,16,256]{2,1,0:T(8,128)}, f32[9,16,256]{2,1,0:T(8,128)S(1)}, u32[]{:S(2)}, u32[]{:S(2)}) collective-permute-start(f32[9,16,256]{2,1,0:T(8,128)} %get-tuple-element.26), channel_id=1, source_target_pairs={{0,16},{1,17},{2,18},{3,19},{4,20},{5,21},{6,22},{7,23},{8,24},{9,... | collective-permute-start | bytes 442376 | tf_op jit(solution)/shard_map/ppermute | solution.py:210
  25.8 11.2 %collective-permute-start.8 = (f32[9,16,256]{2,1,0:T(8,128)}, f32[9,16,256]{2,1,0:T(8,128)S(1)}, u32[]{:S(2)}, u32[]{:S(2)}) collective-permute-start(f32[9,16,256]{2,1,0:T(8,128)} %get-tuple-element.27), channel_id=1, source_target_pairs={{1,2},{2,1},{3,4},{4,3},{5,6},{6,5},{7,8},{8,7},{9,10},{10,9},{11,... | collective-permute-start | bytes 442376 | tf_op jit(solution)/shard_map/ppermute | solution.py:210
  30.0 9.7 %collective-permute-start.9 = (f32[9,16,256]{2,1,0:T(8,128)}, f32[9,16,256]{2,1,0:T(8,128)S(1)}, u32[]{:S(2)}, u32[]{:S(2)}) collective-permute-start(f32[9,16,256]{2,1,0:T(8,128)} %get-tuple-element.28), channel_id=1, source_target_pairs={{2,4},{3,5},{4,2},{5,3},{6,8},{7,9},{8,6},{9,7},{10,12},{11,13},{1... | collective-permute-start | bytes 442376 | tf_op jit(solution)/shard_map/ppermute | solution.py:210
  37.0 2.8 %copy-start.5 = (f32[9,16,256]{2,1,0:T(8,128)}, f32[9,16,256]{2,1,0:T(8,128)S(1)}, u32[]{:S(2)}) copy-start(f32[9,16,256]{2,1,0:T(8,128)S(1)} %collective-permute-done.5.refs_1_) | copy-start | bytes 442372
  37.0 2.8 %copy-start.6 = (f32[9,16,256]{2,1,0:T(8,128)}, f32[9,16,256]{2,1,0:T(8,128)S(1)}, u32[]{:S(2)}) copy-start(f32[9,16,256]{2,1,0:T(8,128)S(1)} %collective-permute-done.6.refs_2_) | copy-start | bytes 442372
  37.0 2.8 %copy-start.7 = (f32[9,16,256]{2,1,0:T(8,128)}, f32[9,16,256]{2,1,0:T(8,128)S(1)}, u32[]{:S(2)}) copy-start(f32[9,16,256]{2,1,0:T(8,128)S(1)} %collective-permute-done.7.refs_3_) | copy-start | bytes 442372
  37.0 2.7 %copy-start.8 = (f32[9,16,256]{2,1,0:T(8,128)}, f32[9,16,256]{2,1,0:T(8,128)S(1)}, u32[]{:S(2)}) copy-start(f32[9,16,256]{2,1,0:T(8,128)S(1)} %collective-permute-done.8.refs_4_) | copy-start | bytes 442372
  39.7 0.6 %copy-start.9 = (f32[9,16,256]{2,1,0:T(8,128)}, f32[9,16,256]{2,1,0:T(8,128)S(1)}, u32[]{:S(2)}) copy-start(f32[9,16,256]{2,1,0:T(8,128)S(1)} %collective-permute-done.9.refs_5_) | copy-start | bytes 442372

commit v17 on v16

--- a/solution.py
+++ b/solution.py
@@ -8,7 +8,6 @@
 from jax.sharding import PartitionSpec as P
 
 STEPS = 2
-HIGHEST = lax.Precision.HIGHEST
 HIGH = lax.Precision.HIGH
 INTERPRET = False
 NT = (((1,), (1,)), ((), ()))
@@ -87,7 +86,7 @@
     for level in range(levels):
         v = values_ref[level]
         x = v + jnp.dot(
-            v, local_ref[level], precision=HIGHEST, preferred_element_type=jnp.float32
+            v, local_ref[level], precision=HIGH, preferred_element_type=jnp.float32
         )
         if level + 1 < levels:
             x = x + mixing_ref[level : level + 1, :] * (values_ref[level + 1] - v)

time: 44.1 us -> 43.7 us (level)
  Pallas kernels: 17.4 us -> 16.2 us
  waiting for transfers between devices: 3.74 us -> 4.89 us
  starting transfers between devices: 18.7 us -> 18.1 us
    ppermute x10, waiting for transfers between devices: 3.74 us -> 4.89 us  [per_device(): lax.ppermute(outgoing[g], 'cells', perm=pair_list(n, partner))]
    pallas_call x2, Pallas kernels: 7.04 us -> 5.89 us  [local_part(): pl.pallas_call(local_kernel, out_shape=jax.ShapeDtypeStruct(values.shape,...]
    ppermute x10, starting transfers between devices: 18.7 us -> 18.1 us  [per_device(): lax.ppermute(outgoing[g], 'cells', perm=pair_list(n, partner))]
  transfers between devices with their start and end apart: 10 -> 10, of which waited for: 2 -> 2; matrix products, arithmetic and copies ran while one was open for 4% -> 4% of each run, Pallas kernels for 16% -> 14%
where the time goes in v17:
time: 43.7 us; the launch traced here: 43.2 us
  starting transfers between devices  18.1 us (41%)
  Pallas kernels  16.2 us (37%)
  waiting for transfers between devices  4.89 us (11%)
  other arithmetic  1.61 us (4%)
  local copies, waits for them, and re-layouts  1.36 us (3%)
  between operations  0.95 us (2%)
    ppermute x10, starting transfers between devices, per_device(): lax.ppermute(outgoing[g], 'cells', perm=pair_list(n, partner))  18.1 us
    pallas_call x2, Pallas kernels, finish(): pl.pallas_call(functools.partial(finish_kernel, groups, hslot, send), out...  7.39 us
    pallas_call x2, Pallas kernels, local_part(): pl.pallas_call(local_kernel, out_shape=jax.ShapeDtypeStruct(values.shape,...  5.89 us
    ppermute x10, waiting for transfers between devices, per_device(): lax.ppermute(outgoing[g], 'cells', perm=pair_list(n, partner))  4.89 us
    pallas_call x1, Pallas kernels, gather_send(): pl.pallas_call(functools.partial(select_kernel, partners, hslot), out_sha...  2.97 us
    add x1, other arithmetic, per_device(): sum((flux_weight[k][:, None, :] * ((row[k][None, :] == slots).astype(f32)...  1.47 us
    unnamed x24, local copies, waits for them, and re-layouts  1.3 us
  transfers between devices with their start and end apart: 10, of which 2 were waited for; matrix products, arithmetic and copies ran while one was open for 4% of the time, Pallas kernels for 14%

profile of v17, /device:TPU:25, one launch (start us, length us, event | category | flops | bytes accessed | tf_op | source)
XLA Modules:
  0.0 43.2 jit_solution(2366080583328674068)
XLA Ops:
  0.0 0.0 copy-start.11
  0.0 0.0 copy-start.10
  0.0 3.0 %gather_send.1 = (f32[9,16,256]{2,1,0:T(8,128)}, f32[9,16,256]{2,1,0:T(8,128)}, f32[9,16,256]{2,1,0:T(8,128)}, f32[9,16,256]{2,1,0:T(8,128)}, f32[9,16,256]{2,1,0:T(8,128)}, /*index=5*/f32[80,128]{1,0:T(8,128)}) custom-call(s32[16,32]{1,0:T(8,128)} %bitcast.38, f32[9,256,128]{2,1,0:T(8,128)} %values_ref.3), custom_call_target="tpu_custom_call" | custom-call | tf_op jit(solution)/shard_map/gather_send/pallas_call | solution.py:75
  3.0 0.7 %collective-permute-start = (f32[9,16,256]{2,1,0:T(8,128)}, f32[9,16,256]{2,1,0:T(8,128)S(1)}, u32[]{:S(2)}, u32[]{:S(2)}) collective-permute-start(f32[9,16,256]{2,1,0:T(8,128)} %get-tuple-element.17), channel_id=1, source_target_pairs={{0,1},{1,0},{2,3},{3,2},{4,5},{5,4},{6,7},{7,6},{8,9},{9,8},{10,11... | collective-permute-start | bytes 442376 | tf_op jit(solution)/shard_map/ppermute | solution.py:209
  3.7 1.2 %collective-permute-start.1 = (f32[9,16,256]{2,1,0:T(8,128)}, f32[9,16,256]{2,1,0:T(8,128)S(1)}, u32[]{:S(2)}, u32[]{:S(2)}) collective-permute-start(f32[9,16,256]{2,1,0:T(8,128)} %get-tuple-element.18), channel_id=1, source_target_pairs={{0,2},{1,3},{2,0},{3,1},{4,6},{5,7},{6,4},{7,5},{8,10},{9,11},{10,... | collective-permute-start | bytes 442376 | tf_op jit(solution)/shard_map/ppermute | solution.py:209
  4.9 0.1 collective-permute-start.2
  4.9 2.6 %collective-permute-start.3 = (f32[9,16,256]{2,1,0:T(8,128)}, f32[9,16,256]{2,1,0:T(8,128)S(1)}, u32[]{:S(2)}, u32[]{:S(2)}) collective-permute-start(f32[9,16,256]{2,1,0:T(8,128)} %get-tuple-element.20), channel_id=1, source_target_pairs={{1,2},{2,1},{3,4},{4,3},{5,6},{6,5},{7,8},{8,7},{9,10},{10,9},{11,... | collective-permute-start | bytes 442376 | tf_op jit(solution)/shard_map/ppermute | solution.py:209
  7.6 4.9 %collective-permute-start.4 = (f32[9,16,256]{2,1,0:T(8,128)}, f32[9,16,256]{2,1,0:T(8,128)S(1)}, u32[]{:S(2)}, u32[]{:S(2)}) collective-permute-start(f32[9,16,256]{2,1,0:T(8,128)} %get-tuple-element.21), channel_id=1, source_target_pairs={{2,4},{3,5},{4,2},{5,3},{6,8},{7,9},{8,6},{9,7},{10,12},{11,13},{1... | collective-permute-start | bytes 442376 | tf_op jit(solution)/shard_map/ppermute | solution.py:209
  13.2 0.0 copy-done.11
  13.2 0.0 copy-done.10
  13.5 1.5 %multiply_add_fusion.local_ref.refs_6_.refs_7_.refs_8_.refs_9_.refs_10_ = f32[9,208,128]{2,1,0:T(8,128)} fusion(f32[208,128]{1,0:T(8,128)S(1)} %get-tuple-element.45, f32[9,128]{1,0:T(8,128)S(1)} %get-tuple-element.53, f32[208,128]{1,0:T(8,128)S(1)} %get-tuple-element.46, f32[9,128]{1,0:T(8,128)S(1)} %get-tuple-element.54, ...), kind=kLoop, calls=%fused_computation | loop fusion | flops 3594240 | bytes 1847296 | tf_op jit(solution)/shard_map/add | solution.py:201
  14.9 2.9 %local_part.2.refs_0_ = f32[9,256,128]{2,1,0:T(8,128)} custom-call(f32[9,256,128]{2,1,0:T(8,128)} %values_ref.3, f32[9,208,128]{2,1,0:T(8,128)} %multiply_add_fusion.local_ref.refs_6_.refs_7_.refs_8_.refs_9_.refs_10_, f32[8,128]{1,0:T(8,128)} %mixing_ref.3), custom_call_target="tpu_custom_call" | custom-call | tf_op jit(solution)/shard_map/local_part/pallas_call | solution.py:102
  17.9 0.0 collective-permute-done.refs_1_
  17.9 0.0 copy-start
  17.9 0.0 collective-permute-done.1.refs_2_
  17.9 0.0 copy-start.1
  17.9 0.0 collective-permute-done.2.refs_3_
  17.9 0.0 copy-start.2
  17.9 0.0 collective-permute-done.3.refs_4_
  17.9 0.0 copy-start.3
  17.9 1.6 %collective-permute-done.4.refs_5_ = f32[9,16,256]{2,1,0:T(8,128)S(1)} collective-permute-done((f32[9,16,256]{2,1,0:T(8,128)}, f32[9,16,256]{2,1,0:T(8,128)S(1)}, u32[]{:S(2)}, u32[]{:S(2)}) %collective-permute-start.4) | collective-permute-done | bytes 147488 | tf_op jit(solution)/shard_map/ppermute | solution.py:209
  19.5 0.0 copy-start.4
  19.5 0.0 copy-done
  19.5 0.0 copy-done.1
  19.5 0.0 copy-done.2
  19.5 0.0 copy-done.3
  19.5 0.6 %copy-done.4 = f32[9,16,256]{2,1,0:T(8,128)} copy-done((f32[9,16,256]{2,1,0:T(8,128)}, f32[9,16,256]{2,1,0:T(8,128)S(1)}, u32[]{:S(2)}) %copy-start.4) | copy-done | bytes 147480
  20.2 4.0 %finish_send.1 = (f32[9,256,128]{2,1,0:T(8,128)}, f32[9,16,256]{2,1,0:T(8,128)}, f32[9,16,256]{2,1,0:T(8,128)}, f32[9,16,256]{2,1,0:T(8,128)}, f32[9,16,256]{2,1,0:T(8,128)}, /*index=5*/f32[9,16,256]{2,1,0:T(8,128)}) custom-call(f32[9,256,128]{2,1,0:T(8,128)} %local_part.2.refs_0_, f32[9,16,256]{2,1,0:T(8,128)} %copy-done, f32[9,16,256]{2,1,0:T(8,128)} %copy-done.1, ...), custom_call_target="tpu_custom_call" | custom-call | tf_op jit(solution)/shard_map/finish_send/pallas_call | solution.py:164
  24.2 0.0 collective-permute-start.5
  24.2 0.1 collective-permute-start.6
  24.3 1.0 %collective-permute-start.7 = (f32[9,16,256]{2,1,0:T(8,128)}, f32[9,16,256]{2,1,0:T(8,128)S(1)}, u32[]{:S(2)}, u32[]{:S(2)}) collective-permute-start(f32[9,16,256]{2,1,0:T(8,128)} %get-tuple-element.26), channel_id=1, source_target_pairs={{0,16},{1,17},{2,18},{3,19},{4,20},{5,21},{6,22},{7,23},{8,24},{9,... | collective-permute-start | bytes 442376 | tf_op jit(solution)/shard_map/ppermute | solution.py:209
  25.3 4.2 %collective-permute-start.8 = (f32[9,16,256]{2,1,0:T(8,128)}, f32[9,16,256]{2,1,0:T(8,128)S(1)}, u32[]{:S(2)}, u32[]{:S(2)}) collective-permute-start(f32[9,16,256]{2,1,0:T(8,128)} %get-tuple-element.27), channel_id=1, source_target_pairs={{1,2},{2,1},{3,4},{4,3},{5,6},{6,5},{7,8},{8,7},{9,10},{10,9},{11,... | collective-permute-start | bytes 442376 | tf_op jit(solution)/shard_map/ppermute | solution.py:209
  29.4 3.4 %collective-permute-start.9 = (f32[9,16,256]{2,1,0:T(8,128)}, f32[9,16,256]{2,1,0:T(8,128)S(1)}, u32[]{:S(2)}, u32[]{:S(2)}) collective-permute-start(f32[9,16,256]{2,1,0:T(8,128)} %get-tuple-element.28), channel_id=1, source_target_pairs={{2,4},{3,5},{4,2},{5,3},{6,8},{7,9},{8,6},{9,7},{10,12},{11,13},{1... | collective-permute-start | bytes 442376 | tf_op jit(solution)/shard_map/ppermute | solution.py:209
  32.9 3.0 %local_part.3.refs_0_ = f32[9,256,128]{2,1,0:T(8,128)} custom-call(f32[9,256,128]{2,1,0:T(8,128)} %get-tuple-element.23.values_ref, f32[9,208,128]{2,1,0:T(8,128)} %multiply_add_fusion.local_ref.refs_6_.refs_7_.refs_8_.refs_9_.refs_10_, f32[8,128]{1,0:T(8,128)} %mixing_ref.3), custom_call_target="tpu_custom_call" | custom-call | tf_op jit(solution)/shard_map/local_part/pallas_call | solution.py:102
  35.8 0.0 collective-permute-done.5.refs_1_
  35.8 0.0 collective-permute-done.6.refs_2_
  35.8 0.0 copy-start.6
  35.8 0.0 collective-permute-done.7.refs_3_
  35.9 0.0 copy-start.7
  35.9 0.0 collective-permute-done.8.refs_4_
  35.9 0.0 copy-start.8
  35.9 3.3 %collective-permute-done.9.refs_5_ = f32[9,16,256]{2,1,0:T(8,128)S(1)} collective-permute-done((f32[9,16,256]{2,1,0:T(8,128)}, f32[9,16,256]{2,1,0:T(8,128)S(1)}, u32[]{:S(2)}, u32[]{:S(2)}) %collective-permute-start.9) | collective-permute-done | bytes 147488 | tf_op jit(solution)/shard_map/ppermute | solution.py:209
  39.2 0.0 copy-done.5
  39.2 0.0 copy-done.6
  39.2 0.0 copy-done.7
  39.2 0.0 copy-done.8
  39.2 0.6 %copy-done.9 = f32[9,16,256]{2,1,0:T(8,128)} copy-done((f32[9,16,256]{2,1,0:T(8,128)}, f32[9,16,256]{2,1,0:T(8,128)S(1)}, u32[]{:S(2)}) %copy-start.9) | copy-done | bytes 147480
  39.8 3.4 %finish.1 = f32[9,256,128]{2,1,0:T(8,128)} custom-call(f32[9,256,128]{2,1,0:T(8,128)} %local_part.3.refs_0_, f32[9,16,256]{2,1,0:T(8,128)} %copy-done.5, f32[9,16,256]{2,1,0:T(8,128)} %copy-done.6, f32[9,16,256]{2,1,0:T(8,128)} %copy-done.7, f32[9,16,256]{2,1,0:T(8,128)} %copy-done.8, f32[9,16,256]{2,1,0:T(8,128)} %copy-done.9, ...), custom_call_target="tpu_custom_call" | custom-call | tf_op jit(solution)/shard_map/finish/pallas_call | solution.py:164
  (13 shorter events, 0.2 us)
Async XLA Ops:
  0.0 13.2 %copy-start.11 = (s32[8,128]{1,0:T(8,128)S(1)}, s32[8,128]{1,0:T(8,128)}, u32[]{:S(2)}) copy-start(s32[8,128]{1,0:T(8,128)} %param.11) | copy-start | bytes 12292
  0.0 13.2 %copy-start.10 = (f32[8,9,128]{2,0,1:T(8,128)S(1)}, f32[8,9,128]{2,0,1:T(8,128)}, u32[]{:S(2)}) copy-start(f32[8,9,128]{2,0,1:T(8,128)} %param.8) | copy-start | bytes 110596
  3.0 14.9 %collective-permute-start = (f32[9,16,256]{2,1,0:T(8,128)}, f32[9,16,256]{2,1,0:T(8,128)S(1)}, u32[]{:S(2)}, u32[]{:S(2)}) collective-permute-start(f32[9,16,256]{2,1,0:T(8,128)} %get-tuple-element.17), channel_id=1, source_target_pairs={{0,1},{1,0},{2,3},{3,2},{4,5},{5,4},{6,7},{7,6},{8,9},{9,8},{10,11... | collective-permute-start | bytes 442376 | tf_op jit(solution)/shard_map/ppermute | solution.py:209
  3.7 14.2 %collective-permute-start.1 = (f32[9,16,256]{2,1,0:T(8,128)}, f32[9,16,256]{2,1,0:T(8,128)S(1)}, u32[]{:S(2)}, u32[]{:S(2)}) collective-permute-start(f32[9,16,256]{2,1,0:T(8,128)} %get-tuple-element.18), channel_id=1, source_target_pairs={{0,2},{1,3},{2,0},{3,1},{4,6},{5,7},{6,4},{7,5},{8,10},{9,11},{10,... | collective-permute-start | bytes 442376 | tf_op jit(solution)/shard_map/ppermute | solution.py:209
  4.9 13.0 %collective-permute-start.2 = (f32[9,16,256]{2,1,0:T(8,128)}, f32[9,16,256]{2,1,0:T(8,128)S(1)}, u32[]{:S(2)}, u32[]{:S(2)}) collective-permute-start(f32[9,16,256]{2,1,0:T(8,128)} %get-tuple-element.19), channel_id=1, source_target_pairs={{0,16},{1,17},{2,18},{3,19},{4,20},{5,21},{6,22},{7,23},{8,24},{9,... | collective-permute-start | bytes 442376 | tf_op jit(solution)/shard_map/ppermute | solution.py:209
  4.9 13.0 %collective-permute-start.3 = (f32[9,16,256]{2,1,0:T(8,128)}, f32[9,16,256]{2,1,0:T(8,128)S(1)}, u32[]{:S(2)}, u32[]{:S(2)}) collective-permute-start(f32[9,16,256]{2,1,0:T(8,128)} %get-tuple-element.20), channel_id=1, source_target_pairs={{1,2},{2,1},{3,4},{4,3},{5,6},{6,5},{7,8},{8,7},{9,10},{10,9},{11,... | collective-permute-start | bytes 442376 | tf_op jit(solution)/shard_map/ppermute | solution.py:209
  7.6 11.9 %collective-permute-start.4 = (f32[9,16,256]{2,1,0:T(8,128)}, f32[9,16,256]{2,1,0:T(8,128)S(1)}, u32[]{:S(2)}, u32[]{:S(2)}) collective-permute-start(f32[9,16,256]{2,1,0:T(8,128)} %get-tuple-element.21), channel_id=1, source_target_pairs={{2,4},{3,5},{4,2},{5,3},{6,8},{7,9},{8,6},{9,7},{10,12},{11,13},{1... | collective-permute-start | bytes 442376 | tf_op jit(solution)/shard_map/ppermute | solution.py:209
  17.9 1.6 %copy-start = (f32[9,16,256]{2,1,0:T(8,128)}, f32[9,16,256]{2,1,0:T(8,128)S(1)}, u32[]{:S(2)}) copy-start(f32[9,16,256]{2,1,0:T(8,128)S(1)} %collective-permute-done.refs_1_) | copy-start | bytes 442372
  17.9 1.6 %copy-start.1 = (f32[9,16,256]{2,1,0:T(8,128)}, f32[9,16,256]{2,1,0:T(8,128)S(1)}, u32[]{:S(2)}) copy-start(f32[9,16,256]{2,1,0:T(8,128)S(1)} %collective-permute-done.1.refs_2_) | copy-start | bytes 442372
  17.9 1.6 %copy-start.2 = (f32[9,16,256]{2,1,0:T(8,128)}, f32[9,16,256]{2,1,0:T(8,128)S(1)}, u32[]{:S(2)}) copy-start(f32[9,16,256]{2,1,0:T(8,128)S(1)} %collective-permute-done.2.refs_3_) | copy-start | bytes 442372
  17.9 1.6 %copy-start.3 = (f32[9,16,256]{2,1,0:T(8,128)}, f32[9,16,256]{2,1,0:T(8,128)S(1)}, u32[]{:S(2)}) copy-start(f32[9,16,256]{2,1,0:T(8,128)S(1)} %collective-permute-done.3.refs_4_) | copy-start | bytes 442372
  19.5 0.7 %copy-start.4 = (f32[9,16,256]{2,1,0:T(8,128)}, f32[9,16,256]{2,1,0:T(8,128)S(1)}, u32[]{:S(2)}) copy-start(f32[9,16,256]{2,1,0:T(8,128)S(1)} %collective-permute-done.4.refs_5_) | copy-start | bytes 442372
  24.2 11.6 %collective-permute-start.5 = (f32[9,16,256]{2,1,0:T(8,128)}, f32[9,16,256]{2,1,0:T(8,128)S(1)}, u32[]{:S(2)}, u32[]{:S(2)}) collective-permute-start(f32[9,16,256]{2,1,0:T(8,128)} %get-tuple-element.24), channel_id=1, source_target_pairs={{0,1},{1,0},{2,3},{3,2},{4,5},{5,4},{6,7},{7,6},{8,9},{9,8},{10,11... | collective-permute-start | bytes 442376 | tf_op jit(solution)/shard_map/ppermute | solution.py:209
  24.2 11.6 %collective-permute-start.6 = (f32[9,16,256]{2,1,0:T(8,128)}, f32[9,16,256]{2,1,0:T(8,128)S(1)}, u32[]{:S(2)}, u32[]{:S(2)}) collective-permute-start(f32[9,16,256]{2,1,0:T(8,128)} %get-tuple-element.25), channel_id=1, source_target_pairs={{0,2},{1,3},{2,0},{3,1},{4,6},{5,7},{6,4},{7,5},{8,10},{9,11},{10,... | collective-permute-start | bytes 442376 | tf_op jit(solution)/shard_map/ppermute | solution.py:209
  24.3 11.6 %collective-permute-start.7 = (f32[9,16,256]{2,1,0:T(8,128)}, f32[9,16,256]{2,1,0:T(8,128)S(1)}, u32[]{:S(2)}, u32[]{:S(2)}) collective-permute-start(f32[9,16,256]{2,1,0:T(8,128)} %get-tuple-element.26), channel_id=1, source_target_pairs={{0,16},{1,17},{2,18},{3,19},{4,20},{5,21},{6,22},{7,23},{8,24},{9,... | collective-permute-start | bytes 442376 | tf_op jit(solution)/shard_map/ppermute | solution.py:209
  25.3 10.6 %collective-permute-start.8 = (f32[9,16,256]{2,1,0:T(8,128)}, f32[9,16,256]{2,1,0:T(8,128)S(1)}, u32[]{:S(2)}, u32[]{:S(2)}) collective-permute-start(f32[9,16,256]{2,1,0:T(8,128)} %get-tuple-element.27), channel_id=1, source_target_pairs={{1,2},{2,1},{3,4},{4,3},{5,6},{6,5},{7,8},{8,7},{9,10},{10,9},{11,... | collective-permute-start | bytes 442376 | tf_op jit(solution)/shard_map/ppermute | solution.py:209
  29.4 9.8 %collective-permute-start.9 = (f32[9,16,256]{2,1,0:T(8,128)}, f32[9,16,256]{2,1,0:T(8,128)S(1)}, u32[]{:S(2)}, u32[]{:S(2)}) collective-permute-start(f32[9,16,256]{2,1,0:T(8,128)} %get-tuple-element.28), channel_id=1, source_target_pairs={{2,4},{3,5},{4,2},{5,3},{6,8},{7,9},{8,6},{9,7},{10,12},{11,13},{1... | collective-permute-start | bytes 442376 | tf_op jit(solution)/shard_map/ppermute | solution.py:209
  35.8 3.4 %copy-start.5 = (f32[9,16,256]{2,1,0:T(8,128)}, f32[9,16,256]{2,1,0:T(8,128)S(1)}, u32[]{:S(2)}) copy-start(f32[9,16,256]{2,1,0:T(8,128)S(1)} %collective-permute-done.5.refs_1_) | copy-start | bytes 442372
  35.8 3.4 %copy-start.6 = (f32[9,16,256]{2,1,0:T(8,128)}, f32[9,16,256]{2,1,0:T(8,128)S(1)}, u32[]{:S(2)}) copy-start(f32[9,16,256]{2,1,0:T(8,128)S(1)} %collective-permute-done.6.refs_2_) | copy-start | bytes 442372
  35.9 3.3 %copy-start.7 = (f32[9,16,256]{2,1,0:T(8,128)}, f32[9,16,256]{2,1,0:T(8,128)S(1)}, u32[]{:S(2)}) copy-start(f32[9,16,256]{2,1,0:T(8,128)S(1)} %collective-permute-done.7.refs_3_) | copy-start | bytes 442372
  35.9 3.3 %copy-start.8 = (f32[9,16,256]{2,1,0:T(8,128)}, f32[9,16,256]{2,1,0:T(8,128)S(1)}, u32[]{:S(2)}) copy-start(f32[9,16,256]{2,1,0:T(8,128)S(1)} %collective-permute-done.8.refs_4_) | copy-start | bytes 442372
  39.2 0.6 %copy-start.9 = (f32[9,16,256]{2,1,0:T(8,128)}, f32[9,16,256]{2,1,0:T(8,128)S(1)}, u32[]{:S(2)}) copy-start(f32[9,16,256]{2,1,0:T(8,128)S(1)} %collective-permute-done.9.refs_5_) | copy-start | bytes 442372

commit v18 on v17

--- a/solution.py
+++ b/solution.py
@@ -35,7 +35,7 @@
 
 
 LEVEL_BLOCKS = 3
-PULSE_BLOCKS = 2
+PULSE_BLOCKS = 4
 
 
 def level_block(levels):

time: 43.7 us -> 44.9 us (1.027)
  waiting for transfers between devices: 4.89 us -> 1.99 us
  Pallas kernels: 16.2 us -> 19 us
  starting transfers between devices: 18.1 us -> 19.6 us
    ppermute x10, waiting for transfers between devices: 4.89 us -> 1.99 us  [per_device(): lax.ppermute(outgoing[g], 'cells', perm=pair_list(n, partner))]
    pallas_call x2, Pallas kernels: 5.89 us -> 8.64 us  [local_part(): pl.pallas_call(local_kernel, out_shape=jax.ShapeDtypeStruct(values.shape,...]
    ppermute x10, starting transfers between devices: 18.1 us -> 19.6 us  [per_device(): lax.ppermute(outgoing[g], 'cells', perm=pair_list(n, partner))]
  transfers between devices with their start and end apart: 10 -> 10, of which waited for: 2 -> 2; matrix products, arithmetic and copies ran while one was open for 4% -> 4% of each run, Pallas kernels for 14% -> 19%
where the time goes in v18:
time: 44.9 us; the launch traced here: 44.5 us
  starting transfers between devices  19.6 us (44%)
  Pallas kernels  19 us (42%)
  waiting for transfers between devices  1.99 us (4%)
  other arithmetic  1.61 us (4%)
  local copies, waits for them, and re-layouts  1.37 us (3%)
  between operations  0.94 us (2%)
    ppermute x10, starting transfers between devices, per_device(): lax.ppermute(outgoing[g], 'cells', perm=pair_list(n, partner))  19.6 us
    pallas_call x2, Pallas kernels, local_part(): pl.pallas_call(local_kernel, out_shape=jax.ShapeDtypeStruct(values.shape,...  8.64 us
    pallas_call x2, Pallas kernels, finish(): pl.pallas_call(functools.partial(finish_kernel, groups, hslot, send), out...  7.39 us
    pallas_call x1, Pallas kernels, gather_send(): pl.pallas_call(functools.partial(select_kernel, partners, hslot), out_sha...  2.97 us
    ppermute x10, waiting for transfers between devices, per_device(): lax.ppermute(outgoing[g], 'cells', perm=pair_list(n, partner))  1.99 us
    add x1, other arithmetic, per_device(): sum((flux_weight[k][:, None, :] * ((row[k][None, :] == slots).astype(f32)...  1.47 us
    unnamed x24, local copies, waits for them, and re-layouts  1.31 us
  transfers between devices with their start and end apart: 10, of which 2 were waited for; matrix products, arithmetic and copies ran while one was open for 4% of the time, Pallas kernels for 19%

profile of v18, /device:TPU:25, one launch (start us, length us, event | category | flops | bytes accessed | tf_op | source)
XLA Modules:
  0.0 44.5 jit_solution(7477227897195773512)
XLA Ops:
  0.0 0.0 copy-start.11
  0.0 0.0 copy-start.10
  0.0 3.0 %gather_send.1 = (f32[9,16,256]{2,1,0:T(8,128)}, f32[9,16,256]{2,1,0:T(8,128)}, f32[9,16,256]{2,1,0:T(8,128)}, f32[9,16,256]{2,1,0:T(8,128)}, f32[9,16,256]{2,1,0:T(8,128)}, /*index=5*/f32[80,128]{1,0:T(8,128)}) custom-call(s32[16,32]{1,0:T(8,128)} %bitcast.38, f32[9,256,128]{2,1,0:T(8,128)} %values_ref.3), custom_call_target="tpu_custom_call" | custom-call | tf_op jit(solution)/shard_map/gather_send/pallas_call | solution.py:75
  3.0 0.7 %collective-permute-start = (f32[9,16,256]{2,1,0:T(8,128)}, f32[9,16,256]{2,1,0:T(8,128)S(1)}, u32[]{:S(2)}, u32[]{:S(2)}) collective-permute-start(f32[9,16,256]{2,1,0:T(8,128)} %get-tuple-element.17), channel_id=1, source_target_pairs={{0,1},{1,0},{2,3},{3,2},{4,5},{5,4},{6,7},{7,6},{8,9},{9,8},{10,11... | collective-permute-start | bytes 442376 | tf_op jit(solution)/shard_map/ppermute | solution.py:209
  3.7 1.2 %collective-permute-start.1 = (f32[9,16,256]{2,1,0:T(8,128)}, f32[9,16,256]{2,1,0:T(8,128)S(1)}, u32[]{:S(2)}, u32[]{:S(2)}) collective-permute-start(f32[9,16,256]{2,1,0:T(8,128)} %get-tuple-element.18), channel_id=1, source_target_pairs={{0,2},{1,3},{2,0},{3,1},{4,6},{5,7},{6,4},{7,5},{8,10},{9,11},{10,... | collective-permute-start | bytes 442376 | tf_op jit(solution)/shard_map/ppermute | solution.py:209
  4.9 0.1 collective-permute-start.2
  4.9 2.6 %collective-permute-start.3 = (f32[9,16,256]{2,1,0:T(8,128)}, f32[9,16,256]{2,1,0:T(8,128)S(1)}, u32[]{:S(2)}, u32[]{:S(2)}) collective-permute-start(f32[9,16,256]{2,1,0:T(8,128)} %get-tuple-element.20), channel_id=1, source_target_pairs={{1,2},{2,1},{3,4},{4,3},{5,6},{6,5},{7,8},{8,7},{9,10},{10,9},{11,... | collective-permute-start | bytes 442376 | tf_op jit(solution)/shard_map/ppermute | solution.py:209
  7.6 4.9 %collective-permute-start.4 = (f32[9,16,256]{2,1,0:T(8,128)}, f32[9,16,256]{2,1,0:T(8,128)S(1)}, u32[]{:S(2)}, u32[]{:S(2)}) collective-permute-start(f32[9,16,256]{2,1,0:T(8,128)} %get-tuple-element.21), channel_id=1, source_target_pairs={{2,4},{3,5},{4,2},{5,3},{6,8},{7,9},{8,6},{9,7},{10,12},{11,13},{1... | collective-permute-start | bytes 442376 | tf_op jit(solution)/shard_map/ppermute | solution.py:209
  13.2 0.0 copy-done.11
  13.2 0.0 copy-done.10
  13.5 1.5 %multiply_add_fusion.local_ref.refs_6_.refs_7_.refs_8_.refs_9_.refs_10_ = f32[9,208,128]{2,1,0:T(8,128)} fusion(f32[208,128]{1,0:T(8,128)S(1)} %get-tuple-element.45, f32[9,128]{1,0:T(8,128)S(1)} %get-tuple-element.53, f32[208,128]{1,0:T(8,128)S(1)} %get-tuple-element.46, f32[9,128]{1,0:T(8,128)S(1)} %get-tuple-element.54, ...), kind=kLoop, calls=%fused_computation | loop fusion | flops 3594240 | bytes 1847296 | tf_op jit(solution)/shard_map/add | solution.py:201
  14.9 4.3 %local_part.2.refs_0_ = f32[9,256,128]{2,1,0:T(8,128)} custom-call(f32[9,256,128]{2,1,0:T(8,128)} %values_ref.3, f32[9,208,128]{2,1,0:T(8,128)} %multiply_add_fusion.local_ref.refs_6_.refs_7_.refs_8_.refs_9_.refs_10_, f32[8,128]{1,0:T(8,128)} %mixing_ref.3), custom_call_target="tpu_custom_call" | custom-call | tf_op jit(solution)/shard_map/local_part/pallas_call | solution.py:102
  19.2 0.0 collective-permute-done.refs_1_
  19.2 0.0 copy-start
  19.2 0.0 collective-permute-done.1.refs_2_
  19.2 0.0 copy-start.1
  19.3 0.0 collective-permute-done.2.refs_3_
  19.3 0.0 copy-start.2
  19.3 0.0 collective-permute-done.3.refs_4_
  19.3 0.0 copy-start.3
  19.3 0.2 collective-permute-done.4.refs_5_
  19.5 0.0 copy-start.4
  19.5 0.4 copy-done
  19.9 0.1 copy-done.1
  19.9 0.1 copy-done.2
  20.0 0.1 copy-done.3
  20.1 0.1 copy-done.4
  20.2 4.0 %finish_send.1 = (f32[9,256,128]{2,1,0:T(8,128)}, f32[9,16,256]{2,1,0:T(8,128)}, f32[9,16,256]{2,1,0:T(8,128)}, f32[9,16,256]{2,1,0:T(8,128)}, f32[9,16,256]{2,1,0:T(8,128)}, /*index=5*/f32[9,16,256]{2,1,0:T(8,128)}) custom-call(f32[9,256,128]{2,1,0:T(8,128)} %local_part.2.refs_0_, f32[9,16,256]{2,1,0:T(8,128)} %copy-done, f32[9,16,256]{2,1,0:T(8,128)} %copy-done.1, ...), custom_call_target="tpu_custom_call" | custom-call | tf_op jit(solution)/shard_map/finish_send/pallas_call | solution.py:164
  24.2 0.0 collective-permute-start.5
  24.2 0.1 collective-permute-start.6
  24.3 2.4 %collective-permute-start.7 = (f32[9,16,256]{2,1,0:T(8,128)}, f32[9,16,256]{2,1,0:T(8,128)S(1)}, u32[]{:S(2)}, u32[]{:S(2)}) collective-permute-start(f32[9,16,256]{2,1,0:T(8,128)} %get-tuple-element.26), channel_id=1, source_target_pairs={{0,16},{1,17},{2,18},{3,19},{4,20},{5,21},{6,22},{7,23},{8,24},{9,... | collective-permute-start | bytes 442376 | tf_op jit(solution)/shard_map/ppermute | solution.py:209
  26.7 4.2 %collective-permute-start.8 = (f32[9,16,256]{2,1,0:T(8,128)}, f32[9,16,256]{2,1,0:T(8,128)S(1)}, u32[]{:S(2)}, u32[]{:S(2)}) collective-permute-start(f32[9,16,256]{2,1,0:T(8,128)} %get-tuple-element.27), channel_id=1, source_target_pairs={{1,2},{2,1},{3,4},{4,3},{5,6},{6,5},{7,8},{8,7},{9,10},{10,9},{11,... | collective-permute-start | bytes 442376 | tf_op jit(solution)/shard_map/ppermute | solution.py:209
  30.9 3.4 %collective-permute-start.9 = (f32[9,16,256]{2,1,0:T(8,128)}, f32[9,16,256]{2,1,0:T(8,128)S(1)}, u32[]{:S(2)}, u32[]{:S(2)}) collective-permute-start(f32[9,16,256]{2,1,0:T(8,128)} %get-tuple-element.28), channel_id=1, source_target_pairs={{2,4},{3,5},{4,2},{5,3},{6,8},{7,9},{8,6},{9,7},{10,12},{11,13},{1... | collective-permute-start | bytes 442376 | tf_op jit(solution)/shard_map/ppermute | solution.py:209
  34.3 4.3 %local_part.3.refs_0_ = f32[9,256,128]{2,1,0:T(8,128)} custom-call(f32[9,256,128]{2,1,0:T(8,128)} %get-tuple-element.23.values_ref, f32[9,208,128]{2,1,0:T(8,128)} %multiply_add_fusion.local_ref.refs_6_.refs_7_.refs_8_.refs_9_.refs_10_, f32[8,128]{1,0:T(8,128)} %mixing_ref.3), custom_call_target="tpu_custom_call" | custom-call | tf_op jit(solution)/shard_map/local_part/pallas_call | solution.py:102
  38.6 0.0 collective-permute-done.5.refs_1_
  38.6 0.0 collective-permute-done.6.refs_2_
  38.7 0.0 copy-start.6
  38.7 0.0 collective-permute-done.7.refs_3_
  38.7 0.0 copy-start.7
  38.7 0.0 collective-permute-done.8.refs_4_
  38.7 0.0 copy-start.8
  38.7 1.8 %collective-permute-done.9.refs_5_ = f32[9,16,256]{2,1,0:T(8,128)S(1)} collective-permute-done((f32[9,16,256]{2,1,0:T(8,128)}, f32[9,16,256]{2,1,0:T(8,128)S(1)}, u32[]{:S(2)}, u32[]{:S(2)}) %collective-permute-start.9) | collective-permute-done | bytes 147488 | tf_op jit(solution)/shard_map/ppermute | solution.py:209
  40.5 0.0 copy-done.5
  40.5 0.0 copy-done.6
  40.5 0.0 copy-done.7
  40.5 0.0 copy-done.8
  40.5 0.6 %copy-done.9 = f32[9,16,256]{2,1,0:T(8,128)} copy-done((f32[9,16,256]{2,1,0:T(8,128)}, f32[9,16,256]{2,1,0:T(8,128)S(1)}, u32[]{:S(2)}) %copy-start.9) | copy-done | bytes 147480
  41.1 3.4 %finish.1 = f32[9,256,128]{2,1,0:T(8,128)} custom-call(f32[9,256,128]{2,1,0:T(8,128)} %local_part.3.refs_0_, f32[9,16,256]{2,1,0:T(8,128)} %copy-done.5, f32[9,16,256]{2,1,0:T(8,128)} %copy-done.6, f32[9,16,256]{2,1,0:T(8,128)} %copy-done.7, f32[9,16,256]{2,1,0:T(8,128)} %copy-done.8, f32[9,16,256]{2,1,0:T(8,128)} %copy-done.9, ...), custom_call_target="tpu_custom_call" | custom-call | tf_op jit(solution)/shard_map/finish/pallas_call | solution.py:164
  (13 shorter events, 0.2 us)
Async XLA Ops:
  0.0 13.2 %copy-start.11 = (s32[8,128]{1,0:T(8,128)S(1)}, s32[8,128]{1,0:T(8,128)}, u32[]{:S(2)}) copy-start(s32[8,128]{1,0:T(8,128)} %param.11) | copy-start | bytes 12292
  0.0 13.2 %copy-start.10 = (f32[8,9,128]{2,0,1:T(8,128)S(1)}, f32[8,9,128]{2,0,1:T(8,128)}, u32[]{:S(2)}) copy-start(f32[8,9,128]{2,0,1:T(8,128)} %param.8) | copy-start | bytes 110596
  3.0 16.3 %collective-permute-start = (f32[9,16,256]{2,1,0:T(8,128)}, f32[9,16,256]{2,1,0:T(8,128)S(1)}, u32[]{:S(2)}, u32[]{:S(2)}) collective-permute-start(f32[9,16,256]{2,1,0:T(8,128)} %get-tuple-element.17), channel_id=1, source_target_pairs={{0,1},{1,0},{2,3},{3,2},{4,5},{5,4},{6,7},{7,6},{8,9},{9,8},{10,11... | collective-permute-start | bytes 442376 | tf_op jit(solution)/shard_map/ppermute | solution.py:209
  3.7 15.6 %collective-permute-start.1 = (f32[9,16,256]{2,1,0:T(8,128)}, f32[9,16,256]{2,1,0:T(8,128)S(1)}, u32[]{:S(2)}, u32[]{:S(2)}) collective-permute-start(f32[9,16,256]{2,1,0:T(8,128)} %get-tuple-element.18), channel_id=1, source_target_pairs={{0,2},{1,3},{2,0},{3,1},{4,6},{5,7},{6,4},{7,5},{8,10},{9,11},{10,... | collective-permute-start | bytes 442376 | tf_op jit(solution)/shard_map/ppermute | solution.py:209
  4.9 14.4 %collective-permute-start.2 = (f32[9,16,256]{2,1,0:T(8,128)}, f32[9,16,256]{2,1,0:T(8,128)S(1)}, u32[]{:S(2)}, u32[]{:S(2)}) collective-permute-start(f32[9,16,256]{2,1,0:T(8,128)} %get-tuple-element.19), channel_id=1, source_target_pairs={{0,16},{1,17},{2,18},{3,19},{4,20},{5,21},{6,22},{7,23},{8,24},{9,... | collective-permute-start | bytes 442376 | tf_op jit(solution)/shard_map/ppermute | solution.py:209
  4.9 14.4 %collective-permute-start.3 = (f32[9,16,256]{2,1,0:T(8,128)}, f32[9,16,256]{2,1,0:T(8,128)S(1)}, u32[]{:S(2)}, u32[]{:S(2)}) collective-permute-start(f32[9,16,256]{2,1,0:T(8,128)} %get-tuple-element.20), channel_id=1, source_target_pairs={{1,2},{2,1},{3,4},{4,3},{5,6},{6,5},{7,8},{8,7},{9,10},{10,9},{11,... | collective-permute-start | bytes 442376 | tf_op jit(solution)/shard_map/ppermute | solution.py:209
  7.6 11.9 %collective-permute-start.4 = (f32[9,16,256]{2,1,0:T(8,128)}, f32[9,16,256]{2,1,0:T(8,128)S(1)}, u32[]{:S(2)}, u32[]{:S(2)}) collective-permute-start(f32[9,16,256]{2,1,0:T(8,128)} %get-tuple-element.21), channel_id=1, source_target_pairs={{2,4},{3,5},{4,2},{5,3},{6,8},{7,9},{8,6},{9,7},{10,12},{11,13},{1... | collective-permute-start | bytes 442376 | tf_op jit(solution)/shard_map/ppermute | solution.py:209
  19.2 0.7 %copy-start = (f32[9,16,256]{2,1,0:T(8,128)}, f32[9,16,256]{2,1,0:T(8,128)S(1)}, u32[]{:S(2)}) copy-start(f32[9,16,256]{2,1,0:T(8,128)S(1)} %collective-permute-done.refs_1_) | copy-start | bytes 442372
  19.2 0.7 %copy-start.1 = (f32[9,16,256]{2,1,0:T(8,128)}, f32[9,16,256]{2,1,0:T(8,128)S(1)}, u32[]{:S(2)}) copy-start(f32[9,16,256]{2,1,0:T(8,128)S(1)} %collective-permute-done.1.refs_2_) | copy-start | bytes 442372
  19.3 0.7 %copy-start.2 = (f32[9,16,256]{2,1,0:T(8,128)}, f32[9,16,256]{2,1,0:T(8,128)S(1)}, u32[]{:S(2)}) copy-start(f32[9,16,256]{2,1,0:T(8,128)S(1)} %collective-permute-done.2.refs_3_) | copy-start | bytes 442372
  19.3 0.8 %copy-start.3 = (f32[9,16,256]{2,1,0:T(8,128)}, f32[9,16,256]{2,1,0:T(8,128)S(1)}, u32[]{:S(2)}) copy-start(f32[9,16,256]{2,1,0:T(8,128)S(1)} %collective-permute-done.3.refs_4_) | copy-start | bytes 442372
  19.5 0.7 %copy-start.4 = (f32[9,16,256]{2,1,0:T(8,128)}, f32[9,16,256]{2,1,0:T(8,128)S(1)}, u32[]{:S(2)}) copy-start(f32[9,16,256]{2,1,0:T(8,128)S(1)} %collective-permute-done.4.refs_5_) | copy-start | bytes 442372
  24.2 14.4 %collective-permute-start.5 = (f32[9,16,256]{2,1,0:T(8,128)}, f32[9,16,256]{2,1,0:T(8,128)S(1)}, u32[]{:S(2)}, u32[]{:S(2)}) collective-permute-start(f32[9,16,256]{2,1,0:T(8,128)} %get-tuple-element.24), channel_id=1, source_target_pairs={{0,1},{1,0},{2,3},{3,2},{4,5},{5,4},{6,7},{7,6},{8,9},{9,8},{10,11... | collective-permute-start | bytes 442376 | tf_op jit(solution)/shard_map/ppermute | solution.py:209
  24.2 14.4 %collective-permute-start.6 = (f32[9,16,256]{2,1,0:T(8,128)}, f32[9,16,256]{2,1,0:T(8,128)S(1)}, u32[]{:S(2)}, u32[]{:S(2)}) collective-permute-start(f32[9,16,256]{2,1,0:T(8,128)} %get-tuple-element.25), channel_id=1, source_target_pairs={{0,2},{1,3},{2,0},{3,1},{4,6},{5,7},{6,4},{7,5},{8,10},{9,11},{10,... | collective-permute-start | bytes 442376 | tf_op jit(solution)/shard_map/ppermute | solution.py:209
  24.3 14.4 %collective-permute-start.7 = (f32[9,16,256]{2,1,0:T(8,128)}, f32[9,16,256]{2,1,0:T(8,128)S(1)}, u32[]{:S(2)}, u32[]{:S(2)}) collective-permute-start(f32[9,16,256]{2,1,0:T(8,128)} %get-tuple-element.26), channel_id=1, source_target_pairs={{0,16},{1,17},{2,18},{3,19},{4,20},{5,21},{6,22},{7,23},{8,24},{9,... | collective-permute-start | bytes 442376 | tf_op jit(solution)/shard_map/ppermute | solution.py:209
  26.7 12.0 %collective-permute-start.8 = (f32[9,16,256]{2,1,0:T(8,128)}, f32[9,16,256]{2,1,0:T(8,128)S(1)}, u32[]{:S(2)}, u32[]{:S(2)}) collective-permute-start(f32[9,16,256]{2,1,0:T(8,128)} %get-tuple-element.27), channel_id=1, source_target_pairs={{1,2},{2,1},{3,4},{4,3},{5,6},{6,5},{7,8},{8,7},{9,10},{10,9},{11,... | collective-permute-start | bytes 442376 | tf_op jit(solution)/shard_map/ppermute | solution.py:209
  30.9 9.6 %collective-permute-start.9 = (f32[9,16,256]{2,1,0:T(8,128)}, f32[9,16,256]{2,1,0:T(8,128)S(1)}, u32[]{:S(2)}, u32[]{:S(2)}) collective-permute-start(f32[9,16,256]{2,1,0:T(8,128)} %get-tuple-element.28), channel_id=1, source_target_pairs={{2,4},{3,5},{4,2},{5,3},{6,8},{7,9},{8,6},{9,7},{10,12},{11,13},{1... | collective-permute-start | bytes 442376 | tf_op jit(solution)/shard_map/ppermute | solution.py:209
  38.6 1.8 %copy-start.5 = (f32[9,16,256]{2,1,0:T(8,128)}, f32[9,16,256]{2,1,0:T(8,128)S(1)}, u32[]{:S(2)}) copy-start(f32[9,16,256]{2,1,0:T(8,128)S(1)} %collective-permute-done.5.refs_1_) | copy-start | bytes 442372
  38.7 1.8 %copy-start.6 = (f32[9,16,256]{2,1,0:T(8,128)}, f32[9,16,256]{2,1,0:T(8,128)S(1)}, u32[]{:S(2)}) copy-start(f32[9,16,256]{2,1,0:T(8,128)S(1)} %collective-permute-done.6.refs_2_) | copy-start | bytes 442372
  38.7 1.8 %copy-start.7 = (f32[9,16,256]{2,1,0:T(8,128)}, f32[9,16,256]{2,1,0:T(8,128)S(1)}, u32[]{:S(2)}) copy-start(f32[9,16,256]{2,1,0:T(8,128)S(1)} %collective-permute-done.7.refs_3_) | copy-start | bytes 442372
  38.7 1.8 %copy-start.8 = (f32[9,16,256]{2,1,0:T(8,128)}, f32[9,16,256]{2,1,0:T(8,128)S(1)}, u32[]{:S(2)}) copy-start(f32[9,16,256]{2,1,0:T(8,128)S(1)} %collective-permute-done.8.refs_4_) | copy-start | bytes 442372
  40.5 0.6 %copy-start.9 = (f32[9,16,256]{2,1,0:T(8,128)}, f32[9,16,256]{2,1,0:T(8,128)S(1)}, u32[]{:S(2)}) copy-start(f32[9,16,256]{2,1,0:T(8,128)S(1)} %collective-permute-done.9.refs_5_) | copy-start | bytes 442372

commit v19 on v18

--- a/solution.py
+++ b/solution.py
@@ -35,7 +35,7 @@
 
 
 LEVEL_BLOCKS = 3
-PULSE_BLOCKS = 4
+PULSE_BLOCKS = 1
 
 
 def level_block(levels):

time: 44.9 us -> 43.7 us (0.973)
  waiting for transfers between devices: 1.99 us -> 4.31 us
  Pallas kernels: 19 us -> 16.7 us
  starting transfers between devices: 19.6 us -> 18.4 us
    ppermute x10, waiting for transfers between devices: 1.99 us -> 4.31 us  [per_device(): lax.ppermute(outgoing[g], 'cells', perm=pair_list(n, partner))]
    pallas_call x2, Pallas kernels: 8.64 us -> 6.32 us  [local_part(): pl.pallas_call(local_kernel, out_shape=jax.ShapeDtypeStruct(values.shape,...]
    ppermute x10, starting transfers between devices: 19.6 us -> 18.4 us  [per_device(): lax.ppermute(outgoing[g], 'cells', perm=pair_list(n, partner))]
  transfers between devices with their start and end apart: 10 -> 10, of which waited for: 2 -> 2; matrix products, arithmetic and copies ran while one was open for 4% -> 4% of each run, Pallas kernels for 19% -> 15%
where the time goes in v19:
time: 43.7 us; the launch traced here: 43.3 us
  starting transfers between devices  18.4 us (42%)
  Pallas kernels  16.7 us (38%)
  waiting for transfers between devices  4.31 us (10%)
  other arithmetic  1.61 us (4%)
  local copies, waits for them, and re-layouts  1.36 us (3%)
  between operations  0.95 us (2%)
    ppermute x10, starting transfers between devices, per_device(): lax.ppermute(outgoing[g], 'cells', perm=pair_list(n, partner))  18.4 us
    pallas_call x2, Pallas kernels, finish(): pl.pallas_call(functools.partial(finish_kernel, groups, hslot, send), out...  7.39 us
    pallas_call x2, Pallas kernels, local_part(): pl.pallas_call(local_kernel, out_shape=jax.ShapeDtypeStruct(values.shape,...  6.32 us
    ppermute x10, waiting for transfers between devices, per_device(): lax.ppermute(outgoing[g], 'cells', perm=pair_list(n, partner))  4.31 us
    pallas_call x1, Pallas kernels, gather_send(): pl.pallas_call(functools.partial(select_kernel, partners, hslot), out_sha...  2.97 us
    add x1, other arithmetic, per_device(): sum((flux_weight[k][:, None, :] * ((row[k][None, :] == slots).astype(f32)...  1.47 us
    unnamed x24, local copies, waits for them, and re-layouts  1.3 us
  transfers between devices with their start and end apart: 10, of which 2 were waited for; matrix products, arithmetic and copies ran while one was open for 4% of the time, Pallas kernels for 15%

profile of v19, /device:TPU:25, one launch (start us, length us, event | category | flops | bytes accessed | tf_op | source)
XLA Modules:
  0.0 43.3 jit_solution(1500100453985259441)
XLA Ops:
  0.0 0.0 copy-start.11
  0.0 0.0 copy-start.10
  0.0 3.0 %gather_send.1 = (f32[9,16,256]{2,1,0:T(8,128)}, f32[9,16,256]{2,1,0:T(8,128)}, f32[9,16,256]{2,1,0:T(8,128)}, f32[9,16,256]{2,1,0:T(8,128)}, f32[9,16,256]{2,1,0:T(8,128)}, /*index=5*/f32[80,128]{1,0:T(8,128)}) custom-call(s32[16,32]{1,0:T(8,128)} %bitcast.38, f32[9,256,128]{2,1,0:T(8,128)} %values_ref.3), custom_call_target="tpu_custom_call" | custom-call | tf_op jit(solution)/shard_map/gather_send/pallas_call | solution.py:75
  3.0 0.7 %collective-permute-start = (f32[9,16,256]{2,1,0:T(8,128)}, f32[9,16,256]{2,1,0:T(8,128)S(1)}, u32[]{:S(2)}, u32[]{:S(2)}) collective-permute-start(f32[9,16,256]{2,1,0:T(8,128)} %get-tuple-element.17), channel_id=1, source_target_pairs={{0,1},{1,0},{2,3},{3,2},{4,5},{5,4},{6,7},{7,6},{8,9},{9,8},{10,11... | collective-permute-start | bytes 442376 | tf_op jit(solution)/shard_map/ppermute | solution.py:209
  3.7 1.2 %collective-permute-start.1 = (f32[9,16,256]{2,1,0:T(8,128)}, f32[9,16,256]{2,1,0:T(8,128)S(1)}, u32[]{:S(2)}, u32[]{:S(2)}) collective-permute-start(f32[9,16,256]{2,1,0:T(8,128)} %get-tuple-element.18), channel_id=1, source_target_pairs={{0,2},{1,3},{2,0},{3,1},{4,6},{5,7},{6,4},{7,5},{8,10},{9,11},{10,... | collective-permute-start | bytes 442376 | tf_op jit(solution)/shard_map/ppermute | solution.py:209
  4.9 0.1 collective-permute-start.2
  4.9 2.6 %collective-permute-start.3 = (f32[9,16,256]{2,1,0:T(8,128)}, f32[9,16,256]{2,1,0:T(8,128)S(1)}, u32[]{:S(2)}, u32[]{:S(2)}) collective-permute-start(f32[9,16,256]{2,1,0:T(8,128)} %get-tuple-element.20), channel_id=1, source_target_pairs={{1,2},{2,1},{3,4},{4,3},{5,6},{6,5},{7,8},{8,7},{9,10},{10,9},{11,... | collective-permute-start | bytes 442376 | tf_op jit(solution)/shard_map/ppermute | solution.py:209
  7.6 4.9 %collective-permute-start.4 = (f32[9,16,256]{2,1,0:T(8,128)}, f32[9,16,256]{2,1,0:T(8,128)S(1)}, u32[]{:S(2)}, u32[]{:S(2)}) collective-permute-start(f32[9,16,256]{2,1,0:T(8,128)} %get-tuple-element.21), channel_id=1, source_target_pairs={{2,4},{3,5},{4,2},{5,3},{6,8},{7,9},{8,6},{9,7},{10,12},{11,13},{1... | collective-permute-start | bytes 442376 | tf_op jit(solution)/shard_map/ppermute | solution.py:209
  13.2 0.0 copy-done.11
  13.2 0.0 copy-done.10
  13.5 1.5 %multiply_add_fusion.local_ref.refs_6_.refs_7_.refs_8_.refs_9_.refs_10_ = f32[9,208,128]{2,1,0:T(8,128)} fusion(f32[208,128]{1,0:T(8,128)S(1)} %get-tuple-element.45, f32[9,128]{1,0:T(8,128)S(1)} %get-tuple-element.53, f32[208,128]{1,0:T(8,128)S(1)} %get-tuple-element.46, f32[9,128]{1,0:T(8,128)S(1)} %get-tuple-element.54, ...), kind=kLoop, calls=%fused_computation | loop fusion | flops 3594240 | bytes 1847296 | tf_op jit(solution)/shard_map/add | solution.py:201
  14.9 3.2 %local_part.2.refs_0_ = f32[9,256,128]{2,1,0:T(8,128)} custom-call(f32[9,256,128]{2,1,0:T(8,128)} %values_ref.3, f32[9,208,128]{2,1,0:T(8,128)} %multiply_add_fusion.local_ref.refs_6_.refs_7_.refs_8_.refs_9_.refs_10_, f32[8,128]{1,0:T(8,128)} %mixing_ref.3), custom_call_target="tpu_custom_call" | custom-call | tf_op jit(solution)/shard_map/local_part/pallas_call | solution.py:102
  18.1 0.0 collective-permute-done.refs_1_
  18.1 0.0 copy-start
  18.1 0.0 collective-permute-done.1.refs_2_
  18.1 0.0 copy-start.1
  18.1 0.0 collective-permute-done.2.refs_3_
  18.1 0.0 copy-start.2
  18.1 0.0 collective-permute-done.3.refs_4_
  18.1 0.0 copy-start.3
  18.1 1.4 %collective-permute-done.4.refs_5_ = f32[9,16,256]{2,1,0:T(8,128)S(1)} collective-permute-done((f32[9,16,256]{2,1,0:T(8,128)}, f32[9,16,256]{2,1,0:T(8,128)S(1)}, u32[]{:S(2)}, u32[]{:S(2)}) %collective-permute-start.4) | collective-permute-done | bytes 147488 | tf_op jit(solution)/shard_map/ppermute | solution.py:209
  19.5 0.0 copy-start.4
  19.5 0.0 copy-done
  19.5 0.0 copy-done.1
  19.5 0.0 copy-done.2
  19.5 0.0 copy-done.3
  19.5 0.6 %copy-done.4 = f32[9,16,256]{2,1,0:T(8,128)} copy-done((f32[9,16,256]{2,1,0:T(8,128)}, f32[9,16,256]{2,1,0:T(8,128)S(1)}, u32[]{:S(2)}) %copy-start.4) | copy-done | bytes 147480
  20.2 4.0 %finish_send.1 = (f32[9,256,128]{2,1,0:T(8,128)}, f32[9,16,256]{2,1,0:T(8,128)}, f32[9,16,256]{2,1,0:T(8,128)}, f32[9,16,256]{2,1,0:T(8,128)}, f32[9,16,256]{2,1,0:T(8,128)}, /*index=5*/f32[9,16,256]{2,1,0:T(8,128)}) custom-call(f32[9,256,128]{2,1,0:T(8,128)} %local_part.2.refs_0_, f32[9,16,256]{2,1,0:T(8,128)} %copy-done, f32[9,16,256]{2,1,0:T(8,128)} %copy-done.1, ...), custom_call_target="tpu_custom_call" | custom-call | tf_op jit(solution)/shard_map/finish_send/pallas_call | solution.py:164
  24.2 0.0 collective-permute-start.5
  24.2 0.1 collective-permute-start.6
  24.3 1.3 %collective-permute-start.7 = (f32[9,16,256]{2,1,0:T(8,128)}, f32[9,16,256]{2,1,0:T(8,128)S(1)}, u32[]{:S(2)}, u32[]{:S(2)}) collective-permute-start(f32[9,16,256]{2,1,0:T(8,128)} %get-tuple-element.26), channel_id=1, source_target_pairs={{0,16},{1,17},{2,18},{3,19},{4,20},{5,21},{6,22},{7,23},{8,24},{9,... | collective-permute-start | bytes 442376 | tf_op jit(solution)/shard_map/ppermute | solution.py:209
  25.5 4.2 %collective-permute-start.8 = (f32[9,16,256]{2,1,0:T(8,128)}, f32[9,16,256]{2,1,0:T(8,128)S(1)}, u32[]{:S(2)}, u32[]{:S(2)}) collective-permute-start(f32[9,16,256]{2,1,0:T(8,128)} %get-tuple-element.27), channel_id=1, source_target_pairs={{1,2},{2,1},{3,4},{4,3},{5,6},{6,5},{7,8},{8,7},{9,10},{10,9},{11,... | collective-permute-start | bytes 442376 | tf_op jit(solution)/shard_map/ppermute | solution.py:209
  29.7 3.4 %collective-permute-start.9 = (f32[9,16,256]{2,1,0:T(8,128)}, f32[9,16,256]{2,1,0:T(8,128)S(1)}, u32[]{:S(2)}, u32[]{:S(2)}) collective-permute-start(f32[9,16,256]{2,1,0:T(8,128)} %get-tuple-element.28), channel_id=1, source_target_pairs={{2,4},{3,5},{4,2},{5,3},{6,8},{7,9},{8,6},{9,7},{10,12},{11,13},{1... | collective-permute-start | bytes 442376 | tf_op jit(solution)/shard_map/ppermute | solution.py:209
  33.2 3.2 %local_part.3.refs_0_ = f32[9,256,128]{2,1,0:T(8,128)} custom-call(f32[9,256,128]{2,1,0:T(8,128)} %get-tuple-element.23.values_ref, f32[9,208,128]{2,1,0:T(8,128)} %multiply_add_fusion.local_ref.refs_6_.refs_7_.refs_8_.refs_9_.refs_10_, f32[8,128]{1,0:T(8,128)} %mixing_ref.3), custom_call_target="tpu_custom_call" | custom-call | tf_op jit(solution)/shard_map/local_part/pallas_call | solution.py:102
  36.3 0.0 collective-permute-done.5.refs_1_
  36.3 0.0 collective-permute-done.6.refs_2_
  36.3 0.0 copy-start.6
  36.3 0.0 collective-permute-done.7.refs_3_
  36.4 0.0 copy-start.7
  36.4 0.0 collective-permute-done.8.refs_4_
  36.4 0.0 copy-start.8
  36.4 2.9 %collective-permute-done.9.refs_5_ = f32[9,16,256]{2,1,0:T(8,128)S(1)} collective-permute-done((f32[9,16,256]{2,1,0:T(8,128)}, f32[9,16,256]{2,1,0:T(8,128)S(1)}, u32[]{:S(2)}, u32[]{:S(2)}) %collective-permute-start.9) | collective-permute-done | bytes 147488 | tf_op jit(solution)/shard_map/ppermute | solution.py:209
  39.3 0.0 copy-done.5
  39.3 0.0 copy-done.6
  39.3 0.0 copy-done.7
  39.3 0.0 copy-done.8
  39.3 0.6 %copy-done.9 = f32[9,16,256]{2,1,0:T(8,128)} copy-done((f32[9,16,256]{2,1,0:T(8,128)}, f32[9,16,256]{2,1,0:T(8,128)S(1)}, u32[]{:S(2)}) %copy-start.9) | copy-done | bytes 147480
  40.0 3.4 %finish.1 = f32[9,256,128]{2,1,0:T(8,128)} custom-call(f32[9,256,128]{2,1,0:T(8,128)} %local_part.3.refs_0_, f32[9,16,256]{2,1,0:T(8,128)} %copy-done.5, f32[9,16,256]{2,1,0:T(8,128)} %copy-done.6, f32[9,16,256]{2,1,0:T(8,128)} %copy-done.7, f32[9,16,256]{2,1,0:T(8,128)} %copy-done.8, f32[9,16,256]{2,1,0:T(8,128)} %copy-done.9, ...), custom_call_target="tpu_custom_call" | custom-call | tf_op jit(solution)/shard_map/finish/pallas_call | solution.py:164
  (13 shorter events, 0.2 us)
Async XLA Ops:
  0.0 13.2 %copy-start.11 = (s32[8,128]{1,0:T(8,128)S(1)}, s32[8,128]{1,0:T(8,128)}, u32[]{:S(2)}) copy-start(s32[8,128]{1,0:T(8,128)} %param.11) | copy-start | bytes 12292
  0.0 13.2 %copy-start.10 = (f32[8,9,128]{2,0,1:T(8,128)S(1)}, f32[8,9,128]{2,0,1:T(8,128)}, u32[]{:S(2)}) copy-start(f32[8,9,128]{2,0,1:T(8,128)} %param.8) | copy-start | bytes 110596
  3.0 15.1 %collective-permute-start = (f32[9,16,256]{2,1,0:T(8,128)}, f32[9,16,256]{2,1,0:T(8,128)S(1)}, u32[]{:S(2)}, u32[]{:S(2)}) collective-permute-start(f32[9,16,256]{2,1,0:T(8,128)} %get-tuple-element.17), channel_id=1, source_target_pairs={{0,1},{1,0},{2,3},{3,2},{4,5},{5,4},{6,7},{7,6},{8,9},{9,8},{10,11... | collective-permute-start | bytes 442376 | tf_op jit(solution)/shard_map/ppermute | solution.py:209
  3.7 14.4 %collective-permute-start.1 = (f32[9,16,256]{2,1,0:T(8,128)}, f32[9,16,256]{2,1,0:T(8,128)S(1)}, u32[]{:S(2)}, u32[]{:S(2)}) collective-permute-start(f32[9,16,256]{2,1,0:T(8,128)} %get-tuple-element.18), channel_id=1, source_target_pairs={{0,2},{1,3},{2,0},{3,1},{4,6},{5,7},{6,4},{7,5},{8,10},{9,11},{10,... | collective-permute-start | bytes 442376 | tf_op jit(solution)/shard_map/ppermute | solution.py:209
  4.9 13.2 %collective-permute-start.2 = (f32[9,16,256]{2,1,0:T(8,128)}, f32[9,16,256]{2,1,0:T(8,128)S(1)}, u32[]{:S(2)}, u32[]{:S(2)}) collective-permute-start(f32[9,16,256]{2,1,0:T(8,128)} %get-tuple-element.19), channel_id=1, source_target_pairs={{0,16},{1,17},{2,18},{3,19},{4,20},{5,21},{6,22},{7,23},{8,24},{9,... | collective-permute-start | bytes 442376 | tf_op jit(solution)/shard_map/ppermute | solution.py:209
  4.9 13.2 %collective-permute-start.3 = (f32[9,16,256]{2,1,0:T(8,128)}, f32[9,16,256]{2,1,0:T(8,128)S(1)}, u32[]{:S(2)}, u32[]{:S(2)}) collective-permute-start(f32[9,16,256]{2,1,0:T(8,128)} %get-tuple-element.20), channel_id=1, source_target_pairs={{1,2},{2,1},{3,4},{4,3},{5,6},{6,5},{7,8},{8,7},{9,10},{10,9},{11,... | collective-permute-start | bytes 442376 | tf_op jit(solution)/shard_map/ppermute | solution.py:209
  7.6 11.9 %collective-permute-start.4 = (f32[9,16,256]{2,1,0:T(8,128)}, f32[9,16,256]{2,1,0:T(8,128)S(1)}, u32[]{:S(2)}, u32[]{:S(2)}) collective-permute-start(f32[9,16,256]{2,1,0:T(8,128)} %get-tuple-element.21), channel_id=1, source_target_pairs={{2,4},{3,5},{4,2},{5,3},{6,8},{7,9},{8,6},{9,7},{10,12},{11,13},{1... | collective-permute-start | bytes 442376 | tf_op jit(solution)/shard_map/ppermute | solution.py:209
  18.1 1.4 %copy-start = (f32[9,16,256]{2,1,0:T(8,128)}, f32[9,16,256]{2,1,0:T(8,128)S(1)}, u32[]{:S(2)}) copy-start(f32[9,16,256]{2,1,0:T(8,128)S(1)} %collective-permute-done.refs_1_) | copy-start | bytes 442372
  18.1 1.4 %copy-start.1 = (f32[9,16,256]{2,1,0:T(8,128)}, f32[9,16,256]{2,1,0:T(8,128)S(1)}, u32[]{:S(2)}) copy-start(f32[9,16,256]{2,1,0:T(8,128)S(1)} %collective-permute-done.1.refs_2_) | copy-start | bytes 442372
  18.1 1.4 %copy-start.2 = (f32[9,16,256]{2,1,0:T(8,128)}, f32[9,16,256]{2,1,0:T(8,128)S(1)}, u32[]{:S(2)}) copy-start(f32[9,16,256]{2,1,0:T(8,128)S(1)} %collective-permute-done.2.refs_3_) | copy-start | bytes 442372
  18.1 1.4 %copy-start.3 = (f32[9,16,256]{2,1,0:T(8,128)}, f32[9,16,256]{2,1,0:T(8,128)S(1)}, u32[]{:S(2)}) copy-start(f32[9,16,256]{2,1,0:T(8,128)S(1)} %collective-permute-done.3.refs_4_) | copy-start | bytes 442372
  19.5 0.7 %copy-start.4 = (f32[9,16,256]{2,1,0:T(8,128)}, f32[9,16,256]{2,1,0:T(8,128)S(1)}, u32[]{:S(2)}) copy-start(f32[9,16,256]{2,1,0:T(8,128)S(1)} %collective-permute-done.4.refs_5_) | copy-start | bytes 442372
  24.2 12.1 %collective-permute-start.5 = (f32[9,16,256]{2,1,0:T(8,128)}, f32[9,16,256]{2,1,0:T(8,128)S(1)}, u32[]{:S(2)}, u32[]{:S(2)}) collective-permute-start(f32[9,16,256]{2,1,0:T(8,128)} %get-tuple-element.24), channel_id=1, source_target_pairs={{0,1},{1,0},{2,3},{3,2},{4,5},{5,4},{6,7},{7,6},{8,9},{9,8},{10,11... | collective-permute-start | bytes 442376 | tf_op jit(solution)/shard_map/ppermute | solution.py:209
  24.2 12.1 %collective-permute-start.6 = (f32[9,16,256]{2,1,0:T(8,128)}, f32[9,16,256]{2,1,0:T(8,128)S(1)}, u32[]{:S(2)}, u32[]{:S(2)}) collective-permute-start(f32[9,16,256]{2,1,0:T(8,128)} %get-tuple-element.25), channel_id=1, source_target_pairs={{0,2},{1,3},{2,0},{3,1},{4,6},{5,7},{6,4},{7,5},{8,10},{9,11},{10,... | collective-permute-start | bytes 442376 | tf_op jit(solution)/shard_map/ppermute | solution.py:209
  24.3 12.1 %collective-permute-start.7 = (f32[9,16,256]{2,1,0:T(8,128)}, f32[9,16,256]{2,1,0:T(8,128)S(1)}, u32[]{:S(2)}, u32[]{:S(2)}) collective-permute-start(f32[9,16,256]{2,1,0:T(8,128)} %get-tuple-element.26), channel_id=1, source_target_pairs={{0,16},{1,17},{2,18},{3,19},{4,20},{5,21},{6,22},{7,23},{8,24},{9,... | collective-permute-start | bytes 442376 | tf_op jit(solution)/shard_map/ppermute | solution.py:209
  25.5 10.8 %collective-permute-start.8 = (f32[9,16,256]{2,1,0:T(8,128)}, f32[9,16,256]{2,1,0:T(8,128)S(1)}, u32[]{:S(2)}, u32[]{:S(2)}) collective-permute-start(f32[9,16,256]{2,1,0:T(8,128)} %get-tuple-element.27), channel_id=1, source_target_pairs={{1,2},{2,1},{3,4},{4,3},{5,6},{6,5},{7,8},{8,7},{9,10},{10,9},{11,... | collective-permute-start | bytes 442376 | tf_op jit(solution)/shard_map/ppermute | solution.py:209
  29.7 9.6 %collective-permute-start.9 = (f32[9,16,256]{2,1,0:T(8,128)}, f32[9,16,256]{2,1,0:T(8,128)S(1)}, u32[]{:S(2)}, u32[]{:S(2)}) collective-permute-start(f32[9,16,256]{2,1,0:T(8,128)} %get-tuple-element.28), channel_id=1, source_target_pairs={{2,4},{3,5},{4,2},{5,3},{6,8},{7,9},{8,6},{9,7},{10,12},{11,13},{1... | collective-permute-start | bytes 442376 | tf_op jit(solution)/shard_map/ppermute | solution.py:209
  36.3 3.0 %copy-start.5 = (f32[9,16,256]{2,1,0:T(8,128)}, f32[9,16,256]{2,1,0:T(8,128)S(1)}, u32[]{:S(2)}) copy-start(f32[9,16,256]{2,1,0:T(8,128)S(1)} %collective-permute-done.5.refs_1_) | copy-start | bytes 442372
  36.3 3.0 %copy-start.6 = (f32[9,16,256]{2,1,0:T(8,128)}, f32[9,16,256]{2,1,0:T(8,128)S(1)}, u32[]{:S(2)}) copy-start(f32[9,16,256]{2,1,0:T(8,128)S(1)} %collective-permute-done.6.refs_2_) | copy-start | bytes 442372
  36.4 3.0 %copy-start.7 = (f32[9,16,256]{2,1,0:T(8,128)}, f32[9,16,256]{2,1,0:T(8,128)S(1)}, u32[]{:S(2)}) copy-start(f32[9,16,256]{2,1,0:T(8,128)S(1)} %collective-permute-done.7.refs_3_) | copy-start | bytes 442372
  36.4 3.0 %copy-start.8 = (f32[9,16,256]{2,1,0:T(8,128)}, f32[9,16,256]{2,1,0:T(8,128)S(1)}, u32[]{:S(2)}) copy-start(f32[9,16,256]{2,1,0:T(8,128)S(1)} %collective-permute-done.8.refs_4_) | copy-start | bytes 442372
  39.3 0.6 %copy-start.9 = (f32[9,16,256]{2,1,0:T(8,128)}, f32[9,16,256]{2,1,0:T(8,128)S(1)}, u32[]{:S(2)}) copy-start(f32[9,16,256]{2,1,0:T(8,128)S(1)} %collective-permute-done.9.refs_5_) | copy-start | bytes 442372
